TPU v7x, 32 devices: a whole 2x2x4 slice. The times are simulated.
32 devices in a mesh: strip: 8 (over z, core), slide: 4 (over y, x).
Axes of the slice: x: 2, y: 2, z: 4, core: 2. Of those that a mesh axis runs over, the one named last changes fastest.
Arguments:
- images: bfloat16 [4, 96, 48, 128], P('slide', None, 'strip'), may hold values from -6 to 6
- cotangent: bfloat16 [4, 96, 48, 128], P('slide', None, 'strip'), may hold values from -16 to 16
- conv_weight: float32 [96, 7, 7], replicated, may hold values from -0.875 to 0.875
- conv_bias: float32 [96], replicated, may hold values from -3 to 3
- norm_gain: float32 [96], replicated, may hold values from 0.5 to 1.5
- norm_bias: float32 [96], replicated, may hold values from -3 to 3
- up_weight: bfloat16 [96, 384], replicated, may hold values from -0.625 to 0.625
- up_bias: float32 [384], replicated, may hold values from -3 to 3
- down_weight: bfloat16 [384, 96], replicated, may hold values from -0.3125 to 0.3125
- down_bias: float32 [96], replicated, may hold values from -3 to 3
- layer_scale: float32 [96], replicated, may hold values from 0.5 to 1.5
Outputs:
- image_grad: bfloat16 [4, 96, 48, 128], P('slide', None, 'strip')
- conv_weight_grad: float32 [96, 7, 7], replicated
- conv_bias_grad: float32 [96], replicated
- norm_gain_grad: float32 [96], replicated
- norm_bias_grad: float32 [96], replicated
- up_weight_grad: float32 [96, 384], replicated
- up_bias_grad: float32 [384], replicated
- down_weight_grad: float32 [384, 96], replicated
- down_bias_grad: float32 [96], replicated
- layer_scale_grad: float32 [96], replicated
All inputs are finite; a program needn't handle non-finite values.
Results may differ from a plain program's by a relative error of at most 0.0065.
Values may be sent and summed in bfloat16 or wider, within the bound.
No kernel may reach another device: no remote copies, remote signals or barrier semaphores. Data moves between devices by JAX's collectives and lax.ppermute only.
A program may use at most 64 MiB of HBM per device.

v0:
```python
import math

import jax
import jax.numpy as jnp
from jax import lax
from jax.sharding import PartitionSpec as P


def with_halo(array, sides, width):
    for axis, dim in sides:
        size, length = (lax.axis_size(axis), array.shape[dim])
        up = [(i, (i + 1) % size) for i in range(size - 1)]
        down = [(j, i) for i, j in up]
        last = lax.slice_in_dim(array, length - width, length, axis=dim)
        first = lax.slice_in_dim(array, 0, width, axis=dim)
        before = lax.ppermute(last, axis, up)
        after = lax.ppermute(first, axis, down)
        array = jnp.concatenate([before, array, after], axis=dim)
    return array


def gelu_slope(value):
    return 0.5 * (1.0 + jax.scipy.special.erf(value / math.sqrt(2.0))) + value * jnp.exp(
        -0.5 * value * value
    ) / math.sqrt(2.0 * math.pi)


def on_device(
    images,
    cotangent,
    conv_weight,
    conv_bias,
    norm_gain,
    norm_bias,
    up_weight,
    up_bias,
    down_weight,
    down_bias,
    layer_scale,
):
    slides_here = images.shape[0]
    chans = images.shape[1]
    rows = images.shape[2]
    cols = images.shape[3]
    kernel = conv_weight.shape[1]
    extended = with_halo(images, (("strip", 2),), 3)
    upstream = cotangent.astype(jnp.float32)
    padded = jnp.pad(extended, ((0, 0), (0, 0), (0, 0), (3, 3)))
    conv = jnp.zeros((slides_here, chans, rows, cols), jnp.float32) + conv_bias[None, :, None, None]
    for a in range(kernel):
        for b in range(kernel):
            conv = (
                conv
                + conv_weight[:, a, b][None, :, None, None]
                * padded[:, :, a : a + rows, b : b + cols]
            )
    centre = conv - jnp.mean(conv, axis=1, keepdims=True)
    inv = lax.rsqrt(jnp.mean(centre * centre, axis=1, keepdims=True) + 1e-06)
    normed = centre * inv
    lifted = (normed * norm_gain[None, :, None, None] + norm_bias[None, :, None, None]).astype(
        jnp.bfloat16
    )
    pre = (
        jnp.einsum("scrw,cf->sfrw", lifted, up_weight, preferred_element_type=jnp.float32)
        + up_bias[None, :, None, None]
    )
    act = jax.nn.gelu(pre, approximate=False).astype(jnp.bfloat16)
    branch = (
        jnp.einsum("sfrw,fc->scrw", act, down_weight, preferred_element_type=jnp.float32)
        + down_bias[None, :, None, None]
    )
    d_branch = (layer_scale[None, :, None, None] * upstream).astype(jnp.bfloat16)
    d_act = jnp.einsum("scrw,fc->sfrw", d_branch, down_weight, preferred_element_type=jnp.float32)
    d_pre = (d_act * gelu_slope(pre)).astype(jnp.bfloat16)
    d_lifted = jnp.einsum("sfrw,cf->scrw", d_pre, up_weight, preferred_element_type=jnp.float32)
    d_normed = d_lifted * norm_gain[None, :, None, None]
    d_conv = inv * (
        d_normed
        - jnp.mean(d_normed, axis=1, keepdims=True)
        - normed * jnp.mean(d_normed * normed, axis=1, keepdims=True)
    )
    d_wide = with_halo(d_conv, (("strip", 2),), 3)
    d_padded = jnp.pad(d_wide, ((0, 0), (0, 0), (0, 0), (3, 3)))
    image_grad = cotangent.astype(jnp.float32)
    taps = []
    for a in range(kernel):
        for b in range(kernel):
            image_grad = (
                image_grad
                + conv_weight[:, a, b][None, :, None, None]
                * d_padded[:, :, 6 - a : 6 - a + rows, 6 - b : 6 - b + cols]
            )
            taps.append(jnp.sum(d_conv * padded[:, :, a : a + rows, b : b + cols], axis=(0, 2, 3)))
    kernel_grad = jnp.stack(taps, axis=1).reshape(chans, kernel, kernel)
    terms = (
        kernel_grad,
        jnp.sum(d_conv, axis=(0, 2, 3)),
        jnp.sum(d_lifted * normed, axis=(0, 2, 3)),
        jnp.sum(d_lifted, axis=(0, 2, 3)),
        jnp.einsum("scrw,sfrw->cf", lifted, d_pre, preferred_element_type=jnp.float32),
        jnp.sum(d_pre.astype(jnp.float32), axis=(0, 2, 3)),
        jnp.einsum("sfrw,scrw->fc", act, d_branch, preferred_element_type=jnp.float32),
        jnp.sum(d_branch.astype(jnp.float32), axis=(0, 2, 3)),
        jnp.sum(upstream * branch, axis=(0, 2, 3)),
    )
    totals = lax.psum(
        (terms[0], terms[1], terms[2], terms[3], terms[4], terms[5], terms[6], terms[7], terms[8]),
        ("strip", "slide"),
    )
    pixel_count = slides_here * lax.axis_size("slide") * rows * lax.axis_size("strip") * cols
    scale = 1.0 / math.sqrt(float(pixel_count))
    g = [item * scale for item in totals]
    return (image_grad.astype(jnp.bfloat16), g[0], g[1], g[2], g[3], g[4], g[5], g[6], g[7], g[8])


def solution(mesh):
    in_specs = (
        P("slide", None, "strip", None),
        P("slide", None, "strip", None),
        P(),
        P(),
        P(),
        P(),
        P(),
        P(),
        P(),
        P(),
        P(),
    )
    out_specs = (P("slide", None, "strip", None), P(), P(), P(), P(), P(), P(), P(), P(), P())
    return jax.shard_map(
        on_device, mesh=mesh, in_specs=in_specs, out_specs=out_specs, check_vma=False
    )
```

profile of v0, /device:TPU:0, one launch (start us, length us, event | category | flops | bytes accessed | tf_op | source)
XLA Modules:
  0.0 224.0 jit_solution(14255228021422578731)
XLA Ops:
  7.2 0.0 copy-start
  7.2 0.0 copy-start.1
  7.2 0.0 all-reduce.6.cloned.1.call-start
  7.3 1.0 fusion.204
  8.2 2.4 %collective-permute-start = (bf16[1,96,3,128]{3,1,2,0:T(8,128)(2,1)S(1)}, bf16[1,96,3,128]{3,1,2,0:T(8,128)(2,1)S(1)}, u32[]{:S(2)}, u32[]{:S(2)}) collective-permute-start(bf16[1,96,3,128]{3,1,2,0:T(8,128)(2,1)S(1)} %get-tuple-element.87), channel_id=1, source_target_pairs={{0,4},{4,8},{8,12},{12,16},{16,20},{20,24},{24,28},{1,5},{5,9},{9,... | collective-permute-start | bytes 221192 | tf_op jit(solution)/shard_map/ppermute | solution.py:16
  10.7 1.3 collective-permute-start.1
  12.0 1.0 slice_bitcast_fusion.48
  12.9 1.0 slice_bitcast_fusion.47
  13.9 0.9 slice_bitcast_fusion.46
  14.8 1.1 convert_reduce_fusion.1
  16.0 1.0 constant_dynamic-update-slice_fusion
  16.9 0.0 collective-permute-done.1
  17.0 0.3 fusion.25
  17.3 0.0 copy-start.3
  17.3 0.0 copy-start.5
  17.3 0.0 copy-start.8
  17.3 3.1 %fusion.201 = (f32[6,128]{1,0:T(8,128)S(1)}, f32[1,96,6,128]{3,1,2,0:T(8,128)S(1)}) fusion(bf16[1,96,12,134]{3,1,2,0:T(8,128)(2,1)S(1)} %fusion.25, f32[96]{0:T(128)S(1)} %get-tuple-element.136, f32[96]{0:T(128)S(1)} %get-tuple-element.137, f32[96]{0:T(128)S(1)} %get-tuple-element.90, bf16[1,96,9,128]{3,1,2,0:T(8,128)(2,1)S(1)} %constant_dynamic-update-slice_fusion.2, ...), kind=kLoop, calls=%fused_computation.442 | loop fusion | flops 10910976 | bytes 7542528 | tf_op jit(solution)/shard_map/reduce_sum | solution.py:57
  20.5 0.0 copy-start.2
  20.5 0.0 copy-start.4
  20.5 0.0 copy-start.7
  20.5 2.8 %fusion.9 = (bf16[384,6,128]{0,2,1:T(8,128)(2,1)S(1)}, f32[384,6,128]{0,2,1:T(8,128)S(1)}) fusion(f32[384]{0:T(512)S(1)} %copy-done.8, bf16[96,384]{1,0:T(8,128)(2,1)S(1)} %copy-done, f32[1,96,6,128]{3,1,2,0:T(8,128)S(1)} %get-tuple-element.82, f32[96]{0:T(128)S(1)} %copy-done.5, f32[96]{0:T(128)S(1)} %copy-done.3, f32[6,128]{1,0:T(8,128)S(1)} %add_rsqrt_fusion, ...), kind=kOutput, calls=%fused_computation.15 | convolution fusion | flops 76455936 | bytes 2146560 | tf_op jit(solution)/shard_map/scrw,cf->sfrw/dot_general | solution.py:64
  23.4 0.7 convert_reduce_fusion
  24.1 0.4 fusion.183
  24.5 0.1 fusion.187
  24.7 1.2 fusion.123
  25.8 0.7 fusion.120
  26.5 1.1 fusion.102
  27.6 1.0 convolution_bitcast_fusion.2
  28.6 0.1 stack.199
  28.8 0.1 reduce_sum.586
  28.9 1.0 convolution_bitcast_fusion.1
  29.9 0.4 fusion.20
  30.3 44.4 %all-reduce.2 = (f32[96,7,7]{0,2,1:T(8,128)S(1)}, f32[96]{0:T(128)S(1)}, f32[96]{0:T(128)S(1)}, f32[96]{0:T(128)S(1)}, f32[384]{0:T(512)S(1)}, /*index=5*/f32[96]{0:T(128)S(1)}, f32[96]{0:T(128)S(1)}) all-reduce(f32[96,7,7]{0,2,1:T(8,128)S(1)} %reshape.338, ...), channel_id=1, replica_groups=mesh['strip'=8,'slide'=4] {'strip','slide'}, use_global_device_ids=true, to_apply=%region_53.54 | all-reduce | flops 5568 | bytes 44544 | tf_op jit(solution)/shard_map/psum | solution.py:106
  74.7 0.6 broadcast_multiply_fusion.2
  75.3 0.6 broadcast_multiply_fusion.6
  75.9 1.3 collective-permute-start.2
  77.2 1.3 collective-permute-start.3
  78.5 0.5 broadcast_multiply_fusion.7
  79.0 0.0 all-reduce.6.cloned.1.call-update
  79.0 0.5 broadcast_multiply_fusion.9
  79.5 0.5 broadcast_multiply_fusion.11
  80.0 129.3 %all-reduce.6.cloned.1.call-done = (f32[96,384]{1,0:T(8,128)}, f32[384,96]{0,1:T(8,128)}) async-done(((f32[96,384]{1,0:T(8,128)}, f32[384,96]{0,1:T(8,128)}), (f32[96,384]{1,0:T(8,128)}, f32[384,96]{0,1:T(8,128)})) %all-reduce.6.cloned.1.call-update) | async-done | bytes 294928 | tf_op jit(solution)/shard_map/psum | solution.py:106
  209.3 1.6 broadcast_multiply_fusion
  210.9 1.6 broadcast_multiply_fusion.1
  212.5 0.0 collective-permute-done.2
  212.5 0.0 collective-permute-done.3
  212.5 0.4 select_maximum_fusion
  212.9 4.3 %fusion.186 = bf16[1,96,6,128]{3,1,2,0:T(8,128)(2,1)} fusion(f32[1,96,12,134]{3,1,2,0:T(8,128)S(1)} %select_maximum_fusion, f32[1,96,6,128]{3,1,2,0:T(8,128)S(1)} %get-tuple-element.80, f32[1,96,3,128]{3,1,2,0:T(8,128)S(1)} %collective-permute-done.2, f32[1,96,3,128]{3,1,2,0:T(8,128)S(1)} %collective-permute-done.3, ...), kind=kLoop, calls=%fused_computation.365 | loop fusion | flops 7815168 | bytes 13289856 | tf_op jit(solution)/shard_map/convert_element_type | solution.py:113
  (22 shorter events, 0.1 us)
Async XLA Ops:
  7.2 13.3 %copy-start = (bf16[96,384]{1,0:T(8,128)(2,1)S(1)}, bf16[96,384]{1,0:T(8,128)(2,1)}, u32[]{:S(2)}) copy-start(bf16[96,384]{1,0:T(8,128)(2,1)} %param.17) | copy-start | bytes 221188
  7.2 9.8 %copy-start.1 = (bf16[1,96,6,128]{3,1,2,0:T(8,128)(2,1)S(1)}, bf16[1,96,6,128]{3,1,2,0:T(8,128)(2,1)}, u32[]{:S(2)}) copy-start(bf16[1,96,6,128]{3,1,2,0:T(8,128)(2,1)} %param.11) | copy-start | bytes 442372
  7.2 10.1 %copy-start.6 = (f32[96]{0:T(128)S(1)}, f32[96]{0:T(128)}, u32[]{:S(2)}) copy-start(f32[96]{0:T(128)} %param.14) | copy-start | bytes 1156
  7.2 202.1 %all-reduce.6.cloned.1.call-start = ((), (), s32[]{:S(2)}) async-start(), calls=%async_computation | async-start | bytes 589824 | tf_op jit(solution)/shard_map/psum | solution.py:106
  8.2 7.7 %collective-permute-start = (bf16[1,96,3,128]{3,1,2,0:T(8,128)(2,1)S(1)}, bf16[1,96,3,128]{3,1,2,0:T(8,128)(2,1)S(1)}, u32[]{:S(2)}, u32[]{:S(2)}) collective-permute-start(bf16[1,96,3,128]{3,1,2,0:T(8,128)(2,1)S(1)} %get-tuple-element.87), channel_id=1, source_target_pairs={{0,4},{4,8},{8,12},{12,16},{16,20},{20,24},{24,28},{1,5},{5,9},{9,... | collective-permute-start | bytes 221192 | tf_op jit(solution)/shard_map/ppermute | solution.py:16
  10.7 6.3 %collective-permute-start.1 = (bf16[1,96,3,128]{3,1,2,0:T(8,128)(2,1)S(1)}, bf16[1,96,3,128]{3,1,2,0:T(8,128)(2,1)S(1)}, u32[]{:S(2)}, u32[]{:S(2)}) collective-permute-start(bf16[1,96,3,128]{3,1,2,0:T(8,128)(2,1)S(1)} %get-tuple-element.88), channel_id=1, source_target_pairs={{4,0},{8,4},{12,8},{16,12},{20,16},{24,20},{28,24},{5,1},{9,5},{13... | collective-permute-start | bytes 221192 | tf_op jit(solution)/shard_map/ppermute | solution.py:17
  17.3 3.2 %copy-start.3 = (f32[96]{0:T(128)S(1)}, f32[96]{0:T(128)}, u32[]{:S(2)}) copy-start(f32[96]{0:T(128)} %param.15) | copy-start | bytes 1156
  17.3 3.2 %copy-start.5 = (f32[96]{0:T(128)S(1)}, f32[96]{0:T(128)}, u32[]{:S(2)}) copy-start(f32[96]{0:T(128)} %param.16) | copy-start | bytes 1156
  17.3 3.2 %copy-start.8 = (f32[384]{0:T(512)S(1)}, f32[384]{0:T(512)}, u32[]{:S(2)}) copy-start(f32[384]{0:T(512)} %param.18) | copy-start | bytes 4612
  20.5 2.9 %copy-start.2 = (bf16[1,96,6,128]{3,1,2,0:T(8,128)(2,1)S(1)}, bf16[1,96,6,128]{3,1,2,0:T(8,128)(2,1)}, u32[]{:S(2)}) copy-start(bf16[1,96,6,128]{3,1,2,0:T(8,128)(2,1)} %param.12) | copy-start | bytes 442372
  20.5 2.9 %copy-start.4 = (f32[96]{0:T(128)S(1)}, f32[96]{0:T(128)}, u32[]{:S(2)}) copy-start(f32[96]{0:T(128)} %param.21) | copy-start | bytes 1156
  20.5 2.9 %copy-start.7 = (bf16[384,96]{0,1:T(8,128)(2,1)S(1)}, bf16[384,96]{0,1:T(8,128)(2,1)}, u32[]{:S(2)}) copy-start(bf16[384,96]{0,1:T(8,128)(2,1)} %param.19) | copy-start | bytes 221188
  28.6 1.3 copy-start.9
  75.9 136.6 %collective-permute-start.2 = (f32[1,96,3,128]{3,1,2,0:T(8,128)S(1)}, f32[1,96,3,128]{3,1,2,0:T(8,128)S(1)}, u32[]{:S(2)}, u32[]{:S(2)}) collective-permute-start(f32[1,96,3,128]{3,1,2,0:T(8,128)S(1)} %get-tuple-element.83), channel_id=1, source_target_pairs={{0,4},{4,8},{8,12},{12,16},{16,20},{20,24},{24,28},{1,5},{5,9},{9,... | collective-permute-start | bytes 442376 | tf_op jit(solution)/shard_map/ppermute | solution.py:16
  77.2 135.3 %collective-permute-start.3 = (f32[1,96,3,128]{3,1,2,0:T(8,128)S(1)}, f32[1,96,3,128]{3,1,2,0:T(8,128)S(1)}, u32[]{:S(2)}, u32[]{:S(2)}) collective-permute-start(f32[1,96,3,128]{3,1,2,0:T(8,128)S(1)} %get-tuple-element.84), channel_id=1, source_target_pairs={{4,0},{8,4},{12,8},{16,12},{20,16},{24,20},{28,24},{5,1},{9,5},{13... | collective-permute-start | bytes 442376 | tf_op jit(solution)/shard_map/ppermute | solution.py:17
Sparse Core Ops, SparseCore 0:
  79.1 130.1 all-reduce.5
where the time goes:
time: 225 us; the launch traced here: 224 us
  waiting for transfers between devices  129 us (57%)
  blocking collectives  44.4 us (20%)
  other arithmetic  18.2 us (8%)
  between operations  14.4 us (6%)
  matrix products  6.34 us (3%)
  starting transfers between devices  6.31 us (3%)
  local copies, waits for them, and re-layouts  5.07 us (2%)
    psum x1, waiting for transfers between devices, on_device(): lax.psum((terms[0], terms[1], terms[2], terms[3], terms[4], terms[5], ter...  129 us
    psum x1, blocking collectives, on_device(): lax.psum((terms[0], terms[1], terms[2], terms[3], terms[4], terms[5], ter...  44.4 us
    mul x7, other arithmetic, on_device(): g = [item * scale for item in totals]  5.91 us
  transfers between devices with their start and end apart: 5, of which 1 were waited for; matrix products, arithmetic and copies ran while one was open for 4% of the time, Pallas kernels for 0%

commit v1 on v0

--- a/solution.py
+++ b/solution.py
@@ -18,6 +18,52 @@
         array = jnp.concatenate([before, array, after], axis=dim)
     return array
 
+
+def butterfly_steps(axes):
+    steps = []
+    for axis in axes:
+        size = lax.axis_size(axis)
+        bit = 1
+        while bit < size:
+            steps.append((axis, bit))
+            bit *= 2
+    order = {"strip": 0, "slide": 1}
+    steps.sort(key=lambda s: (0 if (s[0] == "strip" and s[1] == 1) else 1, s[1], order[s[0]]))
+    return steps
+
+
+def tree_psum(terms, axes):
+    shapes = [t.shape for t in terms]
+    sizes = [math.prod(s) for s in shapes]
+    total = sum(sizes)
+    steps = butterfly_steps(axes)
+    pieces = 2 ** len(steps)
+    rows = -(-total // (pieces * 128))
+    rows = -(-rows // 8) * 8
+    flat = jnp.concatenate([t.reshape(-1) for t in terms])
+    flat = jnp.pad(flat, (0, pieces * rows * 128 - total)).reshape(pieces, rows, 128)
+    for axis, bit in steps:
+        size = lax.axis_size(axis)
+        half = flat.shape[0] // 2
+        mine = (lax.axis_index(axis) // bit) % 2
+        keep = lax.dynamic_slice_in_dim(flat, mine * half, half, axis=0)
+        give = lax.dynamic_slice_in_dim(flat, (1 - mine) * half, half, axis=0)
+        got = lax.ppermute(give, axis, [(i, i ^ bit) for i in range(size)])
+        flat = keep + got
+    for axis, bit in reversed(steps):
+        size = lax.axis_size(axis)
+        mine = (lax.axis_index(axis) // bit) % 2
+        got = lax.ppermute(flat, axis, [(i, i ^ bit) for i in range(size)])
+        low = jnp.where(mine == 0, flat, got)
+        high = jnp.where(mine == 0, got, flat)
+        flat = jnp.concatenate([low, high], axis=0)
+    flat = flat.reshape(-1)
+    out = []
+    offset = 0
+    for shape, size in zip(shapes, sizes):
+        out.append(flat[offset : offset + size].reshape(shape))
+        offset += size
+    return out
 
 def gelu_slope(value):
     return 0.5 * (1.0 + jax.scipy.special.erf(value / math.sqrt(2.0))) + value * jnp.exp(
@@ -103,13 +149,10 @@
         jnp.sum(d_branch.astype(jnp.float32), axis=(0, 2, 3)),
         jnp.sum(upstream * branch, axis=(0, 2, 3)),
     )
-    totals = lax.psum(
-        (terms[0], terms[1], terms[2], terms[3], terms[4], terms[5], terms[6], terms[7], terms[8]),
-        ("strip", "slide"),
-    )
     pixel_count = slides_here * lax.axis_size("slide") * rows * lax.axis_size("strip") * cols
     scale = 1.0 / math.sqrt(float(pixel_count))
-    g = [item * scale for item in totals]
+    g = tree_psum(terms, ("strip", "slide"))
+    g = [item * scale for item in g]
     return (image_grad.astype(jnp.bfloat16), g[0], g[1], g[2], g[3], g[4], g[5], g[6], g[7], g[8])
 
 

time: 225 us -> 75.9 us (0.34)
  waiting for transfers between devices: 129 us -> 18.4 us
  blocking collectives: 44.4 us -> 0 us
  starting transfers between devices: 6.31 us -> 26.7 us
  between operations: 14.4 us -> 1.16 us
  local copies, waits for them, and re-layouts: 5.07 us -> 9.31 us
  other arithmetic: 18.2 us -> 14.3 us
    psum x1 -> x0, waiting for transfers between devices: 129 us -> none  [on_device(): lax.psum((terms[0], terms[1], terms[2], terms[3], terms[4], terms[5], ter...]
    psum x1 -> x0, blocking collectives: 44.4 us -> none  [on_device(): lax.psum((terms[0], terms[1], terms[2], terms[3], terms[4], terms[5], ter...]
    ppermute x0 -> x10, starting transfers between devices: none -> 20.2 us  [the longest x5 11.2 us: tree_psum(): got = lax.ppermute(give, axis, [(i, i ^ bit) for i in range(size)])]
    ppermute x0 -> x10, waiting for transfers between devices: none -> 17.7 us  [the longest x5 11.1 us: tree_psum(): got = lax.ppermute(give, axis, [(i, i ^ bit) for i in range(size)])]
    mul x7 -> x5, other arithmetic: 5.91 us -> 1.88 us  [on_device(): g = [item * scale for item in g]]
  transfers between devices with their start and end apart: 5 -> 14, of which waited for: 1 -> 9; matrix products, arithmetic and copies ran while one was open for 4% -> 13% of each run, Pallas kernels for 0% -> 0%
where the time goes in v1:
time: 75.9 us; the launch traced here: 74.9 us
  starting transfers between devices  26.7 us (35%)
  waiting for transfers between devices  18.4 us (24%)
  other arithmetic  14.3 us (19%)
  local copies, waits for them, and re-layouts  9.31 us (12%)
  matrix products  5.09 us (7%)
  between operations  1.16 us (2%)
    ppermute x5, starting transfers between devices, tree_psum(): got = lax.ppermute(give, axis, [(i, i ^ bit) for i in range(size)])  11.2 us
    ppermute x5, waiting for transfers between devices, tree_psum(): got = lax.ppermute(give, axis, [(i, i ^ bit) for i in range(size)])  11.1 us
    ppermute x5, starting transfers between devices, tree_psum(): got = lax.ppermute(flat, axis, [(i, i ^ bit) for i in range(size)])  9.03 us
    ppermute x5, waiting for transfers between devices, tree_psum(): got = lax.ppermute(flat, axis, [(i, i ^ bit) for i in range(size)])  6.6 us
    convert_element_type x1, other arithmetic, on_device(): image_grad.astype(jnp.bfloat16)  4.21 us
    ppermute x2, starting transfers between devices, with_halo(): before = lax.ppermute(last, axis, up)  3.7 us
    reduce_sum x1, other arithmetic, on_device(): centre = conv - jnp.mean(conv, axis=1, keepdims=True)  3.07 us
    reduce_sum x3, other arithmetic, on_device(): jnp.sum(d_conv * padded[:, :, a:a + rows, b:b + cols], axis=(0, 2, 3))  2.94 us
  transfers between devices with their start and end apart: 14, of which 9 were waited for; matrix products, arithmetic and copies ran while one was open for 13% of the time, Pallas kernels for 0%

profile of v1, /device:TPU:0, one launch (start us, length us, event | category | flops | bytes accessed | tf_op | source)
XLA Modules:
  0.0 74.9 jit_solution(14031437264403059998)
XLA Ops:
  0.7 1.0 %fusion.204 = (bf16[1,96,3,128]{3,1,2,0:T(8,128)(2,1)S(1)}, bf16[1,96,3,128]{3,1,2,0:T(8,128)(2,1)S(1)}) fusion(bf16[1,96,6,128]{3,1,2,0:T(8,128)(2,1)} %param.11), kind=kLoop, calls=%fused_computation.469 | loop fusion | bytes 294912 | tf_op jit(solution)/shard_map/slice | solution.py:14
  1.7 2.4 %collective-permute-start = (bf16[1,96,3,128]{3,1,2,0:T(8,128)(2,1)S(1)}, bf16[1,96,3,128]{3,1,2,0:T(8,128)(2,1)S(1)}, u32[]{:S(2)}, u32[]{:S(2)}) collective-permute-start(bf16[1,96,3,128]{3,1,2,0:T(8,128)(2,1)S(1)} %get-tuple-element.97), channel_id=1, source_target_pairs={{0,4},{4,8},{8,12},{12,16},{16,20},{20,24},{24,28},{1,5},{5,9},{9,... | collective-permute-start | bytes 221192 | tf_op jit(solution)/shard_map/ppermute | solution.py:16
  4.1 1.3 %collective-permute-start.1 = (bf16[1,96,3,128]{3,1,2,0:T(8,128)(2,1)S(1)}, bf16[1,96,3,128]{3,1,2,0:T(8,128)(2,1)S(1)}, u32[]{:S(2)}, u32[]{:S(2)}) collective-permute-start(bf16[1,96,3,128]{3,1,2,0:T(8,128)(2,1)S(1)} %get-tuple-element.98), channel_id=1, source_target_pairs={{4,0},{8,4},{12,8},{16,12},{20,16},{24,20},{28,24},{5,1},{9,5},{13... | collective-permute-start | bytes 221192 | tf_op jit(solution)/shard_map/ppermute | solution.py:17
  5.4 1.0 %slice_bitcast_fusion.48 = (f32[96]{0:T(128)S(1)}, f32[96]{0:T(128)S(1)}, f32[96]{0:T(128)S(1)}, f32[96]{0:T(128)S(1)}, f32[96]{0:T(128)S(1)}, /*index=5*/f32[96...) fusion(f32[96,7,7]{0,2,1:T(8,128)} %param.13), kind=kLoop, calls=%fused_computation.466 | loop fusion | bytes 14592 | tf_op jit(solution)/shard_map/mul | solution.py:136
  6.4 1.0 %slice_bitcast_fusion.47 = (f32[96]{0:T(128)S(1)}, f32[96]{0:T(128)S(1)}, f32[96]{0:T(128)S(1)}, f32[96]{0:T(128)S(1)}, f32[96]{0:T(128)S(1)}, /*index=5*/f32[96...) fusion(f32[96,7,7]{0,2,1:T(8,128)} %param.13), kind=kLoop, calls=%fused_computation.465 | loop fusion | bytes 14592 | tf_op jit(solution)/shard_map/mul | solution.py:100
  7.4 0.9 %slice_bitcast_fusion.46 = (f32[96]{0:T(128)S(1)}, f32[96]{0:T(128)S(1)}, f32[96]{0:T(128)S(1)}, f32[96]{0:T(128)S(1)}, f32[96]{0:T(128)S(1)}, /*index=5*/f32[96...) fusion(f32[96,7,7]{0,2,1:T(8,128)} %param.13), kind=kLoop, calls=%fused_computation.464 | loop fusion | bytes 8448 | tf_op jit(solution)/shard_map/mul | solution.py:100
  8.3 1.1 %convert_reduce_fusion.1 = f32[96]{0:T(128)S(1)} fusion(bf16[1,96,6,128]{3,1,2,0:T(8,128)(2,1)} %param.12, f32[96]{0:T(128)} %param.21), kind=kLoop, calls=%fused_computation.363 | loop fusion | flops 368544 | bytes 148224 | tf_op jit(solution)/shard_map/reduce_sum | solution.py:149
  9.4 1.0 %constant_dynamic-update-slice_fusion = (bf16[1,96,9,128]{3,1,2,0:T(8,128)(2,1)S(1)}, bf16[1,96,9,128]{3,1,2,0:T(8,128)(2,1)S(1)}) fusion(bf16[1,96,9,128]{3,1,2,0:T(8,128)(2,1)S(1)} %constant_dynamic-update-slice_fusion.1, bf16[1,96,6,128]{3,1,2,0:T(8,128)(2,1)} %param.11), kind=kLoop, calls=%fused_computation.397 | loop fusion | bytes 442368 | tf_op jit(solution)/shard_map/concatenate | solution.py:18
  10.4 0.3 fusion.25
  10.8 3.1 %fusion.201 = (f32[6,128]{1,0:T(8,128)S(1)}, f32[1,96,6,128]{3,1,2,0:T(8,128)S(1)}) fusion(bf16[1,96,12,134]{3,1,2,0:T(8,128)(2,1)S(1)} %fusion.25, f32[96]{0:T(128)S(1)} %get-tuple-element.150, f32[96]{0:T(128)S(1)} %get-tuple-element.151, f32[96]{0:T(128)S(1)} %get-tuple-element.104, bf16[1,96,9,128]{3,1,2,0:T(8,128)(2,1)S(1)} %constant_dynamic-update-slice_fusion.2, ...), kind=kLoop, calls=%fused_computation.467 | loop fusion | flops 10910976 | bytes 7542528 | tf_op jit(solution)/shard_map/reduce_sum | solution.py:103
  14.0 2.8 %fusion.9 = (bf16[384,6,128]{0,2,1:T(8,128)(2,1)S(1)}, f32[384,6,128]{0,2,1:T(8,128)S(1)}) fusion(f32[384]{0:T(512)S(1)} %copy-done.8, bf16[96,384]{1,0:T(8,128)(2,1)S(1)} %copy-done, f32[1,96,6,128]{3,1,2,0:T(8,128)S(1)} %get-tuple-element.83, f32[96]{0:T(128)S(1)} %copy-done.5, f32[96]{0:T(128)S(1)} %copy-done.3, f32[6,128]{1,0:T(8,128)S(1)} %add_rsqrt_fusion, ...), kind=kOutput, calls=%fused_computation.15 | convolution fusion | flops 76455936 | bytes 2146560 | tf_op jit(solution)/shard_map/scrw,cf->sfrw/dot_general | solution.py:110
  16.9 0.7 convert_reduce_fusion
  17.6 0.3 convolution_bitcast_fusion.2
  17.9 0.4 fusion.183
  18.4 1.2 %fusion.123 = (f32[96]{0:T(128)S(1)}, f32[96]{0:T(128)S(1)}, f32[96]{0:T(128)S(1)}, f32[96]{0:T(128)S(1)}, f32[96]{0:T(128)S(1)}, /*index=5*/f32[96]{0:T(128)S(1...) fusion(bf16[1,96,12,134]{3,1,2,0:T(8,128)(2,1)S(1)} %fusion.25,, ...), kind=kLoop, calls=%fused_computation.252 | loop fusion | flops 4495680 | bytes 3558528 | tf_op jit(solution)/shard_map/reduce_sum | solution.py:139
  19.6 0.7 fusion.120
  20.3 1.1 %fusion.102 = (f32[96]{0:T(128)S(1)}, f32[96]{0:T(128)S(1)}, f32[96]{0:T(128)S(1)}, f32[96]{0:T(128)S(1)}, f32[96]{0:T(128)S(1)}, /*index=5*/f32[96]{0:T(128)S(1...) fusion(f32[1,96,6,128]{3,1,2,0:T(8,128)S(1)} %get-tuple-element, ...), kind=kLoop, calls=%fused_computation.231 | loop fusion | flops 3979584 | bytes 2956032 | tf_op jit(solution)/shard_map/reduce_sum | solution.py:139
  21.9 0.4 convolution_bitcast_fusion.1
  22.5 0.4 fusion.20
  22.9 1.7 %concatenate.50 = f32[79296]{0:T(1024)S(1)} concatenate(f32[4704]{0:T(1024)S(1)} %reshape_reshape.3, f32[96]{0:T(128)S(1)} %get-tuple-element.70, f32[96]{0:T(128)S(1)} %get-tuple-element.62, f32[96]{0:T(128)S(1)} %reduce_sum.586, f32[36864]{0:T(1024)S(1)} %reshape.356, f32[384]{0:T(512)S(1)} %get-tuple-element.155, f32[36864]{0:T(1024)S(1)} %reshape.357, ...), dimensions={0} | concatenate | bytes 634368 | tf_op jit(solution)/shard_map/concatenate | solution.py:43
  24.7 3.4 %collective-permute-start.4 = (f32[16,24,128]{2,1,0:T(8,128)S(1)}, f32[16,24,128]{2,1,0:T(8,128)S(1)}, u32[]{:S(2)}, u32[]{:S(2)}) collective-permute-start(f32[16,24,128]{2,1,0:T(8,128)S(1)} %constant_dynamic-slice_fusion.4), channel_id=1, source_target_pairs={{0,4},{4,0},{8,12},{12,8},{16,20},{20,16},{24,28},{28,24},{1,5},{5... | collective-permute-start | bytes 589832 | tf_op jit(solution)/shard_map/ppermute | solution.py:51
  28.0 1.1 %collective-permute-done.4 = f32[16,24,128]{2,1,0:T(8,128)S(1)} collective-permute-done((f32[16,24,128]{2,1,0:T(8,128)S(1)}, f32[16,24,128]{2,1,0:T(8,128)S(1)}, u32[]{:S(2)}, u32[]{:S(2)}) %collective-permute-start.4) | collective-permute-done | bytes 196640 | tf_op jit(solution)/shard_map/ppermute | solution.py:51
  29.1 1.6 %collective-permute-start.5 = (f32[8,24,128]{2,1,0:T(8,128)S(1)}, f32[8,24,128]{2,1,0:T(8,128)S(1)}, u32[]{:S(2)}, u32[]{:S(2)}) collective-permute-start(f32[8,24,128]{2,1,0:T(8,128)S(1)} %constant_dynamic-slice_fusion.3), channel_id=1, source_target_pairs={{0,1},{1,0},{2,3},{3,2},{4,5},{5,4},{6,7},{7,6},{8,9},{9,8},{10,11... | collective-permute-start | bytes 294920 | tf_op jit(solution)/shard_map/ppermute | solution.py:51
  30.7 3.6 %collective-permute-done.5 = f32[8,24,128]{2,1,0:T(8,128)S(1)} collective-permute-done((f32[8,24,128]{2,1,0:T(8,128)S(1)}, f32[8,24,128]{2,1,0:T(8,128)S(1)}, u32[]{:S(2)}, u32[]{:S(2)}) %collective-permute-start.5) | collective-permute-done | bytes 98336 | tf_op jit(solution)/shard_map/ppermute | solution.py:51
  34.3 1.8 %collective-permute-start.6 = (f32[4,24,128]{2,1,0:T(8,128)S(1)}, f32[4,24,128]{2,1,0:T(8,128)S(1)}, u32[]{:S(2)}, u32[]{:S(2)}) collective-permute-start(f32[4,24,128]{2,1,0:T(8,128)S(1)} %constant_dynamic-slice_fusion.2), channel_id=1, source_target_pairs={{0,8},{4,12},{8,0},{12,4},{16,24},{20,28},{24,16},{28,20},{1,9},{5... | collective-permute-start | bytes 147464 | tf_op jit(solution)/shard_map/ppermute | solution.py:51
  36.1 2.3 %collective-permute-done.6 = f32[4,24,128]{2,1,0:T(8,128)S(1)} collective-permute-done((f32[4,24,128]{2,1,0:T(8,128)S(1)}, f32[4,24,128]{2,1,0:T(8,128)S(1)}, u32[]{:S(2)}, u32[]{:S(2)}) %collective-permute-start.6) | collective-permute-done | bytes 49184 | tf_op jit(solution)/shard_map/ppermute | solution.py:51
  38.5 1.6 %collective-permute-start.7 = (f32[2,24,128]{2,1,0:T(8,128)S(1)}, f32[2,24,128]{2,1,0:T(8,128)S(1)}, u32[]{:S(2)}, u32[]{:S(2)}) collective-permute-start(f32[2,24,128]{2,1,0:T(8,128)S(1)} %constant_dynamic-slice_fusion.1), channel_id=1, source_target_pairs={{0,2},{1,3},{2,0},{3,1},{4,6},{5,7},{6,4},{7,5},{8,10},{9,11},{10,... | collective-permute-start | bytes 73736 | tf_op jit(solution)/shard_map/ppermute | solution.py:51
  40.1 2.3 %collective-permute-done.7 = f32[2,24,128]{2,1,0:T(8,128)S(1)} collective-permute-done((f32[2,24,128]{2,1,0:T(8,128)S(1)}, f32[2,24,128]{2,1,0:T(8,128)S(1)}, u32[]{:S(2)}, u32[]{:S(2)}) %collective-permute-start.7) | collective-permute-done | bytes 24608 | tf_op jit(solution)/shard_map/ppermute | solution.py:51
  42.4 2.8 %collective-permute-start.8 = (f32[1,24,128]{2,1,0:T(8,128)S(1)}, f32[1,24,128]{2,1,0:T(8,128)S(1)}, u32[]{:S(2)}, u32[]{:S(2)}) collective-permute-start(f32[1,24,128]{2,1,0:T(8,128)S(1)} %constant_dynamic-slice_fusion), channel_id=1, source_target_pairs={{0,16},{4,20},{8,24},{12,28},{16,0},{20,4},{24,8},{28,12},{1,17},{... | collective-permute-start | bytes 36872 | tf_op jit(solution)/shard_map/ppermute | solution.py:51
  45.2 1.8 %collective-permute-done.8 = f32[1,24,128]{2,1,0:T(8,128)S(1)} collective-permute-done((f32[1,24,128]{2,1,0:T(8,128)S(1)}, f32[1,24,128]{2,1,0:T(8,128)S(1)}, u32[]{:S(2)}, u32[]{:S(2)}) %collective-permute-start.8) | collective-permute-done | bytes 12320 | tf_op jit(solution)/shard_map/ppermute | solution.py:51
  47.1 2.8 %collective-permute-start.9 = (f32[1,24,128]{2,1,0:T(8,128)S(1)}, f32[1,24,128]{2,1,0:T(8,128)S(1)}, u32[]{:S(2)}, u32[]{:S(2)}) collective-permute-start(f32[1,24,128]{2,1,0:T(8,128)S(1)} %dynamic-slice_add_fusion.4), channel_id=1, source_target_pairs={{0,16},{4,20},{8,24},{12,28},{16,0},{20,4},{24,8},{28,12},{1,17},{... | collective-permute-start | bytes 36872 | tf_op jit(solution)/shard_map/ppermute | solution.py:56
  49.8 1.8 %collective-permute-done.9 = f32[1,24,128]{2,1,0:T(8,128)S(1)} collective-permute-done((f32[1,24,128]{2,1,0:T(8,128)S(1)}, f32[1,24,128]{2,1,0:T(8,128)S(1)}, u32[]{:S(2)}, u32[]{:S(2)}) %collective-permute-start.9) | collective-permute-done | bytes 12320 | tf_op jit(solution)/shard_map/ppermute | solution.py:56
  51.7 1.6 %collective-permute-start.10 = (f32[2,24,128]{2,1,0:T(8,128)S(1)}, f32[2,24,128]{2,1,0:T(8,128)S(1)}, u32[]{:S(2)}, u32[]{:S(2)}) collective-permute-start(f32[2,24,128]{2,1,0:T(8,128)S(1)} %pad_maximum_fusion.6), channel_id=1, source_target_pairs={{0,2},{1,3},{2,0},{3,1},{4,6},{5,7},{6,4},{7,5},{8,10},{9,11},{10,... | collective-permute-start | bytes 73736 | tf_op jit(solution)/shard_map/ppermute | solution.py:56
  53.3 2.3 %collective-permute-done.10 = f32[2,24,128]{2,1,0:T(8,128)S(1)} collective-permute-done((f32[2,24,128]{2,1,0:T(8,128)S(1)}, f32[2,24,128]{2,1,0:T(8,128)S(1)}, u32[]{:S(2)}, u32[]{:S(2)}) %collective-permute-start.10) | collective-permute-done | bytes 24608 | tf_op jit(solution)/shard_map/ppermute | solution.py:56
  55.6 1.8 %collective-permute-start.11 = (f32[4,24,128]{2,1,0:T(8,128)S(1)}, f32[4,24,128]{2,1,0:T(8,128)S(1)}, u32[]{:S(2)}, u32[]{:S(2)}) collective-permute-start(f32[4,24,128]{2,1,0:T(8,128)S(1)} %pad_maximum_fusion.5), channel_id=1, source_target_pairs={{0,8},{4,12},{8,0},{12,4},{16,24},{20,28},{24,16},{28,20},{1,9},{5... | collective-permute-start | bytes 147464 | tf_op jit(solution)/shard_map/ppermute | solution.py:56
  57.4 1.3 %collective-permute-start.2 = (f32[1,96,3,128]{3,1,2,0:T(8,128)S(1)}, f32[1,96,3,128]{3,1,2,0:T(8,128)S(1)}, u32[]{:S(2)}, u32[]{:S(2)}) collective-permute-start(f32[1,96,3,128]{3,1,2,0:T(8,128)S(1)} %get-tuple-element.91), channel_id=1, source_target_pairs={{0,4},{4,8},{8,12},{12,16},{16,20},{20,24},{24,28},{1,5},{5,9},{9,... | collective-permute-start | bytes 442376 | tf_op jit(solution)/shard_map/ppermute | solution.py:16
  58.7 1.5 %collective-permute-start.3 = (f32[1,96,3,128]{3,1,2,0:T(8,128)S(1)}, f32[1,96,3,128]{3,1,2,0:T(8,128)S(1)}, u32[]{:S(2)}, u32[]{:S(2)}) collective-permute-start(f32[1,96,3,128]{3,1,2,0:T(8,128)S(1)} %get-tuple-element.92), channel_id=1, source_target_pairs={{4,0},{8,4},{12,8},{16,12},{20,16},{24,20},{28,24},{5,1},{9,5},{13... | collective-permute-start | bytes 442376 | tf_op jit(solution)/shard_map/ppermute | solution.py:17
  60.3 1.6 %collective-permute-start.12 = (f32[8,24,128]{2,1,0:T(8,128)S(1)}, f32[8,24,128]{2,1,0:T(8,128)S(1)}, u32[]{:S(2)}, u32[]{:S(2)}) collective-permute-start(f32[8,24,128]{2,1,0:T(8,128)S(1)} %pad_maximum_fusion.4), channel_id=1, source_target_pairs={{0,1},{1,0},{2,3},{3,2},{4,5},{5,4},{6,7},{7,6},{8,9},{9,8},{10,11... | collective-permute-start | bytes 294920 | tf_op jit(solution)/shard_map/ppermute | solution.py:56
  61.8 0.7 collective-permute-done.3
  62.5 0.4 select_maximum_fusion
  62.9 2.5 %collective-permute-done.12 = f32[8,24,128]{2,1,0:T(8,128)S(1)} collective-permute-done((f32[8,24,128]{2,1,0:T(8,128)S(1)}, f32[8,24,128]{2,1,0:T(8,128)S(1)}, u32[]{:S(2)}, u32[]{:S(2)}) %collective-permute-start.12) | collective-permute-done | bytes 98336 | tf_op jit(solution)/shard_map/ppermute | solution.py:56
  65.4 1.3 %collective-permute-start.13 = (f32[16,24,128]{2,1,0:T(8,128)S(1)}, f32[16,24,128]{2,1,0:T(8,128)S(1)}, u32[]{:S(2)}, u32[]{:S(2)}) collective-permute-start(f32[16,24,128]{2,1,0:T(8,128)S(1)} %pad_maximum_fusion.3), channel_id=1, source_target_pairs={{0,4},{4,0},{8,12},{12,8},{16,20},{20,16},{24,28},{28,24},{1,5},{5... | collective-permute-start | bytes 589832 | tf_op jit(solution)/shard_map/ppermute | solution.py:56
  66.7 4.2 %fusion.186 = bf16[1,96,6,128]{3,1,2,0:T(8,128)(2,1)} fusion(f32[1,96,12,134]{3,1,2,0:T(8,128)S(1)} %select_maximum_fusion, f32[1,96,6,128]{3,1,2,0:T(8,128)S(1)} %get-tuple-element.81, f32[1,96,3,128]{3,1,2,0:T(8,128)S(1)} %collective-permute-done.2, f32[1,96,3,128]{3,1,2,0:T(8,128)S(1)} %collective-permute-done.3, ...), kind=kLoop, calls=%fused_computation.366 | loop fusion | flops 7815168 | bytes 13289856 | tf_op jit(solution)/shard_map/convert_element_type | solution.py:156
  71.3 0.6 slice_multiply_fusion.46
  71.9 0.6 slice_multiply_fusion.45
  72.5 0.8 %copy.32 = f32[384,96]{0,1:T(8,128)} copy(f32[384,96]{1,0:T(8,128)S(1)} %slice_multiply_fusion.42) | data formatting | bytes 294912
  73.3 0.7 slice_multiply_fusion.43
  74.2 0.8 %copy.31 = f32[96,7,7]{0,2,1:T(8,128)} copy(f32[96,7,7]{2,1,0:T(8,128)S(1)} %mul.1374) | data formatting | bytes 37632
  (65 shorter events, 1.7 us)
Async XLA Ops:
  0.6 13.3 %copy-start = (bf16[96,384]{1,0:T(8,128)(2,1)S(1)}, bf16[96,384]{1,0:T(8,128)(2,1)}, u32[]{:S(2)}) copy-start(bf16[96,384]{1,0:T(8,128)(2,1)} %param.17) | copy-start | bytes 221188
  0.7 9.7 %copy-start.1 = (bf16[1,96,6,128]{3,1,2,0:T(8,128)(2,1)S(1)}, bf16[1,96,6,128]{3,1,2,0:T(8,128)(2,1)}, u32[]{:S(2)}) copy-start(bf16[1,96,6,128]{3,1,2,0:T(8,128)(2,1)} %param.11) | copy-start | bytes 442372
  0.7 10.0 %copy-start.6 = (f32[96]{0:T(128)S(1)}, f32[96]{0:T(128)}, u32[]{:S(2)}) copy-start(f32[96]{0:T(128)} %param.14) | copy-start | bytes 1156
  1.7 7.7 %collective-permute-start = (bf16[1,96,3,128]{3,1,2,0:T(8,128)(2,1)S(1)}, bf16[1,96,3,128]{3,1,2,0:T(8,128)(2,1)S(1)}, u32[]{:S(2)}, u32[]{:S(2)}) collective-permute-start(bf16[1,96,3,128]{3,1,2,0:T(8,128)(2,1)S(1)} %get-tuple-element.97), channel_id=1, source_target_pairs={{0,4},{4,8},{8,12},{12,16},{16,20},{20,24},{24,28},{1,5},{5,9},{9,... | collective-permute-start | bytes 221192 | tf_op jit(solution)/shard_map/ppermute | solution.py:16
  4.1 6.3 %collective-permute-start.1 = (bf16[1,96,3,128]{3,1,2,0:T(8,128)(2,1)S(1)}, bf16[1,96,3,128]{3,1,2,0:T(8,128)(2,1)S(1)}, u32[]{:S(2)}, u32[]{:S(2)}) collective-permute-start(bf16[1,96,3,128]{3,1,2,0:T(8,128)(2,1)S(1)} %get-tuple-element.98), channel_id=1, source_target_pairs={{4,0},{8,4},{12,8},{16,12},{20,16},{24,20},{28,24},{5,1},{9,5},{13... | collective-permute-start | bytes 221192 | tf_op jit(solution)/shard_map/ppermute | solution.py:17
  10.7 3.2 %copy-start.3 = (f32[96]{0:T(128)S(1)}, f32[96]{0:T(128)}, u32[]{:S(2)}) copy-start(f32[96]{0:T(128)} %param.15) | copy-start | bytes 1156
  10.7 3.2 %copy-start.5 = (f32[96]{0:T(128)S(1)}, f32[96]{0:T(128)}, u32[]{:S(2)}) copy-start(f32[96]{0:T(128)} %param.16) | copy-start | bytes 1156
  10.7 3.2 %copy-start.8 = (f32[384]{0:T(512)S(1)}, f32[384]{0:T(512)}, u32[]{:S(2)}) copy-start(f32[384]{0:T(512)} %param.18) | copy-start | bytes 4612
  13.9 2.9 %copy-start.2 = (bf16[1,96,6,128]{3,1,2,0:T(8,128)(2,1)S(1)}, bf16[1,96,6,128]{3,1,2,0:T(8,128)(2,1)}, u32[]{:S(2)}) copy-start(bf16[1,96,6,128]{3,1,2,0:T(8,128)(2,1)} %param.12) | copy-start | bytes 442372
  14.0 2.9 %copy-start.4 = (f32[96]{0:T(128)S(1)}, f32[96]{0:T(128)}, u32[]{:S(2)}) copy-start(f32[96]{0:T(128)} %param.21) | copy-start | bytes 1156
  14.0 2.9 %copy-start.7 = (bf16[384,96]{0,1:T(8,128)(2,1)S(1)}, bf16[384,96]{0,1:T(8,128)(2,1)}, u32[]{:S(2)}) copy-start(bf16[384,96]{0,1:T(8,128)(2,1)} %param.19) | copy-start | bytes 221188
  21.4 1.1 %copy-start.9 = (f32[96]{0:T(128)S(1)}, f32[96]{0:T(128)}, u32[]{:S(2)}) copy-start(f32[96]{0:T(128)} %param.20) | copy-start | bytes 1156
  24.7 4.4 %collective-permute-start.4 = (f32[16,24,128]{2,1,0:T(8,128)S(1)}, f32[16,24,128]{2,1,0:T(8,128)S(1)}, u32[]{:S(2)}, u32[]{:S(2)}) collective-permute-start(f32[16,24,128]{2,1,0:T(8,128)S(1)} %constant_dynamic-slice_fusion.4), channel_id=1, source_target_pairs={{0,4},{4,0},{8,12},{12,8},{16,20},{20,16},{24,28},{28,24},{1,5},{5... | collective-permute-start | bytes 589832 | tf_op jit(solution)/shard_map/ppermute | solution.py:51
  29.1 5.1 %collective-permute-start.5 = (f32[8,24,128]{2,1,0:T(8,128)S(1)}, f32[8,24,128]{2,1,0:T(8,128)S(1)}, u32[]{:S(2)}, u32[]{:S(2)}) collective-permute-start(f32[8,24,128]{2,1,0:T(8,128)S(1)} %constant_dynamic-slice_fusion.3), channel_id=1, source_target_pairs={{0,1},{1,0},{2,3},{3,2},{4,5},{5,4},{6,7},{7,6},{8,9},{9,8},{10,11... | collective-permute-start | bytes 294920 | tf_op jit(solution)/shard_map/ppermute | solution.py:51
  34.3 4.2 %collective-permute-start.6 = (f32[4,24,128]{2,1,0:T(8,128)S(1)}, f32[4,24,128]{2,1,0:T(8,128)S(1)}, u32[]{:S(2)}, u32[]{:S(2)}) collective-permute-start(f32[4,24,128]{2,1,0:T(8,128)S(1)} %constant_dynamic-slice_fusion.2), channel_id=1, source_target_pairs={{0,8},{4,12},{8,0},{12,4},{16,24},{20,28},{24,16},{28,20},{1,9},{5... | collective-permute-start | bytes 147464 | tf_op jit(solution)/shard_map/ppermute | solution.py:51
  38.5 3.9 %collective-permute-start.7 = (f32[2,24,128]{2,1,0:T(8,128)S(1)}, f32[2,24,128]{2,1,0:T(8,128)S(1)}, u32[]{:S(2)}, u32[]{:S(2)}) collective-permute-start(f32[2,24,128]{2,1,0:T(8,128)S(1)} %constant_dynamic-slice_fusion.1), channel_id=1, source_target_pairs={{0,2},{1,3},{2,0},{3,1},{4,6},{5,7},{6,4},{7,5},{8,10},{9,11},{10,... | collective-permute-start | bytes 73736 | tf_op jit(solution)/shard_map/ppermute | solution.py:51
  42.4 4.7 %collective-permute-start.8 = (f32[1,24,128]{2,1,0:T(8,128)S(1)}, f32[1,24,128]{2,1,0:T(8,128)S(1)}, u32[]{:S(2)}, u32[]{:S(2)}) collective-permute-start(f32[1,24,128]{2,1,0:T(8,128)S(1)} %constant_dynamic-slice_fusion), channel_id=1, source_target_pairs={{0,16},{4,20},{8,24},{12,28},{16,0},{20,4},{24,8},{28,12},{1,17},{... | collective-permute-start | bytes 36872 | tf_op jit(solution)/shard_map/ppermute | solution.py:51
  47.1 4.6 %collective-permute-start.9 = (f32[1,24,128]{2,1,0:T(8,128)S(1)}, f32[1,24,128]{2,1,0:T(8,128)S(1)}, u32[]{:S(2)}, u32[]{:S(2)}) collective-permute-start(f32[1,24,128]{2,1,0:T(8,128)S(1)} %dynamic-slice_add_fusion.4), channel_id=1, source_target_pairs={{0,16},{4,20},{8,24},{12,28},{16,0},{20,4},{24,8},{28,12},{1,17},{... | collective-permute-start | bytes 36872 | tf_op jit(solution)/shard_map/ppermute | solution.py:56
  51.7 3.9 %collective-permute-start.10 = (f32[2,24,128]{2,1,0:T(8,128)S(1)}, f32[2,24,128]{2,1,0:T(8,128)S(1)}, u32[]{:S(2)}, u32[]{:S(2)}) collective-permute-start(f32[2,24,128]{2,1,0:T(8,128)S(1)} %pad_maximum_fusion.6), channel_id=1, source_target_pairs={{0,2},{1,3},{2,0},{3,1},{4,6},{5,7},{6,4},{7,5},{8,10},{9,11},{10,... | collective-permute-start | bytes 73736 | tf_op jit(solution)/shard_map/ppermute | solution.py:56
  55.6 4.6 %collective-permute-start.11 = (f32[4,24,128]{2,1,0:T(8,128)S(1)}, f32[4,24,128]{2,1,0:T(8,128)S(1)}, u32[]{:S(2)}, u32[]{:S(2)}) collective-permute-start(f32[4,24,128]{2,1,0:T(8,128)S(1)} %pad_maximum_fusion.5), channel_id=1, source_target_pairs={{0,8},{4,12},{8,0},{12,4},{16,24},{20,28},{24,16},{28,20},{1,9},{5... | collective-permute-start | bytes 147464 | tf_op jit(solution)/shard_map/ppermute | solution.py:56
  57.4 4.4 %collective-permute-start.2 = (f32[1,96,3,128]{3,1,2,0:T(8,128)S(1)}, f32[1,96,3,128]{3,1,2,0:T(8,128)S(1)}, u32[]{:S(2)}, u32[]{:S(2)}) collective-permute-start(f32[1,96,3,128]{3,1,2,0:T(8,128)S(1)} %get-tuple-element.91), channel_id=1, source_target_pairs={{0,4},{4,8},{8,12},{12,16},{16,20},{20,24},{24,28},{1,5},{5,9},{9,... | collective-permute-start | bytes 442376 | tf_op jit(solution)/shard_map/ppermute | solution.py:16
  58.7 3.8 %collective-permute-start.3 = (f32[1,96,3,128]{3,1,2,0:T(8,128)S(1)}, f32[1,96,3,128]{3,1,2,0:T(8,128)S(1)}, u32[]{:S(2)}, u32[]{:S(2)}) collective-permute-start(f32[1,96,3,128]{3,1,2,0:T(8,128)S(1)} %get-tuple-element.92), channel_id=1, source_target_pairs={{4,0},{8,4},{12,8},{16,12},{20,16},{24,20},{28,24},{5,1},{9,5},{13... | collective-permute-start | bytes 442376 | tf_op jit(solution)/shard_map/ppermute | solution.py:17
  60.3 5.1 %collective-permute-start.12 = (f32[8,24,128]{2,1,0:T(8,128)S(1)}, f32[8,24,128]{2,1,0:T(8,128)S(1)}, u32[]{:S(2)}, u32[]{:S(2)}) collective-permute-start(f32[8,24,128]{2,1,0:T(8,128)S(1)} %pad_maximum_fusion.4), channel_id=1, source_target_pairs={{0,1},{1,0},{2,3},{3,2},{4,5},{5,4},{6,7},{7,6},{8,9},{9,8},{10,11... | collective-permute-start | bytes 294920 | tf_op jit(solution)/shard_map/ppermute | solution.py:56
  65.4 5.5 %collective-permute-start.13 = (f32[16,24,128]{2,1,0:T(8,128)S(1)}, f32[16,24,128]{2,1,0:T(8,128)S(1)}, u32[]{:S(2)}, u32[]{:S(2)}) collective-permute-start(f32[16,24,128]{2,1,0:T(8,128)S(1)} %pad_maximum_fusion.3), channel_id=1, source_target_pairs={{0,4},{4,0},{8,12},{12,8},{16,20},{20,16},{24,28},{28,24},{1,5},{5... | collective-permute-start | bytes 589832 | tf_op jit(solution)/shard_map/ppermute | solution.py:56

commit v2 on v1

--- a/solution.py
+++ b/solution.py
@@ -19,41 +19,52 @@
     return array
 
 
-def butterfly_steps(axes):
-    steps = []
-    for axis in axes:
-        size = lax.axis_size(axis)
-        bit = 1
-        while bit < size:
-            steps.append((axis, bit))
-            bit *= 2
-    order = {"strip": 0, "slide": 1}
-    steps.sort(key=lambda s: (0 if (s[0] == "strip" and s[1] == 1) else 1, s[1], order[s[0]]))
-    return steps
+def xor_pairs(size, mask):
+    return [(i, i ^ mask) for i in range(size)]
 
 
-def tree_psum(terms, axes):
+def low_bits(size):
+    bits = []
+    bit = 1
+    while bit < size:
+        bits.append(bit)
+        bit *= 2
+    return bits
+
+
+def tree_psum(terms):
     shapes = [t.shape for t in terms]
     sizes = [math.prod(s) for s in shapes]
     total = sum(sizes)
-    steps = butterfly_steps(axes)
-    pieces = 2 ** len(steps)
+    strip_bits = low_bits(lax.axis_size("strip"))
+    slide_bits = low_bits(lax.axis_size("slide"))
+    scatter = [("strip", b) for b in strip_bits[:2]]
+    stages = [("slide", slide_bits[i : i + 2]) for i in range(0, len(slide_bits), 2)]
+    stages += [("strip", [b]) for b in strip_bits[2:]]
+    pieces = 2 ** len(scatter)
     rows = -(-total // (pieces * 128))
     rows = -(-rows // 8) * 8
     flat = jnp.concatenate([t.reshape(-1) for t in terms])
     flat = jnp.pad(flat, (0, pieces * rows * 128 - total)).reshape(pieces, rows, 128)
-    for axis, bit in steps:
+    for axis, bit in scatter:
         size = lax.axis_size(axis)
         half = flat.shape[0] // 2
         mine = (lax.axis_index(axis) // bit) % 2
         keep = lax.dynamic_slice_in_dim(flat, mine * half, half, axis=0)
         give = lax.dynamic_slice_in_dim(flat, (1 - mine) * half, half, axis=0)
-        got = lax.ppermute(give, axis, [(i, i ^ bit) for i in range(size)])
-        flat = keep + got
-    for axis, bit in reversed(steps):
+        flat = keep + lax.ppermute(give, axis, xor_pairs(size, bit))
+    for axis, bits in stages:
+        size = lax.axis_size(axis)
+        masks = []
+        for m in range(1, 2 ** len(bits)):
+            masks.append(sum(b for k, b in enumerate(bits) if (m >> k) & 1))
+        got = [lax.ppermute(flat, axis, xor_pairs(size, mask)) for mask in masks]
+        for item in got:
+            flat = flat + item
+    for axis, bit in reversed(scatter):
         size = lax.axis_size(axis)
         mine = (lax.axis_index(axis) // bit) % 2
-        got = lax.ppermute(flat, axis, [(i, i ^ bit) for i in range(size)])
+        got = lax.ppermute(flat, axis, xor_pairs(size, bit))
         low = jnp.where(mine == 0, flat, got)
         high = jnp.where(mine == 0, got, flat)
         flat = jnp.concatenate([low, high], axis=0)
@@ -64,6 +75,7 @@
         out.append(flat[offset : offset + size].reshape(shape))
         offset += size
     return out
+
 
 def gelu_slope(value):
     return 0.5 * (1.0 + jax.scipy.special.erf(value / math.sqrt(2.0))) + value * jnp.exp(
@@ -151,7 +163,7 @@
     )
     pixel_count = slides_here * lax.axis_size("slide") * rows * lax.axis_size("strip") * cols
     scale = 1.0 / math.sqrt(float(pixel_count))
-    g = tree_psum(terms, ("strip", "slide"))
+    g = tree_psum(terms)
     g = [item * scale for item in g]
     return (image_grad.astype(jnp.bfloat16), g[0], g[1], g[2], g[3], g[4], g[5], g[6], g[7], g[8])
 

time: 75.9 us -> 65.3 us (0.86)
  starting transfers between devices: 26.7 us -> 19.4 us
  waiting for transfers between devices: 18.4 us -> 15.9 us
    ppermute x10 -> x8, starting transfers between devices: 20.2 us -> 12.9 us  [the longest x4 7.33 us: tree_psum(): got = [lax.ppermute(flat, axis, xor_pairs(size, mask)) for mask in masks]]
    ppermute x10 -> x8, waiting for transfers between devices: 17.7 us -> 15.9 us  [the longest x4 8.04 us: tree_psum(): got = [lax.ppermute(flat, axis, xor_pairs(size, mask)) for mask in masks]]
    mul x1 -> x3, local copies, waits for them, and re-layouts: 0.2 us -> 0.99 us  [on_device(): g = [item * scale for item in g]]
    mul x5 -> x4, other arithmetic: 1.88 us -> 1.22 us  [on_device(): g = [item * scale for item in g]]
  transfers between devices with their start and end apart: 14 -> 12, of which waited for: 9 -> 6; matrix products, arithmetic and copies ran while one was open for 13% -> 15% of each run, Pallas kernels for 0% -> 0%
where the time goes in v2:
time: 65.3 us; the launch traced here: 65 us
  starting transfers between devices  19.4 us (30%)
  waiting for transfers between devices  15.9 us (24%)
  other arithmetic  13.7 us (21%)
  local copies, waits for them, and re-layouts  9.8 us (15%)
  matrix products  5.09 us (8%)
  between operations  1.16 us (2%)
    ppermute x4, waiting for transfers between devices, tree_psum(): got = [lax.ppermute(flat, axis, xor_pairs(size, mask)) for mask in masks]  8.04 us
    ppermute x4, starting transfers between devices, tree_psum(): got = [lax.ppermute(flat, axis, xor_pairs(size, mask)) for mask in masks]  7.33 us
    ppermute x2, starting transfers between devices, tree_psum(): flat = keep + lax.ppermute(give, axis, xor_pairs(size, bit))  5.42 us
    convert_element_type x1, other arithmetic, on_device(): image_grad.astype(jnp.bfloat16)  4.33 us
    ppermute x2, waiting for transfers between devices, tree_psum(): got = lax.ppermute(flat, axis, xor_pairs(size, bit))  4.03 us
    ppermute x2, waiting for transfers between devices, tree_psum(): flat = keep + lax.ppermute(give, axis, xor_pairs(size, bit))  3.78 us
    ppermute x2, starting transfers between devices, with_halo(): before = lax.ppermute(last, axis, up)  3.7 us
    reduce_sum x1, other arithmetic, on_device(): centre = conv - jnp.mean(conv, axis=1, keepdims=True)  3.07 us
  transfers between devices with their start and end apart: 12, of which 6 were waited for; matrix products, arithmetic and copies ran while one was open for 15% of the time, Pallas kernels for 0%

profile of v2, /device:TPU:0, one launch (start us, length us, event | category | flops | bytes accessed | tf_op | source)
XLA Modules:
  0.0 65.0 jit_solution(1179094182409874114)
XLA Ops:
  0.7 1.0 %fusion.204 = (bf16[1,96,3,128]{3,1,2,0:T(8,128)(2,1)S(1)}, bf16[1,96,3,128]{3,1,2,0:T(8,128)(2,1)S(1)}) fusion(bf16[1,96,6,128]{3,1,2,0:T(8,128)(2,1)} %param.11), kind=kLoop, calls=%fused_computation.455 | loop fusion | bytes 294912 | tf_op jit(solution)/shard_map/slice | solution.py:14
  1.7 2.4 %collective-permute-start = (bf16[1,96,3,128]{3,1,2,0:T(8,128)(2,1)S(1)}, bf16[1,96,3,128]{3,1,2,0:T(8,128)(2,1)S(1)}, u32[]{:S(2)}, u32[]{:S(2)}) collective-permute-start(bf16[1,96,3,128]{3,1,2,0:T(8,128)(2,1)S(1)} %get-tuple-element.99), channel_id=1, source_target_pairs={{0,4},{4,8},{8,12},{12,16},{16,20},{20,24},{24,28},{1,5},{5,9},{9,... | collective-permute-start | bytes 221192 | tf_op jit(solution)/shard_map/ppermute | solution.py:16
  4.1 1.3 %collective-permute-start.1 = (bf16[1,96,3,128]{3,1,2,0:T(8,128)(2,1)S(1)}, bf16[1,96,3,128]{3,1,2,0:T(8,128)(2,1)S(1)}, u32[]{:S(2)}, u32[]{:S(2)}) collective-permute-start(bf16[1,96,3,128]{3,1,2,0:T(8,128)(2,1)S(1)} %get-tuple-element.100), channel_id=1, source_target_pairs={{4,0},{8,4},{12,8},{16,12},{20,16},{24,20},{28,24},{5,1},{9,5},{13... | collective-permute-start | bytes 221192 | tf_op jit(solution)/shard_map/ppermute | solution.py:17
  5.4 1.0 %slice_bitcast_fusion.48 = (f32[96]{0:T(128)S(1)}, f32[96]{0:T(128)S(1)}, f32[96]{0:T(128)S(1)}, f32[96]{0:T(128)S(1)}, f32[96]{0:T(128)S(1)}, /*index=5*/f32[96...) fusion(f32[96,7,7]{0,2,1:T(8,128)} %param.13), kind=kLoop, calls=%fused_computation.452 | loop fusion | bytes 14592 | tf_op jit(solution)/shard_map/mul | solution.py:148
  6.4 1.0 %slice_bitcast_fusion.47 = (f32[96]{0:T(128)S(1)}, f32[96]{0:T(128)S(1)}, f32[96]{0:T(128)S(1)}, f32[96]{0:T(128)S(1)}, f32[96]{0:T(128)S(1)}, /*index=5*/f32[96...) fusion(f32[96,7,7]{0,2,1:T(8,128)} %param.13), kind=kLoop, calls=%fused_computation.451 | loop fusion | bytes 14592 | tf_op jit(solution)/shard_map/mul | solution.py:112
  7.4 0.9 %slice_bitcast_fusion.46 = (f32[96]{0:T(128)S(1)}, f32[96]{0:T(128)S(1)}, f32[96]{0:T(128)S(1)}, f32[96]{0:T(128)S(1)}, f32[96]{0:T(128)S(1)}, /*index=5*/f32[96...) fusion(f32[96,7,7]{0,2,1:T(8,128)} %param.13), kind=kLoop, calls=%fused_computation.450 | loop fusion | bytes 8448 | tf_op jit(solution)/shard_map/mul | solution.py:112
  8.3 1.1 %convert_reduce_fusion.1 = f32[96]{0:T(128)S(1)} fusion(bf16[1,96,6,128]{3,1,2,0:T(8,128)(2,1)} %param.12, f32[96]{0:T(128)} %param.21), kind=kLoop, calls=%fused_computation.363 | loop fusion | flops 368544 | bytes 148224 | tf_op jit(solution)/shard_map/reduce_sum | solution.py:161
  9.4 1.0 %constant_dynamic-update-slice_fusion = (bf16[1,96,9,128]{3,1,2,0:T(8,128)(2,1)S(1)}, bf16[1,96,9,128]{3,1,2,0:T(8,128)(2,1)S(1)}) fusion(bf16[1,96,9,128]{3,1,2,0:T(8,128)(2,1)S(1)} %constant_dynamic-update-slice_fusion.1, bf16[1,96,6,128]{3,1,2,0:T(8,128)(2,1)} %param.11), kind=kLoop, calls=%fused_computation.388 | loop fusion | bytes 442368 | tf_op jit(solution)/shard_map/concatenate | solution.py:18
  10.4 0.3 fusion.25
  10.8 3.1 %fusion.201 = (f32[6,128]{1,0:T(8,128)S(1)}, f32[1,96,6,128]{3,1,2,0:T(8,128)S(1)}) fusion(bf16[1,96,12,134]{3,1,2,0:T(8,128)(2,1)S(1)} %fusion.25, f32[96]{0:T(128)S(1)} %get-tuple-element.148, f32[96]{0:T(128)S(1)} %get-tuple-element.149, f32[96]{0:T(128)S(1)} %get-tuple-element.102, bf16[1,96,9,128]{3,1,2,0:T(8,128)(2,1)S(1)} %constant_dynamic-update-slice_fusion.2, ...), kind=kLoop, calls=%fused_computation.453 | loop fusion | flops 10910976 | bytes 7542528 | tf_op jit(solution)/shard_map/reduce_sum | solution.py:115
  14.0 2.8 %fusion.9 = (bf16[384,6,128]{0,2,1:T(8,128)(2,1)S(1)}, f32[384,6,128]{0,2,1:T(8,128)S(1)}) fusion(f32[384]{0:T(512)S(1)} %copy-done.8, bf16[96,384]{1,0:T(8,128)(2,1)S(1)} %copy-done, f32[1,96,6,128]{3,1,2,0:T(8,128)S(1)} %get-tuple-element.83, f32[96]{0:T(128)S(1)} %copy-done.5, f32[96]{0:T(128)S(1)} %copy-done.3, f32[6,128]{1,0:T(8,128)S(1)} %add_rsqrt_fusion, ...), kind=kOutput, calls=%fused_computation.15 | convolution fusion | flops 76455936 | bytes 2146560 | tf_op jit(solution)/shard_map/scrw,cf->sfrw/dot_general | solution.py:122
  16.8 0.7 %convert_reduce_fusion = (f32[384]{0:T(512)S(1)}, bf16[384,6,128]{0,2,1:T(8,128)(2,1)S(1)}) fusion(f32[384,6,128]{0,2,1:T(8,128)S(1)} %get-tuple-element.154, bf16[384,96]{0,1:T(8,128)(2,1)S(1)} %copy-done.7, bf16[1,96,6,128]{3,1,2,0:T(8,128)(2,1)S(1)} %copy-done.2, f32[96]{0:T(128)S(1)} %copy-done.4), kind=kOutput, calls=%fused_computation.31 | convolution fusion | flops 60382848 | bytes 1992576 | tf_op jit(solution)/shard_map/scrw,fc->sfrw/dot_general | solution.py:131
  17.6 0.3 convolution_bitcast_fusion.2
  17.9 0.4 fusion.183
  18.3 0.1 fusion.187
  18.4 1.2 %fusion.123 = (f32[96]{0:T(128)S(1)}, f32[96]{0:T(128)S(1)}, f32[96]{0:T(128)S(1)}, f32[96]{0:T(128)S(1)}, f32[96]{0:T(128)S(1)}, /*index=5*/f32[96]{0:T(128)S(1...) fusion(bf16[1,96,12,134]{3,1,2,0:T(8,128)(2,1)S(1)} %fusion.25,, ...), kind=kLoop, calls=%fused_computation.252 | loop fusion | flops 4495680 | bytes 3558528 | tf_op jit(solution)/shard_map/reduce_sum | solution.py:151
  19.6 0.7 %fusion.120 = (f32[96]{0:T(128)S(1)}, f32[96]{0:T(128)S(1)}, f32[96]{0:T(128)S(1)}, f32[96]{0:T(128)S(1)}, f32[96]{0:T(128)S(1)}, /*index=5*/f32[96]{0:T(128)S(1...) fusion(f32[1,96,6,128]{3,1,2,0:T(8,128)S(1)} %get-tuple-element, ...), kind=kLoop, calls=%fused_computation.249 | loop fusion | flops 2947776 | bytes 2217216 | tf_op jit(solution)/shard_map/reduce_sum | solution.py:151
  20.3 1.1 %fusion.102 = (f32[96]{0:T(128)S(1)}, f32[96]{0:T(128)S(1)}, f32[96]{0:T(128)S(1)}, f32[96]{0:T(128)S(1)}, f32[96]{0:T(128)S(1)}, /*index=5*/f32[96]{0:T(128)S(1...) fusion(f32[1,96,6,128]{3,1,2,0:T(8,128)S(1)} %get-tuple-element, ...), kind=kLoop, calls=%fused_computation.231 | loop fusion | flops 3979584 | bytes 2956032 | tf_op jit(solution)/shard_map/reduce_sum | solution.py:151
  21.4 0.1 stack.199
  21.6 0.2 reshape_reshape.3
  21.8 0.1 reduce_sum.586
  21.9 0.4 convolution_bitcast_fusion.1
  22.3 0.1 reshape.357
  22.5 0.4 fusion.20
  22.9 1.7 %concatenate.41 = f32[79296]{0:T(1024)S(1)} concatenate(f32[4704]{0:T(1024)S(1)} %reshape_reshape.3, f32[96]{0:T(128)S(1)} %get-tuple-element.70, f32[96]{0:T(128)S(1)} %get-tuple-element.62, f32[96]{0:T(128)S(1)} %reduce_sum.586, f32[36864]{0:T(1024)S(1)} %reshape.356, f32[384]{0:T(512)S(1)} %get-tuple-element.151, f32[36864]{0:T(1024)S(1)} %reshape.357, ...), dimensions={0} | concatenate | bytes 634368 | tf_op jit(solution)/shard_map/concatenate | solution.py:47
  24.6 3.4 %collective-permute-start.4 = (f32[2,160,128]{2,1,0:T(8,128)S(1)}, f32[2,160,128]{2,1,0:T(8,128)S(1)}, u32[]{:S(2)}, u32[]{:S(2)}) collective-permute-start(f32[2,160,128]{2,1,0:T(8,128)S(1)} %constant_dynamic-slice_fusion.1), channel_id=1, source_target_pairs={{0,4},{4,0},{8,12},{12,8},{16,20},{20,16},{24,28},{28,24},{1,5},{5... | collective-permute-start | bytes 491528 | tf_op jit(solution)/shard_map/ppermute | solution.py:55
  28.0 1.0 %collective-permute-done.4 = f32[2,160,128]{2,1,0:T(8,128)S(1)} collective-permute-done((f32[2,160,128]{2,1,0:T(8,128)S(1)}, f32[2,160,128]{2,1,0:T(8,128)S(1)}, u32[]{:S(2)}, u32[]{:S(2)}) %collective-permute-start.4) | collective-permute-done | bytes 163872 | tf_op jit(solution)/shard_map/ppermute | solution.py:55
  29.1 2.1 %collective-permute-start.5 = (f32[1,160,128]{2,1,0:T(8,128)S(1)}, f32[1,160,128]{2,1,0:T(8,128)S(1)}, u32[]{:S(2)}, u32[]{:S(2)}) collective-permute-start(f32[1,160,128]{2,1,0:T(8,128)S(1)} %constant_dynamic-slice_fusion), channel_id=1, source_target_pairs={{0,8},{4,12},{8,0},{12,4},{16,24},{20,28},{24,16},{28,20},{1,9},{5... | collective-permute-start | bytes 245768 | tf_op jit(solution)/shard_map/ppermute | solution.py:55
  31.1 2.8 %collective-permute-done.5 = f32[1,160,128]{2,1,0:T(8,128)S(1)} collective-permute-done((f32[1,160,128]{2,1,0:T(8,128)S(1)}, f32[1,160,128]{2,1,0:T(8,128)S(1)}, u32[]{:S(2)}, u32[]{:S(2)}) %collective-permute-start.5) | collective-permute-done | bytes 81952 | tf_op jit(solution)/shard_map/ppermute | solution.py:55
  33.9 1.6 %collective-permute-start.6 = (f32[1,160,128]{2,1,0:T(8,128)S(1)}, f32[1,160,128]{2,1,0:T(8,128)S(1)}, u32[]{:S(2)}, u32[]{:S(2)}) collective-permute-start(f32[1,160,128]{2,1,0:T(8,128)S(1)} %dynamic-slice_add_fusion.1), channel_id=1, source_target_pairs={{0,1},{1,0},{2,3},{3,2},{4,5},{5,4},{6,7},{7,6},{8,9},{9,8},{10,11... | collective-permute-start | bytes 245768 | tf_op jit(solution)/shard_map/ppermute | solution.py:61
  35.5 1.5 %collective-permute-start.7 = (f32[1,160,128]{2,1,0:T(8,128)S(1)}, f32[1,160,128]{2,1,0:T(8,128)S(1)}, u32[]{:S(2)}, u32[]{:S(2)}) collective-permute-start(f32[1,160,128]{2,1,0:T(8,128)S(1)} %dynamic-slice_add_fusion.1), channel_id=1, source_target_pairs={{0,2},{1,3},{2,0},{3,1},{4,6},{5,7},{6,4},{7,5},{8,10},{9,11},{10,... | collective-permute-start | bytes 245768 | tf_op jit(solution)/shard_map/ppermute | solution.py:61
  37.0 0.5 collective-permute-start.8
  37.5 1.3 %collective-permute-start.2 = (f32[1,96,3,128]{3,1,2,0:T(8,128)S(1)}, f32[1,96,3,128]{3,1,2,0:T(8,128)S(1)}, u32[]{:S(2)}, u32[]{:S(2)}) collective-permute-start(f32[1,96,3,128]{3,1,2,0:T(8,128)S(1)} %get-tuple-element.93), channel_id=1, source_target_pairs={{0,4},{4,8},{8,12},{12,16},{16,20},{20,24},{24,28},{1,5},{5,9},{9,... | collective-permute-start | bytes 442376 | tf_op jit(solution)/shard_map/ppermute | solution.py:16
  38.8 1.5 %collective-permute-start.3 = (f32[1,96,3,128]{3,1,2,0:T(8,128)S(1)}, f32[1,96,3,128]{3,1,2,0:T(8,128)S(1)}, u32[]{:S(2)}, u32[]{:S(2)}) collective-permute-start(f32[1,96,3,128]{3,1,2,0:T(8,128)S(1)} %get-tuple-element.94), channel_id=1, source_target_pairs={{4,0},{8,4},{12,8},{16,12},{20,16},{24,20},{28,24},{5,1},{9,5},{13... | collective-permute-start | bytes 442376 | tf_op jit(solution)/shard_map/ppermute | solution.py:17
  40.3 0.5 collective-permute-done.7
  40.8 1.5 %collective-permute-done.8 = f32[1,160,128]{2,1,0:T(8,128)S(1)} collective-permute-done((f32[1,160,128]{2,1,0:T(8,128)S(1)}, f32[1,160,128]{2,1,0:T(8,128)S(1)}, u32[]{:S(2)}, u32[]{:S(2)}) %collective-permute-start.8) | collective-permute-done | bytes 81952 | tf_op jit(solution)/shard_map/ppermute | solution.py:61
  42.3 3.8 %collective-permute-start.9 = (f32[1,160,128]{2,1,0:T(8,128)S(1)}, f32[1,160,128]{2,1,0:T(8,128)S(1)}, u32[]{:S(2)}, u32[]{:S(2)}) collective-permute-start(f32[1,160,128]{2,1,0:T(8,128)S(1)} %add_add_fusion), channel_id=1, source_target_pairs={{0,16},{4,20},{8,24},{12,28},{16,0},{20,4},{24,8},{28,12},{1,17},{... | collective-permute-start | bytes 245768 | tf_op jit(solution)/shard_map/ppermute | solution.py:61
  46.1 6.0 %collective-permute-done.9 = f32[1,160,128]{2,1,0:T(8,128)S(1)} collective-permute-done((f32[1,160,128]{2,1,0:T(8,128)S(1)}, f32[1,160,128]{2,1,0:T(8,128)S(1)}, u32[]{:S(2)}, u32[]{:S(2)}) %collective-permute-start.9) | collective-permute-done | bytes 81952 | tf_op jit(solution)/shard_map/ppermute | solution.py:61
  52.2 0.4 select_maximum_fusion
  52.6 4.0 %collective-permute-done.10 = f32[1,160,128]{2,1,0:T(8,128)S(1)} collective-permute-done((f32[1,160,128]{2,1,0:T(8,128)S(1)}, f32[1,160,128]{2,1,0:T(8,128)S(1)}, u32[]{:S(2)}, u32[]{:S(2)}) %collective-permute-start.10) | collective-permute-done | bytes 81952 | tf_op jit(solution)/shard_map/ppermute | solution.py:67
  56.8 4.3 %fusion.186 = bf16[1,96,6,128]{3,1,2,0:T(8,128)(2,1)} fusion(f32[1,96,12,134]{3,1,2,0:T(8,128)S(1)} %select_maximum_fusion, f32[1,96,6,128]{3,1,2,0:T(8,128)S(1)} %get-tuple-element.81, f32[1,96,3,128]{3,1,2,0:T(8,128)S(1)} %collective-permute-done.2, f32[1,96,3,128]{3,1,2,0:T(8,128)S(1)} %collective-permute-done.3, ...), kind=kLoop, calls=%fused_computation.366 | loop fusion | flops 7815168 | bytes 13289856 | tf_op jit(solution)/shard_map/convert_element_type | solution.py:168
  61.2 0.6 slice_multiply_fusion.46
  61.8 0.6 slice_multiply_fusion.45
  62.4 0.1 mul.1364
  62.5 0.8 %copy.32 = f32[384,96]{0,1:T(8,128)} copy(f32[384,96]{1,0:T(8,128)S(1)} %mul.1364) | data formatting | bytes 294912
  63.3 0.7 %mul.1360 = f32[96,384]{1,0:T(8,128)} reshape(f32[36864]{0:T(1024)S(1)} %get-tuple-element.90) | data formatting | bytes 294912 | tf_op jit(solution)/shard_map/mul | solution.py:167
  64.0 0.2 mul.1354
  64.2 0.8 %copy.31 = f32[96,7,7]{0,2,1:T(8,128)} copy(f32[96,7,7]{2,1,0:T(8,128)S(1)} %mul.1354) | data formatting | bytes 37632
  (50 shorter events, 0.7 us)
Async XLA Ops:
  0.6 13.3 %copy-start = (bf16[96,384]{1,0:T(8,128)(2,1)S(1)}, bf16[96,384]{1,0:T(8,128)(2,1)}, u32[]{:S(2)}) copy-start(bf16[96,384]{1,0:T(8,128)(2,1)} %param.17) | copy-start | bytes 221188
  0.7 9.7 %copy-start.1 = (bf16[1,96,6,128]{3,1,2,0:T(8,128)(2,1)S(1)}, bf16[1,96,6,128]{3,1,2,0:T(8,128)(2,1)}, u32[]{:S(2)}) copy-start(bf16[1,96,6,128]{3,1,2,0:T(8,128)(2,1)} %param.11) | copy-start | bytes 442372
  0.7 10.0 %copy-start.6 = (f32[96]{0:T(128)S(1)}, f32[96]{0:T(128)}, u32[]{:S(2)}) copy-start(f32[96]{0:T(128)} %param.14) | copy-start | bytes 1156
  1.7 7.7 %collective-permute-start = (bf16[1,96,3,128]{3,1,2,0:T(8,128)(2,1)S(1)}, bf16[1,96,3,128]{3,1,2,0:T(8,128)(2,1)S(1)}, u32[]{:S(2)}, u32[]{:S(2)}) collective-permute-start(bf16[1,96,3,128]{3,1,2,0:T(8,128)(2,1)S(1)} %get-tuple-element.99), channel_id=1, source_target_pairs={{0,4},{4,8},{8,12},{12,16},{16,20},{20,24},{24,28},{1,5},{5,9},{9,... | collective-permute-start | bytes 221192 | tf_op jit(solution)/shard_map/ppermute | solution.py:16
  4.1 6.3 %collective-permute-start.1 = (bf16[1,96,3,128]{3,1,2,0:T(8,128)(2,1)S(1)}, bf16[1,96,3,128]{3,1,2,0:T(8,128)(2,1)S(1)}, u32[]{:S(2)}, u32[]{:S(2)}) collective-permute-start(bf16[1,96,3,128]{3,1,2,0:T(8,128)(2,1)S(1)} %get-tuple-element.100), channel_id=1, source_target_pairs={{4,0},{8,4},{12,8},{16,12},{20,16},{24,20},{28,24},{5,1},{9,5},{13... | collective-permute-start | bytes 221192 | tf_op jit(solution)/shard_map/ppermute | solution.py:17
  10.7 3.2 %copy-start.3 = (f32[96]{0:T(128)S(1)}, f32[96]{0:T(128)}, u32[]{:S(2)}) copy-start(f32[96]{0:T(128)} %param.15) | copy-start | bytes 1156
  10.7 3.2 %copy-start.5 = (f32[96]{0:T(128)S(1)}, f32[96]{0:T(128)}, u32[]{:S(2)}) copy-start(f32[96]{0:T(128)} %param.16) | copy-start | bytes 1156
  10.7 3.2 %copy-start.8 = (f32[384]{0:T(512)S(1)}, f32[384]{0:T(512)}, u32[]{:S(2)}) copy-start(f32[384]{0:T(512)} %param.18) | copy-start | bytes 4612
  13.9 2.9 %copy-start.2 = (bf16[1,96,6,128]{3,1,2,0:T(8,128)(2,1)S(1)}, bf16[1,96,6,128]{3,1,2,0:T(8,128)(2,1)}, u32[]{:S(2)}) copy-start(bf16[1,96,6,128]{3,1,2,0:T(8,128)(2,1)} %param.12) | copy-start | bytes 442372
  14.0 2.9 %copy-start.4 = (f32[96]{0:T(128)S(1)}, f32[96]{0:T(128)}, u32[]{:S(2)}) copy-start(f32[96]{0:T(128)} %param.21) | copy-start | bytes 1156
  14.0 2.9 %copy-start.7 = (bf16[384,96]{0,1:T(8,128)(2,1)S(1)}, bf16[384,96]{0,1:T(8,128)(2,1)}, u32[]{:S(2)}) copy-start(bf16[384,96]{0,1:T(8,128)(2,1)} %param.19) | copy-start | bytes 221188
  21.4 1.1 %copy-start.9 = (f32[96]{0:T(128)S(1)}, f32[96]{0:T(128)}, u32[]{:S(2)}) copy-start(f32[96]{0:T(128)} %param.20) | copy-start | bytes 1156
  24.6 4.4 %collective-permute-start.4 = (f32[2,160,128]{2,1,0:T(8,128)S(1)}, f32[2,160,128]{2,1,0:T(8,128)S(1)}, u32[]{:S(2)}, u32[]{:S(2)}) collective-permute-start(f32[2,160,128]{2,1,0:T(8,128)S(1)} %constant_dynamic-slice_fusion.1), channel_id=1, source_target_pairs={{0,4},{4,0},{8,12},{12,8},{16,20},{20,16},{24,28},{28,24},{1,5},{5... | collective-permute-start | bytes 491528 | tf_op jit(solution)/shard_map/ppermute | solution.py:55
  29.1 4.8 %collective-permute-start.5 = (f32[1,160,128]{2,1,0:T(8,128)S(1)}, f32[1,160,128]{2,1,0:T(8,128)S(1)}, u32[]{:S(2)}, u32[]{:S(2)}) collective-permute-start(f32[1,160,128]{2,1,0:T(8,128)S(1)} %constant_dynamic-slice_fusion), channel_id=1, source_target_pairs={{0,8},{4,12},{8,0},{12,4},{16,24},{20,28},{24,16},{28,20},{1,9},{5... | collective-permute-start | bytes 245768 | tf_op jit(solution)/shard_map/ppermute | solution.py:55
  33.9 6.4 %collective-permute-start.6 = (f32[1,160,128]{2,1,0:T(8,128)S(1)}, f32[1,160,128]{2,1,0:T(8,128)S(1)}, u32[]{:S(2)}, u32[]{:S(2)}) collective-permute-start(f32[1,160,128]{2,1,0:T(8,128)S(1)} %dynamic-slice_add_fusion.1), channel_id=1, source_target_pairs={{0,1},{1,0},{2,3},{3,2},{4,5},{5,4},{6,7},{7,6},{8,9},{9,8},{10,11... | collective-permute-start | bytes 245768 | tf_op jit(solution)/shard_map/ppermute | solution.py:61
  35.5 5.3 %collective-permute-start.7 = (f32[1,160,128]{2,1,0:T(8,128)S(1)}, f32[1,160,128]{2,1,0:T(8,128)S(1)}, u32[]{:S(2)}, u32[]{:S(2)}) collective-permute-start(f32[1,160,128]{2,1,0:T(8,128)S(1)} %dynamic-slice_add_fusion.1), channel_id=1, source_target_pairs={{0,2},{1,3},{2,0},{3,1},{4,6},{5,7},{6,4},{7,5},{8,10},{9,11},{10,... | collective-permute-start | bytes 245768 | tf_op jit(solution)/shard_map/ppermute | solution.py:61
  37.0 5.3 %collective-permute-start.8 = (f32[1,160,128]{2,1,0:T(8,128)S(1)}, f32[1,160,128]{2,1,0:T(8,128)S(1)}, u32[]{:S(2)}, u32[]{:S(2)}) collective-permute-start(f32[1,160,128]{2,1,0:T(8,128)S(1)} %dynamic-slice_add_fusion.1), channel_id=1, source_target_pairs={{0,3},{1,2},{2,1},{3,0},{4,7},{5,6},{6,5},{7,4},{8,11},{9,10},{10,... | collective-permute-start | bytes 245768 | tf_op jit(solution)/shard_map/ppermute | solution.py:61
  37.5 14.7 %collective-permute-start.2 = (f32[1,96,3,128]{3,1,2,0:T(8,128)S(1)}, f32[1,96,3,128]{3,1,2,0:T(8,128)S(1)}, u32[]{:S(2)}, u32[]{:S(2)}) collective-permute-start(f32[1,96,3,128]{3,1,2,0:T(8,128)S(1)} %get-tuple-element.93), channel_id=1, source_target_pairs={{0,4},{4,8},{8,12},{12,16},{16,20},{20,24},{24,28},{1,5},{5,9},{9,... | collective-permute-start | bytes 442376 | tf_op jit(solution)/shard_map/ppermute | solution.py:16
  38.8 13.4 %collective-permute-start.3 = (f32[1,96,3,128]{3,1,2,0:T(8,128)S(1)}, f32[1,96,3,128]{3,1,2,0:T(8,128)S(1)}, u32[]{:S(2)}, u32[]{:S(2)}) collective-permute-start(f32[1,96,3,128]{3,1,2,0:T(8,128)S(1)} %get-tuple-element.94), channel_id=1, source_target_pairs={{4,0},{8,4},{12,8},{16,12},{20,16},{24,20},{28,24},{5,1},{9,5},{13... | collective-permute-start | bytes 442376 | tf_op jit(solution)/shard_map/ppermute | solution.py:17
  42.3 9.8 %collective-permute-start.9 = (f32[1,160,128]{2,1,0:T(8,128)S(1)}, f32[1,160,128]{2,1,0:T(8,128)S(1)}, u32[]{:S(2)}, u32[]{:S(2)}) collective-permute-start(f32[1,160,128]{2,1,0:T(8,128)S(1)} %add_add_fusion), channel_id=1, source_target_pairs={{0,16},{4,20},{8,24},{12,28},{16,0},{20,4},{24,8},{28,12},{1,17},{... | collective-permute-start | bytes 245768 | tf_op jit(solution)/shard_map/ppermute | solution.py:61
  52.1 4.5 %collective-permute-start.10 = (f32[1,160,128]{2,1,0:T(8,128)S(1)}, f32[1,160,128]{2,1,0:T(8,128)S(1)}, u32[]{:S(2)}, u32[]{:S(2)}) collective-permute-start(f32[1,160,128]{2,1,0:T(8,128)S(1)} %add.523), channel_id=1, source_target_pairs={{0,8},{4,12},{8,0},{12,4},{16,24},{20,28},{24,16},{28,20},{1,9},{5... | collective-permute-start | bytes 245768 | tf_op jit(solution)/shard_map/ppermute | solution.py:67
  56.7 4.4 %collective-permute-start.11 = (f32[2,160,128]{2,1,0:T(8,128)S(1)}, f32[2,160,128]{2,1,0:T(8,128)S(1)}, u32[]{:S(2)}, u32[]{:S(2)}) collective-permute-start(f32[2,160,128]{2,1,0:T(8,128)S(1)} %pad_maximum_fusion.3), channel_id=1, source_target_pairs={{0,4},{4,0},{8,12},{12,8},{16,20},{20,16},{24,28},{28,24},{1,5},{5... | collective-permute-start | bytes 491528 | tf_op jit(solution)/shard_map/ppermute | solution.py:67

commit v3 on v2

--- a/solution.py
+++ b/solution.py
@@ -35,7 +35,8 @@
 def tree_psum(terms):
     shapes = [t.shape for t in terms]
     sizes = [math.prod(s) for s in shapes]
-    total = sum(sizes)
+    rooms = [-(-size // 1024) * 1024 for size in sizes]
+    total = sum(rooms)
     strip_bits = low_bits(lax.axis_size("strip"))
     slide_bits = low_bits(lax.axis_size("slide"))
     scatter = [("strip", b) for b in strip_bits[:2]]
@@ -44,7 +45,7 @@
     pieces = 2 ** len(scatter)
     rows = -(-total // (pieces * 128))
     rows = -(-rows // 8) * 8
-    flat = jnp.concatenate([t.reshape(-1) for t in terms])
+    flat = jnp.concatenate([jnp.pad(t.reshape(-1), (0, room - size)) for t, size, room in zip(terms, sizes, rooms)])
     flat = jnp.pad(flat, (0, pieces * rows * 128 - total)).reshape(pieces, rows, 128)
     for axis, bit in scatter:
         size = lax.axis_size(axis)
@@ -71,9 +72,9 @@
     flat = flat.reshape(-1)
     out = []
     offset = 0
-    for shape, size in zip(shapes, sizes):
+    for shape, size, room in zip(shapes, sizes, rooms):
         out.append(flat[offset : offset + size].reshape(shape))
-        offset += size
+        offset += room
     return out
 
 
@@ -149,22 +150,22 @@
                 * d_padded[:, :, 6 - a : 6 - a + rows, 6 - b : 6 - b + cols]
             )
             taps.append(jnp.sum(d_conv * padded[:, :, a : a + rows, b : b + cols], axis=(0, 2, 3)))
-    kernel_grad = jnp.stack(taps, axis=1).reshape(chans, kernel, kernel)
+    pixel_count = slides_here * lax.axis_size("slide") * rows * lax.axis_size("strip") * cols
+    scale = 1.0 / math.sqrt(float(pixel_count))
     terms = (
-        kernel_grad,
+        jnp.stack(taps, axis=0),
         jnp.sum(d_conv, axis=(0, 2, 3)),
         jnp.sum(d_lifted * normed, axis=(0, 2, 3)),
         jnp.sum(d_lifted, axis=(0, 2, 3)),
         jnp.einsum("scrw,sfrw->cf", lifted, d_pre, preferred_element_type=jnp.float32),
         jnp.sum(d_pre.astype(jnp.float32), axis=(0, 2, 3)),
-        jnp.einsum("sfrw,scrw->fc", act, d_branch, preferred_element_type=jnp.float32),
+        jnp.einsum("scrw,sfrw->cf", d_branch, act, preferred_element_type=jnp.float32),
         jnp.sum(d_branch.astype(jnp.float32), axis=(0, 2, 3)),
         jnp.sum(upstream * branch, axis=(0, 2, 3)),
     )
-    pixel_count = slides_here * lax.axis_size("slide") * rows * lax.axis_size("strip") * cols
-    scale = 1.0 / math.sqrt(float(pixel_count))
-    g = tree_psum(terms)
-    g = [item * scale for item in g]
+    g = tree_psum([item * scale for item in terms])
+    g[0] = g[0].reshape(kernel, kernel, chans).transpose(2, 0, 1)
+    g[6] = g[6].T
     return (image_grad.astype(jnp.bfloat16), g[0], g[1], g[2], g[3], g[4], g[5], g[6], g[7], g[8])
 
 

time: 65.3 us -> 63.4 us (0.971)
  other arithmetic: 13.7 us -> 12.6 us
  local copies, waits for them, and re-layouts: 9.8 us -> 8.73 us
    concatenate x1, local copies, waits for them, and re-layouts: 1.69 us -> 0.01 us  [tree_psum(): jnp.concatenate([jnp.pad(t.reshape(-1), (0, room - size)) for t, size, ro...]
    unnamed x23 -> x29, local copies, waits for them, and re-layouts: 1.64 us -> 0.12 us
    slice x0 -> x5, local copies, waits for them, and re-layouts: none -> 1.46 us  [tree_psum(): out.append(flat[offset:offset + size].reshape(shape))]
    transpose x0 -> x2, local copies, waits for them, and re-layouts: none -> 1.28 us  [the longest x1 0.67 us: on_device(): g[6] = g[6].T]
    mul x4 -> x7, other arithmetic: 1.22 us -> 0.03 us  [on_device(): g = tree_psum([item * scale for item in terms])]
    mul x3 -> x1, local copies, waits for them, and re-layouts: 0.99 us -> 0.08 us  [on_device(): g = tree_psum([item * scale for item in terms])]
where the time goes in v3:
time: 63.4 us; the launch traced here: 63 us
  starting transfers between devices  19.3 us (30%)
  waiting for transfers between devices  16.2 us (26%)
  other arithmetic  12.6 us (20%)
  local copies, waits for them, and re-layouts  8.73 us (14%)
  matrix products  4.99 us (8%)
  between operations  1.24 us (2%)
    ppermute x4, waiting for transfers between devices, tree_psum(): got = [lax.ppermute(flat, axis, xor_pairs(size, mask)) for mask in masks]  8.27 us
    ppermute x4, starting transfers between devices, tree_psum(): got = [lax.ppermute(flat, axis, xor_pairs(size, mask)) for mask in masks]  7.27 us
    ppermute x2, starting transfers between devices, tree_psum(): flat = keep + lax.ppermute(give, axis, xor_pairs(size, bit))  5.42 us
    convert_element_type x1, other arithmetic, on_device(): image_grad.astype(jnp.bfloat16)  4.33 us
    ppermute x2, waiting for transfers between devices, tree_psum(): got = lax.ppermute(flat, axis, xor_pairs(size, bit))  4.08 us
    ppermute x2, waiting for transfers between devices, tree_psum(): flat = keep + lax.ppermute(give, axis, xor_pairs(size, bit))  3.88 us
    ppermute x2, starting transfers between devices, with_halo(): before = lax.ppermute(last, axis, up)  3.7 us
    reduce_sum x1, other arithmetic, on_device(): centre = conv - jnp.mean(conv, axis=1, keepdims=True)  3.07 us
  transfers between devices with their start and end apart: 12, of which 6 were waited for; matrix products, arithmetic and copies ran while one was open for 15% of the time, Pallas kernels for 0%

profile of v3, /device:TPU:0, one launch (start us, length us, event | category | flops | bytes accessed | tf_op | source)
XLA Modules:
  0.0 63.0 jit_solution(11891463253630249565)
XLA Ops:
  0.7 1.0 %fusion.207 = (bf16[1,96,3,128]{3,1,2,0:T(8,128)(2,1)S(1)}, bf16[1,96,3,128]{3,1,2,0:T(8,128)(2,1)S(1)}) fusion(bf16[1,96,6,128]{3,1,2,0:T(8,128)(2,1)} %param.11), kind=kLoop, calls=%fused_computation.467 | loop fusion | bytes 294912 | tf_op jit(solution)/shard_map/slice | solution.py:14
  1.7 2.4 %collective-permute-start = (bf16[1,96,3,128]{3,1,2,0:T(8,128)(2,1)S(1)}, bf16[1,96,3,128]{3,1,2,0:T(8,128)(2,1)S(1)}, u32[]{:S(2)}, u32[]{:S(2)}) collective-permute-start(bf16[1,96,3,128]{3,1,2,0:T(8,128)(2,1)S(1)} %get-tuple-element.87), channel_id=1, source_target_pairs={{0,4},{4,8},{8,12},{12,16},{16,20},{20,24},{24,28},{1,5},{5,9},{9,... | collective-permute-start | bytes 221192 | tf_op jit(solution)/shard_map/ppermute | solution.py:16
  4.1 1.3 %collective-permute-start.1 = (bf16[1,96,3,128]{3,1,2,0:T(8,128)(2,1)S(1)}, bf16[1,96,3,128]{3,1,2,0:T(8,128)(2,1)S(1)}, u32[]{:S(2)}, u32[]{:S(2)}) collective-permute-start(bf16[1,96,3,128]{3,1,2,0:T(8,128)(2,1)S(1)} %get-tuple-element.88), channel_id=1, source_target_pairs={{4,0},{8,4},{12,8},{16,12},{20,16},{24,20},{28,24},{5,1},{9,5},{13... | collective-permute-start | bytes 221192 | tf_op jit(solution)/shard_map/ppermute | solution.py:17
  5.4 1.0 %slice_bitcast_fusion.50 = (f32[96]{0:T(128)S(1)}, f32[96]{0:T(128)S(1)}, f32[96]{0:T(128)S(1)}, f32[96]{0:T(128)S(1)}, f32[96]{0:T(128)S(1)}, /*index=5*/f32[96...) fusion(f32[96,7,7]{0,2,1:T(8,128)} %param.13), kind=kLoop, calls=%fused_computation.458 | loop fusion | bytes 14592 | tf_op jit(solution)/shard_map/mul | solution.py:149
  6.4 1.0 %slice_bitcast_fusion.49 = (f32[96]{0:T(128)S(1)}, f32[96]{0:T(128)S(1)}, f32[96]{0:T(128)S(1)}, f32[96]{0:T(128)S(1)}, f32[96]{0:T(128)S(1)}, /*index=5*/f32[96...) fusion(f32[96,7,7]{0,2,1:T(8,128)} %param.13), kind=kLoop, calls=%fused_computation.457 | loop fusion | bytes 14592 | tf_op jit(solution)/shard_map/mul | solution.py:113
  7.4 0.9 %slice_bitcast_fusion.48 = (f32[96]{0:T(128)S(1)}, f32[96]{0:T(128)S(1)}, f32[96]{0:T(128)S(1)}, f32[96]{0:T(128)S(1)}, f32[96]{0:T(128)S(1)}, /*index=5*/f32[96...) fusion(f32[96,7,7]{0,2,1:T(8,128)} %param.13), kind=kLoop, calls=%fused_computation.456 | loop fusion | bytes 8448 | tf_op jit(solution)/shard_map/mul | solution.py:113
  8.3 1.1 %convert_reduce_fusion.1 = f32[96]{0:T(128)S(1)} fusion(bf16[1,96,6,128]{3,1,2,0:T(8,128)(2,1)} %param.12, f32[96]{0:T(128)} %param.21), kind=kLoop, calls=%fused_computation.365 | loop fusion | flops 368544 | bytes 148224 | tf_op jit(solution)/shard_map/reduce_sum | solution.py:163
  9.4 1.0 %constant_dynamic-update-slice_fusion = (bf16[1,96,9,128]{3,1,2,0:T(8,128)(2,1)S(1)}, bf16[1,96,9,128]{3,1,2,0:T(8,128)(2,1)S(1)}) fusion(bf16[1,96,9,128]{3,1,2,0:T(8,128)(2,1)S(1)} %constant_dynamic-update-slice_fusion.1, bf16[1,96,6,128]{3,1,2,0:T(8,128)(2,1)} %param.11), kind=kLoop, calls=%fused_computation.391 | loop fusion | bytes 442368 | tf_op jit(solution)/shard_map/concatenate | solution.py:18
  10.4 0.3 fusion.27
  10.8 3.1 %fusion.203 = (f32[6,128]{1,0:T(8,128)S(1)}, f32[1,96,6,128]{3,1,2,0:T(8,128)S(1)}) fusion(bf16[1,96,12,134]{3,1,2,0:T(8,128)(2,1)S(1)} %fusion.27, f32[96]{0:T(128)S(1)} %get-tuple-element.136, f32[96]{0:T(128)S(1)} %get-tuple-element.137, f32[96]{0:T(128)S(1)} %get-tuple-element.90, bf16[1,96,9,128]{3,1,2,0:T(8,128)(2,1)S(1)} %constant_dynamic-update-slice_fusion.2, ...), kind=kLoop, calls=%fused_computation.464 | loop fusion | flops 10910976 | bytes 7542528 | tf_op jit(solution)/shard_map/reduce_sum | solution.py:116
  14.0 2.8 %fusion.9 = (bf16[384,6,128]{0,2,1:T(8,128)(2,1)S(1)}, f32[384,6,128]{0,2,1:T(8,128)S(1)}) fusion(f32[384]{0:T(512)S(1)} %copy-done.8, bf16[96,384]{1,0:T(8,128)(2,1)S(1)} %copy-done, f32[1,96,6,128]{3,1,2,0:T(8,128)S(1)} %get-tuple-element.73, f32[96]{0:T(128)S(1)} %copy-done.5, f32[96]{0:T(128)S(1)} %copy-done.3, f32[6,128]{1,0:T(8,128)S(1)} %add_rsqrt_fusion, ...), kind=kOutput, calls=%fused_computation.15 | convolution fusion | flops 76455936 | bytes 2146560 | tf_op jit(solution)/shard_map/scrw,cf->sfrw/dot_general | solution.py:123
  16.9 0.7 %convert_reduce_fusion = (f32[384]{0:T(512)S(1)}, bf16[384,6,128]{0,2,1:T(8,128)(2,1)S(1)}) fusion(f32[384,6,128]{0,2,1:T(8,128)S(1)} %get-tuple-element.142, bf16[384,96]{0,1:T(8,128)(2,1)S(1)} %copy-done.7, bf16[1,96,6,128]{3,1,2,0:T(8,128)(2,1)S(1)} %copy-done.2, f32[96]{0:T(128)S(1)} %copy-done.4), kind=kOutput, calls=%fused_computation.31 | convolution fusion | flops 60382848 | bytes 1992576 | tf_op jit(solution)/shard_map/scrw,fc->sfrw/dot_general | solution.py:132
  17.6 0.3 fusion.21
  17.9 0.4 fusion.185
  18.3 0.1 fusion.189
  18.4 1.2 %fusion.125 = (f32[96]{0:T(128)S(1)}, f32[96]{0:T(128)S(1)}, f32[96]{0:T(128)S(1)}, f32[96]{0:T(128)S(1)}, f32[96]{0:T(128)S(1)}, /*index=5*/f32[96]{0:T(128)S(1...) fusion(bf16[1,96,12,134]{3,1,2,0:T(8,128)(2,1)S(1)} %fusion.27,, ...), kind=kLoop, calls=%fused_computation.254 | loop fusion | flops 4495680 | bytes 3558528 | tf_op jit(solution)/shard_map/reduce_sum | solution.py:152
  19.6 0.7 %fusion.122 = (f32[96]{0:T(128)S(1)}, f32[96]{0:T(128)S(1)}, f32[96]{0:T(128)S(1)}, f32[96]{0:T(128)S(1)}, f32[96]{0:T(128)S(1)}, /*index=5*/f32[96]{0:T(128)S(1...) fusion(f32[1,96,6,128]{3,1,2,0:T(8,128)S(1)} %get-tuple-element, ...), kind=kLoop, calls=%fused_computation.251 | loop fusion | flops 2947776 | bytes 2217216 | tf_op jit(solution)/shard_map/reduce_sum | solution.py:152
  20.3 1.1 %fusion.104 = (f32[96]{0:T(128)S(1)}, f32[96]{0:T(128)S(1)}, f32[96]{0:T(128)S(1)}, f32[96]{0:T(128)S(1)}, f32[96]{0:T(128)S(1)}, /*index=5*/f32[96]{0:T(128)S(1...) fusion(f32[1,96,6,128]{3,1,2,0:T(8,128)S(1)} %get-tuple-element, ...), kind=kLoop, calls=%fused_computation.233 | loop fusion | flops 3979584 | bytes 2956032 | tf_op jit(solution)/shard_map/reduce_sum | solution.py:152
  21.4 0.1 stack.199
  21.6 0.1 mul.1338
  21.7 0.1 reduce_sum.586
  21.8 0.3 fusion.22
  22.2 0.4 fusion.20
  22.7 3.4 %collective-permute-start.4 = (f32[2,168,128]{2,1,0:T(8,128)S(1)}, f32[2,168,128]{2,1,0:T(8,128)S(1)}, u32[]{:S(2)}, u32[]{:S(2)}) collective-permute-start(f32[2,168,128]{2,1,0:T(8,128)S(1)} %constant_dynamic-slice_fusion.1), channel_id=1, source_target_pairs={{0,4},{4,0},{8,12},{12,8},{16,20},{20,16},{24,28},{28,24},{1,5},{5... | collective-permute-start | bytes 516104 | tf_op jit(solution)/shard_map/ppermute | solution.py:56
  26.1 1.0 %collective-permute-done.4 = f32[2,168,128]{2,1,0:T(8,128)S(1)} collective-permute-done((f32[2,168,128]{2,1,0:T(8,128)S(1)}, f32[2,168,128]{2,1,0:T(8,128)S(1)}, u32[]{:S(2)}, u32[]{:S(2)}) %collective-permute-start.4) | collective-permute-done | bytes 172064 | tf_op jit(solution)/shard_map/ppermute | solution.py:56
  27.2 2.0 %collective-permute-start.5 = (f32[1,168,128]{2,1,0:T(8,128)S(1)}, f32[1,168,128]{2,1,0:T(8,128)S(1)}, u32[]{:S(2)}, u32[]{:S(2)}) collective-permute-start(f32[1,168,128]{2,1,0:T(8,128)S(1)} %constant_dynamic-slice_fusion), channel_id=1, source_target_pairs={{0,8},{4,12},{8,0},{12,4},{16,24},{20,28},{24,16},{28,20},{1,9},{5... | collective-permute-start | bytes 258056 | tf_op jit(solution)/shard_map/ppermute | solution.py:56
  29.3 2.8 %collective-permute-done.5 = f32[1,168,128]{2,1,0:T(8,128)S(1)} collective-permute-done((f32[1,168,128]{2,1,0:T(8,128)S(1)}, f32[1,168,128]{2,1,0:T(8,128)S(1)}, u32[]{:S(2)}, u32[]{:S(2)}) %collective-permute-start.5) | collective-permute-done | bytes 86048 | tf_op jit(solution)/shard_map/ppermute | solution.py:56
  32.1 1.6 %collective-permute-start.6 = (f32[1,168,128]{2,1,0:T(8,128)S(1)}, f32[1,168,128]{2,1,0:T(8,128)S(1)}, u32[]{:S(2)}, u32[]{:S(2)}) collective-permute-start(f32[1,168,128]{2,1,0:T(8,128)S(1)} %dynamic-slice_add_fusion.1), channel_id=1, source_target_pairs={{0,1},{1,0},{2,3},{3,2},{4,5},{5,4},{6,7},{7,6},{8,9},{9,8},{10,11... | collective-permute-start | bytes 258056 | tf_op jit(solution)/shard_map/ppermute | solution.py:62
  33.7 1.5 %collective-permute-start.7 = (f32[1,168,128]{2,1,0:T(8,128)S(1)}, f32[1,168,128]{2,1,0:T(8,128)S(1)}, u32[]{:S(2)}, u32[]{:S(2)}) collective-permute-start(f32[1,168,128]{2,1,0:T(8,128)S(1)} %dynamic-slice_add_fusion.1), channel_id=1, source_target_pairs={{0,2},{1,3},{2,0},{3,1},{4,6},{5,7},{6,4},{7,5},{8,10},{9,11},{10,... | collective-permute-start | bytes 258056 | tf_op jit(solution)/shard_map/ppermute | solution.py:62
  35.2 0.5 collective-permute-start.8
  35.7 1.3 %collective-permute-start.2 = (f32[1,96,3,128]{3,1,2,0:T(8,128)S(1)}, f32[1,96,3,128]{3,1,2,0:T(8,128)S(1)}, u32[]{:S(2)}, u32[]{:S(2)}) collective-permute-start(f32[1,96,3,128]{3,1,2,0:T(8,128)S(1)} %get-tuple-element.81), channel_id=1, source_target_pairs={{0,4},{4,8},{8,12},{12,16},{16,20},{20,24},{24,28},{1,5},{5,9},{9,... | collective-permute-start | bytes 442376 | tf_op jit(solution)/shard_map/ppermute | solution.py:16
  37.0 1.5 %collective-permute-start.3 = (f32[1,96,3,128]{3,1,2,0:T(8,128)S(1)}, f32[1,96,3,128]{3,1,2,0:T(8,128)S(1)}, u32[]{:S(2)}, u32[]{:S(2)}) collective-permute-start(f32[1,96,3,128]{3,1,2,0:T(8,128)S(1)} %get-tuple-element.82), channel_id=1, source_target_pairs={{4,0},{8,4},{12,8},{16,12},{20,16},{24,20},{28,24},{5,1},{9,5},{13... | collective-permute-start | bytes 442376 | tf_op jit(solution)/shard_map/ppermute | solution.py:17
  38.5 0.6 collective-permute-done.7
  39.1 1.5 %collective-permute-done.8 = f32[1,168,128]{2,1,0:T(8,128)S(1)} collective-permute-done((f32[1,168,128]{2,1,0:T(8,128)S(1)}, f32[1,168,128]{2,1,0:T(8,128)S(1)}, u32[]{:S(2)}, u32[]{:S(2)}) %collective-permute-start.8) | collective-permute-done | bytes 86048 | tf_op jit(solution)/shard_map/ppermute | solution.py:62
  40.6 3.7 %collective-permute-start.9 = (f32[1,168,128]{2,1,0:T(8,128)S(1)}, f32[1,168,128]{2,1,0:T(8,128)S(1)}, u32[]{:S(2)}, u32[]{:S(2)}) collective-permute-start(f32[1,168,128]{2,1,0:T(8,128)S(1)} %add_add_fusion), channel_id=1, source_target_pairs={{0,16},{4,20},{8,24},{12,28},{16,0},{20,4},{24,8},{28,12},{1,17},{... | collective-permute-start | bytes 258056 | tf_op jit(solution)/shard_map/ppermute | solution.py:62
  44.3 6.2 %collective-permute-done.9 = f32[1,168,128]{2,1,0:T(8,128)S(1)} collective-permute-done((f32[1,168,128]{2,1,0:T(8,128)S(1)}, f32[1,168,128]{2,1,0:T(8,128)S(1)}, u32[]{:S(2)}, u32[]{:S(2)}) %collective-permute-start.9) | collective-permute-done | bytes 86048 | tf_op jit(solution)/shard_map/ppermute | solution.py:62
  50.5 0.1 collective-permute-start.10
  50.6 0.4 select_maximum_fusion
  51.0 4.1 %collective-permute-done.10 = f32[1,168,128]{2,1,0:T(8,128)S(1)} collective-permute-done((f32[1,168,128]{2,1,0:T(8,128)S(1)}, f32[1,168,128]{2,1,0:T(8,128)S(1)}, u32[]{:S(2)}, u32[]{:S(2)}) %collective-permute-start.10) | collective-permute-done | bytes 86048 | tf_op jit(solution)/shard_map/ppermute | solution.py:68
  55.1 0.1 collective-permute-start.11
  55.2 4.3 %fusion.188 = bf16[1,96,6,128]{3,1,2,0:T(8,128)(2,1)} fusion(f32[1,96,12,134]{3,1,2,0:T(8,128)S(1)} %select_maximum_fusion, f32[1,96,6,128]{3,1,2,0:T(8,128)S(1)} %get-tuple-element.71, f32[1,96,3,128]{3,1,2,0:T(8,128)S(1)} %collective-permute-done.2, f32[1,96,3,128]{3,1,2,0:T(8,128)S(1)} %collective-permute-done.3, ...), kind=kLoop, calls=%fused_computation.368 | loop fusion | flops 7815168 | bytes 13289856 | tf_op jit(solution)/shard_map/convert_element_type | solution.py:169
  59.6 0.3 slice.755
  59.8 0.1 slice.762
  60.0 0.5 fusion.205
  60.5 0.6 slice.871
  61.1 0.6 slice_bitcast_fusion.1
  61.7 0.7 %slice_bitcast_fusion = f32[384,96]{0,1:T(8,128)} fusion(f32[224,384]{1,0:T(8,128)S(1)} %slice.762), kind=kLoop, calls=%fused_computation.374 | loop fusion | bytes 294912 | tf_op jit(solution)/shard_map/transpose | solution.py:168
  62.3 0.7 %reshape.363 = f32[96,384]{1,0:T(8,128)} reshape(f32[36864]{0:T(1024)S(1)} %slice.870) | data formatting | bytes 294912 | tf_op jit(solution)/shard_map/reshape | solution.py:76
  (63 shorter events, 0.5 us)
Async XLA Ops:
  0.6 13.3 %copy-start = (bf16[96,384]{1,0:T(8,128)(2,1)S(1)}, bf16[96,384]{1,0:T(8,128)(2,1)}, u32[]{:S(2)}) copy-start(bf16[96,384]{1,0:T(8,128)(2,1)} %param.17) | copy-start | bytes 221188
  0.7 9.8 %copy-start.1 = (bf16[1,96,6,128]{3,1,2,0:T(8,128)(2,1)S(1)}, bf16[1,96,6,128]{3,1,2,0:T(8,128)(2,1)}, u32[]{:S(2)}) copy-start(bf16[1,96,6,128]{3,1,2,0:T(8,128)(2,1)} %param.11) | copy-start | bytes 442372
  0.7 10.1 %copy-start.6 = (f32[96]{0:T(128)S(1)}, f32[96]{0:T(128)}, u32[]{:S(2)}) copy-start(f32[96]{0:T(128)} %param.14) | copy-start | bytes 1156
  1.7 7.7 %collective-permute-start = (bf16[1,96,3,128]{3,1,2,0:T(8,128)(2,1)S(1)}, bf16[1,96,3,128]{3,1,2,0:T(8,128)(2,1)S(1)}, u32[]{:S(2)}, u32[]{:S(2)}) collective-permute-start(bf16[1,96,3,128]{3,1,2,0:T(8,128)(2,1)S(1)} %get-tuple-element.87), channel_id=1, source_target_pairs={{0,4},{4,8},{8,12},{12,16},{16,20},{20,24},{24,28},{1,5},{5,9},{9,... | collective-permute-start | bytes 221192 | tf_op jit(solution)/shard_map/ppermute | solution.py:16
  4.1 6.3 %collective-permute-start.1 = (bf16[1,96,3,128]{3,1,2,0:T(8,128)(2,1)S(1)}, bf16[1,96,3,128]{3,1,2,0:T(8,128)(2,1)S(1)}, u32[]{:S(2)}, u32[]{:S(2)}) collective-permute-start(bf16[1,96,3,128]{3,1,2,0:T(8,128)(2,1)S(1)} %get-tuple-element.88), channel_id=1, source_target_pairs={{4,0},{8,4},{12,8},{16,12},{20,16},{24,20},{28,24},{5,1},{9,5},{13... | collective-permute-start | bytes 221192 | tf_op jit(solution)/shard_map/ppermute | solution.py:17
  10.7 3.2 %copy-start.3 = (f32[96]{0:T(128)S(1)}, f32[96]{0:T(128)}, u32[]{:S(2)}) copy-start(f32[96]{0:T(128)} %param.15) | copy-start | bytes 1156
  10.7 3.2 %copy-start.5 = (f32[96]{0:T(128)S(1)}, f32[96]{0:T(128)}, u32[]{:S(2)}) copy-start(f32[96]{0:T(128)} %param.16) | copy-start | bytes 1156
  10.8 3.2 %copy-start.8 = (f32[384]{0:T(512)S(1)}, f32[384]{0:T(512)}, u32[]{:S(2)}) copy-start(f32[384]{0:T(512)} %param.18) | copy-start | bytes 4612
  14.0 2.9 %copy-start.2 = (bf16[1,96,6,128]{3,1,2,0:T(8,128)(2,1)S(1)}, bf16[1,96,6,128]{3,1,2,0:T(8,128)(2,1)}, u32[]{:S(2)}) copy-start(bf16[1,96,6,128]{3,1,2,0:T(8,128)(2,1)} %param.12) | copy-start | bytes 442372
  14.0 2.9 %copy-start.4 = (f32[96]{0:T(128)S(1)}, f32[96]{0:T(128)}, u32[]{:S(2)}) copy-start(f32[96]{0:T(128)} %param.21) | copy-start | bytes 1156
  14.0 2.9 %copy-start.7 = (bf16[384,96]{0,1:T(8,128)(2,1)S(1)}, bf16[384,96]{0,1:T(8,128)(2,1)}, u32[]{:S(2)}) copy-start(bf16[384,96]{0,1:T(8,128)(2,1)} %param.19) | copy-start | bytes 221188
  21.4 0.8 %copy-start.9 = (f32[96]{0:T(128)S(1)}, f32[96]{0:T(128)}, u32[]{:S(2)}) copy-start(f32[96]{0:T(128)} %param.20) | copy-start | bytes 1156
  22.7 4.4 %collective-permute-start.4 = (f32[2,168,128]{2,1,0:T(8,128)S(1)}, f32[2,168,128]{2,1,0:T(8,128)S(1)}, u32[]{:S(2)}, u32[]{:S(2)}) collective-permute-start(f32[2,168,128]{2,1,0:T(8,128)S(1)} %constant_dynamic-slice_fusion.1), channel_id=1, source_target_pairs={{0,4},{4,0},{8,12},{12,8},{16,20},{20,16},{24,28},{28,24},{1,5},{5... | collective-permute-start | bytes 516104 | tf_op jit(solution)/shard_map/ppermute | solution.py:56
  27.2 4.9 %collective-permute-start.5 = (f32[1,168,128]{2,1,0:T(8,128)S(1)}, f32[1,168,128]{2,1,0:T(8,128)S(1)}, u32[]{:S(2)}, u32[]{:S(2)}) collective-permute-start(f32[1,168,128]{2,1,0:T(8,128)S(1)} %constant_dynamic-slice_fusion), channel_id=1, source_target_pairs={{0,8},{4,12},{8,0},{12,4},{16,24},{20,28},{24,16},{28,20},{1,9},{5... | collective-permute-start | bytes 258056 | tf_op jit(solution)/shard_map/ppermute | solution.py:56
  32.1 6.4 %collective-permute-start.6 = (f32[1,168,128]{2,1,0:T(8,128)S(1)}, f32[1,168,128]{2,1,0:T(8,128)S(1)}, u32[]{:S(2)}, u32[]{:S(2)}) collective-permute-start(f32[1,168,128]{2,1,0:T(8,128)S(1)} %dynamic-slice_add_fusion.1), channel_id=1, source_target_pairs={{0,1},{1,0},{2,3},{3,2},{4,5},{5,4},{6,7},{7,6},{8,9},{9,8},{10,11... | collective-permute-start | bytes 258056 | tf_op jit(solution)/shard_map/ppermute | solution.py:62
  33.7 5.4 %collective-permute-start.7 = (f32[1,168,128]{2,1,0:T(8,128)S(1)}, f32[1,168,128]{2,1,0:T(8,128)S(1)}, u32[]{:S(2)}, u32[]{:S(2)}) collective-permute-start(f32[1,168,128]{2,1,0:T(8,128)S(1)} %dynamic-slice_add_fusion.1), channel_id=1, source_target_pairs={{0,2},{1,3},{2,0},{3,1},{4,6},{5,7},{6,4},{7,5},{8,10},{9,11},{10,... | collective-permute-start | bytes 258056 | tf_op jit(solution)/shard_map/ppermute | solution.py:62
  35.2 5.4 %collective-permute-start.8 = (f32[1,168,128]{2,1,0:T(8,128)S(1)}, f32[1,168,128]{2,1,0:T(8,128)S(1)}, u32[]{:S(2)}, u32[]{:S(2)}) collective-permute-start(f32[1,168,128]{2,1,0:T(8,128)S(1)} %dynamic-slice_add_fusion.1), channel_id=1, source_target_pairs={{0,3},{1,2},{2,1},{3,0},{4,7},{5,6},{6,5},{7,4},{8,11},{9,10},{10,... | collective-permute-start | bytes 258056 | tf_op jit(solution)/shard_map/ppermute | solution.py:62
  35.7 14.9 %collective-permute-start.2 = (f32[1,96,3,128]{3,1,2,0:T(8,128)S(1)}, f32[1,96,3,128]{3,1,2,0:T(8,128)S(1)}, u32[]{:S(2)}, u32[]{:S(2)}) collective-permute-start(f32[1,96,3,128]{3,1,2,0:T(8,128)S(1)} %get-tuple-element.81), channel_id=1, source_target_pairs={{0,4},{4,8},{8,12},{12,16},{16,20},{20,24},{24,28},{1,5},{5,9},{9,... | collective-permute-start | bytes 442376 | tf_op jit(solution)/shard_map/ppermute | solution.py:16
  37.0 13.6 %collective-permute-start.3 = (f32[1,96,3,128]{3,1,2,0:T(8,128)S(1)}, f32[1,96,3,128]{3,1,2,0:T(8,128)S(1)}, u32[]{:S(2)}, u32[]{:S(2)}) collective-permute-start(f32[1,96,3,128]{3,1,2,0:T(8,128)S(1)} %get-tuple-element.82), channel_id=1, source_target_pairs={{4,0},{8,4},{12,8},{16,12},{20,16},{24,20},{28,24},{5,1},{9,5},{13... | collective-permute-start | bytes 442376 | tf_op jit(solution)/shard_map/ppermute | solution.py:17
  40.6 9.9 %collective-permute-start.9 = (f32[1,168,128]{2,1,0:T(8,128)S(1)}, f32[1,168,128]{2,1,0:T(8,128)S(1)}, u32[]{:S(2)}, u32[]{:S(2)}) collective-permute-start(f32[1,168,128]{2,1,0:T(8,128)S(1)} %add_add_fusion), channel_id=1, source_target_pairs={{0,16},{4,20},{8,24},{12,28},{16,0},{20,4},{24,8},{28,12},{1,17},{... | collective-permute-start | bytes 258056 | tf_op jit(solution)/shard_map/ppermute | solution.py:62
  50.5 4.6 %collective-permute-start.10 = (f32[1,168,128]{2,1,0:T(8,128)S(1)}, f32[1,168,128]{2,1,0:T(8,128)S(1)}, u32[]{:S(2)}, u32[]{:S(2)}) collective-permute-start(f32[1,168,128]{2,1,0:T(8,128)S(1)} %add.537), channel_id=1, source_target_pairs={{0,8},{4,12},{8,0},{12,4},{16,24},{20,28},{24,16},{28,20},{1,9},{5... | collective-permute-start | bytes 258056 | tf_op jit(solution)/shard_map/ppermute | solution.py:68
  55.1 4.4 %collective-permute-start.11 = (f32[2,168,128]{2,1,0:T(8,128)S(1)}, f32[2,168,128]{2,1,0:T(8,128)S(1)}, u32[]{:S(2)}, u32[]{:S(2)}) collective-permute-start(f32[2,168,128]{2,1,0:T(8,128)S(1)} %pad_maximum_fusion.3), channel_id=1, source_target_pairs={{0,4},{4,0},{8,12},{12,8},{16,20},{20,16},{24,28},{28,24},{1,5},{5... | collective-permute-start | bytes 516104 | tf_op jit(solution)/shard_map/ppermute | solution.py:68

commit v4 on v3

--- a/solution.py
+++ b/solution.py
@@ -163,7 +163,9 @@
         jnp.sum(d_branch.astype(jnp.float32), axis=(0, 2, 3)),
         jnp.sum(upstream * branch, axis=(0, 2, 3)),
     )
-    g = tree_psum([item * scale for item in terms])
+    early = tree_psum([terms[i] * scale for i in (6, 7, 8)])
+    late = tree_psum([terms[i] * scale for i in (0, 1, 2, 3, 4, 5)])
+    g = late + early
     g[0] = g[0].reshape(kernel, kernel, chans).transpose(2, 0, 1)
     g[6] = g[6].T
     return (image_grad.astype(jnp.bfloat16), g[0], g[1], g[2], g[3], g[4], g[5], g[6], g[7], g[8])

time: 63.4 us -> 67 us (1.057)
  starting transfers between devices: 19.3 us -> 28 us
  waiting for transfers between devices: 16.2 us -> 10.6 us
    ppermute x4 -> x8, waiting for transfers between devices: 8.27 us -> 1.53 us  [tree_psum(): got = [lax.ppermute(flat, axis, xor_pairs(size, mask)) for mask in masks]]
    ppermute x4 -> x8, starting transfers between devices: 7.27 us -> 10.6 us  [tree_psum(): got = [lax.ppermute(flat, axis, xor_pairs(size, mask)) for mask in masks]]
    ppermute x2 -> x4, starting transfers between devices: 5.42 us -> 7.59 us  [tree_psum(): flat = keep + lax.ppermute(give, axis, xor_pairs(size, bit))]
    ppermute x2 -> x4, starting transfers between devices: 0.14 us -> 2.23 us  [tree_psum(): got = lax.ppermute(flat, axis, xor_pairs(size, bit))]
    transpose x2 -> x0, local copies, waits for them, and re-layouts: 1.28 us -> none  [the longest x1 0.67 us: on_device(): g[6] = g[6].T]
    ppermute x2 -> x4, waiting for transfers between devices: 4.08 us -> 5.22 us  [tree_psum(): got = lax.ppermute(flat, axis, xor_pairs(size, bit))]
    ppermute x2, starting transfers between devices: 3.7 us -> 4.79 us  [with_halo(): before = lax.ppermute(last, axis, up)]
    reshape x1 -> x2, local copies, waits for them, and re-layouts: 0.7 us -> 1.39 us  [tree_psum(): out.append(flat[offset:offset + size].reshape(shape))]
  transfers between devices with their start and end apart: 12 -> 20, of which waited for: 6 -> 5; matrix products, arithmetic and copies ran while one was open for 15% -> 17% of each run, Pallas kernels for 0% -> 0%
where the time goes in v4:
time: 67 us; the launch traced here: 66.7 us
  starting transfers between devices  28 us (42%)
  other arithmetic  12.5 us (19%)
  waiting for transfers between devices  10.6 us (16%)
  local copies, waits for them, and re-layouts  9.31 us (14%)
  matrix products  4.98 us (7%)
  between operations  1.33 us (2%)
    ppermute x8, starting transfers between devices, tree_psum(): got = [lax.ppermute(flat, axis, xor_pairs(size, mask)) for mask in masks]  10.6 us
    ppermute x4, starting transfers between devices, tree_psum(): flat = keep + lax.ppermute(give, axis, xor_pairs(size, bit))  7.59 us
    ppermute x4, waiting for transfers between devices, tree_psum(): got = lax.ppermute(flat, axis, xor_pairs(size, bit))  5.22 us
    ppermute x2, starting transfers between devices, with_halo(): before = lax.ppermute(last, axis, up)  4.79 us
    convert_element_type x1, other arithmetic, on_device(): image_grad.astype(jnp.bfloat16)  4.2 us
    ppermute x4, waiting for transfers between devices, tree_psum(): flat = keep + lax.ppermute(give, axis, xor_pairs(size, bit))  3.83 us
    reduce_sum x1, other arithmetic, on_device(): centre = conv - jnp.mean(conv, axis=1, keepdims=True)  3.07 us
    reduce_sum x3, other arithmetic, on_device(): jnp.sum(d_conv * padded[:, :, a:a + rows, b:b + cols], axis=(0, 2, 3))  2.94 us
  transfers between devices with their start and end apart: 20, of which 5 were waited for; matrix products, arithmetic and copies ran while one was open for 17% of the time, Pallas kernels for 0%

profile of v4, /device:TPU:0, one launch (start us, length us, event | category | flops | bytes accessed | tf_op | source)
XLA Modules:
  0.0 66.7 jit_solution(11740960725539207647)
XLA Ops:
  0.7 1.0 %fusion.209 = (bf16[1,96,3,128]{3,1,2,0:T(8,128)(2,1)S(1)}, bf16[1,96,3,128]{3,1,2,0:T(8,128)(2,1)S(1)}) fusion(bf16[1,96,6,128]{3,1,2,0:T(8,128)(2,1)} %param.11), kind=kLoop, calls=%fused_computation.480 | loop fusion | bytes 294912 | tf_op jit(solution)/shard_map/slice | solution.py:14
  1.7 2.4 %collective-permute-start = (bf16[1,96,3,128]{3,1,2,0:T(8,128)(2,1)S(1)}, bf16[1,96,3,128]{3,1,2,0:T(8,128)(2,1)S(1)}, u32[]{:S(2)}, u32[]{:S(2)}) collective-permute-start(bf16[1,96,3,128]{3,1,2,0:T(8,128)(2,1)S(1)} %get-tuple-element.87), channel_id=1, source_target_pairs={{0,4},{4,8},{8,12},{12,16},{16,20},{20,24},{24,28},{1,5},{5,9},{9,... | collective-permute-start | bytes 221192 | tf_op jit(solution)/shard_map/ppermute | solution.py:16
  4.1 1.3 %collective-permute-start.1 = (bf16[1,96,3,128]{3,1,2,0:T(8,128)(2,1)S(1)}, bf16[1,96,3,128]{3,1,2,0:T(8,128)(2,1)S(1)}, u32[]{:S(2)}, u32[]{:S(2)}) collective-permute-start(bf16[1,96,3,128]{3,1,2,0:T(8,128)(2,1)S(1)} %get-tuple-element.88), channel_id=1, source_target_pairs={{4,0},{8,4},{12,8},{16,12},{20,16},{24,20},{28,24},{5,1},{9,5},{13... | collective-permute-start | bytes 221192 | tf_op jit(solution)/shard_map/ppermute | solution.py:17
  5.4 1.0 %slice_bitcast_fusion.48 = (f32[96]{0:T(128)S(1)}, f32[96]{0:T(128)S(1)}, f32[96]{0:T(128)S(1)}, f32[96]{0:T(128)S(1)}, f32[96]{0:T(128)S(1)}, /*index=5*/f32[96...) fusion(f32[96,7,7]{0,2,1:T(8,128)} %param.13), kind=kLoop, calls=%fused_computation.470 | loop fusion | bytes 14592 | tf_op jit(solution)/shard_map/mul | solution.py:149
  6.4 1.0 %slice_bitcast_fusion.47 = (f32[96]{0:T(128)S(1)}, f32[96]{0:T(128)S(1)}, f32[96]{0:T(128)S(1)}, f32[96]{0:T(128)S(1)}, f32[96]{0:T(128)S(1)}, /*index=5*/f32[96...) fusion(f32[96,7,7]{0,2,1:T(8,128)} %param.13), kind=kLoop, calls=%fused_computation.469 | loop fusion | bytes 14592 | tf_op jit(solution)/shard_map/mul | solution.py:113
  7.4 0.9 %slice_bitcast_fusion.46 = (f32[96]{0:T(128)S(1)}, f32[96]{0:T(128)S(1)}, f32[96]{0:T(128)S(1)}, f32[96]{0:T(128)S(1)}, f32[96]{0:T(128)S(1)}, /*index=5*/f32[96...) fusion(f32[96,7,7]{0,2,1:T(8,128)} %param.13), kind=kLoop, calls=%fused_computation.468 | loop fusion | bytes 8448 | tf_op jit(solution)/shard_map/mul | solution.py:113
  8.3 1.1 %convert_reduce_fusion.1 = f32[96]{0:T(128)S(1)} fusion(bf16[1,96,6,128]{3,1,2,0:T(8,128)(2,1)} %param.12, f32[96]{0:T(128)} %param.21), kind=kLoop, calls=%fused_computation.364 | loop fusion | flops 368544 | bytes 148224 | tf_op jit(solution)/shard_map/reduce_sum | solution.py:163
  9.5 1.0 %constant_dynamic-update-slice_fusion = (bf16[1,96,9,128]{3,1,2,0:T(8,128)(2,1)S(1)}, bf16[1,96,9,128]{3,1,2,0:T(8,128)(2,1)S(1)}) fusion(bf16[1,96,9,128]{3,1,2,0:T(8,128)(2,1)S(1)} %constant_dynamic-update-slice_fusion.1, bf16[1,96,6,128]{3,1,2,0:T(8,128)(2,1)} %param.11), kind=kLoop, calls=%fused_computation.404 | loop fusion | bytes 442368 | tf_op jit(solution)/shard_map/concatenate | solution.py:18
  10.4 0.3 fusion.27
  10.8 3.1 %fusion.204 = (f32[6,128]{1,0:T(8,128)S(1)}, f32[1,96,6,128]{3,1,2,0:T(8,128)S(1)}) fusion(bf16[1,96,12,134]{3,1,2,0:T(8,128)(2,1)S(1)} %fusion.27, f32[96]{0:T(128)S(1)} %get-tuple-element.140, f32[96]{0:T(128)S(1)} %get-tuple-element.141, f32[96]{0:T(128)S(1)} %get-tuple-element.94, bf16[1,96,9,128]{3,1,2,0:T(8,128)(2,1)S(1)} %constant_dynamic-update-slice_fusion.2, ...), kind=kLoop, calls=%fused_computation.476 | loop fusion | flops 10910976 | bytes 7542528 | tf_op jit(solution)/shard_map/reduce_sum | solution.py:116
  14.0 2.8 %fusion.9 = (bf16[384,6,128]{0,2,1:T(8,128)(2,1)S(1)}, f32[384,6,128]{0,2,1:T(8,128)S(1)}) fusion(f32[384]{0:T(512)S(1)} %copy-done.8, bf16[96,384]{1,0:T(8,128)(2,1)S(1)} %copy-done, f32[1,96,6,128]{3,1,2,0:T(8,128)S(1)} %get-tuple-element.73, f32[96]{0:T(128)S(1)} %copy-done.5, f32[96]{0:T(128)S(1)} %copy-done.3, f32[6,128]{1,0:T(8,128)S(1)} %add_rsqrt_fusion, ...), kind=kOutput, calls=%fused_computation.15 | convolution fusion | flops 76455936 | bytes 2146560 | tf_op jit(solution)/shard_map/scrw,cf->sfrw/dot_general | solution.py:123
  16.9 0.7 %convert_reduce_fusion = (f32[384]{0:T(512)S(1)}, bf16[384,6,128]{0,2,1:T(8,128)(2,1)S(1)}) fusion(f32[384,6,128]{0,2,1:T(8,128)S(1)} %get-tuple-element.146, bf16[384,96]{0,1:T(8,128)(2,1)S(1)} %copy-done.7, bf16[1,96,6,128]{3,1,2,0:T(8,128)(2,1)S(1)} %copy-done.2, f32[96]{0:T(128)S(1)} %copy-done.4), kind=kOutput, calls=%fused_computation.31 | convolution fusion | flops 60382848 | bytes 1992576 | tf_op jit(solution)/shard_map/scrw,fc->sfrw/dot_general | solution.py:132
  17.6 0.3 fusion.21
  17.9 0.4 fusion.185
  18.5 1.2 %fusion.125 = (f32[96]{0:T(128)S(1)}, f32[96]{0:T(128)S(1)}, f32[96]{0:T(128)S(1)}, f32[96]{0:T(128)S(1)}, f32[96]{0:T(128)S(1)}, /*index=5*/f32[96]{0:T(128)S(1...) fusion(bf16[1,96,12,134]{3,1,2,0:T(8,128)(2,1)S(1)} %fusion.27,, ...), kind=kLoop, calls=%fused_computation.253 | loop fusion | flops 4495680 | bytes 3558528 | tf_op jit(solution)/shard_map/reduce_sum | solution.py:152
  19.6 0.7 %fusion.122 = (f32[96]{0:T(128)S(1)}, f32[96]{0:T(128)S(1)}, f32[96]{0:T(128)S(1)}, f32[96]{0:T(128)S(1)}, f32[96]{0:T(128)S(1)}, /*index=5*/f32[96]{0:T(128)S(1...) fusion(f32[1,96,6,128]{3,1,2,0:T(8,128)S(1)} %get-tuple-element, ...), kind=kLoop, calls=%fused_computation.250 | loop fusion | flops 2947776 | bytes 2217216 | tf_op jit(solution)/shard_map/reduce_sum | solution.py:152
  20.3 1.1 %fusion.104 = (f32[96]{0:T(128)S(1)}, f32[96]{0:T(128)S(1)}, f32[96]{0:T(128)S(1)}, f32[96]{0:T(128)S(1)}, f32[96]{0:T(128)S(1)}, /*index=5*/f32[96]{0:T(128)S(1...) fusion(f32[1,96,6,128]{3,1,2,0:T(8,128)S(1)} %get-tuple-element, ...), kind=kLoop, calls=%fused_computation.232 | loop fusion | flops 3979584 | bytes 2956032 | tf_op jit(solution)/shard_map/reduce_sum | solution.py:152
  21.4 0.3 fusion.22
  21.8 0.3 copy-done.9
  22.1 0.4 fusion.20
  22.5 0.1 reduce_sum.586
  22.7 3.4 %collective-permute-start.12 = (f32[2,80,128]{2,1,0:T(8,128)S(1)}, f32[2,80,128]{2,1,0:T(8,128)S(1)}, u32[]{:S(2)}, u32[]{:S(2)}) collective-permute-start(f32[2,80,128]{2,1,0:T(8,128)S(1)} %constant_dynamic-slice_fusion.1), channel_id=1, source_target_pairs={{0,4},{4,0},{8,12},{12,8},{16,20},{20,16},{24,28},{28,24},{1,5},{5... | collective-permute-start | bytes 245768 | tf_op jit(solution)/shard_map/ppermute | solution.py:56
  26.1 0.1 stack.199
  26.5 2.4 %collective-permute-start.2 = (f32[1,96,3,128]{3,1,2,0:T(8,128)S(1)}, f32[1,96,3,128]{3,1,2,0:T(8,128)S(1)}, u32[]{:S(2)}, u32[]{:S(2)}) collective-permute-start(f32[1,96,3,128]{3,1,2,0:T(8,128)S(1)} %get-tuple-element.74), channel_id=1, source_target_pairs={{0,4},{4,8},{8,12},{12,16},{16,20},{20,24},{24,28},{1,5},{5,9},{9,... | collective-permute-start | bytes 442376 | tf_op jit(solution)/shard_map/ppermute | solution.py:16
  28.9 1.5 %collective-permute-start.3 = (f32[1,96,3,128]{3,1,2,0:T(8,128)S(1)}, f32[1,96,3,128]{3,1,2,0:T(8,128)S(1)}, u32[]{:S(2)}, u32[]{:S(2)}) collective-permute-start(f32[1,96,3,128]{3,1,2,0:T(8,128)S(1)} %get-tuple-element.75), channel_id=1, source_target_pairs={{4,0},{8,4},{12,8},{16,12},{20,16},{24,20},{28,24},{5,1},{9,5},{13... | collective-permute-start | bytes 442376 | tf_op jit(solution)/shard_map/ppermute | solution.py:17
  30.5 4.0 %collective-permute-start.13 = (f32[1,80,128]{2,1,0:T(8,128)S(1)}, f32[1,80,128]{2,1,0:T(8,128)S(1)}, u32[]{:S(2)}, u32[]{:S(2)}) collective-permute-start(f32[1,80,128]{2,1,0:T(8,128)S(1)} %constant_dynamic-slice_fusion), channel_id=1, source_target_pairs={{0,8},{4,12},{8,0},{12,4},{16,24},{20,28},{24,16},{28,20},{1,9},{5... | collective-permute-start | bytes 122888 | tf_op jit(solution)/shard_map/ppermute | solution.py:56
  34.7 3.8 %collective-permute-done.13 = f32[1,80,128]{2,1,0:T(8,128)S(1)} collective-permute-done((f32[1,80,128]{2,1,0:T(8,128)S(1)}, f32[1,80,128]{2,1,0:T(8,128)S(1)}, u32[]{:S(2)}, u32[]{:S(2)}) %collective-permute-start.13) | collective-permute-done | bytes 40992 | tf_op jit(solution)/shard_map/ppermute | solution.py:56
  38.5 1.6 %collective-permute-start.14 = (f32[1,80,128]{2,1,0:T(8,128)S(1)}, f32[1,80,128]{2,1,0:T(8,128)S(1)}, u32[]{:S(2)}, u32[]{:S(2)}) collective-permute-start(f32[1,80,128]{2,1,0:T(8,128)S(1)} %dynamic-slice_add_fusion.3), channel_id=1, source_target_pairs={{0,1},{1,0},{2,3},{3,2},{4,5},{5,4},{6,7},{7,6},{8,9},{9,8},{10,11... | collective-permute-start | bytes 122888 | tf_op jit(solution)/shard_map/ppermute | solution.py:62
  40.0 1.5 %collective-permute-start.15 = (f32[1,80,128]{2,1,0:T(8,128)S(1)}, f32[1,80,128]{2,1,0:T(8,128)S(1)}, u32[]{:S(2)}, u32[]{:S(2)}) collective-permute-start(f32[1,80,128]{2,1,0:T(8,128)S(1)} %dynamic-slice_add_fusion.3), channel_id=1, source_target_pairs={{0,2},{1,3},{2,0},{3,1},{4,6},{5,7},{6,4},{7,5},{8,10},{9,11},{10,... | collective-permute-start | bytes 122888 | tf_op jit(solution)/shard_map/ppermute | solution.py:62
  41.6 0.5 collective-permute-start.16
  42.1 1.6 %collective-permute-start.6 = (f32[1,96,128]{2,1,0:T(8,128)S(1)}, f32[1,96,128]{2,1,0:T(8,128)S(1)}, u32[]{:S(2)}, u32[]{:S(2)}) collective-permute-start(f32[1,96,128]{2,1,0:T(8,128)S(1)} %dynamic-slice_add_fusion.2), channel_id=1, source_target_pairs={{0,1},{1,0},{2,3},{3,2},{4,5},{5,4},{6,7},{7,6},{8,9},{9,8},{10,11... | collective-permute-start | bytes 147464 | tf_op jit(solution)/shard_map/ppermute | solution.py:62
  43.6 1.5 %collective-permute-start.7 = (f32[1,96,128]{2,1,0:T(8,128)S(1)}, f32[1,96,128]{2,1,0:T(8,128)S(1)}, u32[]{:S(2)}, u32[]{:S(2)}) collective-permute-start(f32[1,96,128]{2,1,0:T(8,128)S(1)} %dynamic-slice_add_fusion.2), channel_id=1, source_target_pairs={{0,2},{1,3},{2,0},{3,1},{4,6},{5,7},{6,4},{7,5},{8,10},{9,11},{10,... | collective-permute-start | bytes 147464 | tf_op jit(solution)/shard_map/ppermute | solution.py:62
  45.1 0.4 select_maximum_fusion
  45.5 0.5 collective-permute-start.8
  46.1 0.4 collective-permute-done.16
  46.5 2.6 %collective-permute-start.17 = (f32[1,80,128]{2,1,0:T(8,128)S(1)}, f32[1,80,128]{2,1,0:T(8,128)S(1)}, u32[]{:S(2)}, u32[]{:S(2)}) collective-permute-start(f32[1,80,128]{2,1,0:T(8,128)S(1)} %add_add_fusion.1), channel_id=1, source_target_pairs={{0,16},{4,20},{8,24},{12,28},{16,0},{20,4},{24,8},{28,12},{1,17},{... | collective-permute-start | bytes 122888 | tf_op jit(solution)/shard_map/ppermute | solution.py:62
  49.1 4.2 %fusion.188 = bf16[1,96,6,128]{3,1,2,0:T(8,128)(2,1)} fusion(f32[1,96,12,134]{3,1,2,0:T(8,128)S(1)} %select_maximum_fusion, f32[1,96,6,128]{3,1,2,0:T(8,128)S(1)} %get-tuple-element.71, f32[1,96,3,128]{3,1,2,0:T(8,128)S(1)} %collective-permute-done.2, f32[1,96,3,128]{3,1,2,0:T(8,128)S(1)} %collective-permute-done.3, ...), kind=kLoop, calls=%fused_computation.367 | loop fusion | flops 7815168 | bytes 13289856 | tf_op jit(solution)/shard_map/convert_element_type | solution.py:171
  53.5 0.8 %collective-permute-start.9 = (f32[1,96,128]{2,1,0:T(8,128)S(1)}, f32[1,96,128]{2,1,0:T(8,128)S(1)}, u32[]{:S(2)}, u32[]{:S(2)}) collective-permute-start(f32[1,96,128]{2,1,0:T(8,128)S(1)} %add_add_fusion), channel_id=1, source_target_pairs={{0,16},{4,20},{8,24},{12,28},{16,0},{20,4},{24,8},{28,12},{1,17},{... | collective-permute-start | bytes 147464 | tf_op jit(solution)/shard_map/ppermute | solution.py:62
  54.3 3.1 %collective-permute-done.18 = f32[1,80,128]{2,1,0:T(8,128)S(1)} collective-permute-done((f32[1,80,128]{2,1,0:T(8,128)S(1)}, f32[1,80,128]{2,1,0:T(8,128)S(1)}, u32[]{:S(2)}, u32[]{:S(2)}) %collective-permute-start.18) | collective-permute-done | bytes 40992 | tf_op jit(solution)/shard_map/ppermute | solution.py:68
  57.4 1.1 %collective-permute-done.9 = f32[1,96,128]{2,1,0:T(8,128)S(1)} collective-permute-done((f32[1,96,128]{2,1,0:T(8,128)S(1)}, f32[1,96,128]{2,1,0:T(8,128)S(1)}, u32[]{:S(2)}, u32[]{:S(2)}) %collective-permute-start.9) | collective-permute-done | bytes 49184 | tf_op jit(solution)/shard_map/ppermute | solution.py:62
  58.6 2.0 %collective-permute-start.10 = (f32[1,96,128]{2,1,0:T(8,128)S(1)}, f32[1,96,128]{2,1,0:T(8,128)S(1)}, u32[]{:S(2)}, u32[]{:S(2)}) collective-permute-start(f32[1,96,128]{2,1,0:T(8,128)S(1)} %add.561), channel_id=1, source_target_pairs={{0,8},{4,12},{8,0},{12,4},{16,24},{20,28},{24,16},{28,20},{1,9},{5... | collective-permute-start | bytes 147464 | tf_op jit(solution)/shard_map/ppermute | solution.py:68
  60.6 2.1 %collective-permute-done.10 = f32[1,96,128]{2,1,0:T(8,128)S(1)} collective-permute-done((f32[1,96,128]{2,1,0:T(8,128)S(1)}, f32[1,96,128]{2,1,0:T(8,128)S(1)}, u32[]{:S(2)}, u32[]{:S(2)}) %collective-permute-start.10) | collective-permute-done | bytes 49184 | tf_op jit(solution)/shard_map/ppermute | solution.py:68
  62.9 0.5 fusion.208
  63.4 0.7 %reshape.370 = f32[96,384]{1,0:T(8,128)} reshape(f32[36864]{0:T(1024)S(1)} %slice.864) | data formatting | bytes 294912 | tf_op jit(solution)/shard_map/reshape | solution.py:76
  64.2 0.6 slice.863
  64.8 0.5 fusion.207
  65.3 0.7 %reshape.366 = f32[96,384]{1,0:T(8,128)} reshape(f32[36864]{0:T(1024)S(1)} %slice.862) | data formatting | bytes 294912 | tf_op jit(solution)/shard_map/reshape | solution.py:76
  66.0 0.7 %reshape_reshape.3 = f32[7,7,96]{2,1,0:T(8,128)} reshape(f32[4704]{0:T(1024)S(1)} %slice.858) | data formatting | bytes 37632 | tf_op jit(solution)/shard_map/reshape;reshape | solution.py:169
  (88 shorter events, 1.1 us)
Async XLA Ops:
  0.6 13.3 %copy-start = (bf16[96,384]{1,0:T(8,128)(2,1)S(1)}, bf16[96,384]{1,0:T(8,128)(2,1)}, u32[]{:S(2)}) copy-start(bf16[96,384]{1,0:T(8,128)(2,1)} %param.17) | copy-start | bytes 221188
  0.7 9.8 %copy-start.1 = (bf16[1,96,6,128]{3,1,2,0:T(8,128)(2,1)S(1)}, bf16[1,96,6,128]{3,1,2,0:T(8,128)(2,1)}, u32[]{:S(2)}) copy-start(bf16[1,96,6,128]{3,1,2,0:T(8,128)(2,1)} %param.11) | copy-start | bytes 442372
  0.7 10.1 %copy-start.6 = (f32[96]{0:T(128)S(1)}, f32[96]{0:T(128)}, u32[]{:S(2)}) copy-start(f32[96]{0:T(128)} %param.14) | copy-start | bytes 1156
  1.7 7.8 %collective-permute-start = (bf16[1,96,3,128]{3,1,2,0:T(8,128)(2,1)S(1)}, bf16[1,96,3,128]{3,1,2,0:T(8,128)(2,1)S(1)}, u32[]{:S(2)}, u32[]{:S(2)}) collective-permute-start(bf16[1,96,3,128]{3,1,2,0:T(8,128)(2,1)S(1)} %get-tuple-element.87), channel_id=1, source_target_pairs={{0,4},{4,8},{8,12},{12,16},{16,20},{20,24},{24,28},{1,5},{5,9},{9,... | collective-permute-start | bytes 221192 | tf_op jit(solution)/shard_map/ppermute | solution.py:16
  4.1 6.3 %collective-permute-start.1 = (bf16[1,96,3,128]{3,1,2,0:T(8,128)(2,1)S(1)}, bf16[1,96,3,128]{3,1,2,0:T(8,128)(2,1)S(1)}, u32[]{:S(2)}, u32[]{:S(2)}) collective-permute-start(bf16[1,96,3,128]{3,1,2,0:T(8,128)(2,1)S(1)} %get-tuple-element.88), channel_id=1, source_target_pairs={{4,0},{8,4},{12,8},{16,12},{20,16},{24,20},{28,24},{5,1},{9,5},{13... | collective-permute-start | bytes 221192 | tf_op jit(solution)/shard_map/ppermute | solution.py:17
  10.8 3.2 %copy-start.3 = (f32[96]{0:T(128)S(1)}, f32[96]{0:T(128)}, u32[]{:S(2)}) copy-start(f32[96]{0:T(128)} %param.15) | copy-start | bytes 1156
  10.8 3.2 %copy-start.5 = (f32[96]{0:T(128)S(1)}, f32[96]{0:T(128)}, u32[]{:S(2)}) copy-start(f32[96]{0:T(128)} %param.16) | copy-start | bytes 1156
  10.8 3.2 %copy-start.8 = (f32[384]{0:T(512)S(1)}, f32[384]{0:T(512)}, u32[]{:S(2)}) copy-start(f32[384]{0:T(512)} %param.18) | copy-start | bytes 4612
  14.0 2.9 %copy-start.2 = (bf16[1,96,6,128]{3,1,2,0:T(8,128)(2,1)S(1)}, bf16[1,96,6,128]{3,1,2,0:T(8,128)(2,1)}, u32[]{:S(2)}) copy-start(bf16[1,96,6,128]{3,1,2,0:T(8,128)(2,1)} %param.12) | copy-start | bytes 442372
  14.0 2.9 %copy-start.4 = (f32[96]{0:T(128)S(1)}, f32[96]{0:T(128)}, u32[]{:S(2)}) copy-start(f32[96]{0:T(128)} %param.21) | copy-start | bytes 1156
  14.0 2.9 %copy-start.7 = (bf16[384,96]{0,1:T(8,128)(2,1)S(1)}, bf16[384,96]{0,1:T(8,128)(2,1)}, u32[]{:S(2)}) copy-start(bf16[384,96]{0,1:T(8,128)(2,1)} %param.19) | copy-start | bytes 221188
  21.4 0.7 copy-start.9
  22.7 7.8 %collective-permute-start.12 = (f32[2,80,128]{2,1,0:T(8,128)S(1)}, f32[2,80,128]{2,1,0:T(8,128)S(1)}, u32[]{:S(2)}, u32[]{:S(2)}) collective-permute-start(f32[2,80,128]{2,1,0:T(8,128)S(1)} %constant_dynamic-slice_fusion.1), channel_id=1, source_target_pairs={{0,4},{4,0},{8,12},{12,8},{16,20},{20,16},{24,28},{28,24},{1,5},{5... | collective-permute-start | bytes 245768 | tf_op jit(solution)/shard_map/ppermute | solution.py:56
  26.5 8.1 %collective-permute-start.4 = (f32[2,96,128]{2,1,0:T(8,128)S(1)}, f32[2,96,128]{2,1,0:T(8,128)S(1)}, u32[]{:S(2)}, u32[]{:S(2)}) collective-permute-start(f32[2,96,128]{2,1,0:T(8,128)S(1)} %constant_dynamic-slice_fusion.3), channel_id=1, source_target_pairs={{0,4},{4,0},{8,12},{12,8},{16,20},{20,16},{24,28},{28,24},{1,5},{5... | collective-permute-start | bytes 294920 | tf_op jit(solution)/shard_map/ppermute | solution.py:56
  26.5 15.5 %collective-permute-start.2 = (f32[1,96,3,128]{3,1,2,0:T(8,128)S(1)}, f32[1,96,3,128]{3,1,2,0:T(8,128)S(1)}, u32[]{:S(2)}, u32[]{:S(2)}) collective-permute-start(f32[1,96,3,128]{3,1,2,0:T(8,128)S(1)} %get-tuple-element.74), channel_id=1, source_target_pairs={{0,4},{4,8},{8,12},{12,16},{16,20},{20,24},{24,28},{1,5},{5,9},{9,... | collective-permute-start | bytes 442376 | tf_op jit(solution)/shard_map/ppermute | solution.py:16
  28.9 14.7 %collective-permute-start.3 = (f32[1,96,3,128]{3,1,2,0:T(8,128)S(1)}, f32[1,96,3,128]{3,1,2,0:T(8,128)S(1)}, u32[]{:S(2)}, u32[]{:S(2)}) collective-permute-start(f32[1,96,3,128]{3,1,2,0:T(8,128)S(1)} %get-tuple-element.75), channel_id=1, source_target_pairs={{4,0},{8,4},{12,8},{16,12},{20,16},{24,20},{28,24},{5,1},{9,5},{13... | collective-permute-start | bytes 442376 | tf_op jit(solution)/shard_map/ppermute | solution.py:17
  30.5 8.0 %collective-permute-start.13 = (f32[1,80,128]{2,1,0:T(8,128)S(1)}, f32[1,80,128]{2,1,0:T(8,128)S(1)}, u32[]{:S(2)}, u32[]{:S(2)}) collective-permute-start(f32[1,80,128]{2,1,0:T(8,128)S(1)} %constant_dynamic-slice_fusion), channel_id=1, source_target_pairs={{0,8},{4,12},{8,0},{12,4},{16,24},{20,28},{24,16},{28,20},{1,9},{5... | collective-permute-start | bytes 122888 | tf_op jit(solution)/shard_map/ppermute | solution.py:56
  34.6 7.0 %collective-permute-start.5 = (f32[1,96,128]{2,1,0:T(8,128)S(1)}, f32[1,96,128]{2,1,0:T(8,128)S(1)}, u32[]{:S(2)}, u32[]{:S(2)}) collective-permute-start(f32[1,96,128]{2,1,0:T(8,128)S(1)} %constant_dynamic-slice_fusion.2), channel_id=1, source_target_pairs={{0,8},{4,12},{8,0},{12,4},{16,24},{20,28},{24,16},{28,20},{1,9},{5... | collective-permute-start | bytes 147464 | tf_op jit(solution)/shard_map/ppermute | solution.py:56
  38.5 7.0 %collective-permute-start.14 = (f32[1,80,128]{2,1,0:T(8,128)S(1)}, f32[1,80,128]{2,1,0:T(8,128)S(1)}, u32[]{:S(2)}, u32[]{:S(2)}) collective-permute-start(f32[1,80,128]{2,1,0:T(8,128)S(1)} %dynamic-slice_add_fusion.3), channel_id=1, source_target_pairs={{0,1},{1,0},{2,3},{3,2},{4,5},{5,4},{6,7},{7,6},{8,9},{9,8},{10,11... | collective-permute-start | bytes 122888 | tf_op jit(solution)/shard_map/ppermute | solution.py:62
  40.0 6.0 %collective-permute-start.15 = (f32[1,80,128]{2,1,0:T(8,128)S(1)}, f32[1,80,128]{2,1,0:T(8,128)S(1)}, u32[]{:S(2)}, u32[]{:S(2)}) collective-permute-start(f32[1,80,128]{2,1,0:T(8,128)S(1)} %dynamic-slice_add_fusion.3), channel_id=1, source_target_pairs={{0,2},{1,3},{2,0},{3,1},{4,6},{5,7},{6,4},{7,5},{8,10},{9,11},{10,... | collective-permute-start | bytes 122888 | tf_op jit(solution)/shard_map/ppermute | solution.py:62
  41.6 4.9 %collective-permute-start.16 = (f32[1,80,128]{2,1,0:T(8,128)S(1)}, f32[1,80,128]{2,1,0:T(8,128)S(1)}, u32[]{:S(2)}, u32[]{:S(2)}) collective-permute-start(f32[1,80,128]{2,1,0:T(8,128)S(1)} %dynamic-slice_add_fusion.3), channel_id=1, source_target_pairs={{0,3},{1,2},{2,1},{3,0},{4,7},{5,6},{6,5},{7,4},{8,11},{9,10},{10,... | collective-permute-start | bytes 122888 | tf_op jit(solution)/shard_map/ppermute | solution.py:62
  42.1 11.4 %collective-permute-start.6 = (f32[1,96,128]{2,1,0:T(8,128)S(1)}, f32[1,96,128]{2,1,0:T(8,128)S(1)}, u32[]{:S(2)}, u32[]{:S(2)}) collective-permute-start(f32[1,96,128]{2,1,0:T(8,128)S(1)} %dynamic-slice_add_fusion.2), channel_id=1, source_target_pairs={{0,1},{1,0},{2,3},{3,2},{4,5},{5,4},{6,7},{7,6},{8,9},{9,8},{10,11... | collective-permute-start | bytes 147464 | tf_op jit(solution)/shard_map/ppermute | solution.py:62
  43.6 9.8 %collective-permute-start.7 = (f32[1,96,128]{2,1,0:T(8,128)S(1)}, f32[1,96,128]{2,1,0:T(8,128)S(1)}, u32[]{:S(2)}, u32[]{:S(2)}) collective-permute-start(f32[1,96,128]{2,1,0:T(8,128)S(1)} %dynamic-slice_add_fusion.2), channel_id=1, source_target_pairs={{0,2},{1,3},{2,0},{3,1},{4,6},{5,7},{6,4},{7,5},{8,10},{9,11},{10,... | collective-permute-start | bytes 147464 | tf_op jit(solution)/shard_map/ppermute | solution.py:62
  45.5 7.9 %collective-permute-start.8 = (f32[1,96,128]{2,1,0:T(8,128)S(1)}, f32[1,96,128]{2,1,0:T(8,128)S(1)}, u32[]{:S(2)}, u32[]{:S(2)}) collective-permute-start(f32[1,96,128]{2,1,0:T(8,128)S(1)} %dynamic-slice_add_fusion.2), channel_id=1, source_target_pairs={{0,3},{1,2},{2,1},{3,0},{4,7},{5,6},{6,5},{7,4},{8,11},{9,10},{10,... | collective-permute-start | bytes 147464 | tf_op jit(solution)/shard_map/ppermute | solution.py:62
  46.5 6.9 %collective-permute-start.17 = (f32[1,80,128]{2,1,0:T(8,128)S(1)}, f32[1,80,128]{2,1,0:T(8,128)S(1)}, u32[]{:S(2)}, u32[]{:S(2)}) collective-permute-start(f32[1,80,128]{2,1,0:T(8,128)S(1)} %add_add_fusion.1), channel_id=1, source_target_pairs={{0,16},{4,20},{8,24},{12,28},{16,0},{20,4},{24,8},{28,12},{1,17},{... | collective-permute-start | bytes 122888 | tf_op jit(solution)/shard_map/ppermute | solution.py:62
  53.3 4.1 %collective-permute-start.18 = (f32[1,80,128]{2,1,0:T(8,128)S(1)}, f32[1,80,128]{2,1,0:T(8,128)S(1)}, u32[]{:S(2)}, u32[]{:S(2)}) collective-permute-start(f32[1,80,128]{2,1,0:T(8,128)S(1)} %add.571), channel_id=1, source_target_pairs={{0,8},{4,12},{8,0},{12,4},{16,24},{20,28},{24,16},{28,20},{1,9},{5... | collective-permute-start | bytes 122888 | tf_op jit(solution)/shard_map/ppermute | solution.py:68
  53.5 5.1 %collective-permute-start.9 = (f32[1,96,128]{2,1,0:T(8,128)S(1)}, f32[1,96,128]{2,1,0:T(8,128)S(1)}, u32[]{:S(2)}, u32[]{:S(2)}) collective-permute-start(f32[1,96,128]{2,1,0:T(8,128)S(1)} %add_add_fusion), channel_id=1, source_target_pairs={{0,16},{4,20},{8,24},{12,28},{16,0},{20,4},{24,8},{28,12},{1,17},{... | collective-permute-start | bytes 147464 | tf_op jit(solution)/shard_map/ppermute | solution.py:62
  58.6 4.2 %collective-permute-start.10 = (f32[1,96,128]{2,1,0:T(8,128)S(1)}, f32[1,96,128]{2,1,0:T(8,128)S(1)}, u32[]{:S(2)}, u32[]{:S(2)}) collective-permute-start(f32[1,96,128]{2,1,0:T(8,128)S(1)} %add.561), channel_id=1, source_target_pairs={{0,8},{4,12},{8,0},{12,4},{16,24},{20,28},{24,16},{28,20},{1,9},{5... | collective-permute-start | bytes 147464 | tf_op jit(solution)/shard_map/ppermute | solution.py:68
  60.6 2.2 %collective-permute-start.19 = (f32[2,80,128]{2,1,0:T(8,128)S(1)}, f32[2,80,128]{2,1,0:T(8,128)S(1)}, u32[]{:S(2)}, u32[]{:S(2)}) collective-permute-start(f32[2,80,128]{2,1,0:T(8,128)S(1)} %pad_maximum_fusion.5), channel_id=1, source_target_pairs={{0,4},{4,0},{8,12},{12,8},{16,20},{20,16},{24,28},{28,24},{1,5},{5... | collective-permute-start | bytes 245768 | tf_op jit(solution)/shard_map/ppermute | solution.py:68
  62.7 1.4 %collective-permute-start.11 = (f32[2,96,128]{2,1,0:T(8,128)S(1)}, f32[2,96,128]{2,1,0:T(8,128)S(1)}, u32[]{:S(2)}, u32[]{:S(2)}) collective-permute-start(f32[2,96,128]{2,1,0:T(8,128)S(1)} %pad_maximum_fusion.4), channel_id=1, source_target_pairs={{0,4},{4,0},{8,12},{12,8},{16,20},{20,16},{24,28},{28,24},{1,5},{5... | collective-permute-start | bytes 294920 | tf_op jit(solution)/shard_map/ppermute | solution.py:68

commit v5 on v3

--- a/solution.py
+++ b/solution.py
@@ -32,50 +32,68 @@
     return bits
 
 
-def tree_psum(terms):
-    shapes = [t.shape for t in terms]
-    sizes = [math.prod(s) for s in shapes]
-    rooms = [-(-size // 1024) * 1024 for size in sizes]
-    total = sum(rooms)
+def pack(terms, rows_of):
+    flat = jnp.concatenate([t.reshape(-1) for t in terms])
+    total = flat.shape[0]
+    rows = rows_of(-(-total // 128))
+    return jnp.pad(flat, (0, rows * 128 - total)).reshape(rows, 128)
+
+
+def unpack(flat, terms):
+    flat = flat.reshape(-1)
+    out = []
+    offset = 0
+    for t in terms:
+        out.append(flat[offset : offset + t.size].reshape(t.shape))
+        offset += t.size
+    return out
+
+
+def tree_psum(terms, late_fn, late_inputs):
     strip_bits = low_bits(lax.axis_size("strip"))
     slide_bits = low_bits(lax.axis_size("slide"))
     scatter = [("strip", b) for b in strip_bits[:2]]
     stages = [("slide", slide_bits[i : i + 2]) for i in range(0, len(slide_bits), 2)]
     stages += [("strip", [b]) for b in strip_bits[2:]]
     pieces = 2 ** len(scatter)
-    rows = -(-total // (pieces * 128))
-    rows = -(-rows // 8) * 8
-    flat = jnp.concatenate([jnp.pad(t.reshape(-1), (0, room - size)) for t, size, room in zip(terms, sizes, rooms)])
-    flat = jnp.pad(flat, (0, pieces * rows * 128 - total)).reshape(pieces, rows, 128)
+    main = pack(terms, lambda r: -(-r // (8 * pieces)) * 8 * pieces)
+    main = main.reshape(pieces, -1, 128)
     for axis, bit in scatter:
         size = lax.axis_size(axis)
-        half = flat.shape[0] // 2
+        half = main.shape[0] // 2
         mine = (lax.axis_index(axis) // bit) % 2
-        keep = lax.dynamic_slice_in_dim(flat, mine * half, half, axis=0)
-        give = lax.dynamic_slice_in_dim(flat, (1 - mine) * half, half, axis=0)
-        flat = keep + lax.ppermute(give, axis, xor_pairs(size, bit))
+        keep = lax.dynamic_slice_in_dim(main, mine * half, half, axis=0)
+        give = lax.dynamic_slice_in_dim(main, (1 - mine) * half, half, axis=0)
+        main = keep + lax.ppermute(give, axis, xor_pairs(size, bit))
+        if late_inputs is not None:
+            main, late_inputs = lax.optimization_barrier((main, late_inputs))
+            late_terms = late_fn(*late_inputs)
+            late_inputs = None
+    piece_rows = main.shape[1]
+    late = pack(late_terms, lambda r: -(-r // 8) * 8)
+    both = jnp.concatenate([main.reshape(-1, 128), late], axis=0)
     for axis, bits in stages:
         size = lax.axis_size(axis)
         masks = []
         for m in range(1, 2 ** len(bits)):
             masks.append(sum(b for k, b in enumerate(bits) if (m >> k) & 1))
-        got = [lax.ppermute(flat, axis, xor_pairs(size, mask)) for mask in masks]
+        got = [lax.ppermute(both, axis, xor_pairs(size, mask)) for mask in masks]
         for item in got:
-            flat = flat + item
+            both = both + item
+    main = both[:piece_rows][None]
+    late = both[piece_rows:]
     for axis, bit in reversed(scatter):
         size = lax.axis_size(axis)
         mine = (lax.axis_index(axis) // bit) % 2
-        got = lax.ppermute(flat, axis, xor_pairs(size, bit))
-        low = jnp.where(mine == 0, flat, got)
-        high = jnp.where(mine == 0, got, flat)
-        flat = jnp.concatenate([low, high], axis=0)
-    flat = flat.reshape(-1)
-    out = []
-    offset = 0
-    for shape, size, room in zip(shapes, sizes, rooms):
-        out.append(flat[offset : offset + size].reshape(shape))
-        offset += room
-    return out
+        both = jnp.concatenate([main.reshape(-1, 128), late], axis=0)
+        got = lax.ppermute(both, axis, xor_pairs(size, bit))
+        cut = main.shape[0] * piece_rows
+        theirs = got[:cut].reshape(main.shape)
+        late = late + got[cut:]
+        low = jnp.where(mine == 0, main, theirs)
+        high = jnp.where(mine == 0, theirs, main)
+        main = jnp.concatenate([low, high], axis=0)
+    return unpack(main, terms), unpack(late, late_terms)
 
 
 def gelu_slope(value):
@@ -141,7 +159,6 @@
     d_wide = with_halo(d_conv, (("strip", 2),), 3)
     d_padded = jnp.pad(d_wide, ((0, 0), (0, 0), (0, 0), (3, 3)))
     image_grad = cotangent.astype(jnp.float32)
-    taps = []
     for a in range(kernel):
         for b in range(kernel):
             image_grad = (
@@ -149,23 +166,29 @@
                 + conv_weight[:, a, b][None, :, None, None]
                 * d_padded[:, :, 6 - a : 6 - a + rows, 6 - b : 6 - b + cols]
             )
-            taps.append(jnp.sum(d_conv * padded[:, :, a : a + rows, b : b + cols], axis=(0, 2, 3)))
     pixel_count = slides_here * lax.axis_size("slide") * rows * lax.axis_size("strip") * cols
     scale = 1.0 / math.sqrt(float(pixel_count))
+
+    def conv_terms(d_conv, padded):
+        taps = []
+        for a in range(kernel):
+            for b in range(kernel):
+                window = padded[:, :, a : a + rows, b : b + cols]
+                taps.append(jnp.sum(d_conv * window, axis=(0, 2, 3)))
+        return [jnp.stack(taps, axis=0) * scale, jnp.sum(d_conv, axis=(0, 2, 3)) * scale]
+
     terms = (
-        jnp.stack(taps, axis=0),
-        jnp.sum(d_conv, axis=(0, 2, 3)),
+        jnp.einsum("scrw,sfrw->cf", lifted, d_pre, preferred_element_type=jnp.float32),
+        jnp.einsum("scrw,sfrw->cf", d_branch, act, preferred_element_type=jnp.float32),
         jnp.sum(d_lifted * normed, axis=(0, 2, 3)),
         jnp.sum(d_lifted, axis=(0, 2, 3)),
-        jnp.einsum("scrw,sfrw->cf", lifted, d_pre, preferred_element_type=jnp.float32),
         jnp.sum(d_pre.astype(jnp.float32), axis=(0, 2, 3)),
-        jnp.einsum("scrw,sfrw->cf", d_branch, act, preferred_element_type=jnp.float32),
         jnp.sum(d_branch.astype(jnp.float32), axis=(0, 2, 3)),
         jnp.sum(upstream * branch, axis=(0, 2, 3)),
     )
-    g = tree_psum([item * scale for item in terms])
-    g[0] = g[0].reshape(kernel, kernel, chans).transpose(2, 0, 1)
-    g[6] = g[6].T
+    main, late = tree_psum([item * scale for item in terms], conv_terms, (d_conv, padded))
+    g = [late[0].reshape(kernel, kernel, chans).transpose(2, 0, 1), late[1]]
+    g += [main[2], main[3], main[0], main[4], main[1].T, main[5], main[6]]
     return (image_grad.astype(jnp.bfloat16), g[0], g[1], g[2], g[3], g[4], g[5], g[6], g[7], g[8])
 
 

time: 63.4 us -> 65.6 us (1.035)
  local copies, waits for them, and re-layouts: 8.73 us -> 10.8 us
    concatenate x1, local copies, waits for them, and re-layouts: 0.01 us -> 1.56 us  [pack(): flat = jnp.concatenate([t.reshape(-1) for t in terms])]
    transpose x2 -> x0, local copies, waits for them, and re-layouts: 1.28 us -> none  [the longest x1 0.67 us: on_device(): g[6] = g[6].T]
    reshape x3 -> x4, local copies, waits for them, and re-layouts: 0.72 us -> 1.41 us  [the longest x2 1.39 us: unpack(): out.append(flat[offset:offset + t.size].reshape(t.shape))]
    another operation x1 -> x2, local copies, waits for them, and re-layouts: 0.15 us -> 0.83 us  [the longest x1 0.68 us: on_device(): g = [late[0].reshape(kernel, kernel, chans).transpose(2, 0, 1), late[1]]]
  transfers between devices with their start and end apart: 12 -> 12, of which waited for: 6 -> 6; matrix products, arithmetic and copies ran while one was open for 15% -> 16% of each run, Pallas kernels for 0% -> 0%
where the time goes in v5:
time: 65.6 us; the launch traced here: 65.2 us
  starting transfers between devices  18.8 us (29%)
  waiting for transfers between devices  16.6 us (25%)
  other arithmetic  12.8 us (20%)
  local copies, waits for them, and re-layouts  10.8 us (16%)
  matrix products  4.98 us (8%)
  between operations  1.2 us (2%)
    ppermute x4, waiting for transfers between devices, tree_psum(): got = [lax.ppermute(both, axis, xor_pairs(size, mask)) for mask in masks]  9.12 us
    ppermute x4, starting transfers between devices, tree_psum(): got = [lax.ppermute(both, axis, xor_pairs(size, mask)) for mask in masks]  6.97 us
    ppermute x2, starting transfers between devices, tree_psum(): main = keep + lax.ppermute(give, axis, xor_pairs(size, bit))  5.42 us
    convert_element_type x1, other arithmetic, on_device(): image_grad.astype(jnp.bfloat16)  4.33 us
    ppermute x2, waiting for transfers between devices, tree_psum(): got = lax.ppermute(both, axis, xor_pairs(size, bit))  4.21 us
    ppermute x2, starting transfers between devices, with_halo(): before = lax.ppermute(last, axis, up)  3.7 us
    ppermute x2, waiting for transfers between devices, tree_psum(): main = keep + lax.ppermute(give, axis, xor_pairs(size, bit))  3.24 us
    reduce_sum x1, other arithmetic, on_device(): centre = conv - jnp.mean(conv, axis=1, keepdims=True)  3.06 us
  transfers between devices with their start and end apart: 12, of which 6 were waited for; matrix products, arithmetic and copies ran while one was open for 16% of the time, Pallas kernels for 0%

profile of v5, /device:TPU:0, one launch (start us, length us, event | category | flops | bytes accessed | tf_op | source)
XLA Modules:
  0.0 65.2 jit_solution(18369391308050876197)
XLA Ops:
  0.7 1.0 %fusion.110 = (bf16[1,96,3,128]{3,1,2,0:T(8,128)(2,1)S(1)}, bf16[1,96,3,128]{3,1,2,0:T(8,128)(2,1)S(1)}) fusion(bf16[1,96,6,128]{3,1,2,0:T(8,128)(2,1)} %param.11), kind=kLoop, calls=%fused_computation.319 | loop fusion | bytes 294912 | tf_op jit(solution)/shard_map/slice | solution.py:14
  1.7 2.4 %collective-permute-start = (bf16[1,96,3,128]{3,1,2,0:T(8,128)(2,1)S(1)}, bf16[1,96,3,128]{3,1,2,0:T(8,128)(2,1)S(1)}, u32[]{:S(2)}, u32[]{:S(2)}) collective-permute-start(bf16[1,96,3,128]{3,1,2,0:T(8,128)(2,1)S(1)} %get-tuple-element.84), channel_id=1, source_target_pairs={{0,4},{4,8},{8,12},{12,16},{16,20},{20,24},{24,28},{1,5},{5,9},{9,... | collective-permute-start | bytes 221192 | tf_op jit(solution)/shard_map/ppermute | solution.py:16
  4.1 1.3 %collective-permute-start.1 = (bf16[1,96,3,128]{3,1,2,0:T(8,128)(2,1)S(1)}, bf16[1,96,3,128]{3,1,2,0:T(8,128)(2,1)S(1)}, u32[]{:S(2)}, u32[]{:S(2)}) collective-permute-start(bf16[1,96,3,128]{3,1,2,0:T(8,128)(2,1)S(1)} %get-tuple-element.85), channel_id=1, source_target_pairs={{4,0},{8,4},{12,8},{16,12},{20,16},{24,20},{28,24},{5,1},{9,5},{13... | collective-permute-start | bytes 221192 | tf_op jit(solution)/shard_map/ppermute | solution.py:17
  5.4 1.0 %slice_bitcast_fusion.48 = (f32[96]{0:T(128)S(1)}, f32[96]{0:T(128)S(1)}, f32[96]{0:T(128)S(1)}, f32[96]{0:T(128)S(1)}, f32[96]{0:T(128)S(1)}, /*index=5*/f32[96...) fusion(f32[96,7,7]{0,2,1:T(8,128)} %param.13), kind=kLoop, calls=%fused_computation.309 | loop fusion | bytes 14592 | tf_op jit(solution)/shard_map/mul | solution.py:166
  6.4 1.0 %slice_bitcast_fusion.47 = (f32[96]{0:T(128)S(1)}, f32[96]{0:T(128)S(1)}, f32[96]{0:T(128)S(1)}, f32[96]{0:T(128)S(1)}, f32[96]{0:T(128)S(1)}, /*index=5*/f32[96...) fusion(f32[96,7,7]{0,2,1:T(8,128)} %param.13), kind=kLoop, calls=%fused_computation.308 | loop fusion | bytes 14592 | tf_op jit(solution)/shard_map/mul | solution.py:131
  7.4 0.9 %slice_bitcast_fusion.46 = (f32[96]{0:T(128)S(1)}, f32[96]{0:T(128)S(1)}, f32[96]{0:T(128)S(1)}, f32[96]{0:T(128)S(1)}, f32[96]{0:T(128)S(1)}, /*index=5*/f32[96...) fusion(f32[96,7,7]{0,2,1:T(8,128)} %param.13), kind=kLoop, calls=%fused_computation.307 | loop fusion | bytes 8448 | tf_op jit(solution)/shard_map/mul | solution.py:131
  8.3 1.1 %convert_reduce_fusion.1 = f32[96]{0:T(128)S(1)} fusion(bf16[1,96,6,128]{3,1,2,0:T(8,128)(2,1)} %param.12, f32[96]{0:T(128)} %param.21), kind=kLoop, calls=%fused_computation.218 | loop fusion | flops 368544 | bytes 148224 | tf_op jit(solution)/shard_map/reduce_sum | solution.py:186
  9.5 1.0 %constant_dynamic-update-slice_fusion = (bf16[1,96,9,128]{3,1,2,0:T(8,128)(2,1)S(1)}, bf16[1,96,9,128]{3,1,2,0:T(8,128)(2,1)S(1)}) fusion(bf16[1,96,9,128]{3,1,2,0:T(8,128)(2,1)S(1)} %constant_dynamic-update-slice_fusion.1, bf16[1,96,6,128]{3,1,2,0:T(8,128)(2,1)} %param.11), kind=kLoop, calls=%fused_computation.250 | loop fusion | bytes 442368 | tf_op jit(solution)/shard_map/concatenate | solution.py:18
  10.4 0.3 fusion.27
  10.8 3.1 %fusion.106 = (f32[6,128]{1,0:T(8,128)S(1)}, f32[1,96,6,128]{3,1,2,0:T(8,128)S(1)}) fusion(bf16[1,96,12,134]{3,1,2,0:T(8,128)(2,1)S(1)} %fusion.27, f32[96]{0:T(128)S(1)} %get-tuple-element.133, f32[96]{0:T(128)S(1)} %get-tuple-element.134, f32[96]{0:T(128)S(1)} %get-tuple-element.87, bf16[1,96,9,128]{3,1,2,0:T(8,128)(2,1)S(1)} %constant_dynamic-update-slice_fusion.2, ...), kind=kLoop, calls=%fused_computation.315 | loop fusion | flops 10910976 | bytes 7542528 | tf_op jit(solution)/shard_map/reduce_sum | solution.py:134
  14.0 2.8 %fusion.9 = (bf16[384,6,128]{0,2,1:T(8,128)(2,1)S(1)}, f32[384,6,128]{0,2,1:T(8,128)S(1)}) fusion(f32[384]{0:T(512)S(1)} %copy-done.8, bf16[96,384]{1,0:T(8,128)(2,1)S(1)} %copy-done, f32[1,96,6,128]{3,1,2,0:T(8,128)S(1)} %get-tuple-element.69, f32[96]{0:T(128)S(1)} %copy-done.5, f32[96]{0:T(128)S(1)} %copy-done.3, f32[6,128]{1,0:T(8,128)S(1)} %add_rsqrt_fusion, ...), kind=kOutput, calls=%fused_computation.15 | convolution fusion | flops 76455936 | bytes 2146560 | tf_op jit(solution)/shard_map/scrw,cf->sfrw/dot_general | solution.py:141
  16.9 0.7 %convert_reduce_fusion = (f32[384]{0:T(512)S(1)}, bf16[384,6,128]{0,2,1:T(8,128)(2,1)S(1)}) fusion(f32[384,6,128]{0,2,1:T(8,128)S(1)} %get-tuple-element.137, bf16[384,96]{0,1:T(8,128)(2,1)S(1)} %copy-done.7, bf16[1,96,6,128]{3,1,2,0:T(8,128)(2,1)S(1)} %copy-done.2, f32[96]{0:T(128)S(1)} %copy-done.4), kind=kOutput, calls=%fused_computation.18 | convolution fusion | flops 60382848 | bytes 1992576 | tf_op jit(solution)/shard_map/scrw,fc->sfrw/dot_general | solution.py:150
  17.6 0.3 fusion.21
  17.9 0.4 fusion.87
  18.4 0.1 fusion.91
  18.5 0.1 reduce_sum.536
  18.6 0.3 fusion.22
  19.0 0.4 fusion.20
  19.4 1.6 %concatenate.51 = f32[74496]{0:T(1024)S(1)} concatenate(f32[36864]{0:T(1024)S(1)} %reshape.372, f32[36864]{0:T(1024)S(1)} %reshape.373, f32[96]{0:T(128)S(1)} %broadcast_multiply_fusion.9, f32[96]{0:T(128)S(1)} %broadcast_multiply_fusion.8, f32[384]{0:T(512)S(1)} %broadcast_multiply_fusion.4, f32[96]{0:T(128)S(1)} %get-tuple-element.143, f32[96]{0:T(128)S(1)} %get-tuple-element.142), dimensions={0} | concatenate | bytes 595968 | tf_op jit(solution)/shard_map/concatenate | solution.py:36
  21.0 3.4 %collective-permute-start.4 = (f32[2,152,128]{2,1,0:T(8,128)S(1)}, f32[2,152,128]{2,1,0:T(8,128)S(1)}, u32[]{:S(2)}, u32[]{:S(2)}) collective-permute-start(f32[2,152,128]{2,1,0:T(8,128)S(1)} %constant_dynamic-slice_fusion.1), channel_id=1, source_target_pairs={{0,4},{4,0},{8,12},{12,8},{16,20},{20,16},{24,28},{28,24},{1,5},{5... | collective-permute-start | bytes 466952 | tf_op jit(solution)/shard_map/ppermute | solution.py:67
  24.4 0.1 fusion.89
  24.5 0.9 %collective-permute-done.4 = f32[2,152,128]{2,1,0:T(8,128)S(1)} collective-permute-done((f32[2,152,128]{2,1,0:T(8,128)S(1)}, f32[2,152,128]{2,1,0:T(8,128)S(1)}, u32[]{:S(2)}, u32[]{:S(2)}) %collective-permute-start.4) | collective-permute-done | bytes 155680 | tf_op jit(solution)/shard_map/ppermute | solution.py:67
  25.4 1.1 %multiply_reduce_fusion = (f32[96]{0:T(128)S(1)}, f32[96]{0:T(128)S(1)}, f32[96]{0:T(128)S(1)}, f32[96]{0:T(128)S(1)}, f32[96]{0:T(128)S(1)}, /*index=5*/f32[96]...) fusion(f32[1,96,6,128]{3,1,2,0:T(8,128)S(1)} %fusion.89, ...), kind=kLoop, calls=%fused_computation.169 | loop fusion | flops 3979584 | bytes 2956032 | tf_op jit(solution)/shard_map/reduce_sum | solution.py:177
  26.6 1.1 %multiply_reduce_fusion.18 = (f32[96]{0:T(128)S(1)}, f32[96]{0:T(128)S(1)}, f32[96]{0:T(128)S(1)}, f32[96]{0:T(128)S(1)}, f32[96]{0:T(128)S(1)}, /*index=5*/f32[...) fusion(f32[1,96,6,128]{3,1,2,0:T(8,128)S(1)} %fusion.89, ...), kind=kLoop, calls=%fused_computation.187 | loop fusion | flops 3979584 | bytes 2956032 | tf_op jit(solution)/shard_map/reduce_sum | solution.py:177
  27.6 0.8 %multiply_reduce_fusion.36 = (f32[96]{0:T(128)S(1)}, f32[96]{0:T(128)S(1)}, f32[96]{0:T(128)S(1)}, f32[96]{0:T(128)S(1)}, f32[96]{0:T(128)S(1)}, /*index=5*/f32[...) fusion(f32[1,96,6,128]{3,1,2,0:T(8,128)S(1)} %fusion.89, ...), kind=kLoop, calls=%fused_computation.205 | loop fusion | flops 2947776 | bytes 2217216 | tf_op jit(solution)/shard_map/reduce_sum | solution.py:177
  28.5 2.0 %collective-permute-start.5 = (f32[1,152,128]{2,1,0:T(8,128)S(1)}, f32[1,152,128]{2,1,0:T(8,128)S(1)}, u32[]{:S(2)}, u32[]{:S(2)}) collective-permute-start(f32[1,152,128]{2,1,0:T(8,128)S(1)} %constant_dynamic-slice_fusion), channel_id=1, source_target_pairs={{0,8},{4,12},{8,0},{12,4},{16,24},{20,28},{24,16},{28,20},{1,9},{5... | collective-permute-start | bytes 233480 | tf_op jit(solution)/shard_map/ppermute | solution.py:67
  30.5 0.1 stack.199
  30.7 0.1 mul.1353
  30.8 0.1 fusion.101
  30.8 2.3 %collective-permute-done.5 = f32[1,152,128]{2,1,0:T(8,128)S(1)} collective-permute-done((f32[1,152,128]{2,1,0:T(8,128)S(1)}, f32[1,152,128]{2,1,0:T(8,128)S(1)}, u32[]{:S(2)}, u32[]{:S(2)}) %collective-permute-start.5) | collective-permute-done | bytes 77856 | tf_op jit(solution)/shard_map/ppermute | solution.py:67
  33.2 1.6 %collective-permute-start.6 = (f32[192,128]{1,0:T(8,128)S(1)}, f32[192,128]{1,0:T(8,128)S(1)}, u32[]{:S(2)}, u32[]{:S(2)}) collective-permute-start(f32[192,128]{1,0:T(8,128)S(1)} %pad_maximum_fusion.5), channel_id=1, source_target_pairs={{0,1},{1,0},{2,3},{3,2},{4,5},{5,4},{6,7},{7,6},{8,9},{9,8},{10,11... | collective-permute-start | bytes 294920 | tf_op jit(solution)/shard_map/ppermute | solution.py:80
  34.8 1.5 %collective-permute-start.7 = (f32[192,128]{1,0:T(8,128)S(1)}, f32[192,128]{1,0:T(8,128)S(1)}, u32[]{:S(2)}, u32[]{:S(2)}) collective-permute-start(f32[192,128]{1,0:T(8,128)S(1)} %pad_maximum_fusion.5), channel_id=1, source_target_pairs={{0,2},{1,3},{2,0},{3,1},{4,6},{5,7},{6,4},{7,5},{8,10},{9,11},{10,... | collective-permute-start | bytes 294920 | tf_op jit(solution)/shard_map/ppermute | solution.py:80
  36.3 0.5 collective-permute-start.8
  36.8 1.3 %collective-permute-start.2 = (f32[1,96,3,128]{3,1,2,0:T(8,128)S(1)}, f32[1,96,3,128]{3,1,2,0:T(8,128)S(1)}, u32[]{:S(2)}, u32[]{:S(2)}) collective-permute-start(f32[1,96,3,128]{3,1,2,0:T(8,128)S(1)} %get-tuple-element.78), channel_id=1, source_target_pairs={{0,4},{4,8},{8,12},{12,16},{16,20},{20,24},{24,28},{1,5},{5,9},{9,... | collective-permute-start | bytes 442376 | tf_op jit(solution)/shard_map/ppermute | solution.py:16
  38.1 1.3 %collective-permute-start.3 = (f32[1,96,3,128]{3,1,2,0:T(8,128)S(1)}, f32[1,96,3,128]{3,1,2,0:T(8,128)S(1)}, u32[]{:S(2)}, u32[]{:S(2)}) collective-permute-start(f32[1,96,3,128]{3,1,2,0:T(8,128)S(1)} %get-tuple-element.79), channel_id=1, source_target_pairs={{4,0},{8,4},{12,8},{16,12},{20,16},{24,20},{28,24},{5,1},{9,5},{13... | collective-permute-start | bytes 442376 | tf_op jit(solution)/shard_map/ppermute | solution.py:17
  39.4 1.0 %collective-permute-done.7 = f32[192,128]{1,0:T(8,128)S(1)} collective-permute-done((f32[192,128]{1,0:T(8,128)S(1)}, f32[192,128]{1,0:T(8,128)S(1)}, u32[]{:S(2)}, u32[]{:S(2)}) %collective-permute-start.7) | collective-permute-done | bytes 98336 | tf_op jit(solution)/shard_map/ppermute | solution.py:80
  40.4 1.4 %collective-permute-done.8 = f32[192,128]{1,0:T(8,128)S(1)} collective-permute-done((f32[192,128]{1,0:T(8,128)S(1)}, f32[192,128]{1,0:T(8,128)S(1)}, u32[]{:S(2)}, u32[]{:S(2)}) %collective-permute-start.8) | collective-permute-done | bytes 98336 | tf_op jit(solution)/shard_map/ppermute | solution.py:80
  41.8 3.4 %collective-permute-start.9 = (f32[192,128]{1,0:T(8,128)S(1)}, f32[192,128]{1,0:T(8,128)S(1)}, u32[]{:S(2)}, u32[]{:S(2)}) collective-permute-start(f32[192,128]{1,0:T(8,128)S(1)} %add_add_fusion), channel_id=1, source_target_pairs={{0,16},{4,20},{8,24},{12,28},{16,0},{20,4},{24,8},{28,12},{1,17},{... | collective-permute-start | bytes 294920 | tf_op jit(solution)/shard_map/ppermute | solution.py:80
  45.3 6.7 %collective-permute-done.9 = f32[192,128]{1,0:T(8,128)S(1)} collective-permute-done((f32[192,128]{1,0:T(8,128)S(1)}, f32[192,128]{1,0:T(8,128)S(1)}, u32[]{:S(2)}, u32[]{:S(2)}) %collective-permute-start.9) | collective-permute-done | bytes 98336 | tf_op jit(solution)/shard_map/ppermute | solution.py:80
  52.1 0.4 select_maximum_fusion
  52.5 4.2 %collective-permute-done.10 = f32[192,128]{1,0:T(8,128)S(1)} collective-permute-done((f32[192,128]{1,0:T(8,128)S(1)}, f32[192,128]{1,0:T(8,128)S(1)}, u32[]{:S(2)}, u32[]{:S(2)}) %collective-permute-start.10) | collective-permute-done | bytes 98336 | tf_op jit(solution)/shard_map/ppermute | solution.py:89
  56.8 4.3 %fusion.90 = bf16[1,96,6,128]{3,1,2,0:T(8,128)(2,1)} fusion(f32[1,96,12,134]{3,1,2,0:T(8,128)S(1)} %select_maximum_fusion, f32[1,96,6,128]{3,1,2,0:T(8,128)S(1)} %fusion.89, f32[1,96,3,128]{3,1,2,0:T(8,128)S(1)} %collective-permute-done.2, f32[1,96,3,128]{3,1,2,0:T(8,128)S(1)} %collective-permute-done.3, bf16[1,96,6,128]{3,1,2,0:T(8,128)(2,1)S(1)} %copy-done.2, ...), kind=kLoop, calls=%fused_computation.222 | loop fusion | flops 7815168 | bytes 13289856 | tf_op jit(solution)/shard_map/convert_element_type | solution.py:192
  61.3 0.6 fusion.107
  61.9 0.6 slice.1041
  62.5 0.7 %reshape.381 = f32[96,384]{1,0:T(8,128)} reshape(f32[36864]{0:T(1024)S(1)} %get-tuple-element.74) | data formatting | bytes 294912 | tf_op jit(solution)/shard_map/reshape | solution.py:47
  63.2 0.7 %reshape.380 = f32[96,384]{1,0:T(8,128)} reshape(f32[36864]{0:T(1024)S(1)} %get-tuple-element.75) | data formatting | bytes 294912 | tf_op jit(solution)/shard_map/reshape | solution.py:47
  63.9 0.6 slice.1036
  64.5 0.7 %reshape_reshape.7 = f32[7,7,96]{2,1,0:T(8,128)} reshape(f32[4704]{0:T(1024)S(1)} %bitcast.250) | data formatting | bytes 37632 | tf_op jit(solution)/shard_map/reshape;reshape | solution.py:190
  (60 shorter events, 0.7 us)
Async XLA Ops:
  0.6 13.3 %copy-start = (bf16[96,384]{1,0:T(8,128)(2,1)S(1)}, bf16[96,384]{1,0:T(8,128)(2,1)}, u32[]{:S(2)}) copy-start(bf16[96,384]{1,0:T(8,128)(2,1)} %param.17) | copy-start | bytes 221188
  0.7 9.8 %copy-start.1 = (bf16[1,96,6,128]{3,1,2,0:T(8,128)(2,1)S(1)}, bf16[1,96,6,128]{3,1,2,0:T(8,128)(2,1)}, u32[]{:S(2)}) copy-start(bf16[1,96,6,128]{3,1,2,0:T(8,128)(2,1)} %param.11) | copy-start | bytes 442372
  0.7 10.1 %copy-start.6 = (f32[96]{0:T(128)S(1)}, f32[96]{0:T(128)}, u32[]{:S(2)}) copy-start(f32[96]{0:T(128)} %param.14) | copy-start | bytes 1156
  1.7 7.8 %collective-permute-start = (bf16[1,96,3,128]{3,1,2,0:T(8,128)(2,1)S(1)}, bf16[1,96,3,128]{3,1,2,0:T(8,128)(2,1)S(1)}, u32[]{:S(2)}, u32[]{:S(2)}) collective-permute-start(bf16[1,96,3,128]{3,1,2,0:T(8,128)(2,1)S(1)} %get-tuple-element.84), channel_id=1, source_target_pairs={{0,4},{4,8},{8,12},{12,16},{16,20},{20,24},{24,28},{1,5},{5,9},{9,... | collective-permute-start | bytes 221192 | tf_op jit(solution)/shard_map/ppermute | solution.py:16
  4.1 6.3 %collective-permute-start.1 = (bf16[1,96,3,128]{3,1,2,0:T(8,128)(2,1)S(1)}, bf16[1,96,3,128]{3,1,2,0:T(8,128)(2,1)S(1)}, u32[]{:S(2)}, u32[]{:S(2)}) collective-permute-start(bf16[1,96,3,128]{3,1,2,0:T(8,128)(2,1)S(1)} %get-tuple-element.85), channel_id=1, source_target_pairs={{4,0},{8,4},{12,8},{16,12},{20,16},{24,20},{28,24},{5,1},{9,5},{13... | collective-permute-start | bytes 221192 | tf_op jit(solution)/shard_map/ppermute | solution.py:17
  10.8 3.2 %copy-start.3 = (f32[96]{0:T(128)S(1)}, f32[96]{0:T(128)}, u32[]{:S(2)}) copy-start(f32[96]{0:T(128)} %param.15) | copy-start | bytes 1156
  10.8 3.2 %copy-start.5 = (f32[96]{0:T(128)S(1)}, f32[96]{0:T(128)}, u32[]{:S(2)}) copy-start(f32[96]{0:T(128)} %param.16) | copy-start | bytes 1156
  10.8 3.2 %copy-start.8 = (f32[384]{0:T(512)S(1)}, f32[384]{0:T(512)}, u32[]{:S(2)}) copy-start(f32[384]{0:T(512)} %param.18) | copy-start | bytes 4612
  14.0 2.9 %copy-start.2 = (bf16[1,96,6,128]{3,1,2,0:T(8,128)(2,1)S(1)}, bf16[1,96,6,128]{3,1,2,0:T(8,128)(2,1)}, u32[]{:S(2)}) copy-start(bf16[1,96,6,128]{3,1,2,0:T(8,128)(2,1)} %param.12) | copy-start | bytes 442372
  14.0 2.9 %copy-start.4 = (f32[96]{0:T(128)S(1)}, f32[96]{0:T(128)}, u32[]{:S(2)}) copy-start(f32[96]{0:T(128)} %param.21) | copy-start | bytes 1156
  14.0 2.9 %copy-start.7 = (bf16[384,96]{0,1:T(8,128)(2,1)S(1)}, bf16[384,96]{0,1:T(8,128)(2,1)}, u32[]{:S(2)}) copy-start(bf16[384,96]{0,1:T(8,128)(2,1)} %param.19) | copy-start | bytes 221188
  18.3 0.7 %copy-start.9 = (f32[96]{0:T(128)S(1)}, f32[96]{0:T(128)}, u32[]{:S(2)}) copy-start(f32[96]{0:T(128)} %param.20) | copy-start | bytes 1156
  21.0 4.4 %collective-permute-start.4 = (f32[2,152,128]{2,1,0:T(8,128)S(1)}, f32[2,152,128]{2,1,0:T(8,128)S(1)}, u32[]{:S(2)}, u32[]{:S(2)}) collective-permute-start(f32[2,152,128]{2,1,0:T(8,128)S(1)} %constant_dynamic-slice_fusion.1), channel_id=1, source_target_pairs={{0,4},{4,0},{8,12},{12,8},{16,20},{20,16},{24,28},{28,24},{1,5},{5... | collective-permute-start | bytes 466952 | tf_op jit(solution)/shard_map/ppermute | solution.py:67
  28.5 4.7 %collective-permute-start.5 = (f32[1,152,128]{2,1,0:T(8,128)S(1)}, f32[1,152,128]{2,1,0:T(8,128)S(1)}, u32[]{:S(2)}, u32[]{:S(2)}) collective-permute-start(f32[1,152,128]{2,1,0:T(8,128)S(1)} %constant_dynamic-slice_fusion), channel_id=1, source_target_pairs={{0,8},{4,12},{8,0},{12,4},{16,24},{20,28},{24,16},{28,20},{1,9},{5... | collective-permute-start | bytes 233480 | tf_op jit(solution)/shard_map/ppermute | solution.py:67
  33.2 6.2 %collective-permute-start.6 = (f32[192,128]{1,0:T(8,128)S(1)}, f32[192,128]{1,0:T(8,128)S(1)}, u32[]{:S(2)}, u32[]{:S(2)}) collective-permute-start(f32[192,128]{1,0:T(8,128)S(1)} %pad_maximum_fusion.5), channel_id=1, source_target_pairs={{0,1},{1,0},{2,3},{3,2},{4,5},{5,4},{6,7},{7,6},{8,9},{9,8},{10,11... | collective-permute-start | bytes 294920 | tf_op jit(solution)/shard_map/ppermute | solution.py:80
  34.8 5.7 %collective-permute-start.7 = (f32[192,128]{1,0:T(8,128)S(1)}, f32[192,128]{1,0:T(8,128)S(1)}, u32[]{:S(2)}, u32[]{:S(2)}) collective-permute-start(f32[192,128]{1,0:T(8,128)S(1)} %pad_maximum_fusion.5), channel_id=1, source_target_pairs={{0,2},{1,3},{2,0},{3,1},{4,6},{5,7},{6,4},{7,5},{8,10},{9,11},{10,... | collective-permute-start | bytes 294920 | tf_op jit(solution)/shard_map/ppermute | solution.py:80
  36.3 5.5 %collective-permute-start.8 = (f32[192,128]{1,0:T(8,128)S(1)}, f32[192,128]{1,0:T(8,128)S(1)}, u32[]{:S(2)}, u32[]{:S(2)}) collective-permute-start(f32[192,128]{1,0:T(8,128)S(1)} %pad_maximum_fusion.5), channel_id=1, source_target_pairs={{0,3},{1,2},{2,1},{3,0},{4,7},{5,6},{6,5},{7,4},{8,11},{9,10},{10,... | collective-permute-start | bytes 294920 | tf_op jit(solution)/shard_map/ppermute | solution.py:80
  36.8 15.3 %collective-permute-start.2 = (f32[1,96,3,128]{3,1,2,0:T(8,128)S(1)}, f32[1,96,3,128]{3,1,2,0:T(8,128)S(1)}, u32[]{:S(2)}, u32[]{:S(2)}) collective-permute-start(f32[1,96,3,128]{3,1,2,0:T(8,128)S(1)} %get-tuple-element.78), channel_id=1, source_target_pairs={{0,4},{4,8},{8,12},{12,16},{16,20},{20,24},{24,28},{1,5},{5,9},{9,... | collective-permute-start | bytes 442376 | tf_op jit(solution)/shard_map/ppermute | solution.py:16
  38.1 14.0 %collective-permute-start.3 = (f32[1,96,3,128]{3,1,2,0:T(8,128)S(1)}, f32[1,96,3,128]{3,1,2,0:T(8,128)S(1)}, u32[]{:S(2)}, u32[]{:S(2)}) collective-permute-start(f32[1,96,3,128]{3,1,2,0:T(8,128)S(1)} %get-tuple-element.79), channel_id=1, source_target_pairs={{4,0},{8,4},{12,8},{16,12},{20,16},{24,20},{28,24},{5,1},{9,5},{13... | collective-permute-start | bytes 442376 | tf_op jit(solution)/shard_map/ppermute | solution.py:17
  41.8 10.1 %collective-permute-start.9 = (f32[192,128]{1,0:T(8,128)S(1)}, f32[192,128]{1,0:T(8,128)S(1)}, u32[]{:S(2)}, u32[]{:S(2)}) collective-permute-start(f32[192,128]{1,0:T(8,128)S(1)} %add_add_fusion), channel_id=1, source_target_pairs={{0,16},{4,20},{8,24},{12,28},{16,0},{20,4},{24,8},{28,12},{1,17},{... | collective-permute-start | bytes 294920 | tf_op jit(solution)/shard_map/ppermute | solution.py:80
  52.0 4.7 %collective-permute-start.10 = (f32[192,128]{1,0:T(8,128)S(1)}, f32[192,128]{1,0:T(8,128)S(1)}, u32[]{:S(2)}, u32[]{:S(2)}) collective-permute-start(f32[192,128]{1,0:T(8,128)S(1)} %add.531), channel_id=1, source_target_pairs={{0,8},{4,12},{8,0},{12,4},{16,24},{20,28},{24,16},{28,20},{1,9},{5... | collective-permute-start | bytes 294920 | tf_op jit(solution)/shard_map/ppermute | solution.py:89
  56.8 4.4 %collective-permute-start.11 = (f32[344,128]{1,0:T(8,128)S(1)}, f32[344,128]{1,0:T(8,128)S(1)}, u32[]{:S(2)}, u32[]{:S(2)}) collective-permute-start(f32[344,128]{1,0:T(8,128)S(1)} %pad_maximum_fusion.3), channel_id=1, source_target_pairs={{0,4},{4,0},{8,12},{12,8},{16,20},{20,16},{24,28},{28,24},{1,5},{5... | collective-permute-start | bytes 528392 | tf_op jit(solution)/shard_map/ppermute | solution.py:89

commit v6 on v3

--- a/solution.py
+++ b/solution.py
@@ -35,8 +35,7 @@
 def tree_psum(terms):
     shapes = [t.shape for t in terms]
     sizes = [math.prod(s) for s in shapes]
-    rooms = [-(-size // 1024) * 1024 for size in sizes]
-    total = sum(rooms)
+    total = sum(sizes)
     strip_bits = low_bits(lax.axis_size("strip"))
     slide_bits = low_bits(lax.axis_size("slide"))
     scatter = [("strip", b) for b in strip_bits[:2]]
@@ -45,7 +44,8 @@
     pieces = 2 ** len(scatter)
     rows = -(-total // (pieces * 128))
     rows = -(-rows // 8) * 8
-    flat = jnp.concatenate([jnp.pad(t.reshape(-1), (0, room - size)) for t, size, room in zip(terms, sizes, rooms)])
+    order = sorted(range(len(terms)), key=lambda i: -sizes[i])
+    flat = jnp.concatenate([terms[i].reshape(-1) for i in order])
     flat = jnp.pad(flat, (0, pieces * rows * 128 - total)).reshape(pieces, rows, 128)
     for axis, bit in scatter:
         size = lax.axis_size(axis)
@@ -62,6 +62,7 @@
         got = [lax.ppermute(flat, axis, xor_pairs(size, mask)) for mask in masks]
         for item in got:
             flat = flat + item
+    flat = flat.astype(jnp.bfloat16)
     for axis, bit in reversed(scatter):
         size = lax.axis_size(axis)
         mine = (lax.axis_index(axis) // bit) % 2
@@ -70,11 +71,11 @@
         high = jnp.where(mine == 0, got, flat)
         flat = jnp.concatenate([low, high], axis=0)
     flat = flat.reshape(-1)
-    out = []
     offset = 0
-    for shape, size, room in zip(shapes, sizes, rooms):
-        out.append(flat[offset : offset + size].reshape(shape))
-        offset += room
+    out = [None] * len(terms)
+    for i in order:
+        out[i] = flat[offset : offset + sizes[i]].reshape(shapes[i]).astype(jnp.float32)
+        offset += sizes[i]
     return out
 
 

time: 63.4 us -> 63.8 us (level)
  waiting for transfers between devices: 16.2 us -> 11.7 us
  starting transfers between devices: 19.3 us -> 22.8 us
  other arithmetic: 12.6 us -> 13.8 us
    ppermute x2, starting transfers between devices: 0.14 us -> 4.69 us  [tree_psum(): got = lax.ppermute(flat, axis, xor_pairs(size, bit))]
    ppermute x4, waiting for transfers between devices: 8.27 us -> 4.87 us  [tree_psum(): got = [lax.ppermute(flat, axis, xor_pairs(size, mask)) for mask in masks]]
    concatenate x1, local copies, waits for them, and re-layouts: 0.01 us -> 1.74 us  [tree_psum(): flat = jnp.concatenate([terms[i].reshape(-1) for i in order])]
    slice x5 -> x0, local copies, waits for them, and re-layouts: 1.46 us -> none  [tree_psum(): out.append(flat[offset:offset + size].reshape(shape))]
    convert_element_type x0 -> x3, other arithmetic: none -> 1.26 us  [the longest x2 1.25 us: tree_psum(): flat[offset:offset + sizes[i]].reshape(shapes[i]).astype(jnp.float32)]
    ppermute x2, waiting for transfers between devices: 4.08 us -> 3.06 us  [tree_psum(): got = lax.ppermute(flat, axis, xor_pairs(size, bit))]
    ppermute x4, starting transfers between devices: 7.27 us -> 6.37 us  [tree_psum(): got = [lax.ppermute(flat, axis, xor_pairs(size, mask)) for mask in masks]]
    convert_element_type x0 -> x1, local copies, waits for them, and re-layouts: none -> 0.7 us  [tree_psum(): flat[offset:offset + sizes[i]].reshape(shapes[i]).astype(jnp.float32)]
where the time goes in v6:
time: 63.8 us; the launch traced here: 63.4 us
  starting transfers between devices  22.8 us (36%)
  other arithmetic  13.8 us (22%)
  waiting for transfers between devices  11.7 us (18%)
  local copies, waits for them, and re-layouts  9.05 us (14%)
  matrix products  4.98 us (8%)
  between operations  1.15 us (2%)
    ppermute x4, starting transfers between devices, tree_psum(): got = [lax.ppermute(flat, axis, xor_pairs(size, mask)) for mask in masks]  6.37 us
    ppermute x2, starting transfers between devices, tree_psum(): flat = keep + lax.ppermute(give, axis, xor_pairs(size, bit))  5.42 us
    ppermute x4, waiting for transfers between devices, tree_psum(): got = [lax.ppermute(flat, axis, xor_pairs(size, mask)) for mask in masks]  4.87 us
    ppermute x2, starting transfers between devices, tree_psum(): got = lax.ppermute(flat, axis, xor_pairs(size, bit))  4.69 us
    convert_element_type x1, other arithmetic, on_device(): image_grad.astype(jnp.bfloat16)  4.33 us
    ppermute x2, waiting for transfers between devices, tree_psum(): flat = keep + lax.ppermute(give, axis, xor_pairs(size, bit))  3.78 us
    ppermute x2, starting transfers between devices, with_halo(): before = lax.ppermute(last, axis, up)  3.7 us
    reduce_sum x1, other arithmetic, on_device(): centre = conv - jnp.mean(conv, axis=1, keepdims=True)  3.06 us
  transfers between devices with their start and end apart: 12, of which 6 were waited for; matrix products, arithmetic and copies ran while one was open for 15% of the time, Pallas kernels for 0%

profile of v6, /device:TPU:0, one launch (start us, length us, event | category | flops | bytes accessed | tf_op | source)
XLA Modules:
  0.0 63.4 jit_solution(9188617009921583371)
XLA Ops:
  0.6 0.0 copy-start
  0.7 1.0 %fusion.206 = (bf16[1,96,3,128]{3,1,2,0:T(8,128)(2,1)S(1)}, bf16[1,96,3,128]{3,1,2,0:T(8,128)(2,1)S(1)}) fusion(bf16[1,96,6,128]{3,1,2,0:T(8,128)(2,1)} %param.11), kind=kLoop, calls=%fused_computation.465 | loop fusion | bytes 294912 | tf_op jit(solution)/shard_map/slice | solution.py:14
  1.7 2.4 %collective-permute-start = (bf16[1,96,3,128]{3,1,2,0:T(8,128)(2,1)S(1)}, bf16[1,96,3,128]{3,1,2,0:T(8,128)(2,1)S(1)}, u32[]{:S(2)}, u32[]{:S(2)}) collective-permute-start(bf16[1,96,3,128]{3,1,2,0:T(8,128)(2,1)S(1)} %get-tuple-element.87), channel_id=1, source_target_pairs={{0,4},{4,8},{8,12},{12,16},{16,20},{20,24},{24,28},{1,5},{5,9},{9,... | collective-permute-start | bytes 221192 | tf_op jit(solution)/shard_map/ppermute | solution.py:16
  4.1 1.3 %collective-permute-start.1 = (bf16[1,96,3,128]{3,1,2,0:T(8,128)(2,1)S(1)}, bf16[1,96,3,128]{3,1,2,0:T(8,128)(2,1)S(1)}, u32[]{:S(2)}, u32[]{:S(2)}) collective-permute-start(bf16[1,96,3,128]{3,1,2,0:T(8,128)(2,1)S(1)} %get-tuple-element.88), channel_id=1, source_target_pairs={{4,0},{8,4},{12,8},{16,12},{20,16},{24,20},{28,24},{5,1},{9,5},{13... | collective-permute-start | bytes 221192 | tf_op jit(solution)/shard_map/ppermute | solution.py:17
  5.4 1.0 %slice_bitcast_fusion.48 = (f32[96]{0:T(128)S(1)}, f32[96]{0:T(128)S(1)}, f32[96]{0:T(128)S(1)}, f32[96]{0:T(128)S(1)}, f32[96]{0:T(128)S(1)}, /*index=5*/f32[96...) fusion(f32[96,7,7]{0,2,1:T(8,128)} %param.13), kind=kLoop, calls=%fused_computation.457 | loop fusion | bytes 14592 | tf_op jit(solution)/shard_map/mul | solution.py:150
  6.4 1.0 %slice_bitcast_fusion.47 = (f32[96]{0:T(128)S(1)}, f32[96]{0:T(128)S(1)}, f32[96]{0:T(128)S(1)}, f32[96]{0:T(128)S(1)}, f32[96]{0:T(128)S(1)}, /*index=5*/f32[96...) fusion(f32[96,7,7]{0,2,1:T(8,128)} %param.13), kind=kLoop, calls=%fused_computation.456 | loop fusion | bytes 14592 | tf_op jit(solution)/shard_map/mul | solution.py:114
  7.4 0.9 %slice_bitcast_fusion.46 = (f32[96]{0:T(128)S(1)}, f32[96]{0:T(128)S(1)}, f32[96]{0:T(128)S(1)}, f32[96]{0:T(128)S(1)}, f32[96]{0:T(128)S(1)}, /*index=5*/f32[96...) fusion(f32[96,7,7]{0,2,1:T(8,128)} %param.13), kind=kLoop, calls=%fused_computation.455 | loop fusion | bytes 8448 | tf_op jit(solution)/shard_map/mul | solution.py:114
  8.3 1.1 %convert_reduce_fusion.1 = f32[96]{0:T(128)S(1)} fusion(bf16[1,96,6,128]{3,1,2,0:T(8,128)(2,1)} %param.12, f32[96]{0:T(128)} %param.21), kind=kLoop, calls=%fused_computation.364 | loop fusion | flops 368544 | bytes 148224 | tf_op jit(solution)/shard_map/reduce_sum | solution.py:164
  9.4 1.0 %constant_dynamic-update-slice_fusion = (bf16[1,96,9,128]{3,1,2,0:T(8,128)(2,1)S(1)}, bf16[1,96,9,128]{3,1,2,0:T(8,128)(2,1)S(1)}) fusion(bf16[1,96,9,128]{3,1,2,0:T(8,128)(2,1)S(1)} %constant_dynamic-update-slice_fusion.1, bf16[1,96,6,128]{3,1,2,0:T(8,128)(2,1)} %param.11), kind=kLoop, calls=%fused_computation.392 | loop fusion | bytes 442368 | tf_op jit(solution)/shard_map/concatenate | solution.py:18
  10.4 0.3 fusion.27
  10.8 3.1 %fusion.203 = (f32[6,128]{1,0:T(8,128)S(1)}, f32[1,96,6,128]{3,1,2,0:T(8,128)S(1)}) fusion(bf16[1,96,12,134]{3,1,2,0:T(8,128)(2,1)S(1)} %fusion.27, f32[96]{0:T(128)S(1)} %get-tuple-element.138, f32[96]{0:T(128)S(1)} %get-tuple-element.139, f32[96]{0:T(128)S(1)} %get-tuple-element.92, bf16[1,96,9,128]{3,1,2,0:T(8,128)(2,1)S(1)} %constant_dynamic-update-slice_fusion.2, ...), kind=kLoop, calls=%fused_computation.463 | loop fusion | flops 10910976 | bytes 7542528 | tf_op jit(solution)/shard_map/reduce_sum | solution.py:117
  14.0 2.8 %fusion.9 = (bf16[384,6,128]{0,2,1:T(8,128)(2,1)S(1)}, f32[384,6,128]{0,2,1:T(8,128)S(1)}) fusion(f32[384]{0:T(512)S(1)} %copy-done.8, bf16[96,384]{1,0:T(8,128)(2,1)S(1)} %copy-done, f32[1,96,6,128]{3,1,2,0:T(8,128)S(1)} %get-tuple-element.73, f32[96]{0:T(128)S(1)} %copy-done.5, f32[96]{0:T(128)S(1)} %copy-done.3, f32[6,128]{1,0:T(8,128)S(1)} %add_rsqrt_fusion, ...), kind=kOutput, calls=%fused_computation.15 | convolution fusion | flops 76455936 | bytes 2146560 | tf_op jit(solution)/shard_map/scrw,cf->sfrw/dot_general | solution.py:124
  16.8 0.7 %convert_reduce_fusion = (f32[384]{0:T(512)S(1)}, bf16[384,6,128]{0,2,1:T(8,128)(2,1)S(1)}) fusion(f32[384,6,128]{0,2,1:T(8,128)S(1)} %get-tuple-element.142, bf16[384,96]{0,1:T(8,128)(2,1)S(1)} %copy-done.7, bf16[1,96,6,128]{3,1,2,0:T(8,128)(2,1)S(1)} %copy-done.2, f32[96]{0:T(128)S(1)} %copy-done.4), kind=kOutput, calls=%fused_computation.18 | convolution fusion | flops 60382848 | bytes 1992576 | tf_op jit(solution)/shard_map/scrw,fc->sfrw/dot_general | solution.py:133
  17.6 0.4 fusion.185
  18.0 0.1 fusion.189
  18.1 1.2 %fusion.125 = (f32[96]{0:T(128)S(1)}, f32[96]{0:T(128)S(1)}, f32[96]{0:T(128)S(1)}, f32[96]{0:T(128)S(1)}, f32[96]{0:T(128)S(1)}, /*index=5*/f32[96]{0:T(128)S(1...) fusion(bf16[1,96,12,134]{3,1,2,0:T(8,128)(2,1)S(1)} %fusion.27,, ...), kind=kLoop, calls=%fused_computation.253 | loop fusion | flops 4495680 | bytes 3558528 | tf_op jit(solution)/shard_map/reduce_sum | solution.py:153
  19.3 0.7 %fusion.122 = (f32[96]{0:T(128)S(1)}, f32[96]{0:T(128)S(1)}, f32[96]{0:T(128)S(1)}, f32[96]{0:T(128)S(1)}, f32[96]{0:T(128)S(1)}, /*index=5*/f32[96]{0:T(128)S(1...) fusion(f32[1,96,6,128]{3,1,2,0:T(8,128)S(1)} %get-tuple-element, ...), kind=kLoop, calls=%fused_computation.250 | loop fusion | flops 2947776 | bytes 2217216 | tf_op jit(solution)/shard_map/reduce_sum | solution.py:153
  20.0 1.1 %fusion.104 = (f32[96]{0:T(128)S(1)}, f32[96]{0:T(128)S(1)}, f32[96]{0:T(128)S(1)}, f32[96]{0:T(128)S(1)}, f32[96]{0:T(128)S(1)}, /*index=5*/f32[96]{0:T(128)S(1...) fusion(f32[1,96,6,128]{3,1,2,0:T(8,128)S(1)} %get-tuple-element, ...), kind=kLoop, calls=%fused_computation.232 | loop fusion | flops 3979584 | bytes 2956032 | tf_op jit(solution)/shard_map/reduce_sum | solution.py:153
  21.0 0.3 fusion.21
  21.4 0.1 reduce_sum.587
  21.5 0.2 stack.199
  21.6 0.1 mul.1343
  21.8 0.3 fusion.22
  22.1 0.4 fusion.20
  22.5 1.7 %concatenate.41 = f32[79296]{0:T(1024)S(1)} concatenate(f32[36864]{0:T(1024)S(1)} %reshape.362, f32[36864]{0:T(1024)S(1)} %reshape.363, f32[4704]{0:T(1024)S(1)} %mul.1343, f32[384]{0:T(512)S(1)} %broadcast_multiply_fusion.4, f32[96]{0:T(128)S(1)} %broadcast_multiply_fusion.9, f32[96]{0:T(128)S(1)} %get-tuple-element.150, f32[96]{0:T(128)S(1)} %get-tuple-element.149, ...), dimensions={0} | concatenate | bytes 634368 | tf_op jit(solution)/shard_map/concatenate | solution.py:48
  24.3 3.4 %collective-permute-start.4 = (f32[2,160,128]{2,1,0:T(8,128)S(1)}, f32[2,160,128]{2,1,0:T(8,128)S(1)}, u32[]{:S(2)}, u32[]{:S(2)}) collective-permute-start(f32[2,160,128]{2,1,0:T(8,128)S(1)} %constant_dynamic-slice_fusion.1), channel_id=1, source_target_pairs={{0,4},{4,0},{8,12},{12,8},{16,20},{20,16},{24,28},{28,24},{1,5},{5... | collective-permute-start | bytes 491528 | tf_op jit(solution)/shard_map/ppermute | solution.py:56
  27.7 1.0 %collective-permute-done.4 = f32[2,160,128]{2,1,0:T(8,128)S(1)} collective-permute-done((f32[2,160,128]{2,1,0:T(8,128)S(1)}, f32[2,160,128]{2,1,0:T(8,128)S(1)}, u32[]{:S(2)}, u32[]{:S(2)}) %collective-permute-start.4) | collective-permute-done | bytes 163872 | tf_op jit(solution)/shard_map/ppermute | solution.py:56
  28.8 2.0 %collective-permute-start.5 = (f32[1,160,128]{2,1,0:T(8,128)S(1)}, f32[1,160,128]{2,1,0:T(8,128)S(1)}, u32[]{:S(2)}, u32[]{:S(2)}) collective-permute-start(f32[1,160,128]{2,1,0:T(8,128)S(1)} %constant_dynamic-slice_fusion), channel_id=1, source_target_pairs={{0,8},{4,12},{8,0},{12,4},{16,24},{20,28},{24,16},{28,20},{1,9},{5... | collective-permute-start | bytes 245768 | tf_op jit(solution)/shard_map/ppermute | solution.py:56
  30.8 2.8 %collective-permute-done.5 = f32[1,160,128]{2,1,0:T(8,128)S(1)} collective-permute-done((f32[1,160,128]{2,1,0:T(8,128)S(1)}, f32[1,160,128]{2,1,0:T(8,128)S(1)}, u32[]{:S(2)}, u32[]{:S(2)}) %collective-permute-start.5) | collective-permute-done | bytes 81952 | tf_op jit(solution)/shard_map/ppermute | solution.py:56
  33.6 1.6 %collective-permute-start.6 = (f32[1,160,128]{2,1,0:T(8,128)S(1)}, f32[1,160,128]{2,1,0:T(8,128)S(1)}, u32[]{:S(2)}, u32[]{:S(2)}) collective-permute-start(f32[1,160,128]{2,1,0:T(8,128)S(1)} %dynamic-slice_add_fusion.1), channel_id=1, source_target_pairs={{0,1},{1,0},{2,3},{3,2},{4,5},{5,4},{6,7},{7,6},{8,9},{9,8},{10,11... | collective-permute-start | bytes 245768 | tf_op jit(solution)/shard_map/ppermute | solution.py:62
  35.1 1.5 %collective-permute-start.7 = (f32[1,160,128]{2,1,0:T(8,128)S(1)}, f32[1,160,128]{2,1,0:T(8,128)S(1)}, u32[]{:S(2)}, u32[]{:S(2)}) collective-permute-start(f32[1,160,128]{2,1,0:T(8,128)S(1)} %dynamic-slice_add_fusion.1), channel_id=1, source_target_pairs={{0,2},{1,3},{2,0},{3,1},{4,6},{5,7},{6,4},{7,5},{8,10},{9,11},{10,... | collective-permute-start | bytes 245768 | tf_op jit(solution)/shard_map/ppermute | solution.py:62
  36.7 0.5 collective-permute-start.8
  37.1 1.0 %collective-permute-done.6 = f32[1,160,128]{2,1,0:T(8,128)S(1)} collective-permute-done((f32[1,160,128]{2,1,0:T(8,128)S(1)}, f32[1,160,128]{2,1,0:T(8,128)S(1)}, u32[]{:S(2)}, u32[]{:S(2)}) %collective-permute-start.6) | collective-permute-done | bytes 81952 | tf_op jit(solution)/shard_map/ppermute | solution.py:62
  38.1 2.4 %collective-permute-done.7 = f32[1,160,128]{2,1,0:T(8,128)S(1)} collective-permute-done((f32[1,160,128]{2,1,0:T(8,128)S(1)}, f32[1,160,128]{2,1,0:T(8,128)S(1)}, u32[]{:S(2)}, u32[]{:S(2)}) %collective-permute-start.7) | collective-permute-done | bytes 81952 | tf_op jit(solution)/shard_map/ppermute | solution.py:62
  40.5 1.5 %collective-permute-done.8 = f32[1,160,128]{2,1,0:T(8,128)S(1)} collective-permute-done((f32[1,160,128]{2,1,0:T(8,128)S(1)}, f32[1,160,128]{2,1,0:T(8,128)S(1)}, u32[]{:S(2)}, u32[]{:S(2)}) %collective-permute-start.8) | collective-permute-done | bytes 81952 | tf_op jit(solution)/shard_map/ppermute | solution.py:62
  42.0 2.8 %collective-permute-start.9 = (f32[1,160,128]{2,1,0:T(8,128)S(1)}, f32[1,160,128]{2,1,0:T(8,128)S(1)}, u32[]{:S(2)}, u32[]{:S(2)}) collective-permute-start(f32[1,160,128]{2,1,0:T(8,128)S(1)} %add_add_fusion), channel_id=1, source_target_pairs={{0,16},{4,20},{8,24},{12,28},{16,0},{20,4},{24,8},{28,12},{1,17},{... | collective-permute-start | bytes 245768 | tf_op jit(solution)/shard_map/ppermute | solution.py:62
  44.9 1.3 %collective-permute-start.2 = (f32[1,96,3,128]{3,1,2,0:T(8,128)S(1)}, f32[1,96,3,128]{3,1,2,0:T(8,128)S(1)}, u32[]{:S(2)}, u32[]{:S(2)}) collective-permute-start(f32[1,96,3,128]{3,1,2,0:T(8,128)S(1)} %get-tuple-element.74), channel_id=1, source_target_pairs={{0,4},{4,8},{8,12},{12,16},{16,20},{20,24},{24,28},{1,5},{5,9},{9,... | collective-permute-start | bytes 442376 | tf_op jit(solution)/shard_map/ppermute | solution.py:16
  46.2 1.3 %collective-permute-start.3 = (f32[1,96,3,128]{3,1,2,0:T(8,128)S(1)}, f32[1,96,3,128]{3,1,2,0:T(8,128)S(1)}, u32[]{:S(2)}, u32[]{:S(2)}) collective-permute-start(f32[1,96,3,128]{3,1,2,0:T(8,128)S(1)} %get-tuple-element.75), channel_id=1, source_target_pairs={{4,0},{8,4},{12,8},{16,12},{20,16},{24,20},{28,24},{5,1},{9,5},{13... | collective-permute-start | bytes 442376 | tf_op jit(solution)/shard_map/ppermute | solution.py:17
  47.5 4.6 %collective-permute-start.10 = (bf16[1,160,128]{2,1,0:T(8,128)(2,1)S(1)}, bf16[1,160,128]{2,1,0:T(8,128)(2,1)S(1)}, u32[]{:S(2)}, u32[]{:S(2)}) collective-permute-start(bf16[1,160,128]{2,1,0:T(8,128)(2,1)S(1)} %add_convert_fusion.1), channel_id=1, source_target_pairs={{0,8},{4,12},{8,0},{12,4},{16,24},{20,28},{24,16},{28,20},{1,9},{5... | collective-permute-start | bytes 122888 | tf_op jit(solution)/shard_map/ppermute | solution.py:69
  52.1 0.4 select_maximum_fusion
  52.5 3.1 %collective-permute-done.10 = bf16[1,160,128]{2,1,0:T(8,128)(2,1)S(1)} collective-permute-done((bf16[1,160,128]{2,1,0:T(8,128)(2,1)S(1)}, bf16[1,160,128]{2,1,0:T(8,128)(2,1)S(1)}, u32[]{:S(2)}, u32[]{:S(2)}) %collective-permute-start.10) | collective-permute-done | bytes 40992 | tf_op jit(solution)/shard_map/ppermute | solution.py:69
  55.6 0.1 collective-permute-start.11
  55.7 4.3 %fusion.188 = bf16[1,96,6,128]{3,1,2,0:T(8,128)(2,1)} fusion(f32[1,96,12,134]{3,1,2,0:T(8,128)S(1)} %select_maximum_fusion, f32[1,96,6,128]{3,1,2,0:T(8,128)S(1)} %get-tuple-element.71, f32[1,96,3,128]{3,1,2,0:T(8,128)S(1)} %collective-permute-done.2, f32[1,96,3,128]{3,1,2,0:T(8,128)S(1)} %collective-permute-done.3, ...), kind=kLoop, calls=%fused_computation.367 | loop fusion | flops 7815168 | bytes 13289856 | tf_op jit(solution)/shard_map/convert_element_type | solution.py:170
  60.1 0.6 slice_convert_fusion.4
  60.7 0.6 %slice_convert_fusion.3 = f32[384]{0:T(512)} fusion(bf16[81920]{0:T(1024)(128)(2,1)S(1)} %bitcast.236), kind=kLoop, calls=%fused_computation.400 | loop fusion | flops 384 | bytes 2304 | tf_op jit(solution)/shard_map/convert_element_type | solution.py:77
  61.3 0.7 %reshape.368 = f32[96,384]{1,0:T(8,128)} reshape(f32[36864]{0:T(1024)S(1)} %get-tuple-element.81) | data formatting | bytes 294912 | tf_op jit(solution)/shard_map/transpose | solution.py:169
  62.0 0.7 %reshape.366 = f32[96,384]{1,0:T(8,128)} reshape(f32[36864]{0:T(1024)S(1)} %get-tuple-element.82) | data formatting | bytes 294912 | tf_op jit(solution)/shard_map/convert_element_type | solution.py:77
  62.7 0.7 %reshape.367 = f32[7,7,96]{2,1,0:T(8,128)} reshape(f32[4704]{0:T(1024)S(1)} %slice_convert_fusion.2) | data formatting | bytes 37632 | tf_op jit(solution)/shard_map/transpose | solution.py:168
  (52 shorter events, 0.4 us)
Async XLA Ops:
  0.6 13.3 %copy-start = (bf16[96,384]{1,0:T(8,128)(2,1)S(1)}, bf16[96,384]{1,0:T(8,128)(2,1)}, u32[]{:S(2)}) copy-start(bf16[96,384]{1,0:T(8,128)(2,1)} %param.17) | copy-start | bytes 221188
  0.7 9.7 %copy-start.1 = (bf16[1,96,6,128]{3,1,2,0:T(8,128)(2,1)S(1)}, bf16[1,96,6,128]{3,1,2,0:T(8,128)(2,1)}, u32[]{:S(2)}) copy-start(bf16[1,96,6,128]{3,1,2,0:T(8,128)(2,1)} %param.11) | copy-start | bytes 442372
  0.7 10.0 %copy-start.6 = (f32[96]{0:T(128)S(1)}, f32[96]{0:T(128)}, u32[]{:S(2)}) copy-start(f32[96]{0:T(128)} %param.14) | copy-start | bytes 1156
  1.7 7.7 %collective-permute-start = (bf16[1,96,3,128]{3,1,2,0:T(8,128)(2,1)S(1)}, bf16[1,96,3,128]{3,1,2,0:T(8,128)(2,1)S(1)}, u32[]{:S(2)}, u32[]{:S(2)}) collective-permute-start(bf16[1,96,3,128]{3,1,2,0:T(8,128)(2,1)S(1)} %get-tuple-element.87), channel_id=1, source_target_pairs={{0,4},{4,8},{8,12},{12,16},{16,20},{20,24},{24,28},{1,5},{5,9},{9,... | collective-permute-start | bytes 221192 | tf_op jit(solution)/shard_map/ppermute | solution.py:16
  4.1 6.3 %collective-permute-start.1 = (bf16[1,96,3,128]{3,1,2,0:T(8,128)(2,1)S(1)}, bf16[1,96,3,128]{3,1,2,0:T(8,128)(2,1)S(1)}, u32[]{:S(2)}, u32[]{:S(2)}) collective-permute-start(bf16[1,96,3,128]{3,1,2,0:T(8,128)(2,1)S(1)} %get-tuple-element.88), channel_id=1, source_target_pairs={{4,0},{8,4},{12,8},{16,12},{20,16},{24,20},{28,24},{5,1},{9,5},{13... | collective-permute-start | bytes 221192 | tf_op jit(solution)/shard_map/ppermute | solution.py:17
  10.7 3.2 %copy-start.3 = (f32[96]{0:T(128)S(1)}, f32[96]{0:T(128)}, u32[]{:S(2)}) copy-start(f32[96]{0:T(128)} %param.15) | copy-start | bytes 1156
  10.7 3.2 %copy-start.5 = (f32[96]{0:T(128)S(1)}, f32[96]{0:T(128)}, u32[]{:S(2)}) copy-start(f32[96]{0:T(128)} %param.16) | copy-start | bytes 1156
  10.7 3.2 %copy-start.8 = (f32[384]{0:T(512)S(1)}, f32[384]{0:T(512)}, u32[]{:S(2)}) copy-start(f32[384]{0:T(512)} %param.18) | copy-start | bytes 4612
  13.9 2.9 %copy-start.2 = (bf16[1,96,6,128]{3,1,2,0:T(8,128)(2,1)S(1)}, bf16[1,96,6,128]{3,1,2,0:T(8,128)(2,1)}, u32[]{:S(2)}) copy-start(bf16[1,96,6,128]{3,1,2,0:T(8,128)(2,1)} %param.12) | copy-start | bytes 442372
  13.9 2.9 %copy-start.4 = (f32[96]{0:T(128)S(1)}, f32[96]{0:T(128)}, u32[]{:S(2)}) copy-start(f32[96]{0:T(128)} %param.21) | copy-start | bytes 1156
  14.0 2.9 %copy-start.7 = (bf16[384,96]{0,1:T(8,128)(2,1)S(1)}, bf16[384,96]{0,1:T(8,128)(2,1)}, u32[]{:S(2)}) copy-start(bf16[384,96]{0,1:T(8,128)(2,1)} %param.19) | copy-start | bytes 221188
  21.4 0.7 %copy-start.9 = (f32[96]{0:T(128)S(1)}, f32[96]{0:T(128)}, u32[]{:S(2)}) copy-start(f32[96]{0:T(128)} %param.20) | copy-start | bytes 1156
  24.3 4.4 %collective-permute-start.4 = (f32[2,160,128]{2,1,0:T(8,128)S(1)}, f32[2,160,128]{2,1,0:T(8,128)S(1)}, u32[]{:S(2)}, u32[]{:S(2)}) collective-permute-start(f32[2,160,128]{2,1,0:T(8,128)S(1)} %constant_dynamic-slice_fusion.1), channel_id=1, source_target_pairs={{0,4},{4,0},{8,12},{12,8},{16,20},{20,16},{24,28},{28,24},{1,5},{5... | collective-permute-start | bytes 491528 | tf_op jit(solution)/shard_map/ppermute | solution.py:56
  28.8 4.8 %collective-permute-start.5 = (f32[1,160,128]{2,1,0:T(8,128)S(1)}, f32[1,160,128]{2,1,0:T(8,128)S(1)}, u32[]{:S(2)}, u32[]{:S(2)}) collective-permute-start(f32[1,160,128]{2,1,0:T(8,128)S(1)} %constant_dynamic-slice_fusion), channel_id=1, source_target_pairs={{0,8},{4,12},{8,0},{12,4},{16,24},{20,28},{24,16},{28,20},{1,9},{5... | collective-permute-start | bytes 245768 | tf_op jit(solution)/shard_map/ppermute | solution.py:56
  33.6 4.5 %collective-permute-start.6 = (f32[1,160,128]{2,1,0:T(8,128)S(1)}, f32[1,160,128]{2,1,0:T(8,128)S(1)}, u32[]{:S(2)}, u32[]{:S(2)}) collective-permute-start(f32[1,160,128]{2,1,0:T(8,128)S(1)} %dynamic-slice_add_fusion.1), channel_id=1, source_target_pairs={{0,1},{1,0},{2,3},{3,2},{4,5},{5,4},{6,7},{7,6},{8,9},{9,8},{10,11... | collective-permute-start | bytes 245768 | tf_op jit(solution)/shard_map/ppermute | solution.py:62
  35.1 5.3 %collective-permute-start.7 = (f32[1,160,128]{2,1,0:T(8,128)S(1)}, f32[1,160,128]{2,1,0:T(8,128)S(1)}, u32[]{:S(2)}, u32[]{:S(2)}) collective-permute-start(f32[1,160,128]{2,1,0:T(8,128)S(1)} %dynamic-slice_add_fusion.1), channel_id=1, source_target_pairs={{0,2},{1,3},{2,0},{3,1},{4,6},{5,7},{6,4},{7,5},{8,10},{9,11},{10,... | collective-permute-start | bytes 245768 | tf_op jit(solution)/shard_map/ppermute | solution.py:62
  36.7 5.3 %collective-permute-start.8 = (f32[1,160,128]{2,1,0:T(8,128)S(1)}, f32[1,160,128]{2,1,0:T(8,128)S(1)}, u32[]{:S(2)}, u32[]{:S(2)}) collective-permute-start(f32[1,160,128]{2,1,0:T(8,128)S(1)} %dynamic-slice_add_fusion.1), channel_id=1, source_target_pairs={{0,3},{1,2},{2,1},{3,0},{4,7},{5,6},{6,5},{7,4},{8,11},{9,10},{10,... | collective-permute-start | bytes 245768 | tf_op jit(solution)/shard_map/ppermute | solution.py:62
  42.0 5.5 %collective-permute-start.9 = (f32[1,160,128]{2,1,0:T(8,128)S(1)}, f32[1,160,128]{2,1,0:T(8,128)S(1)}, u32[]{:S(2)}, u32[]{:S(2)}) collective-permute-start(f32[1,160,128]{2,1,0:T(8,128)S(1)} %add_add_fusion), channel_id=1, source_target_pairs={{0,16},{4,20},{8,24},{12,28},{16,0},{20,4},{24,8},{28,12},{1,17},{... | collective-permute-start | bytes 245768 | tf_op jit(solution)/shard_map/ppermute | solution.py:62
  44.9 7.3 %collective-permute-start.2 = (f32[1,96,3,128]{3,1,2,0:T(8,128)S(1)}, f32[1,96,3,128]{3,1,2,0:T(8,128)S(1)}, u32[]{:S(2)}, u32[]{:S(2)}) collective-permute-start(f32[1,96,3,128]{3,1,2,0:T(8,128)S(1)} %get-tuple-element.74), channel_id=1, source_target_pairs={{0,4},{4,8},{8,12},{12,16},{16,20},{20,24},{24,28},{1,5},{5,9},{9,... | collective-permute-start | bytes 442376 | tf_op jit(solution)/shard_map/ppermute | solution.py:16
  46.2 6.0 %collective-permute-start.3 = (f32[1,96,3,128]{3,1,2,0:T(8,128)S(1)}, f32[1,96,3,128]{3,1,2,0:T(8,128)S(1)}, u32[]{:S(2)}, u32[]{:S(2)}) collective-permute-start(f32[1,96,3,128]{3,1,2,0:T(8,128)S(1)} %get-tuple-element.75), channel_id=1, source_target_pairs={{4,0},{8,4},{12,8},{16,12},{20,16},{24,20},{28,24},{5,1},{9,5},{13... | collective-permute-start | bytes 442376 | tf_op jit(solution)/shard_map/ppermute | solution.py:17
  47.5 8.1 %collective-permute-start.10 = (bf16[1,160,128]{2,1,0:T(8,128)(2,1)S(1)}, bf16[1,160,128]{2,1,0:T(8,128)(2,1)S(1)}, u32[]{:S(2)}, u32[]{:S(2)}) collective-permute-start(bf16[1,160,128]{2,1,0:T(8,128)(2,1)S(1)} %add_convert_fusion.1), channel_id=1, source_target_pairs={{0,8},{4,12},{8,0},{12,4},{16,24},{20,28},{24,16},{28,20},{1,9},{5... | collective-permute-start | bytes 122888 | tf_op jit(solution)/shard_map/ppermute | solution.py:69
  55.6 4.4 %collective-permute-start.11 = (bf16[2,160,128]{2,1,0:T(8,128)(2,1)S(1)}, bf16[2,160,128]{2,1,0:T(8,128)(2,1)S(1)}, u32[]{:S(2)}, u32[]{:S(2)}) collective-permute-start(bf16[2,160,128]{2,1,0:T(8,128)(2,1)S(1)} %pad_maximum_fusion.3), channel_id=1, source_target_pairs={{0,4},{4,0},{8,12},{12,8},{16,20},{20,16},{24,28},{28,24},{1,5},{5... | collective-permute-start | bytes 245768 | tf_op jit(solution)/shard_map/ppermute | solution.py:69

commit v7 on v3

--- a/solution.py
+++ b/solution.py
@@ -32,7 +32,7 @@
     return bits
 
 
-def tree_psum(terms):
+def tree_psum(terms, hold):
     shapes = [t.shape for t in terms]
     sizes = [math.prod(s) for s in shapes]
     rooms = [-(-size // 1024) * 1024 for size in sizes]
@@ -62,6 +62,7 @@
         got = [lax.ppermute(flat, axis, xor_pairs(size, mask)) for mask in masks]
         for item in got:
             flat = flat + item
+    flat, hold = lax.optimization_barrier((flat, hold))
     for axis, bit in reversed(scatter):
         size = lax.axis_size(axis)
         mine = (lax.axis_index(axis) // bit) % 2
@@ -75,7 +76,7 @@
     for shape, size, room in zip(shapes, sizes, rooms):
         out.append(flat[offset : offset + size].reshape(shape))
         offset += room
-    return out
+    return out, hold
 
 
 def gelu_slope(value):
@@ -163,10 +164,10 @@
         jnp.sum(d_branch.astype(jnp.float32), axis=(0, 2, 3)),
         jnp.sum(upstream * branch, axis=(0, 2, 3)),
     )
-    g = tree_psum([item * scale for item in terms])
+    g, image_grad = tree_psum([item * scale for item in terms], image_grad.astype(jnp.bfloat16))
     g[0] = g[0].reshape(kernel, kernel, chans).transpose(2, 0, 1)
     g[6] = g[6].T
-    return (image_grad.astype(jnp.bfloat16), g[0], g[1], g[2], g[3], g[4], g[5], g[6], g[7], g[8])
+    return (image_grad, g[0], g[1], g[2], g[3], g[4], g[5], g[6], g[7], g[8])
 
 
 def solution(mesh):

time: 63.4 us -> 59 us (0.931)
  waiting for transfers between devices: 16.2 us -> 12.5 us
    ppermute x2, waiting for transfers between devices: 3.88 us -> 1.04 us  [tree_psum(): flat = keep + lax.ppermute(give, axis, xor_pairs(size, bit))]
    ppermute x4, waiting for transfers between devices: 8.27 us -> 5.61 us  [tree_psum(): got = [lax.ppermute(flat, axis, xor_pairs(size, mask)) for mask in masks]]
    ppermute x2, starting transfers between devices: 3.7 us -> 6.25 us  [with_halo(): before = lax.ppermute(last, axis, up)]
    ppermute x4, starting transfers between devices: 7.27 us -> 5.37 us  [tree_psum(): got = [lax.ppermute(flat, axis, xor_pairs(size, mask)) for mask in masks]]
    ppermute x2, waiting for transfers between devices: 4.08 us -> 5.86 us  [tree_psum(): got = lax.ppermute(flat, axis, xor_pairs(size, bit))]
    ppermute x2, starting transfers between devices: 5.42 us -> 4.38 us  [tree_psum(): flat = keep + lax.ppermute(give, axis, xor_pairs(size, bit))]
  transfers between devices with their start and end apart: 12 -> 12, of which waited for: 6 -> 7; matrix products, arithmetic and copies ran while one was open for 15% -> 16% of each run, Pallas kernels for 0% -> 0%
where the time goes in v7:
time: 59 us; the launch traced here: 58.6 us
  starting transfers between devices  18.7 us (32%)
  waiting for transfers between devices  12.5 us (21%)
  other arithmetic  12.4 us (21%)
  local copies, waits for them, and re-layouts  8.73 us (15%)
  matrix products  4.99 us (8%)
  between operations  1.23 us (2%)
    ppermute x2, starting transfers between devices, with_halo(): before = lax.ppermute(last, axis, up)  6.25 us
    ppermute x2, waiting for transfers between devices, tree_psum(): got = lax.ppermute(flat, axis, xor_pairs(size, bit))  5.86 us
    ppermute x4, waiting for transfers between devices, tree_psum(): got = [lax.ppermute(flat, axis, xor_pairs(size, mask)) for mask in masks]  5.61 us
    ppermute x4, starting transfers between devices, tree_psum(): got = [lax.ppermute(flat, axis, xor_pairs(size, mask)) for mask in masks]  5.37 us
    ppermute x2, starting transfers between devices, tree_psum(): flat = keep + lax.ppermute(give, axis, xor_pairs(size, bit))  4.38 us
    convert_element_type x1, other arithmetic, on_device(): image_grad.astype(jnp.bfloat16)  4.21 us
    reduce_sum x1, other arithmetic, on_device(): centre = conv - jnp.mean(conv, axis=1, keepdims=True)  3.06 us
    reduce_sum x3, other arithmetic, on_device(): jnp.sum(d_conv * padded[:, :, a:a + rows, b:b + cols], axis=(0, 2, 3))  2.94 us
  transfers between devices with their start and end apart: 12, of which 7 were waited for; matrix products, arithmetic and copies ran while one was open for 16% of the time, Pallas kernels for 0%

profile of v7, /device:TPU:0, one launch (start us, length us, event | category | flops | bytes accessed | tf_op | source)
XLA Modules:
  0.0 58.6 jit_solution(8381935438792806475)
XLA Ops:
  0.7 1.0 %fusion.203 = (bf16[1,96,3,128]{3,1,2,0:T(8,128)(2,1)S(1)}, bf16[1,96,3,128]{3,1,2,0:T(8,128)(2,1)S(1)}) fusion(bf16[1,96,6,128]{3,1,2,0:T(8,128)(2,1)} %param.11), kind=kLoop, calls=%fused_computation.465 | loop fusion | bytes 294912 | tf_op jit(solution)/shard_map/slice | solution.py:14
  1.7 1.3 %collective-permute-start.1 = (bf16[1,96,3,128]{3,1,2,0:T(8,128)(2,1)S(1)}, bf16[1,96,3,128]{3,1,2,0:T(8,128)(2,1)S(1)}, u32[]{:S(2)}, u32[]{:S(2)}) collective-permute-start(bf16[1,96,3,128]{3,1,2,0:T(8,128)(2,1)S(1)} %get-tuple-element.92), channel_id=1, source_target_pairs={{4,0},{8,4},{12,8},{16,12},{20,16},{24,20},{28,24},{5,1},{9,5},{13... | collective-permute-start | bytes 221192 | tf_op jit(solution)/shard_map/ppermute | solution.py:17
  3.0 3.0 %collective-permute-start = (bf16[1,96,3,128]{3,1,2,0:T(8,128)(2,1)S(1)}, bf16[1,96,3,128]{3,1,2,0:T(8,128)(2,1)S(1)}, u32[]{:S(2)}, u32[]{:S(2)}) collective-permute-start(bf16[1,96,3,128]{3,1,2,0:T(8,128)(2,1)S(1)} %get-tuple-element.91), channel_id=1, source_target_pairs={{0,4},{4,8},{8,12},{12,16},{16,20},{20,24},{24,28},{1,5},{5,9},{9,... | collective-permute-start | bytes 221192 | tf_op jit(solution)/shard_map/ppermute | solution.py:16
  6.0 0.9 %slice_bitcast_fusion.48 = (f32[96]{0:T(128)S(1)}, f32[96]{0:T(128)S(1)}, f32[96]{0:T(128)S(1)}, f32[96]{0:T(128)S(1)}, f32[96]{0:T(128)S(1)}, /*index=5*/f32[96...) fusion(f32[96,7,7]{0,2,1:T(8,128)} %param.13), kind=kLoop, calls=%fused_computation.454 | loop fusion | bytes 8448 | tf_op jit(solution)/shard_map/mul | solution.py:114
  6.9 1.0 %slice_bitcast_fusion.50 = (f32[96]{0:T(128)S(1)}, f32[96]{0:T(128)S(1)}, f32[96]{0:T(128)S(1)}, f32[96]{0:T(128)S(1)}, f32[96]{0:T(128)S(1)}, /*index=5*/f32[96...) fusion(f32[96,7,7]{0,2,1:T(8,128)} %param.13), kind=kLoop, calls=%fused_computation.456 | loop fusion | bytes 14592 | tf_op jit(solution)/shard_map/mul | solution.py:114
  7.9 1.0 %slice_bitcast_fusion.49 = (f32[96]{0:T(128)S(1)}, f32[96]{0:T(128)S(1)}, f32[96]{0:T(128)S(1)}, f32[96]{0:T(128)S(1)}, f32[96]{0:T(128)S(1)}, /*index=5*/f32[96...) fusion(f32[96,7,7]{0,2,1:T(8,128)} %param.13), kind=kLoop, calls=%fused_computation.455 | loop fusion | bytes 14592 | tf_op jit(solution)/shard_map/mul | solution.py:114
  8.9 1.1 %convert_reduce_fusion.1 = f32[96]{0:T(128)S(1)} fusion(bf16[1,96,6,128]{3,1,2,0:T(8,128)(2,1)} %param.12, f32[96]{0:T(128)} %param.21), kind=kLoop, calls=%fused_computation.363 | loop fusion | flops 368544 | bytes 148224 | tf_op jit(solution)/shard_map/reduce_sum | solution.py:164
  10.1 1.0 %constant_dynamic-update-slice_fusion = (bf16[1,96,9,128]{3,1,2,0:T(8,128)(2,1)S(1)}, bf16[1,96,9,128]{3,1,2,0:T(8,128)(2,1)S(1)}) fusion(bf16[1,96,9,128]{3,1,2,0:T(8,128)(2,1)S(1)} %constant_dynamic-update-slice_fusion.1, bf16[1,96,6,128]{3,1,2,0:T(8,128)(2,1)} %param.11), kind=kLoop, calls=%fused_computation.389 | loop fusion | bytes 442368 | tf_op jit(solution)/shard_map/concatenate | solution.py:18
  11.1 0.3 select_maximum_fusion.2
  11.4 3.1 %fusion.199 = (f32[6,128]{1,0:T(8,128)S(1)}, f32[1,96,6,128]{3,1,2,0:T(8,128)S(1)}) fusion(bf16[1,96,12,134]{3,1,2,0:T(8,128)(2,1)S(1)} %select_maximum_fusion.2, f32[96]{0:T(128)S(1)} %get-tuple-element.140, f32[96]{0:T(128)S(1)} %get-tuple-element.141, f32[96]{0:T(128)S(1)} %get-tuple-element.94, ...), kind=kLoop, calls=%fused_computation.462 | loop fusion | flops 10910976 | bytes 7542528 | tf_op jit(solution)/shard_map/reduce_sum | solution.py:117
  14.6 2.8 %fusion.9 = (bf16[384,6,128]{0,2,1:T(8,128)(2,1)S(1)}, f32[384,6,128]{0,2,1:T(8,128)S(1)}) fusion(f32[384]{0:T(512)S(1)} %copy-done.8, bf16[96,384]{1,0:T(8,128)(2,1)S(1)} %copy-done, f32[1,96,6,128]{3,1,2,0:T(8,128)S(1)} %get-tuple-element.77, f32[96]{0:T(128)S(1)} %copy-done.5, f32[96]{0:T(128)S(1)} %copy-done.3, f32[6,128]{1,0:T(8,128)S(1)} %add_rsqrt_fusion, ...), kind=kOutput, calls=%fused_computation.15 | convolution fusion | flops 76455936 | bytes 2146560 | tf_op jit(solution)/shard_map/scrw,cf->sfrw/dot_general | solution.py:124
  17.5 0.7 %convert_reduce_fusion = (f32[384]{0:T(512)S(1)}, bf16[384,6,128]{0,2,1:T(8,128)(2,1)S(1)}) fusion(f32[384,6,128]{0,2,1:T(8,128)S(1)} %get-tuple-element.146, bf16[384,96]{0,1:T(8,128)(2,1)S(1)} %copy-done.7, bf16[1,96,6,128]{3,1,2,0:T(8,128)(2,1)S(1)} %copy-done.2, f32[96]{0:T(128)S(1)} %copy-done.4), kind=kOutput, calls=%fused_computation.31 | convolution fusion | flops 60382848 | bytes 1992576 | tf_op jit(solution)/shard_map/scrw,fc->sfrw/dot_general | solution.py:133
  18.2 0.4 fusion.181
  18.6 0.1 fusion.185
  18.7 1.2 %fusion.121 = (f32[96]{0:T(128)S(1)}, f32[96]{0:T(128)S(1)}, f32[96]{0:T(128)S(1)}, f32[96]{0:T(128)S(1)}, f32[96]{0:T(128)S(1)}, /*index=5*/f32[96]{0:T(128)S(1...) fusion(bf16[1,96,12,134]{3,1,2,0:T(8,128)(2,1)S(1)} %select_max, ...), kind=kLoop, calls=%fused_computation.252 | loop fusion | flops 4495680 | bytes 3558528 | tf_op jit(solution)/shard_map/reduce_sum | solution.py:153
  19.9 0.7 %fusion.118 = (f32[96]{0:T(128)S(1)}, f32[96]{0:T(128)S(1)}, f32[96]{0:T(128)S(1)}, f32[96]{0:T(128)S(1)}, f32[96]{0:T(128)S(1)}, /*index=5*/f32[96]{0:T(128)S(1...) fusion(f32[1,96,6,128]{3,1,2,0:T(8,128)S(1)} %get-tuple-element, ...), kind=kLoop, calls=%fused_computation.249 | loop fusion | flops 2947776 | bytes 2217216 | tf_op jit(solution)/shard_map/reduce_sum | solution.py:153
  20.6 1.1 %fusion.100 = (f32[96]{0:T(128)S(1)}, f32[96]{0:T(128)S(1)}, f32[96]{0:T(128)S(1)}, f32[96]{0:T(128)S(1)}, f32[96]{0:T(128)S(1)}, /*index=5*/f32[96]{0:T(128)S(1...) fusion(f32[1,96,6,128]{3,1,2,0:T(8,128)S(1)} %get-tuple-element, ...), kind=kLoop, calls=%fused_computation.231 | loop fusion | flops 3979584 | bytes 2956032 | tf_op jit(solution)/shard_map/reduce_sum | solution.py:153
  21.7 0.3 fusion.21
  22.0 0.1 stack.199
  22.2 0.1 mul.1289
  22.3 0.1 reduce_sum.586
  22.4 0.3 fusion.22
  22.8 0.4 fusion.20
  23.4 2.7 %collective-permute-start.2 = (f32[2,168,128]{2,1,0:T(8,128)S(1)}, f32[2,168,128]{2,1,0:T(8,128)S(1)}, u32[]{:S(2)}, u32[]{:S(2)}) collective-permute-start(f32[2,168,128]{2,1,0:T(8,128)S(1)} %constant_dynamic-slice_fusion.1), channel_id=1, source_target_pairs={{0,4},{4,0},{8,12},{12,8},{16,20},{20,16},{24,28},{28,24},{1,5},{5... | collective-permute-start | bytes 516104 | tf_op jit(solution)/shard_map/ppermute | solution.py:56
  26.1 1.0 %collective-permute-done.2 = f32[2,168,128]{2,1,0:T(8,128)S(1)} collective-permute-done((f32[2,168,128]{2,1,0:T(8,128)S(1)}, f32[2,168,128]{2,1,0:T(8,128)S(1)}, u32[]{:S(2)}, u32[]{:S(2)}) %collective-permute-start.2) | collective-permute-done | bytes 172064 | tf_op jit(solution)/shard_map/ppermute | solution.py:56
  27.2 1.6 %collective-permute-start.3 = (f32[1,168,128]{2,1,0:T(8,128)S(1)}, f32[1,168,128]{2,1,0:T(8,128)S(1)}, u32[]{:S(2)}, u32[]{:S(2)}) collective-permute-start(f32[1,168,128]{2,1,0:T(8,128)S(1)} %constant_dynamic-slice_fusion), channel_id=1, source_target_pairs={{0,8},{4,12},{8,0},{12,4},{16,24},{20,28},{24,16},{28,20},{1,9},{5... | collective-permute-start | bytes 258056 | tf_op jit(solution)/shard_map/ppermute | solution.py:56
  28.9 1.3 %collective-permute-start.9 = (f32[1,96,3,128]{3,1,2,0:T(8,128)S(1)}, f32[1,96,3,128]{3,1,2,0:T(8,128)S(1)}, u32[]{:S(2)}, u32[]{:S(2)}) collective-permute-start(f32[1,96,3,128]{3,1,2,0:T(8,128)S(1)} %get-tuple-element.86), channel_id=1, source_target_pairs={{4,0},{8,4},{12,8},{16,12},{20,16},{24,20},{28,24},{5,1},{9,5},{13... | collective-permute-start | bytes 442376 | tf_op jit(solution)/shard_map/ppermute | solution.py:17
  30.2 3.2 %collective-permute-start.8 = (f32[1,96,3,128]{3,1,2,0:T(8,128)S(1)}, f32[1,96,3,128]{3,1,2,0:T(8,128)S(1)}, u32[]{:S(2)}, u32[]{:S(2)}) collective-permute-start(f32[1,96,3,128]{3,1,2,0:T(8,128)S(1)} %get-tuple-element.85), channel_id=1, source_target_pairs={{0,4},{4,8},{8,12},{12,16},{16,20},{20,24},{24,28},{1,5},{5,9},{9,... | collective-permute-start | bytes 442376 | tf_op jit(solution)/shard_map/ppermute | solution.py:16
  33.4 2.5 %collective-permute-start.6 = (f32[1,168,128]{2,1,0:T(8,128)S(1)}, f32[1,168,128]{2,1,0:T(8,128)S(1)}, u32[]{:S(2)}, u32[]{:S(2)}) collective-permute-start(f32[1,168,128]{2,1,0:T(8,128)S(1)} %dynamic-slice_add_fusion.1), channel_id=1, source_target_pairs={{0,3},{1,2},{2,1},{3,0},{4,7},{5,6},{6,5},{7,4},{8,11},{9,10},{10,... | collective-permute-start | bytes 258056 | tf_op jit(solution)/shard_map/ppermute | solution.py:62
  35.9 0.5 collective-permute-start.5
  36.4 0.5 collective-permute-start.4
  37.0 0.4 select_maximum_fusion
  37.4 2.1 %collective-permute-done.6 = f32[1,168,128]{2,1,0:T(8,128)S(1)} collective-permute-done((f32[1,168,128]{2,1,0:T(8,128)S(1)}, f32[1,168,128]{2,1,0:T(8,128)S(1)}, u32[]{:S(2)}, u32[]{:S(2)}) %collective-permute-start.6) | collective-permute-done | bytes 86048 | tf_op jit(solution)/shard_map/ppermute | solution.py:62
  39.4 2.2 %collective-permute-done.5 = f32[1,168,128]{2,1,0:T(8,128)S(1)} collective-permute-done((f32[1,168,128]{2,1,0:T(8,128)S(1)}, f32[1,168,128]{2,1,0:T(8,128)S(1)}, u32[]{:S(2)}, u32[]{:S(2)}) %collective-permute-start.5) | collective-permute-done | bytes 86048 | tf_op jit(solution)/shard_map/ppermute | solution.py:62
  41.7 1.8 %collective-permute-start.7 = (f32[1,168,128]{2,1,0:T(8,128)S(1)}, f32[1,168,128]{2,1,0:T(8,128)S(1)}, u32[]{:S(2)}, u32[]{:S(2)}) collective-permute-start(f32[1,168,128]{2,1,0:T(8,128)S(1)} %add_add_fusion), channel_id=1, source_target_pairs={{0,16},{4,20},{8,24},{12,28},{16,0},{20,4},{24,8},{28,12},{1,17},{... | collective-permute-start | bytes 258056 | tf_op jit(solution)/shard_map/ppermute | solution.py:62
  43.5 4.2 %fusion.184 = bf16[1,96,6,128]{3,1,2,0:T(8,128)(2,1)} fusion(f32[1,96,12,134]{3,1,2,0:T(8,128)S(1)} %select_maximum_fusion, f32[1,96,6,128]{3,1,2,0:T(8,128)S(1)} %get-tuple-element.75, f32[1,96,3,128]{3,1,2,0:T(8,128)S(1)} %collective-permute-done.8, f32[1,96,3,128]{3,1,2,0:T(8,128)S(1)} %collective-permute-done.9, ...), kind=kLoop, calls=%fused_computation.366 | loop fusion | flops 7815168 | bytes 13289856 | tf_op jit(solution)/shard_map/convert_element_type | solution.py:167
  47.8 1.3 %collective-permute-done.7 = f32[1,168,128]{2,1,0:T(8,128)S(1)} collective-permute-done((f32[1,168,128]{2,1,0:T(8,128)S(1)}, f32[1,168,128]{2,1,0:T(8,128)S(1)}, u32[]{:S(2)}, u32[]{:S(2)}) %collective-permute-start.7) | collective-permute-done | bytes 86048 | tf_op jit(solution)/shard_map/ppermute | solution.py:62
  49.0 0.1 collective-permute-start.10
  49.1 4.5 %collective-permute-done.10 = f32[1,168,128]{2,1,0:T(8,128)S(1)} collective-permute-done((f32[1,168,128]{2,1,0:T(8,128)S(1)}, f32[1,168,128]{2,1,0:T(8,128)S(1)}, u32[]{:S(2)}, u32[]{:S(2)}) %collective-permute-start.10) | collective-permute-done | bytes 86048 | tf_op jit(solution)/shard_map/ppermute | solution.py:69
  53.6 0.1 collective-permute-start.11
  53.7 1.4 %collective-permute-done.11 = f32[2,168,128]{2,1,0:T(8,128)S(1)} collective-permute-done((f32[2,168,128]{2,1,0:T(8,128)S(1)}, f32[2,168,128]{2,1,0:T(8,128)S(1)}, u32[]{:S(2)}, u32[]{:S(2)}) %collective-permute-start.11) | collective-permute-done | bytes 172064 | tf_op jit(solution)/shard_map/ppermute | solution.py:69
  55.2 0.3 slice.755
  55.4 0.5 fusion.201
  56.0 0.6 slice.871
  56.6 0.1 slice.762
  56.6 0.6 %slice_bitcast_fusion.1 = f32[96,7,7]{0,2,1:T(8,128)} fusion(f32[128,7,96]{2,1,0:T(8,128)S(1)} %slice.755), kind=kLoop, calls=%fused_computation.386 | loop fusion | bytes 37632 | tf_op jit(solution)/shard_map/transpose | solution.py:168
  57.3 0.7 %reshape.363 = f32[96,384]{1,0:T(8,128)} reshape(f32[36864]{0:T(1024)S(1)} %slice.870) | data formatting | bytes 294912 | tf_op jit(solution)/shard_map/reshape | solution.py:77
  58.0 0.7 %slice_bitcast_fusion = f32[384,96]{0,1:T(8,128)} fusion(f32[224,384]{1,0:T(8,128)S(1)} %slice.762), kind=kLoop, calls=%fused_computation.372 | loop fusion | bytes 294912 | tf_op jit(solution)/shard_map/transpose | solution.py:169
  (63 shorter events, 0.6 us)
Async XLA Ops:
  0.6 13.9 %copy-start = (bf16[96,384]{1,0:T(8,128)(2,1)S(1)}, bf16[96,384]{1,0:T(8,128)(2,1)}, u32[]{:S(2)}) copy-start(bf16[96,384]{1,0:T(8,128)(2,1)} %param.17) | copy-start | bytes 221188
  0.7 10.4 %copy-start.1 = (bf16[1,96,6,128]{3,1,2,0:T(8,128)(2,1)S(1)}, bf16[1,96,6,128]{3,1,2,0:T(8,128)(2,1)}, u32[]{:S(2)}) copy-start(bf16[1,96,6,128]{3,1,2,0:T(8,128)(2,1)} %param.11) | copy-start | bytes 442372
  0.7 10.7 %copy-start.6 = (f32[96]{0:T(128)S(1)}, f32[96]{0:T(128)}, u32[]{:S(2)}) copy-start(f32[96]{0:T(128)} %param.14) | copy-start | bytes 1156
  1.7 9.4 %collective-permute-start.1 = (bf16[1,96,3,128]{3,1,2,0:T(8,128)(2,1)S(1)}, bf16[1,96,3,128]{3,1,2,0:T(8,128)(2,1)S(1)}, u32[]{:S(2)}, u32[]{:S(2)}) collective-permute-start(bf16[1,96,3,128]{3,1,2,0:T(8,128)(2,1)S(1)} %get-tuple-element.92), channel_id=1, source_target_pairs={{4,0},{8,4},{12,8},{16,12},{20,16},{24,20},{28,24},{5,1},{9,5},{13... | collective-permute-start | bytes 221192 | tf_op jit(solution)/shard_map/ppermute | solution.py:17
  3.0 7.1 %collective-permute-start = (bf16[1,96,3,128]{3,1,2,0:T(8,128)(2,1)S(1)}, bf16[1,96,3,128]{3,1,2,0:T(8,128)(2,1)S(1)}, u32[]{:S(2)}, u32[]{:S(2)}) collective-permute-start(bf16[1,96,3,128]{3,1,2,0:T(8,128)(2,1)S(1)} %get-tuple-element.91), channel_id=1, source_target_pairs={{0,4},{4,8},{8,12},{12,16},{16,20},{20,24},{24,28},{1,5},{5,9},{9,... | collective-permute-start | bytes 221192 | tf_op jit(solution)/shard_map/ppermute | solution.py:16
  11.4 3.2 %copy-start.3 = (f32[96]{0:T(128)S(1)}, f32[96]{0:T(128)}, u32[]{:S(2)}) copy-start(f32[96]{0:T(128)} %param.15) | copy-start | bytes 1156
  11.4 3.2 %copy-start.5 = (f32[96]{0:T(128)S(1)}, f32[96]{0:T(128)}, u32[]{:S(2)}) copy-start(f32[96]{0:T(128)} %param.16) | copy-start | bytes 1156
  11.4 3.2 %copy-start.8 = (f32[384]{0:T(512)S(1)}, f32[384]{0:T(512)}, u32[]{:S(2)}) copy-start(f32[384]{0:T(512)} %param.18) | copy-start | bytes 4612
  14.6 2.9 %copy-start.2 = (bf16[1,96,6,128]{3,1,2,0:T(8,128)(2,1)S(1)}, bf16[1,96,6,128]{3,1,2,0:T(8,128)(2,1)}, u32[]{:S(2)}) copy-start(bf16[1,96,6,128]{3,1,2,0:T(8,128)(2,1)} %param.12) | copy-start | bytes 442372
  14.6 2.9 %copy-start.4 = (f32[96]{0:T(128)S(1)}, f32[96]{0:T(128)}, u32[]{:S(2)}) copy-start(f32[96]{0:T(128)} %param.21) | copy-start | bytes 1156
  14.6 2.9 %copy-start.7 = (bf16[384,96]{0,1:T(8,128)(2,1)S(1)}, bf16[384,96]{0,1:T(8,128)(2,1)}, u32[]{:S(2)}) copy-start(bf16[384,96]{0,1:T(8,128)(2,1)} %param.19) | copy-start | bytes 221188
  22.0 0.8 %copy-start.9 = (f32[96]{0:T(128)S(1)}, f32[96]{0:T(128)}, u32[]{:S(2)}) copy-start(f32[96]{0:T(128)} %param.20) | copy-start | bytes 1156
  23.4 3.8 %collective-permute-start.2 = (f32[2,168,128]{2,1,0:T(8,128)S(1)}, f32[2,168,128]{2,1,0:T(8,128)S(1)}, u32[]{:S(2)}, u32[]{:S(2)}) collective-permute-start(f32[2,168,128]{2,1,0:T(8,128)S(1)} %constant_dynamic-slice_fusion.1), channel_id=1, source_target_pairs={{0,4},{4,0},{8,12},{12,8},{16,20},{20,16},{24,28},{28,24},{1,5},{5... | collective-permute-start | bytes 516104 | tf_op jit(solution)/shard_map/ppermute | solution.py:56
  27.2 6.2 %collective-permute-start.3 = (f32[1,168,128]{2,1,0:T(8,128)S(1)}, f32[1,168,128]{2,1,0:T(8,128)S(1)}, u32[]{:S(2)}, u32[]{:S(2)}) collective-permute-start(f32[1,168,128]{2,1,0:T(8,128)S(1)} %constant_dynamic-slice_fusion), channel_id=1, source_target_pairs={{0,8},{4,12},{8,0},{12,4},{16,24},{20,28},{24,16},{28,20},{1,9},{5... | collective-permute-start | bytes 258056 | tf_op jit(solution)/shard_map/ppermute | solution.py:56
  28.9 8.1 %collective-permute-start.9 = (f32[1,96,3,128]{3,1,2,0:T(8,128)S(1)}, f32[1,96,3,128]{3,1,2,0:T(8,128)S(1)}, u32[]{:S(2)}, u32[]{:S(2)}) collective-permute-start(f32[1,96,3,128]{3,1,2,0:T(8,128)S(1)} %get-tuple-element.86), channel_id=1, source_target_pairs={{4,0},{8,4},{12,8},{16,12},{20,16},{24,20},{28,24},{5,1},{9,5},{13... | collective-permute-start | bytes 442376 | tf_op jit(solution)/shard_map/ppermute | solution.py:17
  30.2 6.8 %collective-permute-start.8 = (f32[1,96,3,128]{3,1,2,0:T(8,128)S(1)}, f32[1,96,3,128]{3,1,2,0:T(8,128)S(1)}, u32[]{:S(2)}, u32[]{:S(2)}) collective-permute-start(f32[1,96,3,128]{3,1,2,0:T(8,128)S(1)} %get-tuple-element.85), channel_id=1, source_target_pairs={{0,4},{4,8},{8,12},{12,16},{16,20},{20,24},{24,28},{1,5},{5,9},{9,... | collective-permute-start | bytes 442376 | tf_op jit(solution)/shard_map/ppermute | solution.py:16
  33.4 6.0 %collective-permute-start.6 = (f32[1,168,128]{2,1,0:T(8,128)S(1)}, f32[1,168,128]{2,1,0:T(8,128)S(1)}, u32[]{:S(2)}, u32[]{:S(2)}) collective-permute-start(f32[1,168,128]{2,1,0:T(8,128)S(1)} %dynamic-slice_add_fusion.1), channel_id=1, source_target_pairs={{0,3},{1,2},{2,1},{3,0},{4,7},{5,6},{6,5},{7,4},{8,11},{9,10},{10,... | collective-permute-start | bytes 258056 | tf_op jit(solution)/shard_map/ppermute | solution.py:62
  35.9 5.7 %collective-permute-start.5 = (f32[1,168,128]{2,1,0:T(8,128)S(1)}, f32[1,168,128]{2,1,0:T(8,128)S(1)}, u32[]{:S(2)}, u32[]{:S(2)}) collective-permute-start(f32[1,168,128]{2,1,0:T(8,128)S(1)} %dynamic-slice_add_fusion.1), channel_id=1, source_target_pairs={{0,2},{1,3},{2,0},{3,1},{4,6},{5,7},{6,4},{7,5},{8,10},{9,11},{10,... | collective-permute-start | bytes 258056 | tf_op jit(solution)/shard_map/ppermute | solution.py:62
  36.4 5.3 %collective-permute-start.4 = (f32[1,168,128]{2,1,0:T(8,128)S(1)}, f32[1,168,128]{2,1,0:T(8,128)S(1)}, u32[]{:S(2)}, u32[]{:S(2)}) collective-permute-start(f32[1,168,128]{2,1,0:T(8,128)S(1)} %dynamic-slice_add_fusion.1), channel_id=1, source_target_pairs={{0,1},{1,0},{2,3},{3,2},{4,5},{5,4},{6,7},{7,6},{8,9},{9,8},{10,11... | collective-permute-start | bytes 258056 | tf_op jit(solution)/shard_map/ppermute | solution.py:62
  41.7 7.3 %collective-permute-start.7 = (f32[1,168,128]{2,1,0:T(8,128)S(1)}, f32[1,168,128]{2,1,0:T(8,128)S(1)}, u32[]{:S(2)}, u32[]{:S(2)}) collective-permute-start(f32[1,168,128]{2,1,0:T(8,128)S(1)} %add_add_fusion), channel_id=1, source_target_pairs={{0,16},{4,20},{8,24},{12,28},{16,0},{20,4},{24,8},{28,12},{1,17},{... | collective-permute-start | bytes 258056 | tf_op jit(solution)/shard_map/ppermute | solution.py:62
  49.0 4.6 %collective-permute-start.10 = (f32[1,168,128]{2,1,0:T(8,128)S(1)}, f32[1,168,128]{2,1,0:T(8,128)S(1)}, u32[]{:S(2)}, u32[]{:S(2)}) collective-permute-start(f32[1,168,128]{2,1,0:T(8,128)S(1)} %add.488), channel_id=1, source_target_pairs={{0,8},{4,12},{8,0},{12,4},{16,24},{20,28},{24,16},{28,20},{1,9},{5... | collective-permute-start | bytes 258056 | tf_op jit(solution)/shard_map/ppermute | solution.py:69
  53.6 1.5 %collective-permute-start.11 = (f32[2,168,128]{2,1,0:T(8,128)S(1)}, f32[2,168,128]{2,1,0:T(8,128)S(1)}, u32[]{:S(2)}, u32[]{:S(2)}) collective-permute-start(f32[2,168,128]{2,1,0:T(8,128)S(1)} %pad_maximum_fusion.3), channel_id=1, source_target_pairs={{0,4},{4,0},{8,12},{12,8},{16,20},{20,16},{24,28},{28,24},{1,5},{5... | collective-permute-start | bytes 516104 | tf_op jit(solution)/shard_map/ppermute | solution.py:69

commit v8 on v7

--- a/solution.py
+++ b/solution.py
@@ -6,11 +6,18 @@
 from jax.sharding import PartitionSpec as P
 
 
-def with_halo(array, sides, width):
+def with_halo(array, sides, width, whole=False):
     for axis, dim in sides:
         size, length = (lax.axis_size(axis), array.shape[dim])
         up = [(i, (i + 1) % size) for i in range(size - 1)]
         down = [(j, i) for i, j in up]
+        if whole:
+            before = lax.ppermute(array, axis, up)
+            after = lax.ppermute(array, axis, down)
+            before = lax.slice_in_dim(before, length - width, length, axis=dim)
+            after = lax.slice_in_dim(after, 0, width, axis=dim)
+            array = jnp.concatenate([before, array, after], axis=dim)
+            continue
         last = lax.slice_in_dim(array, length - width, length, axis=dim)
         first = lax.slice_in_dim(array, 0, width, axis=dim)
         before = lax.ppermute(last, axis, up)
@@ -103,7 +110,7 @@
     rows = images.shape[2]
     cols = images.shape[3]
     kernel = conv_weight.shape[1]
-    extended = with_halo(images, (("strip", 2),), 3)
+    extended = with_halo(images, (("strip", 2),), 3, whole=True)
     upstream = cotangent.astype(jnp.float32)
     padded = jnp.pad(extended, ((0, 0), (0, 0), (0, 0), (3, 3)))
     conv = jnp.zeros((slides_here, chans, rows, cols), jnp.float32) + conv_bias[None, :, None, None]

time: 59 us -> 58.1 us (0.985)
  local copies, waits for them, and re-layouts: 8.73 us -> 6.78 us
  other arithmetic: 12.4 us -> 13.4 us
    ppermute x0 -> x2, starting transfers between devices: none -> 4.47 us  [the longest x1 3.04 us: with_halo(): before = lax.ppermute(array, axis, up)]
    ppermute x2 -> x1, starting transfers between devices: 6.25 us -> 3.22 us  [with_halo(): before = lax.ppermute(last, axis, up)]
    ppermute x2 -> x1, starting transfers between devices: 2.58 us -> 1.29 us  [with_halo(): after = lax.ppermute(first, axis, down)]
    slice x2 -> x1, local copies, waits for them, and re-layouts: 1.01 us -> 0.02 us  [with_halo(): last = lax.slice_in_dim(array, length - width, length, axis=dim)]
    concatenate x2 -> x0, local copies, waits for them, and re-layouts: 0.98 us -> none  [with_halo(): array = jnp.concatenate([before, array, after], axis=dim)]
    concatenate x2, other arithmetic: 0.64 us -> 1.56 us  [with_halo(): array = jnp.concatenate([before, array, after], axis=dim)]
    reduce_sum x3 -> x4, other arithmetic: 2.94 us -> 2.97 us  [on_device(): jnp.sum(d_conv * padded[:, :, a:a + rows, b:b + cols], axis=(0, 2, 3))]
  transfers between devices with their start and end apart: 12 -> 12, of which waited for: 7 -> 7; matrix products, arithmetic and copies ran while one was open for 16% -> 15% of each run, Pallas kernels for 0% -> 0%
where the time goes in v8:
time: 58.1 us; the launch traced here: 57.8 us
  starting transfers between devices  19 us (33%)
  other arithmetic  13.4 us (23%)
  waiting for transfers between devices  12.3 us (21%)
  local copies, waits for them, and re-layouts  6.78 us (12%)
  matrix products  4.99 us (9%)
  between operations  1.23 us (2%)
    ppermute x2, waiting for transfers between devices, tree_psum(): got = lax.ppermute(flat, axis, xor_pairs(size, bit))  5.86 us
    ppermute x4, starting transfers between devices, tree_psum(): got = [lax.ppermute(flat, axis, xor_pairs(size, mask)) for mask in masks]  5.55 us
    ppermute x4, waiting for transfers between devices, tree_psum(): got = [lax.ppermute(flat, axis, xor_pairs(size, mask)) for mask in masks]  5.43 us
    ppermute x2, starting transfers between devices, tree_psum(): flat = keep + lax.ppermute(give, axis, xor_pairs(size, bit))  4.37 us
    convert_element_type x1, other arithmetic, on_device(): image_grad.astype(jnp.bfloat16)  4.21 us
    ppermute x1, starting transfers between devices, with_halo(): before = lax.ppermute(last, axis, up)  3.22 us
    reduce_sum x1, other arithmetic, on_device(): centre = conv - jnp.mean(conv, axis=1, keepdims=True)  3.07 us
    ppermute x1, starting transfers between devices, with_halo(): before = lax.ppermute(array, axis, up)  3.04 us
  transfers between devices with their start and end apart: 12, of which 7 were waited for; matrix products, arithmetic and copies ran while one was open for 15% of the time, Pallas kernels for 0%

profile of v8, /device:TPU:0, one launch (start us, length us, event | category | flops | bytes accessed | tf_op | source)
XLA Modules:
  0.0 57.8 jit_solution(8526471221745950940)
XLA Ops:
  0.7 1.4 %collective-permute-start.1 = (bf16[1,96,6,128]{3,1,2,0:T(8,128)(2,1)}, bf16[1,96,6,128]{3,1,2,0:T(8,128)(2,1)S(1)}, u32[]{:S(2)}, u32[]{:S(2)}) collective-permute-start(bf16[1,96,6,128]{3,1,2,0:T(8,128)(2,1)} %param.11), channel_id=1, source_target_pairs={{4,0},{8,4},{12,8},{16,12},{20,16},{24,20},{28,24},{5,1},{9,5},{13... | collective-permute-start | bytes 442376 | tf_op jit(solution)/shard_map/ppermute | solution.py:16
  2.1 3.0 %collective-permute-start = (bf16[1,96,6,128]{3,1,2,0:T(8,128)(2,1)}, bf16[1,96,6,128]{3,1,2,0:T(8,128)(2,1)S(1)}, u32[]{:S(2)}, u32[]{:S(2)}) collective-permute-start(bf16[1,96,6,128]{3,1,2,0:T(8,128)(2,1)} %param.11), channel_id=1, source_target_pairs={{0,4},{4,8},{8,12},{12,16},{16,20},{20,24},{24,28},{1,5},{5,9},{9,... | collective-permute-start | bytes 442376 | tf_op jit(solution)/shard_map/ppermute | solution.py:15
  5.2 0.9 %slice_bitcast_fusion.48 = (f32[96]{0:T(128)S(1)}, f32[96]{0:T(128)S(1)}, f32[96]{0:T(128)S(1)}, f32[96]{0:T(128)S(1)}, f32[96]{0:T(128)S(1)}, /*index=5*/f32[96...) fusion(f32[96,7,7]{0,2,1:T(8,128)} %param.13), kind=kLoop, calls=%fused_computation.464 | loop fusion | bytes 8448 | tf_op jit(solution)/shard_map/mul | solution.py:121
  6.1 1.0 %slice_bitcast_fusion.50 = (f32[96]{0:T(128)S(1)}, f32[96]{0:T(128)S(1)}, f32[96]{0:T(128)S(1)}, f32[96]{0:T(128)S(1)}, f32[96]{0:T(128)S(1)}, /*index=5*/f32[96...) fusion(f32[96,7,7]{0,2,1:T(8,128)} %param.13), kind=kLoop, calls=%fused_computation.466 | loop fusion | bytes 14592 | tf_op jit(solution)/shard_map/mul | solution.py:121
  7.0 1.0 %slice_bitcast_fusion.49 = (f32[96]{0:T(128)S(1)}, f32[96]{0:T(128)S(1)}, f32[96]{0:T(128)S(1)}, f32[96]{0:T(128)S(1)}, f32[96]{0:T(128)S(1)}, /*index=5*/f32[96...) fusion(f32[96,7,7]{0,2,1:T(8,128)} %param.13), kind=kLoop, calls=%fused_computation.465 | loop fusion | bytes 14592 | tf_op jit(solution)/shard_map/mul | solution.py:121
  8.1 1.1 %convert_reduce_fusion.1 = f32[96]{0:T(128)S(1)} fusion(bf16[1,96,6,128]{3,1,2,0:T(8,128)(2,1)} %param.12, f32[96]{0:T(128)} %param.21), kind=kLoop, calls=%fused_computation.363 | loop fusion | flops 368544 | bytes 148224 | tf_op jit(solution)/shard_map/reduce_sum | solution.py:171
  9.2 1.2 %select_maximum_fusion.2 = bf16[1,96,12,134]{3,1,2,0:T(8,128)(2,1)S(1)} fusion(bf16[1,96,3,128]{3,1,2,0:T(8,128)(2,1)S(1)} %slice.767, bf16[1,96,6,128]{3,1,2,0:T(8,128)(2,1)} %param.11, bf16[1,96,3,128]{3,1,2,0:T(8,128)(2,1)S(1)} %slice.766), kind=kLoop, calls=%fused_computation.43 | loop fusion | flops 1852416 | bytes 603648 | tf_op jit(solution)/shard_map/concatenate | solution.py:19
  10.5 3.1 %fusion.203 = (f32[6,128]{1,0:T(8,128)S(1)}, f32[1,96,6,128]{3,1,2,0:T(8,128)S(1)}) fusion(bf16[1,96,12,134]{3,1,2,0:T(8,128)(2,1)S(1)} %select_maximum_fusion.2, f32[96]{0:T(128)S(1)} %get-tuple-element.130, f32[96]{0:T(128)S(1)} %get-tuple-element.131, f32[96]{0:T(128)S(1)} %get-tuple-element.84, bf16[1,96,3,128]{3,1,2,0:T(8,128)(2,1)S(1)} %slice.767, ...), kind=kLoop, calls=%fused_computation.472 | loop fusion | flops 11353344 | bytes 6805248 | tf_op jit(solution)/shard_map/reduce_sum | solution.py:124
  13.7 2.8 %fusion.9 = (bf16[384,6,128]{0,2,1:T(8,128)(2,1)S(1)}, f32[384,6,128]{0,2,1:T(8,128)S(1)}) fusion(f32[384]{0:T(512)S(1)} %copy-done.8, bf16[96,384]{1,0:T(8,128)(2,1)S(1)} %copy-done, f32[1,96,6,128]{3,1,2,0:T(8,128)S(1)} %get-tuple-element.71, f32[96]{0:T(128)S(1)} %copy-done.5, f32[96]{0:T(128)S(1)} %copy-done.3, f32[6,128]{1,0:T(8,128)S(1)} %add_rsqrt_fusion, ...), kind=kOutput, calls=%fused_computation.15 | convolution fusion | flops 76455936 | bytes 2146560 | tf_op jit(solution)/shard_map/scrw,cf->sfrw/dot_general | solution.py:131
  16.6 0.7 %convert_reduce_fusion = (f32[384]{0:T(512)S(1)}, bf16[384,6,128]{0,2,1:T(8,128)(2,1)S(1)}) fusion(f32[384,6,128]{0,2,1:T(8,128)S(1)} %get-tuple-element.136, bf16[384,96]{0,1:T(8,128)(2,1)S(1)} %copy-done.7, bf16[1,96,6,128]{3,1,2,0:T(8,128)(2,1)S(1)} %copy-done.2, f32[96]{0:T(128)S(1)} %copy-done.4), kind=kOutput, calls=%fused_computation.31 | convolution fusion | flops 60382848 | bytes 1992576 | tf_op jit(solution)/shard_map/scrw,fc->sfrw/dot_general | solution.py:140
  17.3 0.4 fusion.181
  17.7 0.1 fusion.185
  17.9 1.2 %fusion.121 = (f32[96]{0:T(128)S(1)}, f32[96]{0:T(128)S(1)}, f32[96]{0:T(128)S(1)}, f32[96]{0:T(128)S(1)}, f32[96]{0:T(128)S(1)}, /*index=5*/f32[96]{0:T(128)S(1...) fusion(bf16[1,96,12,134]{3,1,2,0:T(8,128)(2,1)S(1)} %select_max, ...), kind=kLoop, calls=%fused_computation.252 | loop fusion | flops 4495680 | bytes 3558528 | tf_op jit(solution)/shard_map/reduce_sum | solution.py:160
  19.0 0.4 fusion.55
  19.5 0.3 fusion.118
  19.8 1.1 %fusion.100 = (f32[96]{0:T(128)S(1)}, f32[96]{0:T(128)S(1)}, f32[96]{0:T(128)S(1)}, f32[96]{0:T(128)S(1)}, f32[96]{0:T(128)S(1)}, /*index=5*/f32[96]{0:T(128)S(1...) fusion(f32[1,96,6,128]{3,1,2,0:T(8,128)S(1)} %get-tuple-element, ...), kind=kLoop, calls=%fused_computation.231 | loop fusion | flops 3979584 | bytes 2956032 | tf_op jit(solution)/shard_map/reduce_sum | solution.py:160
  20.8 0.3 fusion.21
  21.2 0.1 stack.199
  21.3 0.1 mul.1289
  21.4 0.1 reduce_sum.586
  21.6 0.3 fusion.22
  21.9 0.4 fusion.20
  22.5 2.7 %collective-permute-start.2 = (f32[2,168,128]{2,1,0:T(8,128)S(1)}, f32[2,168,128]{2,1,0:T(8,128)S(1)}, u32[]{:S(2)}, u32[]{:S(2)}) collective-permute-start(f32[2,168,128]{2,1,0:T(8,128)S(1)} %constant_dynamic-slice_fusion.1), channel_id=1, source_target_pairs={{0,4},{4,0},{8,12},{12,8},{16,20},{20,16},{24,28},{28,24},{1,5},{5... | collective-permute-start | bytes 516104 | tf_op jit(solution)/shard_map/ppermute | solution.py:63
  25.3 1.0 %collective-permute-done.2 = f32[2,168,128]{2,1,0:T(8,128)S(1)} collective-permute-done((f32[2,168,128]{2,1,0:T(8,128)S(1)}, f32[2,168,128]{2,1,0:T(8,128)S(1)}, u32[]{:S(2)}, u32[]{:S(2)}) %collective-permute-start.2) | collective-permute-done | bytes 172064 | tf_op jit(solution)/shard_map/ppermute | solution.py:63
  26.3 1.6 %collective-permute-start.3 = (f32[1,168,128]{2,1,0:T(8,128)S(1)}, f32[1,168,128]{2,1,0:T(8,128)S(1)}, u32[]{:S(2)}, u32[]{:S(2)}) collective-permute-start(f32[1,168,128]{2,1,0:T(8,128)S(1)} %constant_dynamic-slice_fusion), channel_id=1, source_target_pairs={{0,8},{4,12},{8,0},{12,4},{16,24},{20,28},{24,16},{28,20},{1,9},{5... | collective-permute-start | bytes 258056 | tf_op jit(solution)/shard_map/ppermute | solution.py:63
  28.0 1.3 %collective-permute-start.9 = (f32[1,96,3,128]{3,1,2,0:T(8,128)S(1)}, f32[1,96,3,128]{3,1,2,0:T(8,128)S(1)}, u32[]{:S(2)}, u32[]{:S(2)}) collective-permute-start(f32[1,96,3,128]{3,1,2,0:T(8,128)S(1)} %get-tuple-element.80), channel_id=1, source_target_pairs={{4,0},{8,4},{12,8},{16,12},{20,16},{24,20},{28,24},{5,1},{9,5},{13... | collective-permute-start | bytes 442376 | tf_op jit(solution)/shard_map/ppermute | solution.py:24
  29.3 3.2 %collective-permute-start.8 = (f32[1,96,3,128]{3,1,2,0:T(8,128)S(1)}, f32[1,96,3,128]{3,1,2,0:T(8,128)S(1)}, u32[]{:S(2)}, u32[]{:S(2)}) collective-permute-start(f32[1,96,3,128]{3,1,2,0:T(8,128)S(1)} %get-tuple-element.79), channel_id=1, source_target_pairs={{0,4},{4,8},{8,12},{12,16},{16,20},{20,24},{24,28},{1,5},{5,9},{9,... | collective-permute-start | bytes 442376 | tf_op jit(solution)/shard_map/ppermute | solution.py:23
  32.6 2.5 %collective-permute-start.6 = (f32[1,168,128]{2,1,0:T(8,128)S(1)}, f32[1,168,128]{2,1,0:T(8,128)S(1)}, u32[]{:S(2)}, u32[]{:S(2)}) collective-permute-start(f32[1,168,128]{2,1,0:T(8,128)S(1)} %dynamic-slice_add_fusion.1), channel_id=1, source_target_pairs={{0,3},{1,2},{2,1},{3,0},{4,7},{5,6},{6,5},{7,4},{8,11},{9,10},{10,... | collective-permute-start | bytes 258056 | tf_op jit(solution)/shard_map/ppermute | solution.py:69
  35.1 0.5 collective-permute-start.5
  35.6 0.5 collective-permute-start.4
  36.1 0.4 select_maximum_fusion
  36.5 2.1 %collective-permute-done.6 = f32[1,168,128]{2,1,0:T(8,128)S(1)} collective-permute-done((f32[1,168,128]{2,1,0:T(8,128)S(1)}, f32[1,168,128]{2,1,0:T(8,128)S(1)}, u32[]{:S(2)}, u32[]{:S(2)}) %collective-permute-start.6) | collective-permute-done | bytes 86048 | tf_op jit(solution)/shard_map/ppermute | solution.py:69
  38.6 2.2 %collective-permute-done.5 = f32[1,168,128]{2,1,0:T(8,128)S(1)} collective-permute-done((f32[1,168,128]{2,1,0:T(8,128)S(1)}, f32[1,168,128]{2,1,0:T(8,128)S(1)}, u32[]{:S(2)}, u32[]{:S(2)}) %collective-permute-start.5) | collective-permute-done | bytes 86048 | tf_op jit(solution)/shard_map/ppermute | solution.py:69
  40.8 0.1 collective-permute-done.4
  40.9 2.0 %collective-permute-start.7 = (f32[1,168,128]{2,1,0:T(8,128)S(1)}, f32[1,168,128]{2,1,0:T(8,128)S(1)}, u32[]{:S(2)}, u32[]{:S(2)}) collective-permute-start(f32[1,168,128]{2,1,0:T(8,128)S(1)} %add_add_fusion), channel_id=1, source_target_pairs={{0,16},{4,20},{8,24},{12,28},{16,0},{20,4},{24,8},{28,12},{1,17},{... | collective-permute-start | bytes 258056 | tf_op jit(solution)/shard_map/ppermute | solution.py:69
  42.9 4.2 %fusion.184 = bf16[1,96,6,128]{3,1,2,0:T(8,128)(2,1)} fusion(f32[1,96,12,134]{3,1,2,0:T(8,128)S(1)} %select_maximum_fusion, f32[1,96,6,128]{3,1,2,0:T(8,128)S(1)} %get-tuple-element.69, f32[1,96,3,128]{3,1,2,0:T(8,128)S(1)} %collective-permute-done.8, f32[1,96,3,128]{3,1,2,0:T(8,128)S(1)} %collective-permute-done.9, ...), kind=kLoop, calls=%fused_computation.366 | loop fusion | flops 7815168 | bytes 13289856 | tf_op jit(solution)/shard_map/convert_element_type | solution.py:174
  47.1 1.1 %collective-permute-done.7 = f32[1,168,128]{2,1,0:T(8,128)S(1)} collective-permute-done((f32[1,168,128]{2,1,0:T(8,128)S(1)}, f32[1,168,128]{2,1,0:T(8,128)S(1)}, u32[]{:S(2)}, u32[]{:S(2)}) %collective-permute-start.7) | collective-permute-done | bytes 86048 | tf_op jit(solution)/shard_map/ppermute | solution.py:69
  48.2 0.1 collective-permute-start.10
  48.3 4.5 %collective-permute-done.10 = f32[1,168,128]{2,1,0:T(8,128)S(1)} collective-permute-done((f32[1,168,128]{2,1,0:T(8,128)S(1)}, f32[1,168,128]{2,1,0:T(8,128)S(1)}, u32[]{:S(2)}, u32[]{:S(2)}) %collective-permute-start.10) | collective-permute-done | bytes 86048 | tf_op jit(solution)/shard_map/ppermute | solution.py:76
  52.8 0.1 collective-permute-start.11
  52.9 1.4 %collective-permute-done.11 = f32[2,168,128]{2,1,0:T(8,128)S(1)} collective-permute-done((f32[2,168,128]{2,1,0:T(8,128)S(1)}, f32[2,168,128]{2,1,0:T(8,128)S(1)}, u32[]{:S(2)}, u32[]{:S(2)}) %collective-permute-start.11) | collective-permute-done | bytes 172064 | tf_op jit(solution)/shard_map/ppermute | solution.py:76
  54.3 0.3 slice.755
  54.6 0.5 fusion.205
  55.1 0.6 %slice.875 = f32[384]{0:T(512)} slice(f32[86016]{0:T(1024)S(1)} %bitcast.235), slice={[45056:45440]} | slice | bytes 3072 | tf_op jit(solution)/shard_map/slice | solution.py:84
  55.7 0.1 slice.762
  55.8 0.6 %slice_bitcast_fusion.1 = f32[96,7,7]{0,2,1:T(8,128)} fusion(f32[128,7,96]{2,1,0:T(8,128)S(1)} %slice.755), kind=kLoop, calls=%fused_computation.400 | loop fusion | bytes 37632 | tf_op jit(solution)/shard_map/transpose | solution.py:175
  56.4 0.7 %reshape.363 = f32[96,384]{1,0:T(8,128)} reshape(f32[36864]{0:T(1024)S(1)} %slice.874) | data formatting | bytes 294912 | tf_op jit(solution)/shard_map/reshape | solution.py:84
  57.1 0.7 %slice_bitcast_fusion = f32[384,96]{0,1:T(8,128)} fusion(f32[224,384]{1,0:T(8,128)S(1)} %slice.762), kind=kLoop, calls=%fused_computation.384 | loop fusion | bytes 294912 | tf_op jit(solution)/shard_map/transpose | solution.py:176
  (62 shorter events, 0.5 us)
Async XLA Ops:
  0.6 13.0 %copy-start = (bf16[96,384]{1,0:T(8,128)(2,1)S(1)}, bf16[96,384]{1,0:T(8,128)(2,1)}, u32[]{:S(2)}) copy-start(bf16[96,384]{1,0:T(8,128)(2,1)} %param.17) | copy-start | bytes 221188
  0.7 9.8 %copy-start.1 = (bf16[1,96,6,128]{3,1,2,0:T(8,128)(2,1)S(1)}, bf16[1,96,6,128]{3,1,2,0:T(8,128)(2,1)}, u32[]{:S(2)}) copy-start(bf16[1,96,6,128]{3,1,2,0:T(8,128)(2,1)} %param.11) | copy-start | bytes 442372
  0.7 9.8 %copy-start.6 = (f32[96]{0:T(128)S(1)}, f32[96]{0:T(128)}, u32[]{:S(2)}) copy-start(f32[96]{0:T(128)} %param.14) | copy-start | bytes 1156
  0.7 8.5 %collective-permute-start.1 = (bf16[1,96,6,128]{3,1,2,0:T(8,128)(2,1)}, bf16[1,96,6,128]{3,1,2,0:T(8,128)(2,1)S(1)}, u32[]{:S(2)}, u32[]{:S(2)}) collective-permute-start(bf16[1,96,6,128]{3,1,2,0:T(8,128)(2,1)} %param.11), channel_id=1, source_target_pairs={{4,0},{8,4},{12,8},{16,12},{20,16},{24,20},{28,24},{5,1},{9,5},{13... | collective-permute-start | bytes 442376 | tf_op jit(solution)/shard_map/ppermute | solution.py:16
  2.1 7.1 %collective-permute-start = (bf16[1,96,6,128]{3,1,2,0:T(8,128)(2,1)}, bf16[1,96,6,128]{3,1,2,0:T(8,128)(2,1)S(1)}, u32[]{:S(2)}, u32[]{:S(2)}) collective-permute-start(bf16[1,96,6,128]{3,1,2,0:T(8,128)(2,1)} %param.11), channel_id=1, source_target_pairs={{0,4},{4,8},{8,12},{12,16},{16,20},{20,24},{24,28},{1,5},{5,9},{9,... | collective-permute-start | bytes 442376 | tf_op jit(solution)/shard_map/ppermute | solution.py:15
  10.5 3.2 %copy-start.3 = (f32[96]{0:T(128)S(1)}, f32[96]{0:T(128)}, u32[]{:S(2)}) copy-start(f32[96]{0:T(128)} %param.15) | copy-start | bytes 1156
  10.5 3.2 %copy-start.5 = (f32[96]{0:T(128)S(1)}, f32[96]{0:T(128)}, u32[]{:S(2)}) copy-start(f32[96]{0:T(128)} %param.16) | copy-start | bytes 1156
  10.5 3.2 %copy-start.8 = (f32[384]{0:T(512)S(1)}, f32[384]{0:T(512)}, u32[]{:S(2)}) copy-start(f32[384]{0:T(512)} %param.18) | copy-start | bytes 4612
  13.7 2.9 %copy-start.2 = (bf16[1,96,6,128]{3,1,2,0:T(8,128)(2,1)S(1)}, bf16[1,96,6,128]{3,1,2,0:T(8,128)(2,1)}, u32[]{:S(2)}) copy-start(bf16[1,96,6,128]{3,1,2,0:T(8,128)(2,1)} %param.12) | copy-start | bytes 442372
  13.7 2.9 %copy-start.4 = (f32[96]{0:T(128)S(1)}, f32[96]{0:T(128)}, u32[]{:S(2)}) copy-start(f32[96]{0:T(128)} %param.21) | copy-start | bytes 1156
  13.7 2.9 %copy-start.7 = (bf16[384,96]{0,1:T(8,128)(2,1)S(1)}, bf16[384,96]{0,1:T(8,128)(2,1)}, u32[]{:S(2)}) copy-start(bf16[384,96]{0,1:T(8,128)(2,1)} %param.19) | copy-start | bytes 221188
  21.2 0.8 %copy-start.9 = (f32[96]{0:T(128)S(1)}, f32[96]{0:T(128)}, u32[]{:S(2)}) copy-start(f32[96]{0:T(128)} %param.20) | copy-start | bytes 1156
  22.5 3.8 %collective-permute-start.2 = (f32[2,168,128]{2,1,0:T(8,128)S(1)}, f32[2,168,128]{2,1,0:T(8,128)S(1)}, u32[]{:S(2)}, u32[]{:S(2)}) collective-permute-start(f32[2,168,128]{2,1,0:T(8,128)S(1)} %constant_dynamic-slice_fusion.1), channel_id=1, source_target_pairs={{0,4},{4,0},{8,12},{12,8},{16,20},{20,16},{24,28},{28,24},{1,5},{5... | collective-permute-start | bytes 516104 | tf_op jit(solution)/shard_map/ppermute | solution.py:63
  26.3 6.2 %collective-permute-start.3 = (f32[1,168,128]{2,1,0:T(8,128)S(1)}, f32[1,168,128]{2,1,0:T(8,128)S(1)}, u32[]{:S(2)}, u32[]{:S(2)}) collective-permute-start(f32[1,168,128]{2,1,0:T(8,128)S(1)} %constant_dynamic-slice_fusion), channel_id=1, source_target_pairs={{0,8},{4,12},{8,0},{12,4},{16,24},{20,28},{24,16},{28,20},{1,9},{5... | collective-permute-start | bytes 258056 | tf_op jit(solution)/shard_map/ppermute | solution.py:63
  28.0 8.1 %collective-permute-start.9 = (f32[1,96,3,128]{3,1,2,0:T(8,128)S(1)}, f32[1,96,3,128]{3,1,2,0:T(8,128)S(1)}, u32[]{:S(2)}, u32[]{:S(2)}) collective-permute-start(f32[1,96,3,128]{3,1,2,0:T(8,128)S(1)} %get-tuple-element.80), channel_id=1, source_target_pairs={{4,0},{8,4},{12,8},{16,12},{20,16},{24,20},{28,24},{5,1},{9,5},{13... | collective-permute-start | bytes 442376 | tf_op jit(solution)/shard_map/ppermute | solution.py:24
  29.3 6.8 %collective-permute-start.8 = (f32[1,96,3,128]{3,1,2,0:T(8,128)S(1)}, f32[1,96,3,128]{3,1,2,0:T(8,128)S(1)}, u32[]{:S(2)}, u32[]{:S(2)}) collective-permute-start(f32[1,96,3,128]{3,1,2,0:T(8,128)S(1)} %get-tuple-element.79), channel_id=1, source_target_pairs={{0,4},{4,8},{8,12},{12,16},{16,20},{20,24},{24,28},{1,5},{5,9},{9,... | collective-permute-start | bytes 442376 | tf_op jit(solution)/shard_map/ppermute | solution.py:23
  32.6 6.0 %collective-permute-start.6 = (f32[1,168,128]{2,1,0:T(8,128)S(1)}, f32[1,168,128]{2,1,0:T(8,128)S(1)}, u32[]{:S(2)}, u32[]{:S(2)}) collective-permute-start(f32[1,168,128]{2,1,0:T(8,128)S(1)} %dynamic-slice_add_fusion.1), channel_id=1, source_target_pairs={{0,3},{1,2},{2,1},{3,0},{4,7},{5,6},{6,5},{7,4},{8,11},{9,10},{10,... | collective-permute-start | bytes 258056 | tf_op jit(solution)/shard_map/ppermute | solution.py:69
  35.1 5.7 %collective-permute-start.5 = (f32[1,168,128]{2,1,0:T(8,128)S(1)}, f32[1,168,128]{2,1,0:T(8,128)S(1)}, u32[]{:S(2)}, u32[]{:S(2)}) collective-permute-start(f32[1,168,128]{2,1,0:T(8,128)S(1)} %dynamic-slice_add_fusion.1), channel_id=1, source_target_pairs={{0,2},{1,3},{2,0},{3,1},{4,6},{5,7},{6,4},{7,5},{8,10},{9,11},{10,... | collective-permute-start | bytes 258056 | tf_op jit(solution)/shard_map/ppermute | solution.py:69
  35.6 5.3 %collective-permute-start.4 = (f32[1,168,128]{2,1,0:T(8,128)S(1)}, f32[1,168,128]{2,1,0:T(8,128)S(1)}, u32[]{:S(2)}, u32[]{:S(2)}) collective-permute-start(f32[1,168,128]{2,1,0:T(8,128)S(1)} %dynamic-slice_add_fusion.1), channel_id=1, source_target_pairs={{0,1},{1,0},{2,3},{3,2},{4,5},{5,4},{6,7},{7,6},{8,9},{9,8},{10,11... | collective-permute-start | bytes 258056 | tf_op jit(solution)/shard_map/ppermute | solution.py:69
  40.9 7.3 %collective-permute-start.7 = (f32[1,168,128]{2,1,0:T(8,128)S(1)}, f32[1,168,128]{2,1,0:T(8,128)S(1)}, u32[]{:S(2)}, u32[]{:S(2)}) collective-permute-start(f32[1,168,128]{2,1,0:T(8,128)S(1)} %add_add_fusion), channel_id=1, source_target_pairs={{0,16},{4,20},{8,24},{12,28},{16,0},{20,4},{24,8},{28,12},{1,17},{... | collective-permute-start | bytes 258056 | tf_op jit(solution)/shard_map/ppermute | solution.py:69
  48.2 4.6 %collective-permute-start.10 = (f32[1,168,128]{2,1,0:T(8,128)S(1)}, f32[1,168,128]{2,1,0:T(8,128)S(1)}, u32[]{:S(2)}, u32[]{:S(2)}) collective-permute-start(f32[1,168,128]{2,1,0:T(8,128)S(1)} %add.488), channel_id=1, source_target_pairs={{0,8},{4,12},{8,0},{12,4},{16,24},{20,28},{24,16},{28,20},{1,9},{5... | collective-permute-start | bytes 258056 | tf_op jit(solution)/shard_map/ppermute | solution.py:76
  52.8 1.5 %collective-permute-start.11 = (f32[2,168,128]{2,1,0:T(8,128)S(1)}, f32[2,168,128]{2,1,0:T(8,128)S(1)}, u32[]{:S(2)}, u32[]{:S(2)}) collective-permute-start(f32[2,168,128]{2,1,0:T(8,128)S(1)} %pad_maximum_fusion.3), channel_id=1, source_target_pairs={{0,4},{4,0},{8,12},{12,8},{16,20},{20,16},{24,28},{28,24},{1,5},{5... | collective-permute-start | bytes 516104 | tf_op jit(solution)/shard_map/ppermute | solution.py:76

commit v9 on v8

--- a/solution.py
+++ b/solution.py
@@ -39,7 +39,7 @@
     return bits
 
 
-def tree_psum(terms, hold):
+def tree_psum(terms, side_fn, side_in):
     shapes = [t.shape for t in terms]
     sizes = [math.prod(s) for s in shapes]
     rooms = [-(-size // 1024) * 1024 for size in sizes]
@@ -61,6 +61,8 @@
         keep = lax.dynamic_slice_in_dim(flat, mine * half, half, axis=0)
         give = lax.dynamic_slice_in_dim(flat, (1 - mine) * half, half, axis=0)
         flat = keep + lax.ppermute(give, axis, xor_pairs(size, bit))
+    flat, side_in = lax.optimization_barrier((flat, side_in))
+    hold = side_fn(*side_in)
     for axis, bits in stages:
         size = lax.axis_size(axis)
         masks = []
@@ -146,17 +148,22 @@
         - jnp.mean(d_normed, axis=1, keepdims=True)
         - normed * jnp.mean(d_normed * normed, axis=1, keepdims=True)
     )
-    d_wide = with_halo(d_conv, (("strip", 2),), 3)
-    d_padded = jnp.pad(d_wide, ((0, 0), (0, 0), (0, 0), (3, 3)))
-    image_grad = cotangent.astype(jnp.float32)
+    def image_grad_of(d_conv, cotangent):
+        d_wide = with_halo(d_conv, (("strip", 2),), 3)
+        d_padded = jnp.pad(d_wide, ((0, 0), (0, 0), (0, 0), (3, 3)))
+        image_grad = cotangent.astype(jnp.float32)
+        for a in range(kernel):
+            for b in range(kernel):
+                image_grad = (
+                    image_grad
+                    + conv_weight[:, a, b][None, :, None, None]
+                    * d_padded[:, :, 6 - a : 6 - a + rows, 6 - b : 6 - b + cols]
+                )
+        return image_grad.astype(jnp.bfloat16)
+
     taps = []
     for a in range(kernel):
         for b in range(kernel):
-            image_grad = (
-                image_grad
-                + conv_weight[:, a, b][None, :, None, None]
-                * d_padded[:, :, 6 - a : 6 - a + rows, 6 - b : 6 - b + cols]
-            )
             taps.append(jnp.sum(d_conv * padded[:, :, a : a + rows, b : b + cols], axis=(0, 2, 3)))
     pixel_count = slides_here * lax.axis_size("slide") * rows * lax.axis_size("strip") * cols
     scale = 1.0 / math.sqrt(float(pixel_count))
@@ -171,7 +178,9 @@
         jnp.sum(d_branch.astype(jnp.float32), axis=(0, 2, 3)),
         jnp.sum(upstream * branch, axis=(0, 2, 3)),
     )
-    g, image_grad = tree_psum([item * scale for item in terms], image_grad.astype(jnp.bfloat16))
+    g, image_grad = tree_psum(
+        [item * scale for item in terms], image_grad_of, (d_conv, cotangent)
+    )
     g[0] = g[0].reshape(kernel, kernel, chans).transpose(2, 0, 1)
     g[6] = g[6].T
     return (image_grad, g[0], g[1], g[2], g[3], g[4], g[5], g[6], g[7], g[8])

time: 58.1 us -> 60.4 us (1.040)
  starting transfers between devices: 19 us -> 20.7 us
    ppermute x2, waiting for transfers between devices: 1.04 us -> 4.26 us  [tree_psum(): flat = keep + lax.ppermute(give, axis, xor_pairs(size, bit))]
    ppermute x4, waiting for transfers between devices: 5.43 us -> 3.43 us  [tree_psum(): got = [lax.ppermute(flat, axis, xor_pairs(size, mask)) for mask in masks]]
    ppermute x1, starting transfers between devices: 3.22 us -> 1.3 us  [with_halo(): before = lax.ppermute(last, axis, up)]
    ppermute x4, starting transfers between devices: 5.55 us -> 7.11 us  [tree_psum(): got = [lax.ppermute(flat, axis, xor_pairs(size, mask)) for mask in masks]]
    ppermute x2, starting transfers between devices: 0.14 us -> 1.55 us  [tree_psum(): got = lax.ppermute(flat, axis, xor_pairs(size, bit))]
    ppermute x2, starting transfers between devices: 4.37 us -> 5.42 us  [tree_psum(): flat = keep + lax.ppermute(give, axis, xor_pairs(size, bit))]
    ppermute x2, waiting for transfers between devices: 5.86 us -> 4.84 us  [tree_psum(): got = lax.ppermute(flat, axis, xor_pairs(size, bit))]
  transfers between devices with their start and end apart: 12 -> 12, of which waited for: 7 -> 8; matrix products, arithmetic and copies ran while one was open for 15% -> 15% of each run, Pallas kernels for 0% -> 0%
where the time goes in v9:
time: 60.4 us; the launch traced here: 60 us
  starting transfers between devices  20.7 us (34%)
  other arithmetic  13.5 us (22%)
  waiting for transfers between devices  12.8 us (21%)
  local copies, waits for them, and re-layouts  6.84 us (11%)
  matrix products  4.98 us (8%)
  between operations  1.22 us (2%)
    ppermute x4, starting transfers between devices, tree_psum(): got = [lax.ppermute(flat, axis, xor_pairs(size, mask)) for mask in masks]  7.11 us
    ppermute x2, starting transfers between devices, tree_psum(): flat = keep + lax.ppermute(give, axis, xor_pairs(size, bit))  5.42 us
    ppermute x2, waiting for transfers between devices, tree_psum(): got = lax.ppermute(flat, axis, xor_pairs(size, bit))  4.84 us
    convert_element_type x1, other arithmetic, image_grad_of(): return image_grad.astype(jnp.bfloat16)  4.32 us
    ppermute x2, waiting for transfers between devices, tree_psum(): flat = keep + lax.ppermute(give, axis, xor_pairs(size, bit))  4.26 us
    ppermute x4, waiting for transfers between devices, tree_psum(): got = [lax.ppermute(flat, axis, xor_pairs(size, mask)) for mask in masks]  3.43 us
    reduce_sum x1, other arithmetic, on_device(): centre = conv - jnp.mean(conv, axis=1, keepdims=True)  3.07 us
    reduce_sum x4, other arithmetic, on_device(): jnp.sum(d_conv * padded[:, :, a:a + rows, b:b + cols], axis=(0, 2, 3))  2.96 us
  transfers between devices with their start and end apart: 12, of which 8 were waited for; matrix products, arithmetic and copies ran while one was open for 15% of the time, Pallas kernels for 0%

profile of v9, /device:TPU:0, one launch (start us, length us, event | category | flops | bytes accessed | tf_op | source)
XLA Modules:
  0.0 60.0 jit_solution(10563143805253427157)
XLA Ops:
  0.7 2.5 %collective-permute-start = (bf16[1,96,6,128]{3,1,2,0:T(8,128)(2,1)}, bf16[1,96,6,128]{3,1,2,0:T(8,128)(2,1)S(1)}, u32[]{:S(2)}, u32[]{:S(2)}) collective-permute-start(bf16[1,96,6,128]{3,1,2,0:T(8,128)(2,1)} %param.11), channel_id=1, source_target_pairs={{0,4},{4,8},{8,12},{12,16},{16,20},{20,24},{24,28},{1,5},{5,9},{9,... | collective-permute-start | bytes 442376 | tf_op jit(solution)/shard_map/ppermute | solution.py:15
  3.2 1.3 %collective-permute-start.1 = (bf16[1,96,6,128]{3,1,2,0:T(8,128)(2,1)}, bf16[1,96,6,128]{3,1,2,0:T(8,128)(2,1)S(1)}, u32[]{:S(2)}, u32[]{:S(2)}) collective-permute-start(bf16[1,96,6,128]{3,1,2,0:T(8,128)(2,1)} %param.11), channel_id=1, source_target_pairs={{4,0},{8,4},{12,8},{16,12},{20,16},{24,20},{28,24},{5,1},{9,5},{13... | collective-permute-start | bytes 442376 | tf_op jit(solution)/shard_map/ppermute | solution.py:16
  4.5 1.0 %slice_bitcast_fusion.50 = (f32[96]{0:T(128)S(1)}, f32[96]{0:T(128)S(1)}, f32[96]{0:T(128)S(1)}, f32[96]{0:T(128)S(1)}, f32[96]{0:T(128)S(1)}, /*index=5*/f32[96...) fusion(f32[96,7,7]{0,2,1:T(8,128)} %param.13), kind=kLoop, calls=%fused_computation.456 | loop fusion | bytes 14592 | tf_op jit(solution)/shard_map/mul | solution.py:123
  5.5 1.0 %slice_bitcast_fusion.49 = (f32[96]{0:T(128)S(1)}, f32[96]{0:T(128)S(1)}, f32[96]{0:T(128)S(1)}, f32[96]{0:T(128)S(1)}, f32[96]{0:T(128)S(1)}, /*index=5*/f32[96...) fusion(f32[96,7,7]{0,2,1:T(8,128)} %param.13), kind=kLoop, calls=%fused_computation.455 | loop fusion | bytes 14592 | tf_op jit(solution)/shard_map/mul | solution.py:123
  6.5 0.9 %slice_bitcast_fusion.48 = (f32[96]{0:T(128)S(1)}, f32[96]{0:T(128)S(1)}, f32[96]{0:T(128)S(1)}, f32[96]{0:T(128)S(1)}, f32[96]{0:T(128)S(1)}, /*index=5*/f32[96...) fusion(f32[96,7,7]{0,2,1:T(8,128)} %param.13), kind=kLoop, calls=%fused_computation.454 | loop fusion | bytes 8448 | tf_op jit(solution)/shard_map/mul | solution.py:123
  7.4 1.1 %convert_reduce_fusion.1 = f32[96]{0:T(128)S(1)} fusion(bf16[1,96,6,128]{3,1,2,0:T(8,128)(2,1)} %param.12, f32[96]{0:T(128)} %param.21), kind=kLoop, calls=%fused_computation.350 | loop fusion | flops 368544 | bytes 148224 | tf_op jit(solution)/shard_map/reduce_sum | solution.py:178
  8.6 0.3 collective-permute-done.1
  8.9 1.2 %select_maximum_fusion.2 = bf16[1,96,12,134]{3,1,2,0:T(8,128)(2,1)S(1)} fusion(bf16[1,96,3,128]{3,1,2,0:T(8,128)(2,1)S(1)} %slice.767, bf16[1,96,6,128]{3,1,2,0:T(8,128)(2,1)} %param.11, bf16[1,96,3,128]{3,1,2,0:T(8,128)(2,1)S(1)} %slice.766), kind=kLoop, calls=%fused_computation.43 | loop fusion | flops 1852416 | bytes 603648 | tf_op jit(solution)/shard_map/concatenate | solution.py:19
  10.1 3.1 %fusion.194 = (f32[6,128]{1,0:T(8,128)S(1)}, f32[1,96,6,128]{3,1,2,0:T(8,128)S(1)}) fusion(bf16[1,96,12,134]{3,1,2,0:T(8,128)(2,1)S(1)} %select_maximum_fusion.2, f32[96]{0:T(128)S(1)} %get-tuple-element.138, f32[96]{0:T(128)S(1)} %get-tuple-element.139, f32[96]{0:T(128)S(1)} %get-tuple-element.92, bf16[1,96,3,128]{3,1,2,0:T(8,128)(2,1)S(1)} %slice.767, ...), kind=kLoop, calls=%fused_computation.462 | loop fusion | flops 11353344 | bytes 6805248 | tf_op jit(solution)/shard_map/reduce_sum | solution.py:126
  13.4 2.8 %fusion.9 = (bf16[384,6,128]{0,2,1:T(8,128)(2,1)S(1)}, f32[384,6,128]{0,2,1:T(8,128)S(1)}) fusion(f32[384]{0:T(512)S(1)} %copy-done.8, bf16[96,384]{1,0:T(8,128)(2,1)S(1)} %copy-done, f32[1,96,6,128]{3,1,2,0:T(8,128)S(1)} %get-tuple-element.77, f32[96]{0:T(128)S(1)} %copy-done.5, f32[96]{0:T(128)S(1)} %copy-done.3, f32[6,128]{1,0:T(8,128)S(1)} %add_rsqrt_fusion, ...), kind=kOutput, calls=%fused_computation.15 | convolution fusion | flops 76455936 | bytes 2146560 | tf_op jit(solution)/shard_map/scrw,cf->sfrw/dot_general | solution.py:133
  16.2 0.7 %convert_reduce_fusion = (f32[384]{0:T(512)S(1)}, bf16[384,6,128]{0,2,1:T(8,128)(2,1)S(1)}) fusion(f32[384,6,128]{0,2,1:T(8,128)S(1)} %get-tuple-element.144, bf16[384,96]{0,1:T(8,128)(2,1)S(1)} %copy-done.7, bf16[1,96,6,128]{3,1,2,0:T(8,128)(2,1)S(1)} %copy-done.1, f32[96]{0:T(128)S(1)} %copy-done.4), kind=kOutput, calls=%fused_computation.31 | convolution fusion | flops 60382848 | bytes 1992576 | tf_op jit(solution)/shard_map/scrw,fc->sfrw/dot_general | solution.py:142
  17.0 0.3 fusion.21
  17.3 0.4 fusion.173
  17.7 0.1 fusion.176
  17.8 1.2 %fusion.121 = (f32[96]{0:T(128)S(1)}, f32[96]{0:T(128)S(1)}, f32[96]{0:T(128)S(1)}, f32[96]{0:T(128)S(1)}, f32[96]{0:T(128)S(1)}, /*index=5*/f32[96]{0:T(128)S(1...) fusion(bf16[1,96,12,134]{3,1,2,0:T(8,128)(2,1)S(1)} %select_max, ...), kind=kLoop, calls=%fused_computation.243 | loop fusion | flops 4495680 | bytes 3558528 | tf_op jit(solution)/shard_map/reduce_sum | solution.py:167
  19.0 1.1 %fusion.100 = (f32[96]{0:T(128)S(1)}, f32[96]{0:T(128)S(1)}, f32[96]{0:T(128)S(1)}, f32[96]{0:T(128)S(1)}, f32[96]{0:T(128)S(1)}, /*index=5*/f32[96]{0:T(128)S(1...) fusion(f32[1,96,6,128]{3,1,2,0:T(8,128)S(1)} %get-tuple-element, ...), kind=kLoop, calls=%fused_computation.222 | loop fusion | flops 3979584 | bytes 2956032 | tf_op jit(solution)/shard_map/reduce_sum | solution.py:167
  20.0 0.3 fusion.118
  20.3 0.4 fusion.55
  20.8 0.1 stack.199
  21.1 0.1 reduce_sum.586
  21.2 0.3 fusion.22
  21.5 0.4 fusion.20
  22.1 3.8 %collective-permute-start.2 = (f32[2,168,128]{2,1,0:T(8,128)S(1)}, f32[2,168,128]{2,1,0:T(8,128)S(1)}, u32[]{:S(2)}, u32[]{:S(2)}) collective-permute-start(f32[2,168,128]{2,1,0:T(8,128)S(1)} %constant_dynamic-slice_fusion.1), channel_id=1, source_target_pairs={{0,4},{4,0},{8,12},{12,8},{16,20},{20,16},{24,28},{28,24},{1,5},{5... | collective-permute-start | bytes 516104 | tf_op jit(solution)/shard_map/ppermute | solution.py:63
  25.9 1.0 %collective-permute-done.2 = f32[2,168,128]{2,1,0:T(8,128)S(1)} collective-permute-done((f32[2,168,128]{2,1,0:T(8,128)S(1)}, f32[2,168,128]{2,1,0:T(8,128)S(1)}, u32[]{:S(2)}, u32[]{:S(2)}) %collective-permute-start.2) | collective-permute-done | bytes 172064 | tf_op jit(solution)/shard_map/ppermute | solution.py:63
  27.0 1.7 %collective-permute-start.3 = (f32[1,168,128]{2,1,0:T(8,128)S(1)}, f32[1,168,128]{2,1,0:T(8,128)S(1)}, u32[]{:S(2)}, u32[]{:S(2)}) collective-permute-start(f32[1,168,128]{2,1,0:T(8,128)S(1)} %constant_dynamic-slice_fusion), channel_id=1, source_target_pairs={{0,8},{4,12},{8,0},{12,4},{16,24},{20,28},{24,16},{28,20},{1,9},{5... | collective-permute-start | bytes 258056 | tf_op jit(solution)/shard_map/ppermute | solution.py:63
  28.6 3.2 %collective-permute-done.3 = f32[1,168,128]{2,1,0:T(8,128)S(1)} collective-permute-done((f32[1,168,128]{2,1,0:T(8,128)S(1)}, f32[1,168,128]{2,1,0:T(8,128)S(1)}, u32[]{:S(2)}, u32[]{:S(2)}) %collective-permute-start.3) | collective-permute-done | bytes 86048 | tf_op jit(solution)/shard_map/ppermute | solution.py:63
  31.9 1.6 %collective-permute-start.4 = (f32[1,168,128]{2,1,0:T(8,128)S(1)}, f32[1,168,128]{2,1,0:T(8,128)S(1)}, u32[]{:S(2)}, u32[]{:S(2)}) collective-permute-start(f32[1,168,128]{2,1,0:T(8,128)S(1)} %dynamic-slice_add_fusion.1), channel_id=1, source_target_pairs={{0,1},{1,0},{2,3},{3,2},{4,5},{5,4},{6,7},{7,6},{8,9},{9,8},{10,11... | collective-permute-start | bytes 258056 | tf_op jit(solution)/shard_map/ppermute | solution.py:71
  33.4 1.5 %collective-permute-start.5 = (f32[1,168,128]{2,1,0:T(8,128)S(1)}, f32[1,168,128]{2,1,0:T(8,128)S(1)}, u32[]{:S(2)}, u32[]{:S(2)}) collective-permute-start(f32[1,168,128]{2,1,0:T(8,128)S(1)} %dynamic-slice_add_fusion.1), channel_id=1, source_target_pairs={{0,2},{1,3},{2,0},{3,1},{4,6},{5,7},{6,4},{7,5},{8,10},{9,11},{10,... | collective-permute-start | bytes 258056 | tf_op jit(solution)/shard_map/ppermute | solution.py:71
  35.0 0.5 collective-permute-start.6
  35.5 1.3 %collective-permute-start.8 = (f32[1,96,3,128]{3,1,2,0:T(8,128)S(1)}, f32[1,96,3,128]{3,1,2,0:T(8,128)S(1)}, u32[]{:S(2)}, u32[]{:S(2)}) collective-permute-start(f32[1,96,3,128]{3,1,2,0:T(8,128)S(1)} %get-tuple-element.87), channel_id=1, source_target_pairs={{0,4},{4,8},{8,12},{12,16},{16,20},{20,24},{24,28},{1,5},{5,9},{9,... | collective-permute-start | bytes 442376 | tf_op jit(solution)/shard_map/ppermute | solution.py:23
  36.8 1.5 %collective-permute-start.9 = (f32[1,96,3,128]{3,1,2,0:T(8,128)S(1)}, f32[1,96,3,128]{3,1,2,0:T(8,128)S(1)}, u32[]{:S(2)}, u32[]{:S(2)}) collective-permute-start(f32[1,96,3,128]{3,1,2,0:T(8,128)S(1)} %get-tuple-element.88), channel_id=1, source_target_pairs={{4,0},{8,4},{12,8},{16,12},{20,16},{24,20},{28,24},{5,1},{9,5},{13... | collective-permute-start | bytes 442376 | tf_op jit(solution)/shard_map/ppermute | solution.py:24
  38.3 0.6 collective-permute-done.5
  38.8 1.5 %collective-permute-done.6 = f32[1,168,128]{2,1,0:T(8,128)S(1)} collective-permute-done((f32[1,168,128]{2,1,0:T(8,128)S(1)}, f32[1,168,128]{2,1,0:T(8,128)S(1)}, u32[]{:S(2)}, u32[]{:S(2)}) %collective-permute-start.6) | collective-permute-done | bytes 86048 | tf_op jit(solution)/shard_map/ppermute | solution.py:71
  40.4 3.6 %collective-permute-start.7 = (f32[1,168,128]{2,1,0:T(8,128)S(1)}, f32[1,168,128]{2,1,0:T(8,128)S(1)}, u32[]{:S(2)}, u32[]{:S(2)}) collective-permute-start(f32[1,168,128]{2,1,0:T(8,128)S(1)} %add_add_fusion), channel_id=1, source_target_pairs={{0,16},{4,20},{8,24},{12,28},{16,0},{20,4},{24,8},{28,12},{1,17},{... | collective-permute-start | bytes 258056 | tf_op jit(solution)/shard_map/ppermute | solution.py:71
  44.0 0.4 select_maximum_fusion
  44.4 4.3 %fusion.124 = bf16[1,96,6,128]{3,1,2,0:T(8,128)(2,1)} fusion(f32[1,96,12,134]{3,1,2,0:T(8,128)S(1)} %select_maximum_fusion, f32[1,96,9,128]{3,1,2,0:T(8,128)S(1)} %get-tuple-element.86, f32[1,96,9,128]{3,1,2,0:T(8,128)S(1)} %constant_dynamic-update-slice_fusion, f32[1,96,6,128]{3,1,2,0:T(8,128)S(1)} %get-tuple-element.17, ...), kind=kLoop, calls=%fused_computation.247 | loop fusion | flops 7372800 | bytes 14764416 | tf_op jit(solution)/shard_map/convert_element_type | solution.py:162
  48.7 1.3 %collective-permute-done.7 = f32[1,168,128]{2,1,0:T(8,128)S(1)} collective-permute-done((f32[1,168,128]{2,1,0:T(8,128)S(1)}, f32[1,168,128]{2,1,0:T(8,128)S(1)}, u32[]{:S(2)}, u32[]{:S(2)}) %collective-permute-start.7) | collective-permute-done | bytes 86048 | tf_op jit(solution)/shard_map/ppermute | solution.py:71
  50.1 0.8 %collective-permute-start.10 = (f32[1,168,128]{2,1,0:T(8,128)S(1)}, f32[1,168,128]{2,1,0:T(8,128)S(1)}, u32[]{:S(2)}, u32[]{:S(2)}) collective-permute-start(f32[1,168,128]{2,1,0:T(8,128)S(1)} %add.488), channel_id=1, source_target_pairs={{0,8},{4,12},{8,0},{12,4},{16,24},{20,28},{24,16},{28,20},{1,9},{5... | collective-permute-start | bytes 258056 | tf_op jit(solution)/shard_map/ppermute | solution.py:78
  50.9 3.8 %collective-permute-done.10 = f32[1,168,128]{2,1,0:T(8,128)S(1)} collective-permute-done((f32[1,168,128]{2,1,0:T(8,128)S(1)}, f32[1,168,128]{2,1,0:T(8,128)S(1)}, u32[]{:S(2)}, u32[]{:S(2)}) %collective-permute-start.10) | collective-permute-done | bytes 86048 | tf_op jit(solution)/shard_map/ppermute | solution.py:78
  54.7 0.7 %collective-permute-start.11 = (f32[2,168,128]{2,1,0:T(8,128)S(1)}, f32[2,168,128]{2,1,0:T(8,128)S(1)}, u32[]{:S(2)}, u32[]{:S(2)}) collective-permute-start(f32[2,168,128]{2,1,0:T(8,128)S(1)} %pad_maximum_fusion.1), channel_id=1, source_target_pairs={{0,4},{4,0},{8,12},{12,8},{16,20},{20,16},{24,28},{28,24},{1,5},{5... | collective-permute-start | bytes 516104 | tf_op jit(solution)/shard_map/ppermute | solution.py:78
  55.5 1.0 %collective-permute-done.11 = f32[2,168,128]{2,1,0:T(8,128)S(1)} collective-permute-done((f32[2,168,128]{2,1,0:T(8,128)S(1)}, f32[2,168,128]{2,1,0:T(8,128)S(1)}, u32[]{:S(2)}, u32[]{:S(2)}) %collective-permute-start.11) | collective-permute-done | bytes 172064 | tf_op jit(solution)/shard_map/ppermute | solution.py:78
  56.6 0.3 slice.755
  56.9 0.1 slice.762
  57.0 0.5 fusion.196
  57.5 0.6 slice.871
  58.1 0.6 %slice_bitcast_fusion.1 = f32[96,7,7]{0,2,1:T(8,128)} fusion(f32[128,7,96]{2,1,0:T(8,128)S(1)} %slice.755), kind=kLoop, calls=%fused_computation.386 | loop fusion | bytes 37632 | tf_op jit(solution)/shard_map/transpose | solution.py:184
  58.7 0.7 %slice_bitcast_fusion = f32[384,96]{0,1:T(8,128)} fusion(f32[224,384]{1,0:T(8,128)S(1)} %slice.762), kind=kLoop, calls=%fused_computation.370 | loop fusion | bytes 294912 | tf_op jit(solution)/shard_map/transpose | solution.py:185
  59.4 0.7 %reshape.363 = f32[96,384]{1,0:T(8,128)} reshape(f32[36864]{0:T(1024)S(1)} %slice.870) | data formatting | bytes 294912 | tf_op jit(solution)/shard_map/reshape | solution.py:86
  (65 shorter events, 0.7 us)
Async XLA Ops:
  0.6 12.6 %copy-start = (bf16[96,384]{1,0:T(8,128)(2,1)S(1)}, bf16[96,384]{1,0:T(8,128)(2,1)}, u32[]{:S(2)}) copy-start(bf16[96,384]{1,0:T(8,128)(2,1)} %param.17) | copy-start | bytes 221188
  0.7 9.4 %copy-start.2 = (bf16[1,96,6,128]{3,1,2,0:T(8,128)(2,1)S(1)}, bf16[1,96,6,128]{3,1,2,0:T(8,128)(2,1)}, u32[]{:S(2)}) copy-start(bf16[1,96,6,128]{3,1,2,0:T(8,128)(2,1)} %param.11) | copy-start | bytes 442372
  0.7 9.4 %copy-start.6 = (f32[96]{0:T(128)S(1)}, f32[96]{0:T(128)}, u32[]{:S(2)}) copy-start(f32[96]{0:T(128)} %param.14) | copy-start | bytes 1156
  0.7 7.9 %collective-permute-start = (bf16[1,96,6,128]{3,1,2,0:T(8,128)(2,1)}, bf16[1,96,6,128]{3,1,2,0:T(8,128)(2,1)S(1)}, u32[]{:S(2)}, u32[]{:S(2)}) collective-permute-start(bf16[1,96,6,128]{3,1,2,0:T(8,128)(2,1)} %param.11), channel_id=1, source_target_pairs={{0,4},{4,8},{8,12},{12,16},{16,20},{20,24},{24,28},{1,5},{5,9},{9,... | collective-permute-start | bytes 442376 | tf_op jit(solution)/shard_map/ppermute | solution.py:15
  3.2 5.7 %collective-permute-start.1 = (bf16[1,96,6,128]{3,1,2,0:T(8,128)(2,1)}, bf16[1,96,6,128]{3,1,2,0:T(8,128)(2,1)S(1)}, u32[]{:S(2)}, u32[]{:S(2)}) collective-permute-start(bf16[1,96,6,128]{3,1,2,0:T(8,128)(2,1)} %param.11), channel_id=1, source_target_pairs={{4,0},{8,4},{12,8},{16,12},{20,16},{24,20},{28,24},{5,1},{9,5},{13... | collective-permute-start | bytes 442376 | tf_op jit(solution)/shard_map/ppermute | solution.py:16
  10.1 3.2 %copy-start.3 = (f32[96]{0:T(128)S(1)}, f32[96]{0:T(128)}, u32[]{:S(2)}) copy-start(f32[96]{0:T(128)} %param.15) | copy-start | bytes 1156
  10.1 3.2 %copy-start.5 = (f32[96]{0:T(128)S(1)}, f32[96]{0:T(128)}, u32[]{:S(2)}) copy-start(f32[96]{0:T(128)} %param.16) | copy-start | bytes 1156
  10.1 3.2 %copy-start.8 = (f32[384]{0:T(512)S(1)}, f32[384]{0:T(512)}, u32[]{:S(2)}) copy-start(f32[384]{0:T(512)} %param.18) | copy-start | bytes 4612
  13.3 2.9 %copy-start.1 = (bf16[1,96,6,128]{3,1,2,0:T(8,128)(2,1)S(1)}, bf16[1,96,6,128]{3,1,2,0:T(8,128)(2,1)}, u32[]{:S(2)}) copy-start(bf16[1,96,6,128]{3,1,2,0:T(8,128)(2,1)} %param.12) | copy-start | bytes 442372
  13.3 2.9 %copy-start.4 = (f32[96]{0:T(128)S(1)}, f32[96]{0:T(128)}, u32[]{:S(2)}) copy-start(f32[96]{0:T(128)} %param.21) | copy-start | bytes 1156
  13.3 2.9 %copy-start.7 = (bf16[384,96]{0,1:T(8,128)(2,1)S(1)}, bf16[384,96]{0,1:T(8,128)(2,1)}, u32[]{:S(2)}) copy-start(bf16[384,96]{0,1:T(8,128)(2,1)} %param.19) | copy-start | bytes 221188
  20.8 0.8 %copy-start.9 = (f32[96]{0:T(128)S(1)}, f32[96]{0:T(128)}, u32[]{:S(2)}) copy-start(f32[96]{0:T(128)} %param.20) | copy-start | bytes 1156
  22.1 4.8 %collective-permute-start.2 = (f32[2,168,128]{2,1,0:T(8,128)S(1)}, f32[2,168,128]{2,1,0:T(8,128)S(1)}, u32[]{:S(2)}, u32[]{:S(2)}) collective-permute-start(f32[2,168,128]{2,1,0:T(8,128)S(1)} %constant_dynamic-slice_fusion.1), channel_id=1, source_target_pairs={{0,4},{4,0},{8,12},{12,8},{16,20},{20,16},{24,28},{28,24},{1,5},{5... | collective-permute-start | bytes 516104 | tf_op jit(solution)/shard_map/ppermute | solution.py:63
  27.0 4.9 %collective-permute-start.3 = (f32[1,168,128]{2,1,0:T(8,128)S(1)}, f32[1,168,128]{2,1,0:T(8,128)S(1)}, u32[]{:S(2)}, u32[]{:S(2)}) collective-permute-start(f32[1,168,128]{2,1,0:T(8,128)S(1)} %constant_dynamic-slice_fusion), channel_id=1, source_target_pairs={{0,8},{4,12},{8,0},{12,4},{16,24},{20,28},{24,16},{28,20},{1,9},{5... | collective-permute-start | bytes 258056 | tf_op jit(solution)/shard_map/ppermute | solution.py:63
  31.9 6.4 %collective-permute-start.4 = (f32[1,168,128]{2,1,0:T(8,128)S(1)}, f32[1,168,128]{2,1,0:T(8,128)S(1)}, u32[]{:S(2)}, u32[]{:S(2)}) collective-permute-start(f32[1,168,128]{2,1,0:T(8,128)S(1)} %dynamic-slice_add_fusion.1), channel_id=1, source_target_pairs={{0,1},{1,0},{2,3},{3,2},{4,5},{5,4},{6,7},{7,6},{8,9},{9,8},{10,11... | collective-permute-start | bytes 258056 | tf_op jit(solution)/shard_map/ppermute | solution.py:71
  33.4 5.4 %collective-permute-start.5 = (f32[1,168,128]{2,1,0:T(8,128)S(1)}, f32[1,168,128]{2,1,0:T(8,128)S(1)}, u32[]{:S(2)}, u32[]{:S(2)}) collective-permute-start(f32[1,168,128]{2,1,0:T(8,128)S(1)} %dynamic-slice_add_fusion.1), channel_id=1, source_target_pairs={{0,2},{1,3},{2,0},{3,1},{4,6},{5,7},{6,4},{7,5},{8,10},{9,11},{10,... | collective-permute-start | bytes 258056 | tf_op jit(solution)/shard_map/ppermute | solution.py:71
  35.0 5.4 %collective-permute-start.6 = (f32[1,168,128]{2,1,0:T(8,128)S(1)}, f32[1,168,128]{2,1,0:T(8,128)S(1)}, u32[]{:S(2)}, u32[]{:S(2)}) collective-permute-start(f32[1,168,128]{2,1,0:T(8,128)S(1)} %dynamic-slice_add_fusion.1), channel_id=1, source_target_pairs={{0,3},{1,2},{2,1},{3,0},{4,7},{5,6},{6,5},{7,4},{8,11},{9,10},{10,... | collective-permute-start | bytes 258056 | tf_op jit(solution)/shard_map/ppermute | solution.py:71
  35.5 8.5 %collective-permute-start.8 = (f32[1,96,3,128]{3,1,2,0:T(8,128)S(1)}, f32[1,96,3,128]{3,1,2,0:T(8,128)S(1)}, u32[]{:S(2)}, u32[]{:S(2)}) collective-permute-start(f32[1,96,3,128]{3,1,2,0:T(8,128)S(1)} %get-tuple-element.87), channel_id=1, source_target_pairs={{0,4},{4,8},{8,12},{12,16},{16,20},{20,24},{24,28},{1,5},{5,9},{9,... | collective-permute-start | bytes 442376 | tf_op jit(solution)/shard_map/ppermute | solution.py:23
  36.8 7.2 %collective-permute-start.9 = (f32[1,96,3,128]{3,1,2,0:T(8,128)S(1)}, f32[1,96,3,128]{3,1,2,0:T(8,128)S(1)}, u32[]{:S(2)}, u32[]{:S(2)}) collective-permute-start(f32[1,96,3,128]{3,1,2,0:T(8,128)S(1)} %get-tuple-element.88), channel_id=1, source_target_pairs={{4,0},{8,4},{12,8},{16,12},{20,16},{24,20},{28,24},{5,1},{9,5},{13... | collective-permute-start | bytes 442376 | tf_op jit(solution)/shard_map/ppermute | solution.py:24
  40.4 9.7 %collective-permute-start.7 = (f32[1,168,128]{2,1,0:T(8,128)S(1)}, f32[1,168,128]{2,1,0:T(8,128)S(1)}, u32[]{:S(2)}, u32[]{:S(2)}) collective-permute-start(f32[1,168,128]{2,1,0:T(8,128)S(1)} %add_add_fusion), channel_id=1, source_target_pairs={{0,16},{4,20},{8,24},{12,28},{16,0},{20,4},{24,8},{28,12},{1,17},{... | collective-permute-start | bytes 258056 | tf_op jit(solution)/shard_map/ppermute | solution.py:71
  50.1 4.6 %collective-permute-start.10 = (f32[1,168,128]{2,1,0:T(8,128)S(1)}, f32[1,168,128]{2,1,0:T(8,128)S(1)}, u32[]{:S(2)}, u32[]{:S(2)}) collective-permute-start(f32[1,168,128]{2,1,0:T(8,128)S(1)} %add.488), channel_id=1, source_target_pairs={{0,8},{4,12},{8,0},{12,4},{16,24},{20,28},{24,16},{28,20},{1,9},{5... | collective-permute-start | bytes 258056 | tf_op jit(solution)/shard_map/ppermute | solution.py:78
  54.7 1.8 %collective-permute-start.11 = (f32[2,168,128]{2,1,0:T(8,128)S(1)}, f32[2,168,128]{2,1,0:T(8,128)S(1)}, u32[]{:S(2)}, u32[]{:S(2)}) collective-permute-start(f32[2,168,128]{2,1,0:T(8,128)S(1)} %pad_maximum_fusion.1), channel_id=1, source_target_pairs={{0,4},{4,0},{8,12},{12,8},{16,20},{20,16},{24,28},{28,24},{1,5},{5... | collective-permute-start | bytes 516104 | tf_op jit(solution)/shard_map/ppermute | solution.py:78

commit v10 on v9

--- a/solution.py
+++ b/solution.py
@@ -61,8 +61,6 @@
         keep = lax.dynamic_slice_in_dim(flat, mine * half, half, axis=0)
         give = lax.dynamic_slice_in_dim(flat, (1 - mine) * half, half, axis=0)
         flat = keep + lax.ppermute(give, axis, xor_pairs(size, bit))
-    flat, side_in = lax.optimization_barrier((flat, side_in))
-    hold = side_fn(*side_in)
     for axis, bits in stages:
         size = lax.axis_size(axis)
         masks = []
@@ -71,8 +69,11 @@
         got = [lax.ppermute(flat, axis, xor_pairs(size, mask)) for mask in masks]
         for item in got:
             flat = flat + item
-    flat, hold = lax.optimization_barrier((flat, hold))
-    for axis, bit in reversed(scatter):
+    flat, side_in = lax.optimization_barrier((flat, side_in))
+    hold = side_fn(*side_in)
+    for step, (axis, bit) in enumerate(reversed(scatter)):
+        if step == len(scatter) - 1:
+            flat, hold = lax.optimization_barrier((flat, hold))
         size = lax.axis_size(axis)
         mine = (lax.axis_index(axis) // bit) % 2
         got = lax.ppermute(flat, axis, xor_pairs(size, bit))
@@ -148,9 +149,9 @@
         - jnp.mean(d_normed, axis=1, keepdims=True)
         - normed * jnp.mean(d_normed * normed, axis=1, keepdims=True)
     )
-    def image_grad_of(d_conv, cotangent):
-        d_wide = with_halo(d_conv, (("strip", 2),), 3)
-        d_padded = jnp.pad(d_wide, ((0, 0), (0, 0), (0, 0), (3, 3)))
+    d_wide = with_halo(d_conv, (("strip", 2),), 3)
+    d_padded = jnp.pad(d_wide, ((0, 0), (0, 0), (0, 0), (3, 3)))
+    def image_grad_of(d_padded, cotangent):
         image_grad = cotangent.astype(jnp.float32)
         for a in range(kernel):
             for b in range(kernel):
@@ -179,7 +180,7 @@
         jnp.sum(upstream * branch, axis=(0, 2, 3)),
     )
     g, image_grad = tree_psum(
-        [item * scale for item in terms], image_grad_of, (d_conv, cotangent)
+        [item * scale for item in terms], image_grad_of, (d_padded, cotangent)
     )
     g[0] = g[0].reshape(kernel, kernel, chans).transpose(2, 0, 1)
     g[6] = g[6].T

time: 60.4 us -> 57.7 us (0.955)
  waiting for transfers between devices: 12.8 us -> 10.5 us
  starting transfers between devices: 20.7 us -> 19.9 us
    ppermute x2, waiting for transfers between devices: 4.84 us -> 1.31 us  [tree_psum(): got = lax.ppermute(flat, axis, xor_pairs(size, bit))]
    ppermute x1, starting transfers between devices: 1.3 us -> 3.22 us  [with_halo(): before = lax.ppermute(last, axis, up)]
    ppermute x4, waiting for transfers between devices: 3.43 us -> 4.95 us  [tree_psum(): got = [lax.ppermute(flat, axis, xor_pairs(size, mask)) for mask in masks]]
    ppermute x2, starting transfers between devices: 1.55 us -> 0.37 us  [tree_psum(): got = lax.ppermute(flat, axis, xor_pairs(size, bit))]
    ppermute x2, starting transfers between devices: 5.42 us -> 4.38 us  [tree_psum(): flat = keep + lax.ppermute(give, axis, xor_pairs(size, bit))]
    ppermute x4, starting transfers between devices: 7.11 us -> 6.2 us  [tree_psum(): got = [lax.ppermute(flat, axis, xor_pairs(size, mask)) for mask in masks]]
  transfers between devices with their start and end apart: 12 -> 12, of which waited for: 8 -> 4; matrix products, arithmetic and copies ran while one was open for 15% -> 16% of each run, Pallas kernels for 0% -> 0%
where the time goes in v10:
time: 57.7 us; the launch traced here: 57.3 us
  starting transfers between devices  19.9 us (34%)
  other arithmetic  13.9 us (24%)
  waiting for transfers between devices  10.5 us (18%)
  local copies, waits for them, and re-layouts  6.77 us (12%)
  matrix products  4.99 us (9%)
  between operations  1.22 us (2%)
    ppermute x4, starting transfers between devices, tree_psum(): got = [lax.ppermute(flat, axis, xor_pairs(size, mask)) for mask in masks]  6.2 us
    ppermute x4, waiting for transfers between devices, tree_psum(): got = [lax.ppermute(flat, axis, xor_pairs(size, mask)) for mask in masks]  4.95 us
    convert_element_type x1, other arithmetic, image_grad_of(): return image_grad.astype(jnp.bfloat16)  4.71 us
    ppermute x2, starting transfers between devices, tree_psum(): flat = keep + lax.ppermute(give, axis, xor_pairs(size, bit))  4.38 us
    ppermute x2, waiting for transfers between devices, tree_psum(): flat = keep + lax.ppermute(give, axis, xor_pairs(size, bit))  4.26 us
    ppermute x1, starting transfers between devices, with_halo(): before = lax.ppermute(last, axis, up)  3.22 us
    reduce_sum x1, other arithmetic, on_device(): centre = conv - jnp.mean(conv, axis=1, keepdims=True)  3.07 us
    ppermute x1, starting transfers between devices, with_halo(): before = lax.ppermute(array, axis, up)  3.04 us
  transfers between devices with their start and end apart: 12, of which 4 were waited for; matrix products, arithmetic and copies ran while one was open for 16% of the time, Pallas kernels for 0%

profile of v10, /device:TPU:0, one launch (start us, length us, event | category | flops | bytes accessed | tf_op | source)
XLA Modules:
  0.0 57.3 jit_solution(9865524199471765077)
XLA Ops:
  0.6 0.0 copy-start
  0.7 1.4 %collective-permute-start.1 = (bf16[1,96,6,128]{3,1,2,0:T(8,128)(2,1)}, bf16[1,96,6,128]{3,1,2,0:T(8,128)(2,1)S(1)}, u32[]{:S(2)}, u32[]{:S(2)}) collective-permute-start(bf16[1,96,6,128]{3,1,2,0:T(8,128)(2,1)} %param.11), channel_id=1, source_target_pairs={{4,0},{8,4},{12,8},{16,12},{20,16},{24,20},{28,24},{5,1},{9,5},{13... | collective-permute-start | bytes 442376 | tf_op jit(solution)/shard_map/ppermute | solution.py:16
  2.1 3.0 %collective-permute-start = (bf16[1,96,6,128]{3,1,2,0:T(8,128)(2,1)}, bf16[1,96,6,128]{3,1,2,0:T(8,128)(2,1)S(1)}, u32[]{:S(2)}, u32[]{:S(2)}) collective-permute-start(bf16[1,96,6,128]{3,1,2,0:T(8,128)(2,1)} %param.11), channel_id=1, source_target_pairs={{0,4},{4,8},{8,12},{12,16},{16,20},{20,24},{24,28},{1,5},{5,9},{9,... | collective-permute-start | bytes 442376 | tf_op jit(solution)/shard_map/ppermute | solution.py:15
  5.2 0.9 %slice_bitcast_fusion.48 = (f32[96]{0:T(128)S(1)}, f32[96]{0:T(128)S(1)}, f32[96]{0:T(128)S(1)}, f32[96]{0:T(128)S(1)}, f32[96]{0:T(128)S(1)}, /*index=5*/f32[96...) fusion(f32[96,7,7]{0,2,1:T(8,128)} %param.13), kind=kLoop, calls=%fused_computation.353 | loop fusion | bytes 8448 | tf_op jit(solution)/shard_map/mul | solution.py:124
  6.1 1.0 %slice_bitcast_fusion.50 = (f32[96]{0:T(128)S(1)}, f32[96]{0:T(128)S(1)}, f32[96]{0:T(128)S(1)}, f32[96]{0:T(128)S(1)}, f32[96]{0:T(128)S(1)}, /*index=5*/f32[96...) fusion(f32[96,7,7]{0,2,1:T(8,128)} %param.13), kind=kLoop, calls=%fused_computation.355 | loop fusion | bytes 14592 | tf_op jit(solution)/shard_map/mul | solution.py:124
  7.0 1.0 %slice_bitcast_fusion.49 = (f32[96]{0:T(128)S(1)}, f32[96]{0:T(128)S(1)}, f32[96]{0:T(128)S(1)}, f32[96]{0:T(128)S(1)}, f32[96]{0:T(128)S(1)}, /*index=5*/f32[96...) fusion(f32[96,7,7]{0,2,1:T(8,128)} %param.13), kind=kLoop, calls=%fused_computation.354 | loop fusion | bytes 14592 | tf_op jit(solution)/shard_map/mul | solution.py:124
  8.1 1.1 %convert_reduce_fusion.1 = f32[96]{0:T(128)S(1)} fusion(bf16[1,96,6,128]{3,1,2,0:T(8,128)(2,1)} %param.12, f32[96]{0:T(128)} %param.21), kind=kLoop, calls=%fused_computation.253 | loop fusion | flops 368544 | bytes 148224 | tf_op jit(solution)/shard_map/reduce_sum | solution.py:179
  9.2 1.2 %select_maximum_fusion.2 = bf16[1,96,12,134]{3,1,2,0:T(8,128)(2,1)S(1)} fusion(bf16[1,96,3,128]{3,1,2,0:T(8,128)(2,1)S(1)} %slice.757, bf16[1,96,6,128]{3,1,2,0:T(8,128)(2,1)} %param.11, bf16[1,96,3,128]{3,1,2,0:T(8,128)(2,1)S(1)} %slice.756), kind=kLoop, calls=%fused_computation.43 | loop fusion | flops 1852416 | bytes 603648 | tf_op jit(solution)/shard_map/concatenate | solution.py:19
  10.5 0.0 copy-start.3
  10.5 0.0 copy-start.8
  10.5 3.1 %fusion.144 = (f32[6,128]{1,0:T(8,128)S(1)}, f32[1,96,6,128]{3,1,2,0:T(8,128)S(1)}) fusion(bf16[1,96,12,134]{3,1,2,0:T(8,128)(2,1)S(1)} %select_maximum_fusion.2, f32[96]{0:T(128)S(1)} %get-tuple-element.136, f32[96]{0:T(128)S(1)} %get-tuple-element.137, f32[96]{0:T(128)S(1)} %get-tuple-element.90, bf16[1,96,3,128]{3,1,2,0:T(8,128)(2,1)S(1)} %slice.757, ...), kind=kLoop, calls=%fused_computation.361 | loop fusion | flops 11353344 | bytes 6805248 | tf_op jit(solution)/shard_map/reduce_sum | solution.py:127
  13.7 2.8 %fusion.9 = (bf16[384,6,128]{0,2,1:T(8,128)(2,1)S(1)}, f32[384,6,128]{0,2,1:T(8,128)S(1)}) fusion(f32[384]{0:T(512)S(1)} %copy-done.8, bf16[96,384]{1,0:T(8,128)(2,1)S(1)} %copy-done, f32[1,96,6,128]{3,1,2,0:T(8,128)S(1)} %get-tuple-element.77, f32[96]{0:T(128)S(1)} %copy-done.5, f32[96]{0:T(128)S(1)} %copy-done.3, f32[6,128]{1,0:T(8,128)S(1)} %add_rsqrt_fusion, ...), kind=kOutput, calls=%fused_computation.15 | convolution fusion | flops 76455936 | bytes 2146560 | tf_op jit(solution)/shard_map/scrw,cf->sfrw/dot_general | solution.py:134
  16.6 0.7 %convert_reduce_fusion = (f32[384]{0:T(512)S(1)}, bf16[384,6,128]{0,2,1:T(8,128)(2,1)S(1)}) fusion(f32[384,6,128]{0,2,1:T(8,128)S(1)} %get-tuple-element.142, bf16[384,96]{0,1:T(8,128)(2,1)S(1)} %copy-done.7, bf16[1,96,6,128]{3,1,2,0:T(8,128)(2,1)S(1)} %copy-done.1, f32[96]{0:T(128)S(1)} %copy-done.4), kind=kOutput, calls=%fused_computation.31 | convolution fusion | flops 60382848 | bytes 1992576 | tf_op jit(solution)/shard_map/scrw,fc->sfrw/dot_general | solution.py:143
  17.3 0.4 fusion.123
  17.7 0.1 fusion.126
  17.9 1.2 %fusion.121 = (f32[96]{0:T(128)S(1)}, f32[96]{0:T(128)S(1)}, f32[96]{0:T(128)S(1)}, f32[96]{0:T(128)S(1)}, f32[96]{0:T(128)S(1)}, /*index=5*/f32[96]{0:T(128)S(1...) fusion(bf16[1,96,12,134]{3,1,2,0:T(8,128)(2,1)S(1)} %select_max, ...), kind=kLoop, calls=%fused_computation.243 | loop fusion | flops 4495680 | bytes 3558528 | tf_op jit(solution)/shard_map/reduce_sum | solution.py:168
  19.0 0.4 fusion.55
  19.5 0.3 fusion.118
  19.8 1.1 %fusion.100 = (f32[96]{0:T(128)S(1)}, f32[96]{0:T(128)S(1)}, f32[96]{0:T(128)S(1)}, f32[96]{0:T(128)S(1)}, f32[96]{0:T(128)S(1)}, /*index=5*/f32[96]{0:T(128)S(1...) fusion(f32[1,96,6,128]{3,1,2,0:T(8,128)S(1)} %get-tuple-element, ...), kind=kLoop, calls=%fused_computation.222 | loop fusion | flops 3979584 | bytes 2956032 | tf_op jit(solution)/shard_map/reduce_sum | solution.py:168
  20.8 0.3 fusion.21
  21.2 0.1 stack.199
  21.3 0.1 mul.1289
  21.4 0.1 reduce_sum.586
  21.6 0.3 fusion.22
  21.9 0.4 fusion.20
  22.5 2.7 %collective-permute-start.2 = (f32[2,168,128]{2,1,0:T(8,128)S(1)}, f32[2,168,128]{2,1,0:T(8,128)S(1)}, u32[]{:S(2)}, u32[]{:S(2)}) collective-permute-start(f32[2,168,128]{2,1,0:T(8,128)S(1)} %constant_dynamic-slice_fusion.1), channel_id=1, source_target_pairs={{0,4},{4,0},{8,12},{12,8},{16,20},{20,16},{24,28},{28,24},{1,5},{5... | collective-permute-start | bytes 516104 | tf_op jit(solution)/shard_map/ppermute | solution.py:63
  25.2 1.0 %collective-permute-done.2 = f32[2,168,128]{2,1,0:T(8,128)S(1)} collective-permute-done((f32[2,168,128]{2,1,0:T(8,128)S(1)}, f32[2,168,128]{2,1,0:T(8,128)S(1)}, u32[]{:S(2)}, u32[]{:S(2)}) %collective-permute-start.2) | collective-permute-done | bytes 172064 | tf_op jit(solution)/shard_map/ppermute | solution.py:63
  26.3 1.6 %collective-permute-start.3 = (f32[1,168,128]{2,1,0:T(8,128)S(1)}, f32[1,168,128]{2,1,0:T(8,128)S(1)}, u32[]{:S(2)}, u32[]{:S(2)}) collective-permute-start(f32[1,168,128]{2,1,0:T(8,128)S(1)} %constant_dynamic-slice_fusion), channel_id=1, source_target_pairs={{0,8},{4,12},{8,0},{12,4},{16,24},{20,28},{24,16},{28,20},{1,9},{5... | collective-permute-start | bytes 258056 | tf_op jit(solution)/shard_map/ppermute | solution.py:63
  28.0 3.2 %collective-permute-done.3 = f32[1,168,128]{2,1,0:T(8,128)S(1)} collective-permute-done((f32[1,168,128]{2,1,0:T(8,128)S(1)}, f32[1,168,128]{2,1,0:T(8,128)S(1)}, u32[]{:S(2)}, u32[]{:S(2)}) %collective-permute-start.3) | collective-permute-done | bytes 86048 | tf_op jit(solution)/shard_map/ppermute | solution.py:63
  31.2 2.5 %collective-permute-start.6 = (f32[1,168,128]{2,1,0:T(8,128)S(1)}, f32[1,168,128]{2,1,0:T(8,128)S(1)}, u32[]{:S(2)}, u32[]{:S(2)}) collective-permute-start(f32[1,168,128]{2,1,0:T(8,128)S(1)} %dynamic-slice_add_fusion.1), channel_id=1, source_target_pairs={{0,3},{1,2},{2,1},{3,0},{4,7},{5,6},{6,5},{7,4},{8,11},{9,10},{10,... | collective-permute-start | bytes 258056 | tf_op jit(solution)/shard_map/ppermute | solution.py:69
  33.7 0.5 collective-permute-start.5
  34.2 0.5 collective-permute-start.4
  34.8 1.3 %collective-permute-start.9 = (f32[1,96,3,128]{3,1,2,0:T(8,128)S(1)}, f32[1,96,3,128]{3,1,2,0:T(8,128)S(1)}, u32[]{:S(2)}, u32[]{:S(2)}) collective-permute-start(f32[1,96,3,128]{3,1,2,0:T(8,128)S(1)} %get-tuple-element.86), channel_id=1, source_target_pairs={{4,0},{8,4},{12,8},{16,12},{20,16},{24,20},{28,24},{5,1},{9,5},{13... | collective-permute-start | bytes 442376 | tf_op jit(solution)/shard_map/ppermute | solution.py:24
  36.1 3.2 %collective-permute-start.8 = (f32[1,96,3,128]{3,1,2,0:T(8,128)S(1)}, f32[1,96,3,128]{3,1,2,0:T(8,128)S(1)}, u32[]{:S(2)}, u32[]{:S(2)}) collective-permute-start(f32[1,96,3,128]{3,1,2,0:T(8,128)S(1)} %get-tuple-element.85), channel_id=1, source_target_pairs={{0,4},{4,8},{8,12},{12,16},{16,20},{20,24},{24,28},{1,5},{5,9},{9,... | collective-permute-start | bytes 442376 | tf_op jit(solution)/shard_map/ppermute | solution.py:23
  39.4 2.6 %collective-permute-start.7 = (f32[1,168,128]{2,1,0:T(8,128)S(1)}, f32[1,168,128]{2,1,0:T(8,128)S(1)}, u32[]{:S(2)}, u32[]{:S(2)}) collective-permute-start(f32[1,168,128]{2,1,0:T(8,128)S(1)} %add_add_fusion), channel_id=1, source_target_pairs={{0,16},{4,20},{8,24},{12,28},{16,0},{20,4},{24,8},{28,12},{1,17},{... | collective-permute-start | bytes 258056 | tf_op jit(solution)/shard_map/ppermute | solution.py:69
  42.0 0.4 select_maximum_fusion
  42.4 4.9 %collective-permute-done.7 = f32[1,168,128]{2,1,0:T(8,128)S(1)} collective-permute-done((f32[1,168,128]{2,1,0:T(8,128)S(1)}, f32[1,168,128]{2,1,0:T(8,128)S(1)}, u32[]{:S(2)}, u32[]{:S(2)}) %collective-permute-start.7) | collective-permute-done | bytes 86048 | tf_op jit(solution)/shard_map/ppermute | solution.py:69
  47.4 0.2 collective-permute-start.10
  47.6 4.7 %add_convert_fusion = bf16[1,96,6,128]{3,1,2,0:T(8,128)(2,1)} fusion(f32[1,96,12,134]{3,1,2,0:T(8,128)S(1)} %select_maximum_fusion, bf16[1,96,6,128]{3,1,2,0:T(8,128)(2,1)S(1)} %copy-done.1, f32[96]{0:T(128)S(1)} %get-tuple-element.136, f32[96]{0:T(128)S(1)} %get-tuple-element.137, f32[96]{0:T(128)S(1)} %get-tuple-element.90, f32[96]{0:T(128)S(1)} %get-tuple-element.91, ...), kind=kLoop, calls=%fused_computation.252 | loop fusion | flops 7372800 | bytes 14764416 | tf_op jit(solution)/shard_map/convert_element_type | solution.py:163
  52.3 0.2 collective-permute-start.11
  52.5 1.3 %collective-permute-done.11 = f32[2,168,128]{2,1,0:T(8,128)S(1)} collective-permute-done((f32[2,168,128]{2,1,0:T(8,128)S(1)}, f32[2,168,128]{2,1,0:T(8,128)S(1)}, u32[]{:S(2)}, u32[]{:S(2)}) %collective-permute-start.11) | collective-permute-done | bytes 172064 | tf_op jit(solution)/shard_map/ppermute | solution.py:79
  53.9 0.3 slice.745
  54.1 0.5 fusion.146
  54.7 0.6 %slice.815 = f32[384]{0:T(512)} slice(f32[86016]{0:T(1024)S(1)} %bitcast.235), slice={[45056:45440]} | slice | bytes 3072 | tf_op jit(solution)/shard_map/slice | solution.py:87
  55.3 0.1 slice.752
  55.4 0.6 %slice_bitcast_fusion.1 = f32[96,7,7]{0,2,1:T(8,128)} fusion(f32[128,7,96]{2,1,0:T(8,128)S(1)} %slice.745), kind=kLoop, calls=%fused_computation.289 | loop fusion | bytes 37632 | tf_op jit(solution)/shard_map/transpose | solution.py:185
  56.0 0.7 %reshape.363 = f32[96,384]{1,0:T(8,128)} reshape(f32[36864]{0:T(1024)S(1)} %slice.814) | data formatting | bytes 294912 | tf_op jit(solution)/shard_map/reshape | solution.py:87
  56.7 0.7 %slice_bitcast_fusion = f32[384,96]{0,1:T(8,128)} fusion(f32[224,384]{1,0:T(8,128)S(1)} %slice.752), kind=kLoop, calls=%fused_computation.273 | loop fusion | bytes 294912 | tf_op jit(solution)/shard_map/transpose | solution.py:186
  (62 shorter events, 0.5 us)
Async XLA Ops:
  0.6 13.0 %copy-start = (bf16[96,384]{1,0:T(8,128)(2,1)S(1)}, bf16[96,384]{1,0:T(8,128)(2,1)}, u32[]{:S(2)}) copy-start(bf16[96,384]{1,0:T(8,128)(2,1)} %param.17) | copy-start | bytes 221188
  0.7 9.8 %copy-start.2 = (bf16[1,96,6,128]{3,1,2,0:T(8,128)(2,1)S(1)}, bf16[1,96,6,128]{3,1,2,0:T(8,128)(2,1)}, u32[]{:S(2)}) copy-start(bf16[1,96,6,128]{3,1,2,0:T(8,128)(2,1)} %param.11) | copy-start | bytes 442372
  0.7 9.8 %copy-start.6 = (f32[96]{0:T(128)S(1)}, f32[96]{0:T(128)}, u32[]{:S(2)}) copy-start(f32[96]{0:T(128)} %param.14) | copy-start | bytes 1156
  0.7 8.5 %collective-permute-start.1 = (bf16[1,96,6,128]{3,1,2,0:T(8,128)(2,1)}, bf16[1,96,6,128]{3,1,2,0:T(8,128)(2,1)S(1)}, u32[]{:S(2)}, u32[]{:S(2)}) collective-permute-start(bf16[1,96,6,128]{3,1,2,0:T(8,128)(2,1)} %param.11), channel_id=1, source_target_pairs={{4,0},{8,4},{12,8},{16,12},{20,16},{24,20},{28,24},{5,1},{9,5},{13... | collective-permute-start | bytes 442376 | tf_op jit(solution)/shard_map/ppermute | solution.py:16
  2.1 7.1 %collective-permute-start = (bf16[1,96,6,128]{3,1,2,0:T(8,128)(2,1)}, bf16[1,96,6,128]{3,1,2,0:T(8,128)(2,1)S(1)}, u32[]{:S(2)}, u32[]{:S(2)}) collective-permute-start(bf16[1,96,6,128]{3,1,2,0:T(8,128)(2,1)} %param.11), channel_id=1, source_target_pairs={{0,4},{4,8},{8,12},{12,16},{16,20},{20,24},{24,28},{1,5},{5,9},{9,... | collective-permute-start | bytes 442376 | tf_op jit(solution)/shard_map/ppermute | solution.py:15
  10.5 3.2 %copy-start.3 = (f32[96]{0:T(128)S(1)}, f32[96]{0:T(128)}, u32[]{:S(2)}) copy-start(f32[96]{0:T(128)} %param.15) | copy-start | bytes 1156
  10.5 3.2 %copy-start.5 = (f32[96]{0:T(128)S(1)}, f32[96]{0:T(128)}, u32[]{:S(2)}) copy-start(f32[96]{0:T(128)} %param.16) | copy-start | bytes 1156
  10.5 3.2 %copy-start.8 = (f32[384]{0:T(512)S(1)}, f32[384]{0:T(512)}, u32[]{:S(2)}) copy-start(f32[384]{0:T(512)} %param.18) | copy-start | bytes 4612
  13.7 2.9 %copy-start.1 = (bf16[1,96,6,128]{3,1,2,0:T(8,128)(2,1)S(1)}, bf16[1,96,6,128]{3,1,2,0:T(8,128)(2,1)}, u32[]{:S(2)}) copy-start(bf16[1,96,6,128]{3,1,2,0:T(8,128)(2,1)} %param.12) | copy-start | bytes 442372
  13.7 2.9 %copy-start.4 = (f32[96]{0:T(128)S(1)}, f32[96]{0:T(128)}, u32[]{:S(2)}) copy-start(f32[96]{0:T(128)} %param.21) | copy-start | bytes 1156
  13.7 2.9 %copy-start.7 = (bf16[384,96]{0,1:T(8,128)(2,1)S(1)}, bf16[384,96]{0,1:T(8,128)(2,1)}, u32[]{:S(2)}) copy-start(bf16[384,96]{0,1:T(8,128)(2,1)} %param.19) | copy-start | bytes 221188
  21.2 0.8 %copy-start.9 = (f32[96]{0:T(128)S(1)}, f32[96]{0:T(128)}, u32[]{:S(2)}) copy-start(f32[96]{0:T(128)} %param.20) | copy-start | bytes 1156
  22.5 3.8 %collective-permute-start.2 = (f32[2,168,128]{2,1,0:T(8,128)S(1)}, f32[2,168,128]{2,1,0:T(8,128)S(1)}, u32[]{:S(2)}, u32[]{:S(2)}) collective-permute-start(f32[2,168,128]{2,1,0:T(8,128)S(1)} %constant_dynamic-slice_fusion.1), channel_id=1, source_target_pairs={{0,4},{4,0},{8,12},{12,8},{16,20},{20,16},{24,28},{28,24},{1,5},{5... | collective-permute-start | bytes 516104 | tf_op jit(solution)/shard_map/ppermute | solution.py:63
  26.3 4.9 %collective-permute-start.3 = (f32[1,168,128]{2,1,0:T(8,128)S(1)}, f32[1,168,128]{2,1,0:T(8,128)S(1)}, u32[]{:S(2)}, u32[]{:S(2)}) collective-permute-start(f32[1,168,128]{2,1,0:T(8,128)S(1)} %constant_dynamic-slice_fusion), channel_id=1, source_target_pairs={{0,8},{4,12},{8,0},{12,4},{16,24},{20,28},{24,16},{28,20},{1,9},{5... | collective-permute-start | bytes 258056 | tf_op jit(solution)/shard_map/ppermute | solution.py:63
  31.2 8.1 %collective-permute-start.6 = (f32[1,168,128]{2,1,0:T(8,128)S(1)}, f32[1,168,128]{2,1,0:T(8,128)S(1)}, u32[]{:S(2)}, u32[]{:S(2)}) collective-permute-start(f32[1,168,128]{2,1,0:T(8,128)S(1)} %dynamic-slice_add_fusion.1), channel_id=1, source_target_pairs={{0,3},{1,2},{2,1},{3,0},{4,7},{5,6},{6,5},{7,4},{8,11},{9,10},{10,... | collective-permute-start | bytes 258056 | tf_op jit(solution)/shard_map/ppermute | solution.py:69
  33.7 5.6 %collective-permute-start.5 = (f32[1,168,128]{2,1,0:T(8,128)S(1)}, f32[1,168,128]{2,1,0:T(8,128)S(1)}, u32[]{:S(2)}, u32[]{:S(2)}) collective-permute-start(f32[1,168,128]{2,1,0:T(8,128)S(1)} %dynamic-slice_add_fusion.1), channel_id=1, source_target_pairs={{0,2},{1,3},{2,0},{3,1},{4,6},{5,7},{6,4},{7,5},{8,10},{9,11},{10,... | collective-permute-start | bytes 258056 | tf_op jit(solution)/shard_map/ppermute | solution.py:69
  34.2 5.1 %collective-permute-start.4 = (f32[1,168,128]{2,1,0:T(8,128)S(1)}, f32[1,168,128]{2,1,0:T(8,128)S(1)}, u32[]{:S(2)}, u32[]{:S(2)}) collective-permute-start(f32[1,168,128]{2,1,0:T(8,128)S(1)} %dynamic-slice_add_fusion.1), channel_id=1, source_target_pairs={{0,1},{1,0},{2,3},{3,2},{4,5},{5,4},{6,7},{7,6},{8,9},{9,8},{10,11... | collective-permute-start | bytes 258056 | tf_op jit(solution)/shard_map/ppermute | solution.py:69
  34.8 7.2 %collective-permute-start.9 = (f32[1,96,3,128]{3,1,2,0:T(8,128)S(1)}, f32[1,96,3,128]{3,1,2,0:T(8,128)S(1)}, u32[]{:S(2)}, u32[]{:S(2)}) collective-permute-start(f32[1,96,3,128]{3,1,2,0:T(8,128)S(1)} %get-tuple-element.86), channel_id=1, source_target_pairs={{4,0},{8,4},{12,8},{16,12},{20,16},{24,20},{28,24},{5,1},{9,5},{13... | collective-permute-start | bytes 442376 | tf_op jit(solution)/shard_map/ppermute | solution.py:24
  36.1 5.9 %collective-permute-start.8 = (f32[1,96,3,128]{3,1,2,0:T(8,128)S(1)}, f32[1,96,3,128]{3,1,2,0:T(8,128)S(1)}, u32[]{:S(2)}, u32[]{:S(2)}) collective-permute-start(f32[1,96,3,128]{3,1,2,0:T(8,128)S(1)} %get-tuple-element.85), channel_id=1, source_target_pairs={{0,4},{4,8},{8,12},{12,16},{16,20},{20,24},{24,28},{1,5},{5,9},{9,... | collective-permute-start | bytes 442376 | tf_op jit(solution)/shard_map/ppermute | solution.py:23
  39.4 8.0 %collective-permute-start.7 = (f32[1,168,128]{2,1,0:T(8,128)S(1)}, f32[1,168,128]{2,1,0:T(8,128)S(1)}, u32[]{:S(2)}, u32[]{:S(2)}) collective-permute-start(f32[1,168,128]{2,1,0:T(8,128)S(1)} %add_add_fusion), channel_id=1, source_target_pairs={{0,16},{4,20},{8,24},{12,28},{16,0},{20,4},{24,8},{28,12},{1,17},{... | collective-permute-start | bytes 258056 | tf_op jit(solution)/shard_map/ppermute | solution.py:69
  47.4 4.9 %collective-permute-start.10 = (f32[1,168,128]{2,1,0:T(8,128)S(1)}, f32[1,168,128]{2,1,0:T(8,128)S(1)}, u32[]{:S(2)}, u32[]{:S(2)}) collective-permute-start(f32[1,168,128]{2,1,0:T(8,128)S(1)} %add.488), channel_id=1, source_target_pairs={{0,8},{4,12},{8,0},{12,4},{16,24},{20,28},{24,16},{28,20},{1,9},{5... | collective-permute-start | bytes 258056 | tf_op jit(solution)/shard_map/ppermute | solution.py:79
  52.3 1.5 %collective-permute-start.11 = (f32[2,168,128]{2,1,0:T(8,128)S(1)}, f32[2,168,128]{2,1,0:T(8,128)S(1)}, u32[]{:S(2)}, u32[]{:S(2)}) collective-permute-start(f32[2,168,128]{2,1,0:T(8,128)S(1)} %pad_maximum_fusion.1), channel_id=1, source_target_pairs={{0,4},{4,0},{8,12},{12,8},{16,20},{20,16},{24,28},{28,24},{1,5},{5... | collective-permute-start | bytes 516104 | tf_op jit(solution)/shard_map/ppermute | solution.py:79

commit v11 on v10

--- a/solution.py
+++ b/solution.py
@@ -116,14 +116,15 @@
     extended = with_halo(images, (("strip", 2),), 3, whole=True)
     upstream = cotangent.astype(jnp.float32)
     padded = jnp.pad(extended, ((0, 0), (0, 0), (0, 0), (3, 3)))
-    conv = jnp.zeros((slides_here, chans, rows, cols), jnp.float32) + conv_bias[None, :, None, None]
-    for a in range(kernel):
-        for b in range(kernel):
-            conv = (
-                conv
-                + conv_weight[:, a, b][None, :, None, None]
-                * padded[:, :, a : a + rows, b : b + cols]
-            )
+    conv = lax.conv_general_dilated(
+        extended.astype(jnp.float32),
+        conv_weight[:, None],
+        window_strides=(1, 1),
+        padding=((0, 0), (3, 3)),
+        dimension_numbers=("NCHW", "OIHW", "NCHW"),
+        feature_group_count=chans,
+        precision=lax.Precision.HIGHEST,
+    ) + conv_bias[None, :, None, None]
     centre = conv - jnp.mean(conv, axis=1, keepdims=True)
     inv = lax.rsqrt(jnp.mean(centre * centre, axis=1, keepdims=True) + 1e-06)
     normed = centre * inv

time: 57.7 us -> 57.1 us (0.990)
  other arithmetic: 13.9 us -> 10.9 us
  starting transfers between devices: 19.9 us -> 21.6 us
  matrix products: 4.99 us -> 6.49 us
  waiting for transfers between devices: 10.5 us -> 9.9 us
    reduce_sum x1, other arithmetic: 3.07 us -> 0.03 us  [on_device(): centre = conv - jnp.mean(conv, axis=1, keepdims=True)]
    mul x3, local copies, waits for them, and re-layouts: 2.87 us -> 0.98 us  [image_grad_of(): conv_weight[:, a, b][None, :, None, None]]
    conv_general_dilated x0 -> x1, matrix products: none -> 1.5 us  [on_device(): lax.conv_general_dilated(extended.astype(jnp.float32), conv_weight[:, Non...]
    ppermute x2, starting transfers between devices: 4.38 us -> 5.6 us  [tree_psum(): flat = keep + lax.ppermute(give, axis, xor_pairs(size, bit))]
    unnamed x28 -> x34, local copies, waits for them, and re-layouts: 0.12 us -> 1.32 us
  transfers between devices with their start and end apart: 12 -> 12, of which waited for: 4 -> 4; matrix products, arithmetic and copies ran while one was open for 16% -> 13% of each run, Pallas kernels for 0% -> 0%
where the time goes in v11:
time: 57.1 us; the launch traced here: 56.7 us
  starting transfers between devices  21.6 us (38%)
  other arithmetic  10.9 us (19%)
  waiting for transfers between devices  9.9 us (17%)
  local copies, waits for them, and re-layouts  6.63 us (12%)
  matrix products  6.49 us (11%)
  between operations  1.28 us (2%)
    ppermute x4, starting transfers between devices, tree_psum(): got = [lax.ppermute(flat, axis, xor_pairs(size, mask)) for mask in masks]  6.37 us
    ppermute x2, starting transfers between devices, tree_psum(): flat = keep + lax.ppermute(give, axis, xor_pairs(size, bit))  5.6 us
    convert_element_type x1, other arithmetic, image_grad_of(): return image_grad.astype(jnp.bfloat16)  4.7 us
    ppermute x4, waiting for transfers between devices, tree_psum(): got = [lax.ppermute(flat, axis, xor_pairs(size, mask)) for mask in masks]  4.64 us
    ppermute x2, waiting for transfers between devices, tree_psum(): flat = keep + lax.ppermute(give, axis, xor_pairs(size, bit))  3.86 us
    reduce_sum x4, other arithmetic, on_device(): jnp.sum(d_conv * padded[:, :, a:a + rows, b:b + cols], axis=(0, 2, 3))  3.23 us
    ppermute x1, starting transfers between devices, with_halo(): before = lax.ppermute(last, axis, up)  3.22 us
    ppermute x1, starting transfers between devices, with_halo(): before = lax.ppermute(array, axis, up)  3.04 us
  transfers between devices with their start and end apart: 12, of which 4 were waited for; matrix products, arithmetic and copies ran while one was open for 13% of the time, Pallas kernels for 0%

profile of v11, /device:TPU:0, one launch (start us, length us, event | category | flops | bytes accessed | tf_op | source)
XLA Modules:
  0.0 56.7 jit_solution(16372399106720464996)
XLA Ops:
  0.7 1.4 %collective-permute-start.1 = (bf16[1,96,6,128]{3,1,2,0:T(8,128)(2,1)}, bf16[1,96,6,128]{3,1,2,0:T(8,128)(2,1)S(1)}, u32[]{:S(2)}, u32[]{:S(2)}) collective-permute-start(bf16[1,96,6,128]{3,1,2,0:T(8,128)(2,1)} %param.11), channel_id=1, source_target_pairs={{4,0},{8,4},{12,8},{16,12},{20,16},{24,20},{28,24},{5,1},{9,5},{13... | collective-permute-start | bytes 442376 | tf_op jit(solution)/shard_map/ppermute | solution.py:16
  2.1 3.0 %collective-permute-start = (bf16[1,96,6,128]{3,1,2,0:T(8,128)(2,1)}, bf16[1,96,6,128]{3,1,2,0:T(8,128)(2,1)S(1)}, u32[]{:S(2)}, u32[]{:S(2)}) collective-permute-start(bf16[1,96,6,128]{3,1,2,0:T(8,128)(2,1)} %param.11), channel_id=1, source_target_pairs={{0,4},{4,8},{8,12},{12,16},{16,20},{20,24},{24,28},{1,5},{5,9},{9,... | collective-permute-start | bytes 442376 | tf_op jit(solution)/shard_map/ppermute | solution.py:15
  5.2 1.0 %slice_bitcast_fusion.50 = (f32[96]{0:T(128)S(1)}, f32[96]{0:T(128)S(1)}, f32[96]{0:T(128)S(1)}, f32[96]{0:T(128)S(1)}, f32[96]{0:T(128)S(1)}, /*index=5*/f32[96...) fusion(f32[96,7,7]{0,2,1:T(8,128)} %param.13), kind=kLoop, calls=%fused_computation.261 | loop fusion | bytes 14592 | tf_op jit(solution)/shard_map/mul | solution.py:161
  6.2 1.1 %convert_reduce_fusion.1 = f32[96]{0:T(128)S(1)} fusion(bf16[1,96,6,128]{3,1,2,0:T(8,128)(2,1)} %param.12, f32[96]{0:T(128)} %param.21), kind=kLoop, calls=%fused_computation.108 | loop fusion | flops 368544 | bytes 148224 | tf_op jit(solution)/shard_map/reduce_sum | solution.py:180
  7.4 1.0 %fusion.58 = (bf16[96,12,1,128]{3,0,1,2:T(8,128)(2,1)S(1)}, bf16[1,96,12,128]{3,1,2,0:T(8,128)(2,1)S(1)}) fusion(bf16[1,96,3,128]{3,1,2,0:T(8,128)(2,1)S(1)} %slice.661, bf16[1,96,6,128]{3,1,2,0:T(8,128)(2,1)} %param.11, bf16[1,96,3,128]{3,1,2,0:T(8,128)(2,1)S(1)} %slice.660), kind=kLoop, calls=%fused_computation.270 | loop fusion | flops 294912 | bytes 884736 | tf_op jit(solution)/shard_map/concatenate | solution.py:19
  8.3 0.2 copy.41
  8.6 0.1 pad.46.clone
  8.7 0.1 reshape.366
  9.0 0.5 copy-done.3
  9.5 1.5 %fusion.20 = f32[6,8,17,96]{3,1,2,0:T(8,128)S(1)} fusion(bf16[96,12,1,7,6]{0,3,4,1,2:T(8,128)(2,1)S(1)} %slice.662, bf16[96,12,1,8,17]{0,3,4,1,2:T(8,128)(2,1)S(1)} %copy.28, f32[96]{0:T(128)S(1)} %copy-done.9, pred[8,17]{0,1:T(8,128)(4,1)S(1)} %copy-done.11, f32[96,1,7,7]{0,3,2,1:T(8,128)S(1)} %bitcast.270), kind=kOutput, calls=%fused_computation.81 | convolution fusion | flops 47490048 | bytes 742792 | tf_op jit(solution)/shard_map/conv_general_dilated | solution.py:119
  11.0 0.1 copy.30
  11.2 0.2 copy.40
  11.5 0.3 copy-done.4
  11.8 2.8 %fusion.9 = (bf16[384,6,128]{0,2,1:T(8,128)(2,1)S(1)}, f32[384,6,128]{0,2,1:T(8,128)S(1)}) fusion(f32[384]{0:T(512)S(1)} %copy-done.8, bf16[96,384]{1,0:T(8,128)(2,1)S(1)} %copy-done, f32[6,1,128,96]{2,3,0,1:T(8,128)S(1)} %copy.40, f32[96]{0:T(128)S(1)} %copy-done.6, f32[96]{0:T(128)S(1)} %copy-done.4, f32[6,128]{1,0:T(8,128)S(1)} %add_rsqrt_fusion, ...), kind=kOutput, calls=%fused_computation.57 | convolution fusion | flops 76455936 | bytes 2146560 | tf_op jit(solution)/shard_map/scrw,cf->sfrw/dot_general | solution.py:135
  14.7 0.7 %convert_reduce_fusion = (f32[384]{0:T(512)S(1)}, bf16[384,6,128]{0,2,1:T(8,128)(2,1)S(1)}) fusion(f32[384,6,128]{0,2,1:T(8,128)S(1)} %get-tuple-element.142, bf16[384,96]{0,1:T(8,128)(2,1)S(1)} %copy-done.7, bf16[1,96,6,128]{3,1,2,0:T(8,128)(2,1)S(1)} %copy-done.1, f32[96]{0:T(128)S(1)} %copy-done.5), kind=kOutput, calls=%fused_computation.73 | convolution fusion | flops 60382848 | bytes 1992576 | tf_op jit(solution)/shard_map/scrw,fc->sfrw/dot_general | solution.py:144
  15.4 0.4 fusion.32
  15.8 0.1 fusion.37
  16.0 1.2 %multiply_reduce_fusion = (f32[96]{0:T(128)S(1)}, f32[96]{0:T(128)S(1)}, f32[96]{0:T(128)S(1)}, f32[96]{0:T(128)S(1)}, f32[96]{0:T(128)S(1)}, /*index=5*/f32[96]...) fusion(bf16[1,96,12,128]{3,1,2,0:T(8,128)(2,1)S(1)} %get-tuple-, ...), kind=kLoop, calls=%fused_computation.109 | loop fusion | flops 4495680 | bytes 1199232 | tf_op jit(solution)/shard_map/reduce_sum | solution.py:169
  17.2 0.5 multiply_reduce_fusion.42
  17.7 0.3 multiply_reduce_fusion.3
  18.0 1.2 %multiply_reduce_fusion.21 = (f32[96]{0:T(128)S(1)}, f32[96]{0:T(128)S(1)}, f32[96]{0:T(128)S(1)}, f32[96]{0:T(128)S(1)}, f32[96]{0:T(128)S(1)}, /*index=5*/f32[...) fusion(f32[1,96,6,128]{3,1,2,0:T(8,128)S(1)} %get-tuple-element, ...), kind=kLoop, calls=%fused_computation.130 | loop fusion | flops 3979584 | bytes 596736 | tf_op jit(solution)/shard_map/reduce_sum | solution.py:169
  19.2 0.3 fusion.22
  19.5 0.1 stack.199
  19.8 0.1 reduce_sum.586
  20.0 0.3 fusion.23
  20.3 0.4 fusion.21
  20.9 2.9 %collective-permute-start.2 = (f32[2,168,128]{2,1,0:T(8,128)S(1)}, f32[2,168,128]{2,1,0:T(8,128)S(1)}, u32[]{:S(2)}, u32[]{:S(2)}) collective-permute-start(f32[2,168,128]{2,1,0:T(8,128)S(1)} %constant_dynamic-slice_fusion.1), channel_id=1, source_target_pairs={{0,4},{4,0},{8,12},{12,8},{16,20},{20,16},{24,28},{28,24},{1,5},{5... | collective-permute-start | bytes 516104 | tf_op jit(solution)/shard_map/ppermute | solution.py:63
  23.8 1.0 %collective-permute-done.2 = f32[2,168,128]{2,1,0:T(8,128)S(1)} collective-permute-done((f32[2,168,128]{2,1,0:T(8,128)S(1)}, f32[2,168,128]{2,1,0:T(8,128)S(1)}, u32[]{:S(2)}, u32[]{:S(2)}) %collective-permute-start.2) | collective-permute-done | bytes 172064 | tf_op jit(solution)/shard_map/ppermute | solution.py:63
  24.9 2.7 %collective-permute-start.3 = (f32[1,168,128]{2,1,0:T(8,128)S(1)}, f32[1,168,128]{2,1,0:T(8,128)S(1)}, u32[]{:S(2)}, u32[]{:S(2)}) collective-permute-start(f32[1,168,128]{2,1,0:T(8,128)S(1)} %constant_dynamic-slice_fusion), channel_id=1, source_target_pairs={{0,8},{4,12},{8,0},{12,4},{16,24},{20,28},{24,16},{28,20},{1,9},{5... | collective-permute-start | bytes 258056 | tf_op jit(solution)/shard_map/ppermute | solution.py:63
  27.6 2.8 %collective-permute-done.3 = f32[1,168,128]{2,1,0:T(8,128)S(1)} collective-permute-done((f32[1,168,128]{2,1,0:T(8,128)S(1)}, f32[1,168,128]{2,1,0:T(8,128)S(1)}, u32[]{:S(2)}, u32[]{:S(2)}) %collective-permute-start.3) | collective-permute-done | bytes 86048 | tf_op jit(solution)/shard_map/ppermute | solution.py:63
  30.4 2.5 %collective-permute-start.6 = (f32[1,168,128]{2,1,0:T(8,128)S(1)}, f32[1,168,128]{2,1,0:T(8,128)S(1)}, u32[]{:S(2)}, u32[]{:S(2)}) collective-permute-start(f32[1,168,128]{2,1,0:T(8,128)S(1)} %dynamic-slice_add_fusion.1), channel_id=1, source_target_pairs={{0,3},{1,2},{2,1},{3,0},{4,7},{5,6},{6,5},{7,4},{8,11},{9,10},{10,... | collective-permute-start | bytes 258056 | tf_op jit(solution)/shard_map/ppermute | solution.py:69
  32.9 0.5 collective-permute-start.5
  33.4 0.5 collective-permute-start.4
  34.0 1.3 %collective-permute-start.9 = (f32[1,96,3,128]{3,1,2,0:T(8,128)S(1)}, f32[1,96,3,128]{3,1,2,0:T(8,128)S(1)}, u32[]{:S(2)}, u32[]{:S(2)}) collective-permute-start(f32[1,96,3,128]{3,1,2,0:T(8,128)S(1)} %get-tuple-element.84), channel_id=1, source_target_pairs={{4,0},{8,4},{12,8},{16,12},{20,16},{24,20},{28,24},{5,1},{9,5},{13... | collective-permute-start | bytes 442376 | tf_op jit(solution)/shard_map/ppermute | solution.py:24
  35.3 3.2 %collective-permute-start.8 = (f32[1,96,3,128]{3,1,2,0:T(8,128)S(1)}, f32[1,96,3,128]{3,1,2,0:T(8,128)S(1)}, u32[]{:S(2)}, u32[]{:S(2)}) collective-permute-start(f32[1,96,3,128]{3,1,2,0:T(8,128)S(1)} %get-tuple-element.83), channel_id=1, source_target_pairs={{0,4},{4,8},{8,12},{12,16},{16,20},{20,24},{24,28},{1,5},{5,9},{9,... | collective-permute-start | bytes 442376 | tf_op jit(solution)/shard_map/ppermute | solution.py:23
  38.6 2.8 %collective-permute-start.7 = (f32[1,168,128]{2,1,0:T(8,128)S(1)}, f32[1,168,128]{2,1,0:T(8,128)S(1)}, u32[]{:S(2)}, u32[]{:S(2)}) collective-permute-start(f32[1,168,128]{2,1,0:T(8,128)S(1)} %add_add_fusion), channel_id=1, source_target_pairs={{0,16},{4,20},{8,24},{12,28},{16,0},{20,4},{24,8},{28,12},{1,17},{... | collective-permute-start | bytes 258056 | tf_op jit(solution)/shard_map/ppermute | solution.py:69
  41.4 0.4 select_maximum_fusion
  41.8 4.6 %collective-permute-done.7 = f32[1,168,128]{2,1,0:T(8,128)S(1)} collective-permute-done((f32[1,168,128]{2,1,0:T(8,128)S(1)}, f32[1,168,128]{2,1,0:T(8,128)S(1)}, u32[]{:S(2)}, u32[]{:S(2)}) %collective-permute-start.7) | collective-permute-done | bytes 86048 | tf_op jit(solution)/shard_map/ppermute | solution.py:69
  46.4 0.6 collective-permute-start.10
  47.0 4.7 %add_convert_fusion = bf16[1,96,6,128]{3,1,2,0:T(8,128)(2,1)} fusion(f32[1,96,12,134]{3,1,2,0:T(8,128)S(1)} %select_maximum_fusion, bf16[1,96,6,128]{3,1,2,0:T(8,128)(2,1)S(1)} %copy-done.1, f32[96]{0:T(128)S(1)} %get-tuple-element.136, f32[96]{0:T(128)S(1)} %get-tuple-element.137, f32[96]{0:T(128)S(1)} %get-tuple-element.90, f32[96]{0:T(128)S(1)} %get-tuple-element.91, ...), kind=kLoop, calls=%fused_computation.107 | loop fusion | flops 7372800 | bytes 14764416 | tf_op jit(solution)/shard_map/convert_element_type | solution.py:164
  51.8 1.4 %collective-permute-done.11 = f32[2,168,128]{2,1,0:T(8,128)S(1)} collective-permute-done((f32[2,168,128]{2,1,0:T(8,128)S(1)}, f32[2,168,128]{2,1,0:T(8,128)S(1)}, u32[]{:S(2)}, u32[]{:S(2)}) %collective-permute-start.11) | collective-permute-done | bytes 172064 | tf_op jit(solution)/shard_map/ppermute | solution.py:79
  53.3 0.3 slice.647
  53.5 0.5 fusion.60
  54.1 0.6 %slice.679 = f32[384]{0:T(512)} slice(f32[86016]{0:T(1024)S(1)} %bitcast.267), slice={[45056:45440]} | slice | bytes 3072 | tf_op jit(solution)/shard_map/slice | solution.py:87
  54.7 0.1 slice.654
  54.8 0.6 %slice_bitcast_fusion.1 = f32[96,7,7]{0,2,1:T(8,128)} fusion(f32[128,7,96]{2,1,0:T(8,128)S(1)} %slice.647), kind=kLoop, calls=%fused_computation.194 | loop fusion | bytes 37632 | tf_op jit(solution)/shard_map/transpose | solution.py:186
  55.4 0.7 %reshape.363 = f32[96,384]{1,0:T(8,128)} reshape(f32[36864]{0:T(1024)S(1)} %slice.678) | data formatting | bytes 294912 | tf_op jit(solution)/shard_map/reshape | solution.py:87
  56.1 0.7 %slice_bitcast_fusion = f32[384,96]{0,1:T(8,128)} fusion(f32[224,384]{1,0:T(8,128)S(1)} %slice.654), kind=kLoop, calls=%fused_computation.178 | loop fusion | bytes 294912 | tf_op jit(solution)/shard_map/transpose | solution.py:187
  (76 shorter events, 0.9 us)
Async XLA Ops:
  0.6 10.8 %copy-start = (bf16[96,384]{1,0:T(8,128)(2,1)S(1)}, bf16[96,384]{1,0:T(8,128)(2,1)}, u32[]{:S(2)}) copy-start(bf16[96,384]{1,0:T(8,128)(2,1)} %param.17) | copy-start | bytes 221188
  0.7 6.6 %collective-permute-start.1 = (bf16[1,96,6,128]{3,1,2,0:T(8,128)(2,1)}, bf16[1,96,6,128]{3,1,2,0:T(8,128)(2,1)S(1)}, u32[]{:S(2)}, u32[]{:S(2)}) collective-permute-start(bf16[1,96,6,128]{3,1,2,0:T(8,128)(2,1)} %param.11), channel_id=1, source_target_pairs={{4,0},{8,4},{12,8},{16,12},{20,16},{24,20},{28,24},{5,1},{9,5},{13... | collective-permute-start | bytes 442376 | tf_op jit(solution)/shard_map/ppermute | solution.py:16
  2.1 5.2 %collective-permute-start = (bf16[1,96,6,128]{3,1,2,0:T(8,128)(2,1)}, bf16[1,96,6,128]{3,1,2,0:T(8,128)(2,1)S(1)}, u32[]{:S(2)}, u32[]{:S(2)}) collective-permute-start(bf16[1,96,6,128]{3,1,2,0:T(8,128)(2,1)} %param.11), channel_id=1, source_target_pairs={{0,4},{4,8},{8,12},{12,16},{16,20},{20,24},{24,28},{1,5},{5,9},{9,... | collective-permute-start | bytes 442376 | tf_op jit(solution)/shard_map/ppermute | solution.py:15
  8.7 0.8 %copy-start.3 = (f32[96,7,7]{0,2,1:T(8,128)S(1)}, f32[96,7,7]{0,2,1:T(8,128)}, u32[]{:S(2)}) copy-start(f32[96,7,7]{0,2,1:T(8,128)} %param.13) | copy-start | bytes 56452
  8.7 0.7 %copy-start.9 = (f32[96]{0:T(128)S(1)}, f32[96]{0:T(128)}, u32[]{:S(2)}) copy-start(f32[96]{0:T(128)} %param.14) | copy-start | bytes 1156
  8.7 0.7 %copy-start.11 = (pred[8,17]{0,1:T(8,128)(4,1)S(1)}, pred[8,17]{0,1:T(8,128)(4,1)}, u32[]{:S(2)}) copy-start(pred[8,17]{0,1:T(8,128)(4,1)} %constant.168) | copy-start | bytes 412
  11.1 0.7 %copy-start.4 = (f32[96]{0:T(128)S(1)}, f32[96]{0:T(128)}, u32[]{:S(2)}) copy-start(f32[96]{0:T(128)} %param.15) | copy-start | bytes 1156
  11.1 0.7 %copy-start.6 = (f32[96]{0:T(128)S(1)}, f32[96]{0:T(128)}, u32[]{:S(2)}) copy-start(f32[96]{0:T(128)} %param.16) | copy-start | bytes 1156
  11.1 0.7 %copy-start.8 = (f32[384]{0:T(512)S(1)}, f32[384]{0:T(512)}, u32[]{:S(2)}) copy-start(f32[384]{0:T(512)} %param.18) | copy-start | bytes 4612
  11.8 2.8 %copy-start.1 = (bf16[1,96,6,128]{3,1,2,0:T(8,128)(2,1)S(1)}, bf16[1,96,6,128]{3,1,2,0:T(8,128)(2,1)}, u32[]{:S(2)}) copy-start(bf16[1,96,6,128]{3,1,2,0:T(8,128)(2,1)} %param.12) | copy-start | bytes 442372
  11.8 2.9 %copy-start.5 = (f32[96]{0:T(128)S(1)}, f32[96]{0:T(128)}, u32[]{:S(2)}) copy-start(f32[96]{0:T(128)} %param.21) | copy-start | bytes 1156
  11.8 2.9 %copy-start.7 = (bf16[384,96]{0,1:T(8,128)(2,1)S(1)}, bf16[384,96]{0,1:T(8,128)(2,1)}, u32[]{:S(2)}) copy-start(bf16[384,96]{0,1:T(8,128)(2,1)} %param.19) | copy-start | bytes 221188
  15.8 1.9 %copy-start.2 = (bf16[1,96,6,128]{3,1,2,0:T(8,128)(2,1)S(1)}, bf16[1,96,6,128]{3,1,2,0:T(8,128)(2,1)}, u32[]{:S(2)}) copy-start(bf16[1,96,6,128]{3,1,2,0:T(8,128)(2,1)} %param.11) | copy-start | bytes 442372
  19.5 0.8 %copy-start.10 = (f32[96]{0:T(128)S(1)}, f32[96]{0:T(128)}, u32[]{:S(2)}) copy-start(f32[96]{0:T(128)} %param.20) | copy-start | bytes 1156
  20.9 4.0 %collective-permute-start.2 = (f32[2,168,128]{2,1,0:T(8,128)S(1)}, f32[2,168,128]{2,1,0:T(8,128)S(1)}, u32[]{:S(2)}, u32[]{:S(2)}) collective-permute-start(f32[2,168,128]{2,1,0:T(8,128)S(1)} %constant_dynamic-slice_fusion.1), channel_id=1, source_target_pairs={{0,4},{4,0},{8,12},{12,8},{16,20},{20,16},{24,28},{28,24},{1,5},{5... | collective-permute-start | bytes 516104 | tf_op jit(solution)/shard_map/ppermute | solution.py:63
  24.9 5.5 %collective-permute-start.3 = (f32[1,168,128]{2,1,0:T(8,128)S(1)}, f32[1,168,128]{2,1,0:T(8,128)S(1)}, u32[]{:S(2)}, u32[]{:S(2)}) collective-permute-start(f32[1,168,128]{2,1,0:T(8,128)S(1)} %constant_dynamic-slice_fusion), channel_id=1, source_target_pairs={{0,8},{4,12},{8,0},{12,4},{16,24},{20,28},{24,16},{28,20},{1,9},{5... | collective-permute-start | bytes 258056 | tf_op jit(solution)/shard_map/ppermute | solution.py:63
  30.4 8.1 %collective-permute-start.6 = (f32[1,168,128]{2,1,0:T(8,128)S(1)}, f32[1,168,128]{2,1,0:T(8,128)S(1)}, u32[]{:S(2)}, u32[]{:S(2)}) collective-permute-start(f32[1,168,128]{2,1,0:T(8,128)S(1)} %dynamic-slice_add_fusion.1), channel_id=1, source_target_pairs={{0,3},{1,2},{2,1},{3,0},{4,7},{5,6},{6,5},{7,4},{8,11},{9,10},{10,... | collective-permute-start | bytes 258056 | tf_op jit(solution)/shard_map/ppermute | solution.py:69
  32.9 5.6 %collective-permute-start.5 = (f32[1,168,128]{2,1,0:T(8,128)S(1)}, f32[1,168,128]{2,1,0:T(8,128)S(1)}, u32[]{:S(2)}, u32[]{:S(2)}) collective-permute-start(f32[1,168,128]{2,1,0:T(8,128)S(1)} %dynamic-slice_add_fusion.1), channel_id=1, source_target_pairs={{0,2},{1,3},{2,0},{3,1},{4,6},{5,7},{6,4},{7,5},{8,10},{9,11},{10,... | collective-permute-start | bytes 258056 | tf_op jit(solution)/shard_map/ppermute | solution.py:69
  33.4 5.1 %collective-permute-start.4 = (f32[1,168,128]{2,1,0:T(8,128)S(1)}, f32[1,168,128]{2,1,0:T(8,128)S(1)}, u32[]{:S(2)}, u32[]{:S(2)}) collective-permute-start(f32[1,168,128]{2,1,0:T(8,128)S(1)} %dynamic-slice_add_fusion.1), channel_id=1, source_target_pairs={{0,1},{1,0},{2,3},{3,2},{4,5},{5,4},{6,7},{7,6},{8,9},{9,8},{10,11... | collective-permute-start | bytes 258056 | tf_op jit(solution)/shard_map/ppermute | solution.py:69
  34.0 7.4 %collective-permute-start.9 = (f32[1,96,3,128]{3,1,2,0:T(8,128)S(1)}, f32[1,96,3,128]{3,1,2,0:T(8,128)S(1)}, u32[]{:S(2)}, u32[]{:S(2)}) collective-permute-start(f32[1,96,3,128]{3,1,2,0:T(8,128)S(1)} %get-tuple-element.84), channel_id=1, source_target_pairs={{4,0},{8,4},{12,8},{16,12},{20,16},{24,20},{28,24},{5,1},{9,5},{13... | collective-permute-start | bytes 442376 | tf_op jit(solution)/shard_map/ppermute | solution.py:24
  35.3 6.1 %collective-permute-start.8 = (f32[1,96,3,128]{3,1,2,0:T(8,128)S(1)}, f32[1,96,3,128]{3,1,2,0:T(8,128)S(1)}, u32[]{:S(2)}, u32[]{:S(2)}) collective-permute-start(f32[1,96,3,128]{3,1,2,0:T(8,128)S(1)} %get-tuple-element.83), channel_id=1, source_target_pairs={{0,4},{4,8},{8,12},{12,16},{16,20},{20,24},{24,28},{1,5},{5,9},{9,... | collective-permute-start | bytes 442376 | tf_op jit(solution)/shard_map/ppermute | solution.py:23
  38.6 7.8 %collective-permute-start.7 = (f32[1,168,128]{2,1,0:T(8,128)S(1)}, f32[1,168,128]{2,1,0:T(8,128)S(1)}, u32[]{:S(2)}, u32[]{:S(2)}) collective-permute-start(f32[1,168,128]{2,1,0:T(8,128)S(1)} %add_add_fusion), channel_id=1, source_target_pairs={{0,16},{4,20},{8,24},{12,28},{16,0},{20,4},{24,8},{28,12},{1,17},{... | collective-permute-start | bytes 258056 | tf_op jit(solution)/shard_map/ppermute | solution.py:69
  46.4 5.3 %collective-permute-start.10 = (f32[1,168,128]{2,1,0:T(8,128)S(1)}, f32[1,168,128]{2,1,0:T(8,128)S(1)}, u32[]{:S(2)}, u32[]{:S(2)}) collective-permute-start(f32[1,168,128]{2,1,0:T(8,128)S(1)} %add.296), channel_id=1, source_target_pairs={{0,8},{4,12},{8,0},{12,4},{16,24},{20,28},{24,16},{28,20},{1,9},{5... | collective-permute-start | bytes 258056 | tf_op jit(solution)/shard_map/ppermute | solution.py:79
  51.7 1.5 %collective-permute-start.11 = (f32[2,168,128]{2,1,0:T(8,128)S(1)}, f32[2,168,128]{2,1,0:T(8,128)S(1)}, u32[]{:S(2)}, u32[]{:S(2)}) collective-permute-start(f32[2,168,128]{2,1,0:T(8,128)S(1)} %pad_maximum_fusion.2), channel_id=1, source_target_pairs={{0,4},{4,0},{8,12},{12,8},{16,20},{20,16},{24,28},{28,24},{1,5},{5... | collective-permute-start | bytes 516104 | tf_op jit(solution)/shard_map/ppermute | solution.py:79

commit v12 on v10

--- a/solution.py
+++ b/solution.py
@@ -116,14 +116,19 @@
     extended = with_halo(images, (("strip", 2),), 3, whole=True)
     upstream = cotangent.astype(jnp.float32)
     padded = jnp.pad(extended, ((0, 0), (0, 0), (0, 0), (3, 3)))
-    conv = jnp.zeros((slides_here, chans, rows, cols), jnp.float32) + conv_bias[None, :, None, None]
-    for a in range(kernel):
-        for b in range(kernel):
-            conv = (
-                conv
-                + conv_weight[:, a, b][None, :, None, None]
-                * padded[:, :, a : a + rows, b : b + cols]
-            )
+    def depthwise(weight):
+        return lax.conv_general_dilated(
+            extended.astype(jnp.float32),
+            weight[:, None],
+            window_strides=(1, 1),
+            padding=((0, 0), (3, 3)),
+            dimension_numbers=("NCHW", "OIHW", "NCHW"),
+            feature_group_count=chans,
+            precision=lax.Precision.HIGHEST,
+        )
+
+    conv, weight_vjp = jax.vjp(depthwise, conv_weight)
+    conv = conv + conv_bias[None, :, None, None]
     centre = conv - jnp.mean(conv, axis=1, keepdims=True)
     inv = lax.rsqrt(jnp.mean(centre * centre, axis=1, keepdims=True) + 1e-06)
     normed = centre * inv
@@ -162,14 +167,11 @@
                 )
         return image_grad.astype(jnp.bfloat16)
 
-    taps = []
-    for a in range(kernel):
-        for b in range(kernel):
-            taps.append(jnp.sum(d_conv * padded[:, :, a : a + rows, b : b + cols], axis=(0, 2, 3)))
+    (kernel_grad,) = weight_vjp(d_conv)
     pixel_count = slides_here * lax.axis_size("slide") * rows * lax.axis_size("strip") * cols
     scale = 1.0 / math.sqrt(float(pixel_count))
     terms = (
-        jnp.stack(taps, axis=0),
+        kernel_grad.transpose(1, 2, 0),
         jnp.sum(d_conv, axis=(0, 2, 3)),
         jnp.sum(d_lifted * normed, axis=(0, 2, 3)),
         jnp.sum(d_lifted, axis=(0, 2, 3)),

time: 57.7 us -> 73.5 us (1.27)
  matrix products: 4.99 us -> 25 us
  other arithmetic: 13.9 us -> 7.84 us
  starting transfers between devices: 19.9 us -> 21.6 us
  local copies, waits for them, and re-layouts: 6.77 us -> 7.6 us
    conv_general_dilated x0 -> x2, matrix products: none -> 20 us  [depthwise(): lax.conv_general_dilated(extended.astype(jnp.float32), weight[:, None], w...]
    reduce_sum x1, other arithmetic: 3.07 us -> 0.03 us  [on_device(): centre = conv - jnp.mean(conv, axis=1, keepdims=True)]
    reduce_sum x4 -> x1, other arithmetic: 2.97 us -> 0.21 us  [on_device(): jnp.sum(d_conv, axis=(0, 2, 3))]
    mul x4, local copies, waits for them, and re-layouts: 2.95 us -> 1.48 us  [the longest x3 0.98 us: image_grad_of(): conv_weight[:, a, b][None, :, None, None]]
    unnamed x28 -> x33, local copies, waits for them, and re-layouts: 0.12 us -> 1.37 us
    ppermute x2, starting transfers between devices: 4.38 us -> 5.6 us  [tree_psum(): flat = keep + lax.ppermute(give, axis, xor_pairs(size, bit))]
  transfers between devices with their start and end apart: 12 -> 12, of which waited for: 4 -> 4; matrix products, arithmetic and copies ran while one was open for 16% -> 10% of each run, Pallas kernels for 0% -> 0%
where the time goes in v12:
time: 73.5 us; the launch traced here: 73.1 us
  matrix products  25 us (34%)
  starting transfers between devices  21.6 us (29%)
  waiting for transfers between devices  9.9 us (13%)
  other arithmetic  7.84 us (11%)
  local copies, waits for them, and re-layouts  7.6 us (10%)
  between operations  1.27 us (2%)
    conv_general_dilated x2, matrix products, depthwise(): lax.conv_general_dilated(extended.astype(jnp.float32), weight[:, None], w...  20 us
    ppermute x4, starting transfers between devices, tree_psum(): got = [lax.ppermute(flat, axis, xor_pairs(size, mask)) for mask in masks]  6.37 us
    ppermute x2, starting transfers between devices, tree_psum(): flat = keep + lax.ppermute(give, axis, xor_pairs(size, bit))  5.6 us
    convert_element_type x1, other arithmetic, image_grad_of(): return image_grad.astype(jnp.bfloat16)  4.71 us
    ppermute x4, waiting for transfers between devices, tree_psum(): got = [lax.ppermute(flat, axis, xor_pairs(size, mask)) for mask in masks]  4.64 us
    ppermute x2, waiting for transfers between devices, tree_psum(): flat = keep + lax.ppermute(give, axis, xor_pairs(size, bit))  3.86 us
    ppermute x1, starting transfers between devices, with_halo(): before = lax.ppermute(array, axis, up)  3.04 us
    ppermute x1, starting transfers between devices, with_halo(): before = lax.ppermute(last, axis, up)  3.04 us
  transfers between devices with their start and end apart: 12, of which 4 were waited for; matrix products, arithmetic and copies ran while one was open for 10% of the time, Pallas kernels for 0%

profile of v12, /device:TPU:0, one launch (start us, length us, event | category | flops | bytes accessed | tf_op | source)
XLA Modules:
  0.0 73.1 jit_solution(1436712084416347349)
XLA Ops:
  0.7 1.4 %collective-permute-start.1 = (bf16[1,96,6,128]{3,1,2,0:T(8,128)(2,1)}, bf16[1,96,6,128]{3,1,2,0:T(8,128)(2,1)S(1)}, u32[]{:S(2)}, u32[]{:S(2)}) collective-permute-start(bf16[1,96,6,128]{3,1,2,0:T(8,128)(2,1)} %param.11), channel_id=1, source_target_pairs={{4,0},{8,4},{12,8},{16,12},{20,16},{24,20},{28,24},{5,1},{9,5},{13... | collective-permute-start | bytes 442376 | tf_op jit(solution)/shard_map/ppermute | solution.py:16
  2.1 3.0 %collective-permute-start = (bf16[1,96,6,128]{3,1,2,0:T(8,128)(2,1)}, bf16[1,96,6,128]{3,1,2,0:T(8,128)(2,1)S(1)}, u32[]{:S(2)}, u32[]{:S(2)}) collective-permute-start(bf16[1,96,6,128]{3,1,2,0:T(8,128)(2,1)} %param.11), channel_id=1, source_target_pairs={{0,4},{4,8},{8,12},{12,16},{16,20},{20,24},{24,28},{1,5},{5,9},{9,... | collective-permute-start | bytes 442376 | tf_op jit(solution)/shard_map/ppermute | solution.py:15
  5.2 1.0 %slice_bitcast_fusion.50 = (f32[96]{0:T(128)S(1)}, f32[96]{0:T(128)S(1)}, f32[96]{0:T(128)S(1)}, f32[96]{0:T(128)S(1)}, f32[96]{0:T(128)S(1)}, /*index=5*/f32[96...) fusion(f32[96,7,7]{0,2,1:T(8,128)} %param.13), kind=kLoop, calls=%fused_computation.157 | loop fusion | bytes 14592 | tf_op jit(solution)/shard_map/mul | solution.py:165
  6.2 1.1 %convert_reduce_fusion.1 = f32[96]{0:T(128)S(1)} fusion(bf16[1,96,6,128]{3,1,2,0:T(8,128)(2,1)} %param.12, f32[96]{0:T(128)} %param.21), kind=kLoop, calls=%fused_computation.67 | loop fusion | flops 368544 | bytes 148224 | tf_op jit(solution)/shard_map/reduce_sum | solution.py:181
  7.4 1.0 %fusion.54 = (bf16[96,12,1,128]{3,0,2,1:T(8,128)(2,1)S(1)}, bf16[1,96,12,128]{3,1,2,0:T(8,128)(2,1)S(1)}) fusion(bf16[1,96,3,128]{3,1,2,0:T(8,128)(2,1)S(1)} %slice.455, bf16[1,96,6,128]{3,1,2,0:T(8,128)(2,1)} %param.11, bf16[1,96,3,128]{3,1,2,0:T(8,128)(2,1)S(1)} %slice.454), kind=kLoop, calls=%fused_computation.166 | loop fusion | flops 294912 | bytes 884736 | tf_op jit(solution)/shard_map/concatenate | solution.py:19
  8.3 0.2 copy.63
  8.6 0.1 pad.41.clone
  8.7 0.1 reshape.370
  9.0 0.5 copy-done.2
  9.5 1.5 %fusion.20 = f32[6,8,17,96]{3,1,2,0:T(8,128)S(1)} fusion(bf16[96,12,1,7,6]{0,3,4,1,2:T(8,128)(2,1)S(1)} %slice.456, bf16[96,12,1,8,17]{0,3,4,1,2:T(8,128)(2,1)S(1)} %copy.47, f32[96]{0:T(128)S(1)} %copy-done.8, pred[8,17]{0,1:T(8,128)(4,1)S(1)} %copy-done.10, f32[96,1,7,7]{0,3,2,1:T(8,128)S(1)} %bitcast.229), kind=kOutput, calls=%fused_computation.39 | convolution fusion | flops 47490048 | bytes 742792 | tf_op jit(solution)/shard_map/jvp()/conv_general_dilated | solution.py:120
  11.0 0.1 copy.49
  11.2 0.2 copy.62
  11.5 0.3 copy-done.3
  11.9 2.8 %fusion.9 = (bf16[384,6,128]{0,2,1:T(8,128)(2,1)S(1)}, f32[384,6,128]{0,2,1:T(8,128)S(1)}) fusion(f32[384]{0:T(512)S(1)} %copy-done.7, bf16[96,384]{1,0:T(8,128)(2,1)S(1)} %copy-done, f32[6,1,128,96]{2,3,0,1:T(8,128)S(1)} %copy.62, f32[96]{0:T(128)S(1)} %copy-done.5, f32[96]{0:T(128)S(1)} %copy-done.3, f32[6,128]{1,0:T(8,128)S(1)} %add_rsqrt_fusion, ...), kind=kOutput, calls=%fused_computation.15 | convolution fusion | flops 76455936 | bytes 2146560 | tf_op jit(solution)/shard_map/scrw,cf->sfrw/dot_general | solution.py:139
  14.7 0.7 convert_reduce_fusion
  15.5 0.4 fusion.32
  15.9 0.3 fusion.22
  16.2 0.6 copy.52
  16.8 0.1 fusion.37
  16.9 0.2 fusion.55
  17.1 0.5 copy.53
  17.6 18.4 %convolution_multiply_fusion = f32[96,1,7,7]{0,1,3,2:T(1,128)S(1)} fusion(bf16[1,96,12,128]{1,0,3,2:T(2,128)(2,1)S(1)} %copy.52, f32[1,96,6,128]{1,0,3,2:T(1,128)S(1)} %copy.53), kind=kOutput, calls=%fused_computation.47 | convolution fusion | flops 42776160 | bytes 608640 | tf_op jit(solution)/shard_map/transpose(jvp())/conv_general_dilated | solution.py:120
  36.1 0.1 reshape.362
  36.2 0.1 reduce_sum.100
  36.3 0.3 fusion.23
  36.7 0.4 fusion.21
  37.3 2.9 %collective-permute-start.2 = (f32[2,168,128]{2,1,0:T(8,128)S(1)}, f32[2,168,128]{2,1,0:T(8,128)S(1)}, u32[]{:S(2)}, u32[]{:S(2)}) collective-permute-start(f32[2,168,128]{2,1,0:T(8,128)S(1)} %constant_dynamic-slice_fusion.1), channel_id=1, source_target_pairs={{0,4},{4,0},{8,12},{12,8},{16,20},{20,16},{24,28},{28,24},{1,5},{5... | collective-permute-start | bytes 516104 | tf_op jit(solution)/shard_map/ppermute | solution.py:63
  40.2 1.0 %collective-permute-done.2 = f32[2,168,128]{2,1,0:T(8,128)S(1)} collective-permute-done((f32[2,168,128]{2,1,0:T(8,128)S(1)}, f32[2,168,128]{2,1,0:T(8,128)S(1)}, u32[]{:S(2)}, u32[]{:S(2)}) %collective-permute-start.2) | collective-permute-done | bytes 172064 | tf_op jit(solution)/shard_map/ppermute | solution.py:63
  41.3 2.7 %collective-permute-start.3 = (f32[1,168,128]{2,1,0:T(8,128)S(1)}, f32[1,168,128]{2,1,0:T(8,128)S(1)}, u32[]{:S(2)}, u32[]{:S(2)}) collective-permute-start(f32[1,168,128]{2,1,0:T(8,128)S(1)} %constant_dynamic-slice_fusion), channel_id=1, source_target_pairs={{0,8},{4,12},{8,0},{12,4},{16,24},{20,28},{24,16},{28,20},{1,9},{5... | collective-permute-start | bytes 258056 | tf_op jit(solution)/shard_map/ppermute | solution.py:63
  44.0 2.8 %collective-permute-done.3 = f32[1,168,128]{2,1,0:T(8,128)S(1)} collective-permute-done((f32[1,168,128]{2,1,0:T(8,128)S(1)}, f32[1,168,128]{2,1,0:T(8,128)S(1)}, u32[]{:S(2)}, u32[]{:S(2)}) %collective-permute-start.3) | collective-permute-done | bytes 86048 | tf_op jit(solution)/shard_map/ppermute | solution.py:63
  46.8 2.5 %collective-permute-start.6 = (f32[1,168,128]{2,1,0:T(8,128)S(1)}, f32[1,168,128]{2,1,0:T(8,128)S(1)}, u32[]{:S(2)}, u32[]{:S(2)}) collective-permute-start(f32[1,168,128]{2,1,0:T(8,128)S(1)} %dynamic-slice_add_fusion.1), channel_id=1, source_target_pairs={{0,3},{1,2},{2,1},{3,0},{4,7},{5,6},{6,5},{7,4},{8,11},{9,10},{10,... | collective-permute-start | bytes 258056 | tf_op jit(solution)/shard_map/ppermute | solution.py:69
  49.3 0.5 collective-permute-start.5
  49.8 0.5 collective-permute-start.4
  50.4 1.3 %collective-permute-start.9 = (f32[1,96,3,128]{3,1,2,0:T(8,128)S(1)}, f32[1,96,3,128]{3,1,2,0:T(8,128)S(1)}, u32[]{:S(2)}, u32[]{:S(2)}) collective-permute-start(f32[1,96,3,128]{3,1,2,0:T(8,128)S(1)} %get-tuple-element.32), channel_id=1, source_target_pairs={{4,0},{8,4},{12,8},{16,12},{20,16},{24,20},{28,24},{5,1},{9,5},{13... | collective-permute-start | bytes 442376 | tf_op jit(solution)/shard_map/ppermute | solution.py:24
  51.7 3.0 %collective-permute-start.8 = (f32[1,96,3,128]{3,1,2,0:T(8,128)S(1)}, f32[1,96,3,128]{3,1,2,0:T(8,128)S(1)}, u32[]{:S(2)}, u32[]{:S(2)}) collective-permute-start(f32[1,96,3,128]{3,1,2,0:T(8,128)S(1)} %get-tuple-element.31), channel_id=1, source_target_pairs={{0,4},{4,8},{8,12},{12,16},{16,20},{20,24},{24,28},{1,5},{5,9},{9,... | collective-permute-start | bytes 442376 | tf_op jit(solution)/shard_map/ppermute | solution.py:23
  54.8 2.8 %collective-permute-start.7 = (f32[1,168,128]{2,1,0:T(8,128)S(1)}, f32[1,168,128]{2,1,0:T(8,128)S(1)}, u32[]{:S(2)}, u32[]{:S(2)}) collective-permute-start(f32[1,168,128]{2,1,0:T(8,128)S(1)} %add_add_fusion), channel_id=1, source_target_pairs={{0,16},{4,20},{8,24},{12,28},{16,0},{20,4},{24,8},{28,12},{1,17},{... | collective-permute-start | bytes 258056 | tf_op jit(solution)/shard_map/ppermute | solution.py:69
  57.6 0.4 select_maximum_fusion
  58.0 4.6 %collective-permute-done.7 = f32[1,168,128]{2,1,0:T(8,128)S(1)} collective-permute-done((f32[1,168,128]{2,1,0:T(8,128)S(1)}, f32[1,168,128]{2,1,0:T(8,128)S(1)}, u32[]{:S(2)}, u32[]{:S(2)}) %collective-permute-start.7) | collective-permute-done | bytes 86048 | tf_op jit(solution)/shard_map/ppermute | solution.py:69
  62.7 0.7 %collective-permute-start.10 = (f32[1,168,128]{2,1,0:T(8,128)S(1)}, f32[1,168,128]{2,1,0:T(8,128)S(1)}, u32[]{:S(2)}, u32[]{:S(2)}) collective-permute-start(f32[1,168,128]{2,1,0:T(8,128)S(1)} %add.294), channel_id=1, source_target_pairs={{0,8},{4,12},{8,0},{12,4},{16,24},{20,28},{24,16},{28,20},{1,9},{5... | collective-permute-start | bytes 258056 | tf_op jit(solution)/shard_map/ppermute | solution.py:79
  63.4 4.7 %add_convert_fusion = bf16[1,96,6,128]{3,1,2,0:T(8,128)(2,1)} fusion(f32[1,96,12,134]{3,1,2,0:T(8,128)S(1)} %select_maximum_fusion, bf16[1,96,6,128]{3,1,2,0:T(8,128)(2,1)S(1)} %copy-done.1, f32[96]{0:T(128)S(1)} %get-tuple-element.84, f32[96]{0:T(128)S(1)} %get-tuple-element.85, f32[96]{0:T(128)S(1)} %get-tuple-element.38, f32[96]{0:T(128)S(1)} %get-tuple-element.39, ...), kind=kLoop, calls=%fused_computation.66 | loop fusion | flops 7372800 | bytes 14764416 | tf_op jit(solution)/shard_map/convert_element_type | solution.py:168
  68.2 1.4 %collective-permute-done.11 = f32[2,168,128]{2,1,0:T(8,128)S(1)} collective-permute-done((f32[2,168,128]{2,1,0:T(8,128)S(1)}, f32[2,168,128]{2,1,0:T(8,128)S(1)}, u32[]{:S(2)}, u32[]{:S(2)}) %collective-permute-start.11) | collective-permute-done | bytes 172064 | tf_op jit(solution)/shard_map/ppermute | solution.py:79
  69.7 0.3 slice.441
  69.9 0.5 fusion.57
  70.5 0.6 slice.465
  71.1 0.1 slice.448
  71.2 0.6 slice_bitcast_fusion.1
  71.8 0.7 reshape.367
  72.5 0.7 slice_bitcast_fusion
  (73 shorter events, 0.9 us)
Async XLA Ops:
  0.6 10.8 %copy-start = (bf16[96,384]{1,0:T(8,128)(2,1)S(1)}, bf16[96,384]{1,0:T(8,128)(2,1)}, u32[]{:S(2)}) copy-start(bf16[96,384]{1,0:T(8,128)(2,1)} %param.17) | copy-start | bytes 221188
  0.7 6.6 %collective-permute-start.1 = (bf16[1,96,6,128]{3,1,2,0:T(8,128)(2,1)}, bf16[1,96,6,128]{3,1,2,0:T(8,128)(2,1)S(1)}, u32[]{:S(2)}, u32[]{:S(2)}) collective-permute-start(bf16[1,96,6,128]{3,1,2,0:T(8,128)(2,1)} %param.11), channel_id=1, source_target_pairs={{4,0},{8,4},{12,8},{16,12},{20,16},{24,20},{28,24},{5,1},{9,5},{13... | collective-permute-start | bytes 442376 | tf_op jit(solution)/shard_map/ppermute | solution.py:16
  2.1 5.2 %collective-permute-start = (bf16[1,96,6,128]{3,1,2,0:T(8,128)(2,1)}, bf16[1,96,6,128]{3,1,2,0:T(8,128)(2,1)S(1)}, u32[]{:S(2)}, u32[]{:S(2)}) collective-permute-start(bf16[1,96,6,128]{3,1,2,0:T(8,128)(2,1)} %param.11), channel_id=1, source_target_pairs={{0,4},{4,8},{8,12},{12,16},{16,20},{20,24},{24,28},{1,5},{5,9},{9,... | collective-permute-start | bytes 442376 | tf_op jit(solution)/shard_map/ppermute | solution.py:15
  8.7 0.8 %copy-start.2 = (f32[96,7,7]{0,2,1:T(8,128)S(1)}, f32[96,7,7]{0,2,1:T(8,128)}, u32[]{:S(2)}) copy-start(f32[96,7,7]{0,2,1:T(8,128)} %param.13) | copy-start | bytes 56452
  8.7 0.7 %copy-start.8 = (f32[96]{0:T(128)S(1)}, f32[96]{0:T(128)}, u32[]{:S(2)}) copy-start(f32[96]{0:T(128)} %param.14) | copy-start | bytes 1156
  8.7 0.7 %copy-start.10 = (pred[8,17]{0,1:T(8,128)(4,1)S(1)}, pred[8,17]{0,1:T(8,128)(4,1)}, u32[]{:S(2)}) copy-start(pred[8,17]{0,1:T(8,128)(4,1)} %constant.164) | copy-start | bytes 412
  11.1 0.7 copy-start.3
  11.2 0.7 copy-start.5
  11.2 0.7 copy-start.7
  11.9 2.8 %copy-start.1 = (bf16[1,96,6,128]{3,1,2,0:T(8,128)(2,1)S(1)}, bf16[1,96,6,128]{3,1,2,0:T(8,128)(2,1)}, u32[]{:S(2)}) copy-start(bf16[1,96,6,128]{3,1,2,0:T(8,128)(2,1)} %param.12) | copy-start | bytes 442372
  11.9 2.9 %copy-start.4 = (f32[96]{0:T(128)S(1)}, f32[96]{0:T(128)}, u32[]{:S(2)}) copy-start(f32[96]{0:T(128)} %param.21) | copy-start | bytes 1156
  11.9 2.9 %copy-start.6 = (bf16[384,96]{0,1:T(8,128)(2,1)S(1)}, bf16[384,96]{0,1:T(8,128)(2,1)}, u32[]{:S(2)}) copy-start(bf16[384,96]{0,1:T(8,128)(2,1)} %param.19) | copy-start | bytes 221188
  36.0 0.7 copy-start.9
  37.3 4.0 %collective-permute-start.2 = (f32[2,168,128]{2,1,0:T(8,128)S(1)}, f32[2,168,128]{2,1,0:T(8,128)S(1)}, u32[]{:S(2)}, u32[]{:S(2)}) collective-permute-start(f32[2,168,128]{2,1,0:T(8,128)S(1)} %constant_dynamic-slice_fusion.1), channel_id=1, source_target_pairs={{0,4},{4,0},{8,12},{12,8},{16,20},{20,16},{24,28},{28,24},{1,5},{5... | collective-permute-start | bytes 516104 | tf_op jit(solution)/shard_map/ppermute | solution.py:63
  41.3 5.5 %collective-permute-start.3 = (f32[1,168,128]{2,1,0:T(8,128)S(1)}, f32[1,168,128]{2,1,0:T(8,128)S(1)}, u32[]{:S(2)}, u32[]{:S(2)}) collective-permute-start(f32[1,168,128]{2,1,0:T(8,128)S(1)} %constant_dynamic-slice_fusion), channel_id=1, source_target_pairs={{0,8},{4,12},{8,0},{12,4},{16,24},{20,28},{24,16},{28,20},{1,9},{5... | collective-permute-start | bytes 258056 | tf_op jit(solution)/shard_map/ppermute | solution.py:63
  46.8 7.9 %collective-permute-start.6 = (f32[1,168,128]{2,1,0:T(8,128)S(1)}, f32[1,168,128]{2,1,0:T(8,128)S(1)}, u32[]{:S(2)}, u32[]{:S(2)}) collective-permute-start(f32[1,168,128]{2,1,0:T(8,128)S(1)} %dynamic-slice_add_fusion.1), channel_id=1, source_target_pairs={{0,3},{1,2},{2,1},{3,0},{4,7},{5,6},{6,5},{7,4},{8,11},{9,10},{10,... | collective-permute-start | bytes 258056 | tf_op jit(solution)/shard_map/ppermute | solution.py:69
  49.3 5.4 %collective-permute-start.5 = (f32[1,168,128]{2,1,0:T(8,128)S(1)}, f32[1,168,128]{2,1,0:T(8,128)S(1)}, u32[]{:S(2)}, u32[]{:S(2)}) collective-permute-start(f32[1,168,128]{2,1,0:T(8,128)S(1)} %dynamic-slice_add_fusion.1), channel_id=1, source_target_pairs={{0,2},{1,3},{2,0},{3,1},{4,6},{5,7},{6,4},{7,5},{8,10},{9,11},{10,... | collective-permute-start | bytes 258056 | tf_op jit(solution)/shard_map/ppermute | solution.py:69
  49.8 4.9 %collective-permute-start.4 = (f32[1,168,128]{2,1,0:T(8,128)S(1)}, f32[1,168,128]{2,1,0:T(8,128)S(1)}, u32[]{:S(2)}, u32[]{:S(2)}) collective-permute-start(f32[1,168,128]{2,1,0:T(8,128)S(1)} %dynamic-slice_add_fusion.1), channel_id=1, source_target_pairs={{0,1},{1,0},{2,3},{3,2},{4,5},{5,4},{6,7},{7,6},{8,9},{9,8},{10,11... | collective-permute-start | bytes 258056 | tf_op jit(solution)/shard_map/ppermute | solution.py:69
  50.4 7.2 %collective-permute-start.9 = (f32[1,96,3,128]{3,1,2,0:T(8,128)S(1)}, f32[1,96,3,128]{3,1,2,0:T(8,128)S(1)}, u32[]{:S(2)}, u32[]{:S(2)}) collective-permute-start(f32[1,96,3,128]{3,1,2,0:T(8,128)S(1)} %get-tuple-element.32), channel_id=1, source_target_pairs={{4,0},{8,4},{12,8},{16,12},{20,16},{24,20},{28,24},{5,1},{9,5},{13... | collective-permute-start | bytes 442376 | tf_op jit(solution)/shard_map/ppermute | solution.py:24
  51.7 5.9 %collective-permute-start.8 = (f32[1,96,3,128]{3,1,2,0:T(8,128)S(1)}, f32[1,96,3,128]{3,1,2,0:T(8,128)S(1)}, u32[]{:S(2)}, u32[]{:S(2)}) collective-permute-start(f32[1,96,3,128]{3,1,2,0:T(8,128)S(1)} %get-tuple-element.31), channel_id=1, source_target_pairs={{0,4},{4,8},{8,12},{12,16},{16,20},{20,24},{24,28},{1,5},{5,9},{9,... | collective-permute-start | bytes 442376 | tf_op jit(solution)/shard_map/ppermute | solution.py:23
  54.8 7.8 %collective-permute-start.7 = (f32[1,168,128]{2,1,0:T(8,128)S(1)}, f32[1,168,128]{2,1,0:T(8,128)S(1)}, u32[]{:S(2)}, u32[]{:S(2)}) collective-permute-start(f32[1,168,128]{2,1,0:T(8,128)S(1)} %add_add_fusion), channel_id=1, source_target_pairs={{0,16},{4,20},{8,24},{12,28},{16,0},{20,4},{24,8},{28,12},{1,17},{... | collective-permute-start | bytes 258056 | tf_op jit(solution)/shard_map/ppermute | solution.py:69
  62.7 5.4 %collective-permute-start.10 = (f32[1,168,128]{2,1,0:T(8,128)S(1)}, f32[1,168,128]{2,1,0:T(8,128)S(1)}, u32[]{:S(2)}, u32[]{:S(2)}) collective-permute-start(f32[1,168,128]{2,1,0:T(8,128)S(1)} %add.294), channel_id=1, source_target_pairs={{0,8},{4,12},{8,0},{12,4},{16,24},{20,28},{24,16},{28,20},{1,9},{5... | collective-permute-start | bytes 258056 | tf_op jit(solution)/shard_map/ppermute | solution.py:79
  68.1 1.5 %collective-permute-start.11 = (f32[2,168,128]{2,1,0:T(8,128)S(1)}, f32[2,168,128]{2,1,0:T(8,128)S(1)}, u32[]{:S(2)}, u32[]{:S(2)}) collective-permute-start(f32[2,168,128]{2,1,0:T(8,128)S(1)} %pad_maximum_fusion.2), channel_id=1, source_target_pairs={{0,4},{4,0},{8,12},{12,8},{16,20},{20,16},{24,28},{28,24},{1,5},{5... | collective-permute-start | bytes 516104 | tf_op jit(solution)/shard_map/ppermute | solution.py:79

commit v13 on v11

--- a/solution.py
+++ b/solution.py
@@ -12,10 +12,15 @@
         up = [(i, (i + 1) % size) for i in range(size - 1)]
         down = [(j, i) for i, j in up]
         if whole:
-            before = lax.ppermute(array, axis, up)
-            after = lax.ppermute(array, axis, down)
-            before = lax.slice_in_dim(before, length - width, length, axis=dim)
-            after = lax.slice_in_dim(after, 0, width, axis=dim)
+            pairs = [(i, i + 1) for i in range(1, size - 1, 2)]
+            pairs += [(j, i) for i, j in pairs]
+            from_pair = lax.ppermute(array, axis, [(i, i ^ 1) for i in range(size)])
+            from_chip = lax.ppermute(array, axis, pairs)
+            even = lax.axis_index(axis) % 2 == 0
+            above = jnp.where(even, from_chip, from_pair)
+            below = jnp.where(even, from_pair, from_chip)
+            before = lax.slice_in_dim(above, length - width, length, axis=dim)
+            after = lax.slice_in_dim(below, 0, width, axis=dim)
             array = jnp.concatenate([before, array, after], axis=dim)
             continue
         last = lax.slice_in_dim(array, length - width, length, axis=dim)

time: 57.1 us -> 55.5 us (0.972)
  starting transfers between devices: 21.6 us -> 19.7 us
    ppermute x2, starting transfers between devices: 4.47 us -> 1.22 us  [the longest x1 0.66 us: with_halo(): from_chip = lax.ppermute(array, axis, pairs)]
    ppermute x2, starting transfers between devices: 5.6 us -> 7.01 us  [tree_psum(): flat = keep + lax.ppermute(give, axis, xor_pairs(size, bit))]
where the time goes in v13:
time: 55.5 us; the launch traced here: 55.1 us
  starting transfers between devices  19.7 us (35%)
  other arithmetic  10.9 us (20%)
  waiting for transfers between devices  10.1 us (18%)
  local copies, waits for them, and re-layouts  6.62 us (12%)
  matrix products  6.49 us (12%)
  between operations  1.26 us (2%)
    ppermute x2, starting transfers between devices, tree_psum(): flat = keep + lax.ppermute(give, axis, xor_pairs(size, bit))  7.01 us
    ppermute x4, starting transfers between devices, tree_psum(): got = [lax.ppermute(flat, axis, xor_pairs(size, mask)) for mask in masks]  6.37 us
    convert_element_type x1, other arithmetic, image_grad_of(): return image_grad.astype(jnp.bfloat16)  4.7 us
    ppermute x4, waiting for transfers between devices, tree_psum(): got = [lax.ppermute(flat, axis, xor_pairs(size, mask)) for mask in masks]  4.63 us
    ppermute x2, waiting for transfers between devices, tree_psum(): flat = keep + lax.ppermute(give, axis, xor_pairs(size, bit))  4.09 us
    reduce_sum x4, other arithmetic, on_device(): jnp.sum(d_conv * padded[:, :, a:a + rows, b:b + cols], axis=(0, 2, 3))  3.23 us
    ppermute x1, starting transfers between devices, with_halo(): before = lax.ppermute(last, axis, up)  3.22 us
    dot_general x1, matrix products, on_device(): jnp.einsum('scrw,cf->sfrw', lifted, up_weight, preferred_element_type=jnp...  2.83 us
  transfers between devices with their start and end apart: 12, of which 4 were waited for; matrix products, arithmetic and copies ran while one was open for 13% of the time, Pallas kernels for 0%

profile of v13, /device:TPU:0, one launch (start us, length us, event | category | flops | bytes accessed | tf_op | source)
XLA Modules:
  0.0 55.1 jit_solution(17637973100512516072)
XLA Ops:
  0.7 0.6 %collective-permute-start.1 = (bf16[1,96,6,128]{3,1,2,0:T(8,128)(2,1)}, bf16[1,96,6,128]{3,1,2,0:T(8,128)(2,1)S(1)}, u32[]{:S(2)}, u32[]{:S(2)}) collective-permute-start(bf16[1,96,6,128]{3,1,2,0:T(8,128)(2,1)} %param.11), channel_id=1, source_target_pairs={{0,4},{4,0},{8,12},{12,8},{16,20},{20,16},{24,28},{28,24},{1,5},{5... | collective-permute-start | bytes 442376 | tf_op jit(solution)/shard_map/ppermute | solution.py:17
  1.2 0.7 %collective-permute-start = (bf16[1,96,6,128]{3,1,2,0:T(8,128)(2,1)}, bf16[1,96,6,128]{3,1,2,0:T(8,128)(2,1)S(1)}, u32[]{:S(2)}, u32[]{:S(2)}) collective-permute-start(bf16[1,96,6,128]{3,1,2,0:T(8,128)(2,1)} %param.11), channel_id=1, source_target_pairs={{4,8},{12,16},{20,24},{8,4},{16,12},{24,20},{5,9},{13,17},{21,25},... | collective-permute-start | bytes 442376 | tf_op jit(solution)/shard_map/ppermute | solution.py:18
  1.9 1.0 %slice_bitcast_fusion.50 = (f32[96]{0:T(128)S(1)}, f32[96]{0:T(128)S(1)}, f32[96]{0:T(128)S(1)}, f32[96]{0:T(128)S(1)}, f32[96]{0:T(128)S(1)}, /*index=5*/f32[96...) fusion(f32[96,7,7]{0,2,1:T(8,128)} %param.13), kind=kLoop, calls=%fused_computation.263 | loop fusion | bytes 14592 | tf_op jit(solution)/shard_map/mul | solution.py:166
  2.9 1.1 %convert_reduce_fusion.1 = f32[96]{0:T(128)S(1)} fusion(bf16[1,96,6,128]{3,1,2,0:T(8,128)(2,1)} %param.12, f32[96]{0:T(128)} %param.21), kind=kLoop, calls=%fused_computation.108 | loop fusion | flops 368544 | bytes 148224 | tf_op jit(solution)/shard_map/reduce_sum | solution.py:185
  4.1 1.0 %fusion.58 = (bf16[96,12,1,128]{3,0,1,2:T(8,128)(2,1)S(1)}, bf16[1,96,12,128]{3,1,2,0:T(8,128)(2,1)S(1)}) fusion(bf16[1,96,3,128]{3,1,2,0:T(8,128)(2,1)S(1)} %get-tuple-element.88, bf16[1,96,6,128]{3,1,2,0:T(8,128)(2,1)} %param.11, bf16[1,96,3,128]{3,1,2,0:T(8,128)(2,1)S(1)} %get-tuple-element.87), kind=kLoop, calls=%fused_computation.272 | loop fusion | flops 294912 | bytes 884736 | tf_op jit(solution)/shard_map/concatenate | solution.py:24
  5.1 0.2 copy.41
  5.3 0.1 pad.46.clone
  5.5 0.1 reshape.366
  5.7 0.5 copy-done.3
  6.2 1.5 %fusion.20 = f32[6,8,17,96]{3,1,2,0:T(8,128)S(1)} fusion(bf16[96,12,1,7,6]{0,3,4,1,2:T(8,128)(2,1)S(1)} %slice.664, bf16[96,12,1,8,17]{0,3,4,1,2:T(8,128)(2,1)S(1)} %copy.28, f32[96]{0:T(128)S(1)} %copy-done.9, pred[8,17]{0,1:T(8,128)(4,1)S(1)} %copy-done.11, f32[96,1,7,7]{0,3,2,1:T(8,128)S(1)} %bitcast.270), kind=kOutput, calls=%fused_computation.81 | convolution fusion | flops 47490048 | bytes 742792 | tf_op jit(solution)/shard_map/conv_general_dilated | solution.py:124
  7.7 0.1 copy.30
  7.9 0.2 copy.40
  8.2 0.3 copy-done.4
  8.6 2.8 %fusion.9 = (bf16[384,6,128]{0,2,1:T(8,128)(2,1)S(1)}, f32[384,6,128]{0,2,1:T(8,128)S(1)}) fusion(f32[384]{0:T(512)S(1)} %copy-done.8, bf16[96,384]{1,0:T(8,128)(2,1)S(1)} %copy-done, f32[6,1,128,96]{2,3,0,1:T(8,128)S(1)} %copy.40, f32[96]{0:T(128)S(1)} %copy-done.6, f32[96]{0:T(128)S(1)} %copy-done.4, f32[6,128]{1,0:T(8,128)S(1)} %add_rsqrt_fusion, ...), kind=kOutput, calls=%fused_computation.57 | convolution fusion | flops 76455936 | bytes 2146560 | tf_op jit(solution)/shard_map/scrw,cf->sfrw/dot_general | solution.py:140
  11.4 0.7 %convert_reduce_fusion = (f32[384]{0:T(512)S(1)}, bf16[384,6,128]{0,2,1:T(8,128)(2,1)S(1)}) fusion(f32[384,6,128]{0,2,1:T(8,128)S(1)} %get-tuple-element.144, bf16[384,96]{0,1:T(8,128)(2,1)S(1)} %copy-done.7, bf16[1,96,6,128]{3,1,2,0:T(8,128)(2,1)S(1)} %copy-done.1, f32[96]{0:T(128)S(1)} %copy-done.5), kind=kOutput, calls=%fused_computation.73 | convolution fusion | flops 60382848 | bytes 1992576 | tf_op jit(solution)/shard_map/scrw,fc->sfrw/dot_general | solution.py:149
  12.2 0.4 fusion.32
  12.6 0.1 fusion.37
  12.7 1.2 %multiply_reduce_fusion = (f32[96]{0:T(128)S(1)}, f32[96]{0:T(128)S(1)}, f32[96]{0:T(128)S(1)}, f32[96]{0:T(128)S(1)}, f32[96]{0:T(128)S(1)}, /*index=5*/f32[96]...) fusion(bf16[1,96,12,128]{3,1,2,0:T(8,128)(2,1)S(1)} %get-tuple-, ...), kind=kLoop, calls=%fused_computation.109 | loop fusion | flops 4495680 | bytes 1199232 | tf_op jit(solution)/shard_map/reduce_sum | solution.py:174
  13.9 0.5 multiply_reduce_fusion.42
  14.5 0.3 multiply_reduce_fusion.3
  14.8 1.2 %multiply_reduce_fusion.21 = (f32[96]{0:T(128)S(1)}, f32[96]{0:T(128)S(1)}, f32[96]{0:T(128)S(1)}, f32[96]{0:T(128)S(1)}, f32[96]{0:T(128)S(1)}, /*index=5*/f32[...) fusion(f32[1,96,6,128]{3,1,2,0:T(8,128)S(1)} %get-tuple-element, ...), kind=kLoop, calls=%fused_computation.130 | loop fusion | flops 3979584 | bytes 596736 | tf_op jit(solution)/shard_map/reduce_sum | solution.py:174
  16.0 0.3 fusion.22
  16.3 0.1 stack.199
  16.5 0.1 reduce_sum.586
  16.7 0.3 fusion.23
  17.0 0.4 fusion.21
  17.6 4.8 %collective-permute-start.2 = (f32[2,168,128]{2,1,0:T(8,128)S(1)}, f32[2,168,128]{2,1,0:T(8,128)S(1)}, u32[]{:S(2)}, u32[]{:S(2)}) collective-permute-start(f32[2,168,128]{2,1,0:T(8,128)S(1)} %constant_dynamic-slice_fusion.1), channel_id=1, source_target_pairs={{0,4},{4,0},{8,12},{12,8},{16,20},{20,16},{24,28},{28,24},{1,5},{5... | collective-permute-start | bytes 516104 | tf_op jit(solution)/shard_map/ppermute | solution.py:68
  22.5 1.0 %collective-permute-done.2 = f32[2,168,128]{2,1,0:T(8,128)S(1)} collective-permute-done((f32[2,168,128]{2,1,0:T(8,128)S(1)}, f32[2,168,128]{2,1,0:T(8,128)S(1)}, u32[]{:S(2)}, u32[]{:S(2)}) %collective-permute-start.2) | collective-permute-done | bytes 172064 | tf_op jit(solution)/shard_map/ppermute | solution.py:68
  23.6 2.2 %collective-permute-start.3 = (f32[1,168,128]{2,1,0:T(8,128)S(1)}, f32[1,168,128]{2,1,0:T(8,128)S(1)}, u32[]{:S(2)}, u32[]{:S(2)}) collective-permute-start(f32[1,168,128]{2,1,0:T(8,128)S(1)} %constant_dynamic-slice_fusion), channel_id=1, source_target_pairs={{0,8},{4,12},{8,0},{12,4},{16,24},{20,28},{24,16},{28,20},{1,9},{5... | collective-permute-start | bytes 258056 | tf_op jit(solution)/shard_map/ppermute | solution.py:68
  25.7 3.1 %collective-permute-done.3 = f32[1,168,128]{2,1,0:T(8,128)S(1)} collective-permute-done((f32[1,168,128]{2,1,0:T(8,128)S(1)}, f32[1,168,128]{2,1,0:T(8,128)S(1)}, u32[]{:S(2)}, u32[]{:S(2)}) %collective-permute-start.3) | collective-permute-done | bytes 86048 | tf_op jit(solution)/shard_map/ppermute | solution.py:68
  28.8 2.7 %collective-permute-start.6 = (f32[1,168,128]{2,1,0:T(8,128)S(1)}, f32[1,168,128]{2,1,0:T(8,128)S(1)}, u32[]{:S(2)}, u32[]{:S(2)}) collective-permute-start(f32[1,168,128]{2,1,0:T(8,128)S(1)} %dynamic-slice_add_fusion.1), channel_id=1, source_target_pairs={{0,3},{1,2},{2,1},{3,0},{4,7},{5,6},{6,5},{7,4},{8,11},{9,10},{10,... | collective-permute-start | bytes 258056 | tf_op jit(solution)/shard_map/ppermute | solution.py:74
  31.5 0.5 collective-permute-start.5
  32.0 0.4 collective-permute-start.4
  32.4 1.3 %collective-permute-start.9 = (f32[1,96,3,128]{3,1,2,0:T(8,128)S(1)}, f32[1,96,3,128]{3,1,2,0:T(8,128)S(1)}, u32[]{:S(2)}, u32[]{:S(2)}) collective-permute-start(f32[1,96,3,128]{3,1,2,0:T(8,128)S(1)} %get-tuple-element.84), channel_id=1, source_target_pairs={{4,0},{8,4},{12,8},{16,12},{20,16},{24,20},{28,24},{5,1},{9,5},{13... | collective-permute-start | bytes 442376 | tf_op jit(solution)/shard_map/ppermute | solution.py:29
  33.7 3.2 %collective-permute-start.8 = (f32[1,96,3,128]{3,1,2,0:T(8,128)S(1)}, f32[1,96,3,128]{3,1,2,0:T(8,128)S(1)}, u32[]{:S(2)}, u32[]{:S(2)}) collective-permute-start(f32[1,96,3,128]{3,1,2,0:T(8,128)S(1)} %get-tuple-element.83), channel_id=1, source_target_pairs={{0,4},{4,8},{8,12},{12,16},{16,20},{20,24},{24,28},{1,5},{5,9},{9,... | collective-permute-start | bytes 442376 | tf_op jit(solution)/shard_map/ppermute | solution.py:28
  37.0 2.8 %collective-permute-start.7 = (f32[1,168,128]{2,1,0:T(8,128)S(1)}, f32[1,168,128]{2,1,0:T(8,128)S(1)}, u32[]{:S(2)}, u32[]{:S(2)}) collective-permute-start(f32[1,168,128]{2,1,0:T(8,128)S(1)} %add_add_fusion), channel_id=1, source_target_pairs={{0,16},{4,20},{8,24},{12,28},{16,0},{20,4},{24,8},{28,12},{1,17},{... | collective-permute-start | bytes 258056 | tf_op jit(solution)/shard_map/ppermute | solution.py:74
  39.8 0.4 select_maximum_fusion
  40.2 4.6 %collective-permute-done.7 = f32[1,168,128]{2,1,0:T(8,128)S(1)} collective-permute-done((f32[1,168,128]{2,1,0:T(8,128)S(1)}, f32[1,168,128]{2,1,0:T(8,128)S(1)}, u32[]{:S(2)}, u32[]{:S(2)}) %collective-permute-start.7) | collective-permute-done | bytes 86048 | tf_op jit(solution)/shard_map/ppermute | solution.py:74
  44.8 0.6 %collective-permute-start.10 = (f32[1,168,128]{2,1,0:T(8,128)S(1)}, f32[1,168,128]{2,1,0:T(8,128)S(1)}, u32[]{:S(2)}, u32[]{:S(2)}) collective-permute-start(f32[1,168,128]{2,1,0:T(8,128)S(1)} %add.297), channel_id=1, source_target_pairs={{0,8},{4,12},{8,0},{12,4},{16,24},{20,28},{24,16},{28,20},{1,9},{5... | collective-permute-start | bytes 258056 | tf_op jit(solution)/shard_map/ppermute | solution.py:84
  45.4 4.7 %add_convert_fusion = bf16[1,96,6,128]{3,1,2,0:T(8,128)(2,1)} fusion(f32[1,96,12,134]{3,1,2,0:T(8,128)S(1)} %select_maximum_fusion, bf16[1,96,6,128]{3,1,2,0:T(8,128)(2,1)S(1)} %copy-done.1, f32[96]{0:T(128)S(1)} %get-tuple-element.138, f32[96]{0:T(128)S(1)} %get-tuple-element.139, f32[96]{0:T(128)S(1)} %get-tuple-element.92, f32[96]{0:T(128)S(1)} %get-tuple-element.93, ...), kind=kLoop, calls=%fused_computation.107 | loop fusion | flops 7372800 | bytes 14764416 | tf_op jit(solution)/shard_map/convert_element_type | solution.py:169
  50.2 1.4 %collective-permute-done.11 = f32[2,168,128]{2,1,0:T(8,128)S(1)} collective-permute-done((f32[2,168,128]{2,1,0:T(8,128)S(1)}, f32[2,168,128]{2,1,0:T(8,128)S(1)}, u32[]{:S(2)}, u32[]{:S(2)}) %collective-permute-start.11) | collective-permute-done | bytes 172064 | tf_op jit(solution)/shard_map/ppermute | solution.py:84
  51.7 0.3 slice.647
  51.9 0.5 fusion.60
  52.5 0.6 %slice.681 = f32[384]{0:T(512)} slice(f32[86016]{0:T(1024)S(1)} %bitcast.267), slice={[45056:45440]} | slice | bytes 3072 | tf_op jit(solution)/shard_map/slice | solution.py:92
  53.1 0.1 slice.654
  53.1 0.6 %slice_bitcast_fusion.1 = f32[96,7,7]{0,2,1:T(8,128)} fusion(f32[128,7,96]{2,1,0:T(8,128)S(1)} %slice.647), kind=kLoop, calls=%fused_computation.196 | loop fusion | bytes 37632 | tf_op jit(solution)/shard_map/transpose | solution.py:191
  53.8 0.7 %reshape.363 = f32[96,384]{1,0:T(8,128)} reshape(f32[36864]{0:T(1024)S(1)} %slice.680) | data formatting | bytes 294912 | tf_op jit(solution)/shard_map/reshape | solution.py:92
  54.4 0.7 %slice_bitcast_fusion = f32[384,96]{0,1:T(8,128)} fusion(f32[224,384]{1,0:T(8,128)S(1)} %slice.654), kind=kLoop, calls=%fused_computation.178 | loop fusion | bytes 294912 | tf_op jit(solution)/shard_map/transpose | solution.py:192
  (75 shorter events, 0.9 us)
Async XLA Ops:
  0.6 7.5 %copy-start = (bf16[96,384]{1,0:T(8,128)(2,1)S(1)}, bf16[96,384]{1,0:T(8,128)(2,1)}, u32[]{:S(2)}) copy-start(bf16[96,384]{1,0:T(8,128)(2,1)} %param.17) | copy-start | bytes 221188
  0.7 3.4 %collective-permute-start.1 = (bf16[1,96,6,128]{3,1,2,0:T(8,128)(2,1)}, bf16[1,96,6,128]{3,1,2,0:T(8,128)(2,1)S(1)}, u32[]{:S(2)}, u32[]{:S(2)}) collective-permute-start(bf16[1,96,6,128]{3,1,2,0:T(8,128)(2,1)} %param.11), channel_id=1, source_target_pairs={{0,4},{4,0},{8,12},{12,8},{16,20},{20,16},{24,28},{28,24},{1,5},{5... | collective-permute-start | bytes 442376 | tf_op jit(solution)/shard_map/ppermute | solution.py:17
  1.2 2.8 %collective-permute-start = (bf16[1,96,6,128]{3,1,2,0:T(8,128)(2,1)}, bf16[1,96,6,128]{3,1,2,0:T(8,128)(2,1)S(1)}, u32[]{:S(2)}, u32[]{:S(2)}) collective-permute-start(bf16[1,96,6,128]{3,1,2,0:T(8,128)(2,1)} %param.11), channel_id=1, source_target_pairs={{4,8},{12,16},{20,24},{8,4},{16,12},{24,20},{5,9},{13,17},{21,25},... | collective-permute-start | bytes 442376 | tf_op jit(solution)/shard_map/ppermute | solution.py:18
  5.4 0.8 %copy-start.3 = (f32[96,7,7]{0,2,1:T(8,128)S(1)}, f32[96,7,7]{0,2,1:T(8,128)}, u32[]{:S(2)}) copy-start(f32[96,7,7]{0,2,1:T(8,128)} %param.13) | copy-start | bytes 56452
  5.5 0.7 %copy-start.9 = (f32[96]{0:T(128)S(1)}, f32[96]{0:T(128)}, u32[]{:S(2)}) copy-start(f32[96]{0:T(128)} %param.14) | copy-start | bytes 1156
  5.5 0.7 %copy-start.11 = (pred[8,17]{0,1:T(8,128)(4,1)S(1)}, pred[8,17]{0,1:T(8,128)(4,1)}, u32[]{:S(2)}) copy-start(pred[8,17]{0,1:T(8,128)(4,1)} %constant.172) | copy-start | bytes 412
  7.8 0.7 %copy-start.4 = (f32[96]{0:T(128)S(1)}, f32[96]{0:T(128)}, u32[]{:S(2)}) copy-start(f32[96]{0:T(128)} %param.15) | copy-start | bytes 1156
  7.9 0.7 %copy-start.6 = (f32[96]{0:T(128)S(1)}, f32[96]{0:T(128)}, u32[]{:S(2)}) copy-start(f32[96]{0:T(128)} %param.16) | copy-start | bytes 1156
  7.9 0.7 %copy-start.8 = (f32[384]{0:T(512)S(1)}, f32[384]{0:T(512)}, u32[]{:S(2)}) copy-start(f32[384]{0:T(512)} %param.18) | copy-start | bytes 4612
  8.6 2.8 %copy-start.1 = (bf16[1,96,6,128]{3,1,2,0:T(8,128)(2,1)S(1)}, bf16[1,96,6,128]{3,1,2,0:T(8,128)(2,1)}, u32[]{:S(2)}) copy-start(bf16[1,96,6,128]{3,1,2,0:T(8,128)(2,1)} %param.12) | copy-start | bytes 442372
  8.6 2.9 %copy-start.5 = (f32[96]{0:T(128)S(1)}, f32[96]{0:T(128)}, u32[]{:S(2)}) copy-start(f32[96]{0:T(128)} %param.21) | copy-start | bytes 1156
  8.6 2.9 %copy-start.7 = (bf16[384,96]{0,1:T(8,128)(2,1)S(1)}, bf16[384,96]{0,1:T(8,128)(2,1)}, u32[]{:S(2)}) copy-start(bf16[384,96]{0,1:T(8,128)(2,1)} %param.19) | copy-start | bytes 221188
  12.6 1.9 %copy-start.2 = (bf16[1,96,6,128]{3,1,2,0:T(8,128)(2,1)S(1)}, bf16[1,96,6,128]{3,1,2,0:T(8,128)(2,1)}, u32[]{:S(2)}) copy-start(bf16[1,96,6,128]{3,1,2,0:T(8,128)(2,1)} %param.11) | copy-start | bytes 442372
  16.3 0.8 %copy-start.10 = (f32[96]{0:T(128)S(1)}, f32[96]{0:T(128)}, u32[]{:S(2)}) copy-start(f32[96]{0:T(128)} %param.20) | copy-start | bytes 1156
  17.6 5.9 %collective-permute-start.2 = (f32[2,168,128]{2,1,0:T(8,128)S(1)}, f32[2,168,128]{2,1,0:T(8,128)S(1)}, u32[]{:S(2)}, u32[]{:S(2)}) collective-permute-start(f32[2,168,128]{2,1,0:T(8,128)S(1)} %constant_dynamic-slice_fusion.1), channel_id=1, source_target_pairs={{0,4},{4,0},{8,12},{12,8},{16,20},{20,16},{24,28},{28,24},{1,5},{5... | collective-permute-start | bytes 516104 | tf_op jit(solution)/shard_map/ppermute | solution.py:68
  23.6 5.2 %collective-permute-start.3 = (f32[1,168,128]{2,1,0:T(8,128)S(1)}, f32[1,168,128]{2,1,0:T(8,128)S(1)}, u32[]{:S(2)}, u32[]{:S(2)}) collective-permute-start(f32[1,168,128]{2,1,0:T(8,128)S(1)} %constant_dynamic-slice_fusion), channel_id=1, source_target_pairs={{0,8},{4,12},{8,0},{12,4},{16,24},{20,28},{24,16},{28,20},{1,9},{5... | collective-permute-start | bytes 258056 | tf_op jit(solution)/shard_map/ppermute | solution.py:68
  28.8 8.1 %collective-permute-start.6 = (f32[1,168,128]{2,1,0:T(8,128)S(1)}, f32[1,168,128]{2,1,0:T(8,128)S(1)}, u32[]{:S(2)}, u32[]{:S(2)}) collective-permute-start(f32[1,168,128]{2,1,0:T(8,128)S(1)} %dynamic-slice_add_fusion.1), channel_id=1, source_target_pairs={{0,3},{1,2},{2,1},{3,0},{4,7},{5,6},{6,5},{7,4},{8,11},{9,10},{10,... | collective-permute-start | bytes 258056 | tf_op jit(solution)/shard_map/ppermute | solution.py:74
  31.5 5.4 %collective-permute-start.5 = (f32[1,168,128]{2,1,0:T(8,128)S(1)}, f32[1,168,128]{2,1,0:T(8,128)S(1)}, u32[]{:S(2)}, u32[]{:S(2)}) collective-permute-start(f32[1,168,128]{2,1,0:T(8,128)S(1)} %dynamic-slice_add_fusion.1), channel_id=1, source_target_pairs={{0,2},{1,3},{2,0},{3,1},{4,6},{5,7},{6,4},{7,5},{8,10},{9,11},{10,... | collective-permute-start | bytes 258056 | tf_op jit(solution)/shard_map/ppermute | solution.py:74
  32.0 4.9 %collective-permute-start.4 = (f32[1,168,128]{2,1,0:T(8,128)S(1)}, f32[1,168,128]{2,1,0:T(8,128)S(1)}, u32[]{:S(2)}, u32[]{:S(2)}) collective-permute-start(f32[1,168,128]{2,1,0:T(8,128)S(1)} %dynamic-slice_add_fusion.1), channel_id=1, source_target_pairs={{0,1},{1,0},{2,3},{3,2},{4,5},{5,4},{6,7},{7,6},{8,9},{9,8},{10,11... | collective-permute-start | bytes 258056 | tf_op jit(solution)/shard_map/ppermute | solution.py:74
  32.4 7.4 %collective-permute-start.9 = (f32[1,96,3,128]{3,1,2,0:T(8,128)S(1)}, f32[1,96,3,128]{3,1,2,0:T(8,128)S(1)}, u32[]{:S(2)}, u32[]{:S(2)}) collective-permute-start(f32[1,96,3,128]{3,1,2,0:T(8,128)S(1)} %get-tuple-element.84), channel_id=1, source_target_pairs={{4,0},{8,4},{12,8},{16,12},{20,16},{24,20},{28,24},{5,1},{9,5},{13... | collective-permute-start | bytes 442376 | tf_op jit(solution)/shard_map/ppermute | solution.py:29
  33.7 6.1 %collective-permute-start.8 = (f32[1,96,3,128]{3,1,2,0:T(8,128)S(1)}, f32[1,96,3,128]{3,1,2,0:T(8,128)S(1)}, u32[]{:S(2)}, u32[]{:S(2)}) collective-permute-start(f32[1,96,3,128]{3,1,2,0:T(8,128)S(1)} %get-tuple-element.83), channel_id=1, source_target_pairs={{0,4},{4,8},{8,12},{12,16},{16,20},{20,24},{24,28},{1,5},{5,9},{9,... | collective-permute-start | bytes 442376 | tf_op jit(solution)/shard_map/ppermute | solution.py:28
  37.0 7.8 %collective-permute-start.7 = (f32[1,168,128]{2,1,0:T(8,128)S(1)}, f32[1,168,128]{2,1,0:T(8,128)S(1)}, u32[]{:S(2)}, u32[]{:S(2)}) collective-permute-start(f32[1,168,128]{2,1,0:T(8,128)S(1)} %add_add_fusion), channel_id=1, source_target_pairs={{0,16},{4,20},{8,24},{12,28},{16,0},{20,4},{24,8},{28,12},{1,17},{... | collective-permute-start | bytes 258056 | tf_op jit(solution)/shard_map/ppermute | solution.py:74
  44.8 5.3 %collective-permute-start.10 = (f32[1,168,128]{2,1,0:T(8,128)S(1)}, f32[1,168,128]{2,1,0:T(8,128)S(1)}, u32[]{:S(2)}, u32[]{:S(2)}) collective-permute-start(f32[1,168,128]{2,1,0:T(8,128)S(1)} %add.297), channel_id=1, source_target_pairs={{0,8},{4,12},{8,0},{12,4},{16,24},{20,28},{24,16},{28,20},{1,9},{5... | collective-permute-start | bytes 258056 | tf_op jit(solution)/shard_map/ppermute | solution.py:84
  50.1 1.5 %collective-permute-start.11 = (f32[2,168,128]{2,1,0:T(8,128)S(1)}, f32[2,168,128]{2,1,0:T(8,128)S(1)}, u32[]{:S(2)}, u32[]{:S(2)}) collective-permute-start(f32[2,168,128]{2,1,0:T(8,128)S(1)} %pad_maximum_fusion.2), channel_id=1, source_target_pairs={{0,4},{4,0},{8,12},{12,8},{16,20},{20,16},{24,28},{28,24},{1,5},{5... | collective-permute-start | bytes 516104 | tf_op jit(solution)/shard_map/ppermute | solution.py:84

commit v14 on v13

--- a/solution.py
+++ b/solution.py
@@ -9,8 +9,6 @@
 def with_halo(array, sides, width, whole=False):
     for axis, dim in sides:
         size, length = (lax.axis_size(axis), array.shape[dim])
-        up = [(i, (i + 1) % size) for i in range(size - 1)]
-        down = [(j, i) for i, j in up]
         if whole:
             pairs = [(i, i + 1) for i in range(1, size - 1, 2)]
             pairs += [(j, i) for i, j in pairs]
@@ -25,8 +23,13 @@
             continue
         last = lax.slice_in_dim(array, length - width, length, axis=dim)
         first = lax.slice_in_dim(array, 0, width, axis=dim)
-        before = lax.ppermute(last, axis, up)
-        after = lax.ppermute(first, axis, down)
+        pairs = [(i, i + 1) for i in range(1, size - 1, 2)]
+        pairs += [(j, i) for i, j in pairs]
+        even = lax.axis_index(axis) % 2 == 0
+        from_pair = lax.ppermute(jnp.where(even, last, first), axis, [(i, i ^ 1) for i in range(size)])
+        from_chip = lax.ppermute(jnp.where(even, first, last), axis, pairs)
+        before = jnp.where(even, from_chip, from_pair)
+        after = jnp.where(even, from_pair, from_chip)
         array = jnp.concatenate([before, array, after], axis=dim)
     return array
 

time: 55.5 us -> 54.4 us (0.980)
  starting transfers between devices: 19.7 us -> 16.3 us
  waiting for transfers between devices: 10.1 us -> 11.4 us
  local copies, waits for them, and re-layouts: 6.62 us -> 7.6 us
    ppermute x4, waiting for transfers between devices: 4.63 us -> 8.3 us  [tree_psum(): got = [lax.ppermute(flat, axis, xor_pairs(size, mask)) for mask in masks]]
    ppermute x2, waiting for transfers between devices: 4.09 us -> 1.67 us  [tree_psum(): flat = keep + lax.ppermute(give, axis, xor_pairs(size, bit))]
    ppermute x2, starting transfers between devices: 4.51 us -> 2.39 us  [the longest x1 1.54 us: with_halo(): lax.ppermute(jnp.where(even, last, first), axis, [(i, i ^ 1) for i in ran...]
    ppermute x2, starting transfers between devices: 7.01 us -> 5.98 us  [tree_psum(): flat = keep + lax.ppermute(give, axis, xor_pairs(size, bit))]
    mul x3, local copies, waits for them, and re-layouts: 0.98 us -> 1.99 us  [image_grad_of(): conv_weight[:, a, b][None, :, None, None]]
  transfers between devices with their start and end apart: 12 -> 12, of which waited for: 4 -> 7; matrix products, arithmetic and copies ran while one was open for 13% -> 15% of each run, Pallas kernels for 0% -> 0%
where the time goes in v14:
time: 54.4 us; the launch traced here: 54 us
  starting transfers between devices  16.3 us (30%)
  waiting for transfers between devices  11.4 us (21%)
  other arithmetic  10.9 us (20%)
  local copies, waits for them, and re-layouts  7.6 us (14%)
  matrix products  6.49 us (12%)
  between operations  1.26 us (2%)
    ppermute x4, waiting for transfers between devices, tree_psum(): got = [lax.ppermute(flat, axis, xor_pairs(size, mask)) for mask in masks]  8.3 us
    ppermute x4, starting transfers between devices, tree_psum(): got = [lax.ppermute(flat, axis, xor_pairs(size, mask)) for mask in masks]  6.21 us
    ppermute x2, starting transfers between devices, tree_psum(): flat = keep + lax.ppermute(give, axis, xor_pairs(size, bit))  5.98 us
    convert_element_type x1, other arithmetic, image_grad_of(): return image_grad.astype(jnp.bfloat16)  4.7 us
    reduce_sum x4, other arithmetic, on_device(): jnp.sum(d_conv * padded[:, :, a:a + rows, b:b + cols], axis=(0, 2, 3))  3.23 us
    dot_general x1, matrix products, on_device(): jnp.einsum('scrw,cf->sfrw', lifted, up_weight, preferred_element_type=jnp...  2.83 us
    mul x3, local copies, waits for them, and re-layouts, image_grad_of(): conv_weight[:, a, b][None, :, None, None]  1.99 us
    ppermute x2, waiting for transfers between devices, tree_psum(): flat = keep + lax.ppermute(give, axis, xor_pairs(size, bit))  1.67 us
  transfers between devices with their start and end apart: 12, of which 7 were waited for; matrix products, arithmetic and copies ran while one was open for 15% of the time, Pallas kernels for 0%

profile of v14, /device:TPU:0, one launch (start us, length us, event | category | flops | bytes accessed | tf_op | source)
XLA Modules:
  0.0 54.0 jit_solution(7376319588241862488)
XLA Ops:
  0.7 0.6 %collective-permute-start.1 = (bf16[1,96,6,128]{3,1,2,0:T(8,128)(2,1)}, bf16[1,96,6,128]{3,1,2,0:T(8,128)(2,1)S(1)}, u32[]{:S(2)}, u32[]{:S(2)}) collective-permute-start(bf16[1,96,6,128]{3,1,2,0:T(8,128)(2,1)} %param.11), channel_id=1, source_target_pairs={{0,4},{4,0},{8,12},{12,8},{16,20},{20,16},{24,28},{28,24},{1,5},{5... | collective-permute-start | bytes 442376 | tf_op jit(solution)/shard_map/ppermute | solution.py:15
  1.2 0.7 %collective-permute-start = (bf16[1,96,6,128]{3,1,2,0:T(8,128)(2,1)}, bf16[1,96,6,128]{3,1,2,0:T(8,128)(2,1)S(1)}, u32[]{:S(2)}, u32[]{:S(2)}) collective-permute-start(bf16[1,96,6,128]{3,1,2,0:T(8,128)(2,1)} %param.11), channel_id=1, source_target_pairs={{4,8},{12,16},{20,24},{8,4},{16,12},{24,20},{5,9},{13,17},{21,25},... | collective-permute-start | bytes 442376 | tf_op jit(solution)/shard_map/ppermute | solution.py:16
  1.9 1.0 %slice_bitcast_fusion.50 = (f32[96]{0:T(128)S(1)}, f32[96]{0:T(128)S(1)}, f32[96]{0:T(128)S(1)}, f32[96]{0:T(128)S(1)}, f32[96]{0:T(128)S(1)}, /*index=5*/f32[96...) fusion(f32[96,7,7]{0,2,1:T(8,128)} %param.13), kind=kLoop, calls=%fused_computation.267 | loop fusion | bytes 14592 | tf_op jit(solution)/shard_map/mul | solution.py:169
  2.9 1.0 %slice_bitcast_fusion.49 = (f32[96]{0:T(128)S(1)}, f32[96]{0:T(128)S(1)}, f32[96]{0:T(128)S(1)}, f32[96]{0:T(128)S(1)}, f32[96]{0:T(128)S(1)}, /*index=5*/f32[96...) fusion(f32[96,7,7]{0,2,1:T(8,128)} %param.13), kind=kLoop, calls=%fused_computation.266 | loop fusion | bytes 14592 | tf_op jit(solution)/shard_map/mul | solution.py:169
  3.9 1.1 %convert_reduce_fusion.1 = f32[96]{0:T(128)S(1)} fusion(bf16[1,96,6,128]{3,1,2,0:T(8,128)(2,1)} %param.12, f32[96]{0:T(128)} %param.21), kind=kLoop, calls=%fused_computation.108 | loop fusion | flops 368544 | bytes 148224 | tf_op jit(solution)/shard_map/reduce_sum | solution.py:188
  5.1 1.0 %fusion.58 = (bf16[96,12,1,128]{3,0,1,2:T(8,128)(2,1)S(1)}, bf16[1,96,12,128]{3,1,2,0:T(8,128)(2,1)S(1)}) fusion(bf16[1,96,3,128]{3,1,2,0:T(8,128)(2,1)S(1)} %get-tuple-element.90, bf16[1,96,6,128]{3,1,2,0:T(8,128)(2,1)} %param.11, bf16[1,96,3,128]{3,1,2,0:T(8,128)(2,1)S(1)} %get-tuple-element.89), kind=kLoop, calls=%fused_computation.276 | loop fusion | flops 294912 | bytes 884736 | tf_op jit(solution)/shard_map/concatenate | solution.py:22
  6.1 0.2 copy.41
  6.3 0.1 pad.46.clone
  6.5 0.1 reshape.366
  6.8 0.5 copy-done.3
  7.2 1.5 %fusion.20 = f32[6,8,17,96]{3,1,2,0:T(8,128)S(1)} fusion(bf16[96,12,1,7,6]{0,3,4,1,2:T(8,128)(2,1)S(1)} %slice.664, bf16[96,12,1,8,17]{0,3,4,1,2:T(8,128)(2,1)S(1)} %copy.28, f32[96]{0:T(128)S(1)} %copy-done.9, pred[8,17]{0,1:T(8,128)(4,1)S(1)} %copy-done.11, f32[96,1,7,7]{0,3,2,1:T(8,128)S(1)} %bitcast.270), kind=kOutput, calls=%fused_computation.81 | convolution fusion | flops 47490048 | bytes 742792 | tf_op jit(solution)/shard_map/conv_general_dilated | solution.py:127
  8.9 0.2 copy.40
  9.2 0.3 copy-done.4
  9.6 2.8 %fusion.9 = (bf16[384,6,128]{0,2,1:T(8,128)(2,1)S(1)}, f32[384,6,128]{0,2,1:T(8,128)S(1)}) fusion(f32[384]{0:T(512)S(1)} %copy-done.8, bf16[96,384]{1,0:T(8,128)(2,1)S(1)} %copy-done, f32[6,1,128,96]{2,3,0,1:T(8,128)S(1)} %copy.40, f32[96]{0:T(128)S(1)} %copy-done.6, f32[96]{0:T(128)S(1)} %copy-done.4, f32[6,128]{1,0:T(8,128)S(1)} %add_rsqrt_fusion, ...), kind=kOutput, calls=%fused_computation.57 | convolution fusion | flops 76455936 | bytes 2146560 | tf_op jit(solution)/shard_map/scrw,cf->sfrw/dot_general | solution.py:143
  12.5 0.7 %convert_reduce_fusion = (f32[384]{0:T(512)S(1)}, bf16[384,6,128]{0,2,1:T(8,128)(2,1)S(1)}) fusion(f32[384,6,128]{0,2,1:T(8,128)S(1)} %get-tuple-element.146, bf16[384,96]{0,1:T(8,128)(2,1)S(1)} %copy-done.7, bf16[1,96,6,128]{3,1,2,0:T(8,128)(2,1)S(1)} %copy-done.1, f32[96]{0:T(128)S(1)} %copy-done.5), kind=kOutput, calls=%fused_computation.73 | convolution fusion | flops 60382848 | bytes 1992576 | tf_op jit(solution)/shard_map/scrw,fc->sfrw/dot_general | solution.py:152
  13.2 0.4 fusion.32
  13.7 1.2 %multiply_reduce_fusion = (f32[96]{0:T(128)S(1)}, f32[96]{0:T(128)S(1)}, f32[96]{0:T(128)S(1)}, f32[96]{0:T(128)S(1)}, f32[96]{0:T(128)S(1)}, /*index=5*/f32[96]...) fusion(bf16[1,96,12,128]{3,1,2,0:T(8,128)(2,1)S(1)} %get-tuple-, ...), kind=kLoop, calls=%fused_computation.109 | loop fusion | flops 4495680 | bytes 1199232 | tf_op jit(solution)/shard_map/reduce_sum | solution.py:177
  15.0 0.5 multiply_reduce_fusion.42
  15.5 0.3 multiply_reduce_fusion.3
  15.8 1.2 %multiply_reduce_fusion.21 = (f32[96]{0:T(128)S(1)}, f32[96]{0:T(128)S(1)}, f32[96]{0:T(128)S(1)}, f32[96]{0:T(128)S(1)}, f32[96]{0:T(128)S(1)}, /*index=5*/f32[...) fusion(f32[1,96,6,128]{3,1,2,0:T(8,128)S(1)} %get-tuple-element, ...), kind=kLoop, calls=%fused_computation.130 | loop fusion | flops 3979584 | bytes 596736 | tf_op jit(solution)/shard_map/reduce_sum | solution.py:177
  17.0 0.3 fusion.22
  17.3 0.1 stack.199
  17.7 0.3 fusion.23
  18.1 0.4 fusion.21
  18.7 4.0 %collective-permute-start.2 = (f32[2,168,128]{2,1,0:T(8,128)S(1)}, f32[2,168,128]{2,1,0:T(8,128)S(1)}, u32[]{:S(2)}, u32[]{:S(2)}) collective-permute-start(f32[2,168,128]{2,1,0:T(8,128)S(1)} %constant_dynamic-slice_fusion.1), channel_id=1, source_target_pairs={{0,4},{4,0},{8,12},{12,8},{16,20},{20,16},{24,28},{28,24},{1,5},{5... | collective-permute-start | bytes 516104 | tf_op jit(solution)/shard_map/ppermute | solution.py:71
  22.7 1.0 %collective-permute-done.2 = f32[2,168,128]{2,1,0:T(8,128)S(1)} collective-permute-done((f32[2,168,128]{2,1,0:T(8,128)S(1)}, f32[2,168,128]{2,1,0:T(8,128)S(1)}, u32[]{:S(2)}, u32[]{:S(2)}) %collective-permute-start.2) | collective-permute-done | bytes 172064 | tf_op jit(solution)/shard_map/ppermute | solution.py:71
  23.8 2.0 %collective-permute-start.3 = (f32[1,168,128]{2,1,0:T(8,128)S(1)}, f32[1,168,128]{2,1,0:T(8,128)S(1)}, u32[]{:S(2)}, u32[]{:S(2)}) collective-permute-start(f32[1,168,128]{2,1,0:T(8,128)S(1)} %constant_dynamic-slice_fusion), channel_id=1, source_target_pairs={{0,8},{4,12},{8,0},{12,4},{16,24},{20,28},{24,16},{28,20},{1,9},{5... | collective-permute-start | bytes 258056 | tf_op jit(solution)/shard_map/ppermute | solution.py:71
  25.8 0.9 %collective-permute-start.8 = (f32[1,96,3,128]{3,1,2,0:T(8,128)S(1)}, f32[1,96,3,128]{3,1,2,0:T(8,128)S(1)}, u32[]{:S(2)}, u32[]{:S(2)}) collective-permute-start(f32[1,96,3,128]{3,1,2,0:T(8,128)S(1)} %get-tuple-element.85), channel_id=1, source_target_pairs={{4,8},{12,16},{20,24},{8,4},{16,12},{24,20},{5,9},{13,17},{21,25},... | collective-permute-start | bytes 442376 | tf_op jit(solution)/shard_map/ppermute | solution.py:30
  26.6 1.5 %collective-permute-start.9 = (f32[1,96,3,128]{3,1,2,0:T(8,128)S(1)}, f32[1,96,3,128]{3,1,2,0:T(8,128)S(1)}, u32[]{:S(2)}, u32[]{:S(2)}) collective-permute-start(f32[1,96,3,128]{3,1,2,0:T(8,128)S(1)} %get-tuple-element.86), channel_id=1, source_target_pairs={{0,4},{4,0},{8,12},{12,8},{16,20},{20,16},{24,28},{28,24},{1,5},{5... | collective-permute-start | bytes 442376 | tf_op jit(solution)/shard_map/ppermute | solution.py:29
  28.2 0.6 %collective-permute-done.3 = f32[1,168,128]{2,1,0:T(8,128)S(1)} collective-permute-done((f32[1,168,128]{2,1,0:T(8,128)S(1)}, f32[1,168,128]{2,1,0:T(8,128)S(1)}, u32[]{:S(2)}, u32[]{:S(2)}) %collective-permute-start.3) | collective-permute-done | bytes 86048 | tf_op jit(solution)/shard_map/ppermute | solution.py:71
  28.8 2.7 %collective-permute-start.6 = (f32[1,168,128]{2,1,0:T(8,128)S(1)}, f32[1,168,128]{2,1,0:T(8,128)S(1)}, u32[]{:S(2)}, u32[]{:S(2)}) collective-permute-start(f32[1,168,128]{2,1,0:T(8,128)S(1)} %dynamic-slice_add_fusion.1), channel_id=1, source_target_pairs={{0,3},{1,2},{2,1},{3,0},{4,7},{5,6},{6,5},{7,4},{8,11},{9,10},{10,... | collective-permute-start | bytes 258056 | tf_op jit(solution)/shard_map/ppermute | solution.py:77
  31.5 0.5 collective-permute-start.5
  32.0 0.4 collective-permute-start.4
  32.4 2.0 %collective-permute-done.6 = f32[1,168,128]{2,1,0:T(8,128)S(1)} collective-permute-done((f32[1,168,128]{2,1,0:T(8,128)S(1)}, f32[1,168,128]{2,1,0:T(8,128)S(1)}, u32[]{:S(2)}, u32[]{:S(2)}) %collective-permute-start.6) | collective-permute-done | bytes 86048 | tf_op jit(solution)/shard_map/ppermute | solution.py:77
  34.4 1.7 %collective-permute-done.5 = f32[1,168,128]{2,1,0:T(8,128)S(1)} collective-permute-done((f32[1,168,128]{2,1,0:T(8,128)S(1)}, f32[1,168,128]{2,1,0:T(8,128)S(1)}, u32[]{:S(2)}, u32[]{:S(2)}) %collective-permute-start.5) | collective-permute-done | bytes 86048 | tf_op jit(solution)/shard_map/ppermute | solution.py:77
  36.1 0.4 collective-permute-done.4
  36.5 2.7 %collective-permute-start.7 = (f32[1,168,128]{2,1,0:T(8,128)S(1)}, f32[1,168,128]{2,1,0:T(8,128)S(1)}, u32[]{:S(2)}, u32[]{:S(2)}) collective-permute-start(f32[1,168,128]{2,1,0:T(8,128)S(1)} %add_add_fusion), channel_id=1, source_target_pairs={{0,16},{4,20},{8,24},{12,28},{16,0},{20,4},{24,8},{28,12},{1,17},{... | collective-permute-start | bytes 258056 | tf_op jit(solution)/shard_map/ppermute | solution.py:77
  39.2 0.4 select_maximum_fusion
  39.5 4.2 %collective-permute-done.7 = f32[1,168,128]{2,1,0:T(8,128)S(1)} collective-permute-done((f32[1,168,128]{2,1,0:T(8,128)S(1)}, f32[1,168,128]{2,1,0:T(8,128)S(1)}, u32[]{:S(2)}, u32[]{:S(2)}) %collective-permute-start.7) | collective-permute-done | bytes 86048 | tf_op jit(solution)/shard_map/ppermute | solution.py:77
  43.8 0.5 collective-permute-start.10
  44.3 4.7 %add_convert_fusion = bf16[1,96,6,128]{3,1,2,0:T(8,128)(2,1)} fusion(f32[1,96,12,134]{3,1,2,0:T(8,128)S(1)} %select_maximum_fusion, bf16[1,96,6,128]{3,1,2,0:T(8,128)(2,1)S(1)} %copy-done.1, f32[96]{0:T(128)S(1)} %get-tuple-element.140, f32[96]{0:T(128)S(1)} %get-tuple-element.141, f32[96]{0:T(128)S(1)} %get-tuple-element.94, f32[96]{0:T(128)S(1)} %get-tuple-element.95, ...), kind=kLoop, calls=%fused_computation.107 | loop fusion | flops 7372800 | bytes 14764416 | tf_op jit(solution)/shard_map/convert_element_type | solution.py:172
  49.1 1.4 %collective-permute-done.11 = f32[2,168,128]{2,1,0:T(8,128)S(1)} collective-permute-done((f32[2,168,128]{2,1,0:T(8,128)S(1)}, f32[2,168,128]{2,1,0:T(8,128)S(1)}, u32[]{:S(2)}, u32[]{:S(2)}) %collective-permute-start.11) | collective-permute-done | bytes 172064 | tf_op jit(solution)/shard_map/ppermute | solution.py:87
  50.5 0.3 slice.647
  50.8 0.5 fusion.60
  51.3 0.6 %slice.681 = f32[384]{0:T(512)} slice(f32[86016]{0:T(1024)S(1)} %bitcast.267), slice={[45056:45440]} | slice | bytes 3072 | tf_op jit(solution)/shard_map/slice | solution.py:95
  52.0 0.6 %slice_bitcast_fusion.1 = f32[96,7,7]{0,2,1:T(8,128)} fusion(f32[128,7,96]{2,1,0:T(8,128)S(1)} %slice.647), kind=kLoop, calls=%fused_computation.200 | loop fusion | bytes 37632 | tf_op jit(solution)/shard_map/transpose | solution.py:194
  52.6 0.7 %reshape.363 = f32[96,384]{1,0:T(8,128)} reshape(f32[36864]{0:T(1024)S(1)} %slice.680) | data formatting | bytes 294912 | tf_op jit(solution)/shard_map/reshape | solution.py:95
  53.3 0.7 %slice_bitcast_fusion = f32[384,96]{0,1:T(8,128)} fusion(f32[224,384]{1,0:T(8,128)S(1)} %slice.654), kind=kLoop, calls=%fused_computation.178 | loop fusion | bytes 294912 | tf_op jit(solution)/shard_map/transpose | solution.py:195
  (76 shorter events, 1.3 us)
Async XLA Ops:
  0.6 8.6 %copy-start = (bf16[96,384]{1,0:T(8,128)(2,1)S(1)}, bf16[96,384]{1,0:T(8,128)(2,1)}, u32[]{:S(2)}) copy-start(bf16[96,384]{1,0:T(8,128)(2,1)} %param.17) | copy-start | bytes 221188
  0.7 4.4 %collective-permute-start.1 = (bf16[1,96,6,128]{3,1,2,0:T(8,128)(2,1)}, bf16[1,96,6,128]{3,1,2,0:T(8,128)(2,1)S(1)}, u32[]{:S(2)}, u32[]{:S(2)}) collective-permute-start(bf16[1,96,6,128]{3,1,2,0:T(8,128)(2,1)} %param.11), channel_id=1, source_target_pairs={{0,4},{4,0},{8,12},{12,8},{16,20},{20,16},{24,28},{28,24},{1,5},{5... | collective-permute-start | bytes 442376 | tf_op jit(solution)/shard_map/ppermute | solution.py:15
  1.2 3.9 %collective-permute-start = (bf16[1,96,6,128]{3,1,2,0:T(8,128)(2,1)}, bf16[1,96,6,128]{3,1,2,0:T(8,128)(2,1)S(1)}, u32[]{:S(2)}, u32[]{:S(2)}) collective-permute-start(bf16[1,96,6,128]{3,1,2,0:T(8,128)(2,1)} %param.11), channel_id=1, source_target_pairs={{4,8},{12,16},{20,24},{8,4},{16,12},{24,20},{5,9},{13,17},{21,25},... | collective-permute-start | bytes 442376 | tf_op jit(solution)/shard_map/ppermute | solution.py:16
  6.5 0.8 %copy-start.3 = (f32[96,7,7]{0,2,1:T(8,128)S(1)}, f32[96,7,7]{0,2,1:T(8,128)}, u32[]{:S(2)}) copy-start(f32[96,7,7]{0,2,1:T(8,128)} %param.13) | copy-start | bytes 56452
  6.5 0.7 %copy-start.9 = (f32[96]{0:T(128)S(1)}, f32[96]{0:T(128)}, u32[]{:S(2)}) copy-start(f32[96]{0:T(128)} %param.14) | copy-start | bytes 1156
  6.5 0.7 %copy-start.11 = (pred[8,17]{0,1:T(8,128)(4,1)S(1)}, pred[8,17]{0,1:T(8,128)(4,1)}, u32[]{:S(2)}) copy-start(pred[8,17]{0,1:T(8,128)(4,1)} %constant.174) | copy-start | bytes 412
  8.9 0.7 %copy-start.4 = (f32[96]{0:T(128)S(1)}, f32[96]{0:T(128)}, u32[]{:S(2)}) copy-start(f32[96]{0:T(128)} %param.15) | copy-start | bytes 1156
  8.9 0.7 %copy-start.6 = (f32[96]{0:T(128)S(1)}, f32[96]{0:T(128)}, u32[]{:S(2)}) copy-start(f32[96]{0:T(128)} %param.16) | copy-start | bytes 1156
  8.9 0.7 %copy-start.8 = (f32[384]{0:T(512)S(1)}, f32[384]{0:T(512)}, u32[]{:S(2)}) copy-start(f32[384]{0:T(512)} %param.18) | copy-start | bytes 4612
  9.6 2.8 %copy-start.1 = (bf16[1,96,6,128]{3,1,2,0:T(8,128)(2,1)S(1)}, bf16[1,96,6,128]{3,1,2,0:T(8,128)(2,1)}, u32[]{:S(2)}) copy-start(bf16[1,96,6,128]{3,1,2,0:T(8,128)(2,1)} %param.12) | copy-start | bytes 442372
  9.6 2.9 %copy-start.5 = (f32[96]{0:T(128)S(1)}, f32[96]{0:T(128)}, u32[]{:S(2)}) copy-start(f32[96]{0:T(128)} %param.21) | copy-start | bytes 1156
  9.6 2.9 %copy-start.7 = (bf16[384,96]{0,1:T(8,128)(2,1)S(1)}, bf16[384,96]{0,1:T(8,128)(2,1)}, u32[]{:S(2)}) copy-start(bf16[384,96]{0,1:T(8,128)(2,1)} %param.19) | copy-start | bytes 221188
  13.6 1.9 %copy-start.2 = (bf16[1,96,6,128]{3,1,2,0:T(8,128)(2,1)S(1)}, bf16[1,96,6,128]{3,1,2,0:T(8,128)(2,1)}, u32[]{:S(2)}) copy-start(bf16[1,96,6,128]{3,1,2,0:T(8,128)(2,1)} %param.11) | copy-start | bytes 442372
  17.3 0.8 %copy-start.10 = (f32[96]{0:T(128)S(1)}, f32[96]{0:T(128)}, u32[]{:S(2)}) copy-start(f32[96]{0:T(128)} %param.20) | copy-start | bytes 1156
  18.7 5.1 %collective-permute-start.2 = (f32[2,168,128]{2,1,0:T(8,128)S(1)}, f32[2,168,128]{2,1,0:T(8,128)S(1)}, u32[]{:S(2)}, u32[]{:S(2)}) collective-permute-start(f32[2,168,128]{2,1,0:T(8,128)S(1)} %constant_dynamic-slice_fusion.1), channel_id=1, source_target_pairs={{0,4},{4,0},{8,12},{12,8},{16,20},{20,16},{24,28},{28,24},{1,5},{5... | collective-permute-start | bytes 516104 | tf_op jit(solution)/shard_map/ppermute | solution.py:71
  23.8 5.0 %collective-permute-start.3 = (f32[1,168,128]{2,1,0:T(8,128)S(1)}, f32[1,168,128]{2,1,0:T(8,128)S(1)}, u32[]{:S(2)}, u32[]{:S(2)}) collective-permute-start(f32[1,168,128]{2,1,0:T(8,128)S(1)} %constant_dynamic-slice_fusion), channel_id=1, source_target_pairs={{0,8},{4,12},{8,0},{12,4},{16,24},{20,28},{24,16},{28,20},{1,9},{5... | collective-permute-start | bytes 258056 | tf_op jit(solution)/shard_map/ppermute | solution.py:71
  25.8 6.6 %collective-permute-start.8 = (f32[1,96,3,128]{3,1,2,0:T(8,128)S(1)}, f32[1,96,3,128]{3,1,2,0:T(8,128)S(1)}, u32[]{:S(2)}, u32[]{:S(2)}) collective-permute-start(f32[1,96,3,128]{3,1,2,0:T(8,128)S(1)} %get-tuple-element.85), channel_id=1, source_target_pairs={{4,8},{12,16},{20,24},{8,4},{16,12},{24,20},{5,9},{13,17},{21,25},... | collective-permute-start | bytes 442376 | tf_op jit(solution)/shard_map/ppermute | solution.py:30
  26.6 5.8 %collective-permute-start.9 = (f32[1,96,3,128]{3,1,2,0:T(8,128)S(1)}, f32[1,96,3,128]{3,1,2,0:T(8,128)S(1)}, u32[]{:S(2)}, u32[]{:S(2)}) collective-permute-start(f32[1,96,3,128]{3,1,2,0:T(8,128)S(1)} %get-tuple-element.86), channel_id=1, source_target_pairs={{0,4},{4,0},{8,12},{12,8},{16,20},{20,16},{24,28},{28,24},{1,5},{5... | collective-permute-start | bytes 442376 | tf_op jit(solution)/shard_map/ppermute | solution.py:29
  28.8 5.5 %collective-permute-start.6 = (f32[1,168,128]{2,1,0:T(8,128)S(1)}, f32[1,168,128]{2,1,0:T(8,128)S(1)}, u32[]{:S(2)}, u32[]{:S(2)}) collective-permute-start(f32[1,168,128]{2,1,0:T(8,128)S(1)} %dynamic-slice_add_fusion.1), channel_id=1, source_target_pairs={{0,3},{1,2},{2,1},{3,0},{4,7},{5,6},{6,5},{7,4},{8,11},{9,10},{10,... | collective-permute-start | bytes 258056 | tf_op jit(solution)/shard_map/ppermute | solution.py:77
  31.5 4.6 %collective-permute-start.5 = (f32[1,168,128]{2,1,0:T(8,128)S(1)}, f32[1,168,128]{2,1,0:T(8,128)S(1)}, u32[]{:S(2)}, u32[]{:S(2)}) collective-permute-start(f32[1,168,128]{2,1,0:T(8,128)S(1)} %dynamic-slice_add_fusion.1), channel_id=1, source_target_pairs={{0,2},{1,3},{2,0},{3,1},{4,6},{5,7},{6,4},{7,5},{8,10},{9,11},{10,... | collective-permute-start | bytes 258056 | tf_op jit(solution)/shard_map/ppermute | solution.py:77
  32.0 4.5 %collective-permute-start.4 = (f32[1,168,128]{2,1,0:T(8,128)S(1)}, f32[1,168,128]{2,1,0:T(8,128)S(1)}, u32[]{:S(2)}, u32[]{:S(2)}) collective-permute-start(f32[1,168,128]{2,1,0:T(8,128)S(1)} %dynamic-slice_add_fusion.1), channel_id=1, source_target_pairs={{0,1},{1,0},{2,3},{3,2},{4,5},{5,4},{6,7},{7,6},{8,9},{9,8},{10,11... | collective-permute-start | bytes 258056 | tf_op jit(solution)/shard_map/ppermute | solution.py:77
  36.5 7.3 %collective-permute-start.7 = (f32[1,168,128]{2,1,0:T(8,128)S(1)}, f32[1,168,128]{2,1,0:T(8,128)S(1)}, u32[]{:S(2)}, u32[]{:S(2)}) collective-permute-start(f32[1,168,128]{2,1,0:T(8,128)S(1)} %add_add_fusion), channel_id=1, source_target_pairs={{0,16},{4,20},{8,24},{12,28},{16,0},{20,4},{24,8},{28,12},{1,17},{... | collective-permute-start | bytes 258056 | tf_op jit(solution)/shard_map/ppermute | solution.py:77
  43.8 5.2 %collective-permute-start.10 = (f32[1,168,128]{2,1,0:T(8,128)S(1)}, f32[1,168,128]{2,1,0:T(8,128)S(1)}, u32[]{:S(2)}, u32[]{:S(2)}) collective-permute-start(f32[1,168,128]{2,1,0:T(8,128)S(1)} %add.298), channel_id=1, source_target_pairs={{0,8},{4,12},{8,0},{12,4},{16,24},{20,28},{24,16},{28,20},{1,9},{5... | collective-permute-start | bytes 258056 | tf_op jit(solution)/shard_map/ppermute | solution.py:87
  49.0 1.5 %collective-permute-start.11 = (f32[2,168,128]{2,1,0:T(8,128)S(1)}, f32[2,168,128]{2,1,0:T(8,128)S(1)}, u32[]{:S(2)}, u32[]{:S(2)}) collective-permute-start(f32[2,168,128]{2,1,0:T(8,128)S(1)} %pad_maximum_fusion.2), channel_id=1, source_target_pairs={{0,4},{4,0},{8,12},{12,8},{16,20},{20,16},{24,28},{28,24},{1,5},{5... | collective-permute-start | bytes 516104 | tf_op jit(solution)/shard_map/ppermute | solution.py:87

commit v15 on v14

--- a/solution.py
+++ b/solution.py
@@ -6,14 +6,17 @@
 from jax.sharding import PartitionSpec as P
 
 
-def with_halo(array, sides, width, whole=False):
+def with_halo(array, sides, width, whole=False, pair_after=None):
     for axis, dim in sides:
         size, length = (lax.axis_size(axis), array.shape[dim])
         if whole:
             pairs = [(i, i + 1) for i in range(1, size - 1, 2)]
             pairs += [(j, i) for i, j in pairs]
-            from_pair = lax.ppermute(array, axis, [(i, i ^ 1) for i in range(size)])
             from_chip = lax.ppermute(array, axis, pairs)
+            paired = array
+            if pair_after is not None:
+                paired, _ = lax.optimization_barrier((array, pair_after))
+            from_pair = lax.ppermute(paired, axis, [(i, i ^ 1) for i in range(size)])
             even = lax.axis_index(axis) % 2 == 0
             above = jnp.where(even, from_chip, from_pair)
             below = jnp.where(even, from_pair, from_chip)
@@ -121,7 +124,10 @@
     rows = images.shape[2]
     cols = images.shape[3]
     kernel = conv_weight.shape[1]
-    extended = with_halo(images, (("strip", 2),), 3, whole=True)
+    upstream = cotangent.astype(jnp.float32)
+    d_branch = (layer_scale[None, :, None, None] * upstream).astype(jnp.bfloat16)
+    d_branch_sum = jnp.sum(d_branch.astype(jnp.float32), axis=(0, 2, 3))
+    extended = with_halo(images, (("strip", 2),), 3, whole=True, pair_after=d_branch_sum)
     upstream = cotangent.astype(jnp.float32)
     padded = jnp.pad(extended, ((0, 0), (0, 0), (0, 0), (3, 3)))
     conv = lax.conv_general_dilated(
@@ -148,7 +154,6 @@
         jnp.einsum("sfrw,fc->scrw", act, down_weight, preferred_element_type=jnp.float32)
         + down_bias[None, :, None, None]
     )
-    d_branch = (layer_scale[None, :, None, None] * upstream).astype(jnp.bfloat16)
     d_act = jnp.einsum("scrw,fc->sfrw", d_branch, down_weight, preferred_element_type=jnp.float32)
     d_pre = (d_act * gelu_slope(pre)).astype(jnp.bfloat16)
     d_lifted = jnp.einsum("sfrw,cf->scrw", d_pre, up_weight, preferred_element_type=jnp.float32)
@@ -185,7 +190,7 @@
         jnp.einsum("scrw,sfrw->cf", lifted, d_pre, preferred_element_type=jnp.float32),
         jnp.sum(d_pre.astype(jnp.float32), axis=(0, 2, 3)),
         jnp.einsum("scrw,sfrw->cf", d_branch, act, preferred_element_type=jnp.float32),
-        jnp.sum(d_branch.astype(jnp.float32), axis=(0, 2, 3)),
+        d_branch_sum,
         jnp.sum(upstream * branch, axis=(0, 2, 3)),
     )
     g, image_grad = tree_psum(

time: 54.4 us -> 54.4 us (level)
    ppermute x2, starting transfers between devices: 5.98 us -> 1.78 us  [tree_psum(): flat = keep + lax.ppermute(give, axis, xor_pairs(size, bit))]
    ppermute x1, starting transfers between devices: 0.56 us -> 4.47 us  [with_halo(): from_pair = lax.ppermute(paired, axis, [(i, i ^ 1) for i in range(size)])]
where the time goes in v15:
time: 54.4 us; the launch traced here: 54 us
  starting transfers between devices  16.7 us (31%)
  waiting for transfers between devices  11.2 us (21%)
  other arithmetic  10.9 us (20%)
  local copies, waits for them, and re-layouts  7.59 us (14%)
  matrix products  6.49 us (12%)
  between operations  1.21 us (2%)
    ppermute x4, waiting for transfers between devices, tree_psum(): got = [lax.ppermute(flat, axis, xor_pairs(size, mask)) for mask in masks]  8.18 us
    ppermute x4, starting transfers between devices, tree_psum(): got = [lax.ppermute(flat, axis, xor_pairs(size, mask)) for mask in masks]  6.21 us
    convert_element_type x1, other arithmetic, image_grad_of(): return image_grad.astype(jnp.bfloat16)  4.7 us
    ppermute x1, starting transfers between devices, with_halo(): from_pair = lax.ppermute(paired, axis, [(i, i ^ 1) for i in range(size)])  4.47 us
    reduce_sum x4, other arithmetic, on_device(): jnp.sum(d_conv * padded[:, :, a:a + rows, b:b + cols], axis=(0, 2, 3))  3.23 us
    dot_general x1, matrix products, on_device(): jnp.einsum('scrw,cf->sfrw', lifted, up_weight, preferred_element_type=jnp...  2.83 us
    mul x3, local copies, waits for them, and re-layouts, image_grad_of(): conv_weight[:, a, b][None, :, None, None]  1.98 us
    ppermute x1, starting transfers between devices, with_halo(): lax.ppermute(jnp.where(even, last, first), axis, [(i, i ^ 1) for i in ran...  1.87 us
  transfers between devices with their start and end apart: 12, of which 7 were waited for; matrix products, arithmetic and copies ran while one was open for 15% of the time, Pallas kernels for 0%

profile of v15, /device:TPU:0, one launch (start us, length us, event | category | flops | bytes accessed | tf_op | source)
XLA Modules:
  0.0 54.0 jit_solution(18258572555787602243)
XLA Ops:
  0.7 0.8 %collective-permute-start = (bf16[1,96,6,128]{3,1,2,0:T(8,128)(2,1)}, bf16[1,96,6,128]{3,1,2,0:T(8,128)(2,1)S(1)}, u32[]{:S(2)}, u32[]{:S(2)}) collective-permute-start(bf16[1,96,6,128]{3,1,2,0:T(8,128)(2,1)} %param.11), channel_id=1, source_target_pairs={{4,8},{12,16},{20,24},{8,4},{16,12},{24,20},{5,9},{13,17},{21,25},... | collective-permute-start | bytes 442376 | tf_op jit(solution)/shard_map/ppermute | solution.py:15
  1.5 1.1 %convert_reduce_fusion.1 = f32[96]{0:T(128)S(1)} fusion(bf16[1,96,6,128]{3,1,2,0:T(8,128)(2,1)} %param.12, f32[96]{0:T(128)} %param.21), kind=kLoop, calls=%fused_computation.159 | loop fusion | flops 368544 | bytes 148224 | tf_op jit(solution)/shard_map/reduce_sum | solution.py:129
  2.6 4.5 %collective-permute-start.1 = (bf16[1,96,6,128]{3,1,2,0:T(8,128)(2,1)}, bf16[1,96,6,128]{3,1,2,0:T(8,128)(2,1)S(1)}, u32[]{:S(2)}, u32[]{:S(2)}) collective-permute-start(bf16[1,96,6,128]{3,1,2,0:T(8,128)(2,1)} %param.11), channel_id=1, source_target_pairs={{0,4},{4,0},{8,12},{12,8},{16,20},{20,16},{24,28},{28,24},{1,5},{5... | collective-permute-start | bytes 442376 | tf_op jit(solution)/shard_map/ppermute | solution.py:19
  7.1 1.0 %slice_bitcast_fusion.50 = (f32[96]{0:T(128)S(1)}, f32[96]{0:T(128)S(1)}, f32[96]{0:T(128)S(1)}, f32[96]{0:T(128)S(1)}, f32[96]{0:T(128)S(1)}, /*index=5*/f32[96...) fusion(f32[96,7,7]{0,2,1:T(8,128)} %param.13), kind=kLoop, calls=%fused_computation.267 | loop fusion | bytes 14592 | tf_op jit(solution)/shard_map/mul | solution.py:174
  8.0 1.0 %slice_bitcast_fusion.49 = (f32[96]{0:T(128)S(1)}, f32[96]{0:T(128)S(1)}, f32[96]{0:T(128)S(1)}, f32[96]{0:T(128)S(1)}, f32[96]{0:T(128)S(1)}, /*index=5*/f32[96...) fusion(f32[96,7,7]{0,2,1:T(8,128)} %param.13), kind=kLoop, calls=%fused_computation.266 | loop fusion | bytes 14592 | tf_op jit(solution)/shard_map/mul | solution.py:174
  9.1 1.0 %fusion.58 = (bf16[96,12,1,128]{3,0,1,2:T(8,128)(2,1)S(1)}, bf16[1,96,12,128]{3,1,2,0:T(8,128)(2,1)S(1)}) fusion(bf16[1,96,3,128]{3,1,2,0:T(8,128)(2,1)S(1)} %get-tuple-element.92, bf16[1,96,6,128]{3,1,2,0:T(8,128)(2,1)} %param.11, bf16[1,96,3,128]{3,1,2,0:T(8,128)(2,1)S(1)} %get-tuple-element.91), kind=kLoop, calls=%fused_computation.276 | loop fusion | flops 294912 | bytes 884736 | tf_op jit(solution)/shard_map/concatenate | solution.py:25
  10.1 0.2 copy.41
  10.3 0.1 pad.46.clone
  10.5 0.1 reshape.366
  10.8 0.5 copy-done.3
  11.2 1.5 %fusion.20 = f32[6,8,17,96]{3,1,2,0:T(8,128)S(1)} fusion(bf16[96,12,1,7,6]{0,3,4,1,2:T(8,128)(2,1)S(1)} %slice.664, bf16[96,12,1,8,17]{0,3,4,1,2:T(8,128)(2,1)S(1)} %copy.28, f32[96]{0:T(128)S(1)} %copy-done.9, pred[8,17]{0,1:T(8,128)(4,1)S(1)} %copy-done.11, f32[96,1,7,7]{0,3,2,1:T(8,128)S(1)} %bitcast.270), kind=kOutput, calls=%fused_computation.81 | convolution fusion | flops 47490048 | bytes 742792 | tf_op jit(solution)/shard_map/conv_general_dilated | solution.py:133
  12.9 0.2 copy.40
  13.2 0.3 copy-done.4
  13.6 2.8 %fusion.9 = (bf16[384,6,128]{0,2,1:T(8,128)(2,1)S(1)}, f32[384,6,128]{0,2,1:T(8,128)S(1)}) fusion(f32[384]{0:T(512)S(1)} %copy-done.8, bf16[96,384]{1,0:T(8,128)(2,1)S(1)} %copy-done, f32[6,1,128,96]{2,3,0,1:T(8,128)S(1)} %copy.40, f32[96]{0:T(128)S(1)} %copy-done.6, f32[96]{0:T(128)S(1)} %copy-done.4, f32[6,128]{1,0:T(8,128)S(1)} %add_rsqrt_fusion, ...), kind=kOutput, calls=%fused_computation.57 | convolution fusion | flops 76455936 | bytes 2146560 | tf_op jit(solution)/shard_map/scrw,cf->sfrw/dot_general | solution.py:149
  16.5 0.7 %convert_reduce_fusion = (f32[384]{0:T(512)S(1)}, bf16[384,6,128]{0,2,1:T(8,128)(2,1)S(1)}) fusion(f32[384,6,128]{0,2,1:T(8,128)S(1)} %get-tuple-element.148, bf16[384,96]{0,1:T(8,128)(2,1)S(1)} %copy-done.7, bf16[1,96,6,128]{3,1,2,0:T(8,128)(2,1)S(1)} %copy-done.1, f32[96]{0:T(128)S(1)} %copy-done.5), kind=kOutput, calls=%fused_computation.73 | convolution fusion | flops 60382848 | bytes 1992576 | tf_op jit(solution)/shard_map/scrw,fc->sfrw/dot_general | solution.py:157
  17.2 0.4 fusion.32
  17.7 1.2 %multiply_reduce_fusion = (f32[96]{0:T(128)S(1)}, f32[96]{0:T(128)S(1)}, f32[96]{0:T(128)S(1)}, f32[96]{0:T(128)S(1)}, f32[96]{0:T(128)S(1)}, /*index=5*/f32[96]...) fusion(bf16[1,96,12,128]{3,1,2,0:T(8,128)(2,1)S(1)} %get-tuple-, ...), kind=kLoop, calls=%fused_computation.108 | loop fusion | flops 4495680 | bytes 1199232 | tf_op jit(solution)/shard_map/reduce_sum | solution.py:182
  19.0 0.5 multiply_reduce_fusion.42
  19.5 0.3 multiply_reduce_fusion.3
  19.8 1.2 %multiply_reduce_fusion.21 = (f32[96]{0:T(128)S(1)}, f32[96]{0:T(128)S(1)}, f32[96]{0:T(128)S(1)}, f32[96]{0:T(128)S(1)}, f32[96]{0:T(128)S(1)}, /*index=5*/f32[...) fusion(f32[1,96,6,128]{3,1,2,0:T(8,128)S(1)} %get-tuple-element, ...), kind=kLoop, calls=%fused_computation.129 | loop fusion | flops 3979584 | bytes 596736 | tf_op jit(solution)/shard_map/reduce_sum | solution.py:182
  21.0 0.3 fusion.22
  21.3 0.1 stack.199
  21.7 0.3 fusion.23
  22.1 0.4 fusion.21
  22.7 0.1 collective-permute-start.2
  22.8 1.3 %collective-permute-done.2 = f32[2,168,128]{2,1,0:T(8,128)S(1)} collective-permute-done((f32[2,168,128]{2,1,0:T(8,128)S(1)}, f32[2,168,128]{2,1,0:T(8,128)S(1)}, u32[]{:S(2)}, u32[]{:S(2)}) %collective-permute-start.2) | collective-permute-done | bytes 172064 | tf_op jit(solution)/shard_map/ppermute | solution.py:74
  24.2 1.6 %collective-permute-start.3 = (f32[1,168,128]{2,1,0:T(8,128)S(1)}, f32[1,168,128]{2,1,0:T(8,128)S(1)}, u32[]{:S(2)}, u32[]{:S(2)}) collective-permute-start(f32[1,168,128]{2,1,0:T(8,128)S(1)} %constant_dynamic-slice_fusion), channel_id=1, source_target_pairs={{0,8},{4,12},{8,0},{12,4},{16,24},{20,28},{24,16},{28,20},{1,9},{5... | collective-permute-start | bytes 258056 | tf_op jit(solution)/shard_map/ppermute | solution.py:74
  25.8 0.9 %collective-permute-start.8 = (f32[1,96,3,128]{3,1,2,0:T(8,128)S(1)}, f32[1,96,3,128]{3,1,2,0:T(8,128)S(1)}, u32[]{:S(2)}, u32[]{:S(2)}) collective-permute-start(f32[1,96,3,128]{3,1,2,0:T(8,128)S(1)} %get-tuple-element.87), channel_id=1, source_target_pairs={{4,8},{12,16},{20,24},{8,4},{16,12},{24,20},{5,9},{13,17},{21,25},... | collective-permute-start | bytes 442376 | tf_op jit(solution)/shard_map/ppermute | solution.py:33
  26.7 1.9 %collective-permute-start.9 = (f32[1,96,3,128]{3,1,2,0:T(8,128)S(1)}, f32[1,96,3,128]{3,1,2,0:T(8,128)S(1)}, u32[]{:S(2)}, u32[]{:S(2)}) collective-permute-start(f32[1,96,3,128]{3,1,2,0:T(8,128)S(1)} %get-tuple-element.88), channel_id=1, source_target_pairs={{0,4},{4,0},{8,12},{12,8},{16,20},{20,16},{24,28},{28,24},{1,5},{5... | collective-permute-start | bytes 442376 | tf_op jit(solution)/shard_map/ppermute | solution.py:32
  28.6 0.2 collective-permute-done.3
  28.8 2.5 %collective-permute-start.6 = (f32[1,168,128]{2,1,0:T(8,128)S(1)}, f32[1,168,128]{2,1,0:T(8,128)S(1)}, u32[]{:S(2)}, u32[]{:S(2)}) collective-permute-start(f32[1,168,128]{2,1,0:T(8,128)S(1)} %dynamic-slice_add_fusion.1), channel_id=1, source_target_pairs={{0,3},{1,2},{2,1},{3,0},{4,7},{5,6},{6,5},{7,4},{8,11},{9,10},{10,... | collective-permute-start | bytes 258056 | tf_op jit(solution)/shard_map/ppermute | solution.py:80
  31.3 0.5 collective-permute-start.5
  31.9 0.5 collective-permute-start.4
  32.4 1.9 %collective-permute-done.6 = f32[1,168,128]{2,1,0:T(8,128)S(1)} collective-permute-done((f32[1,168,128]{2,1,0:T(8,128)S(1)}, f32[1,168,128]{2,1,0:T(8,128)S(1)}, u32[]{:S(2)}, u32[]{:S(2)}) %collective-permute-start.6) | collective-permute-done | bytes 86048 | tf_op jit(solution)/shard_map/ppermute | solution.py:80
  34.4 1.8 %collective-permute-done.5 = f32[1,168,128]{2,1,0:T(8,128)S(1)} collective-permute-done((f32[1,168,128]{2,1,0:T(8,128)S(1)}, f32[1,168,128]{2,1,0:T(8,128)S(1)}, u32[]{:S(2)}, u32[]{:S(2)}) %collective-permute-start.5) | collective-permute-done | bytes 86048 | tf_op jit(solution)/shard_map/ppermute | solution.py:80
  36.1 0.2 collective-permute-done.4
  36.4 2.7 %collective-permute-start.7 = (f32[1,168,128]{2,1,0:T(8,128)S(1)}, f32[1,168,128]{2,1,0:T(8,128)S(1)}, u32[]{:S(2)}, u32[]{:S(2)}) collective-permute-start(f32[1,168,128]{2,1,0:T(8,128)S(1)} %add_add_fusion), channel_id=1, source_target_pairs={{0,16},{4,20},{8,24},{12,28},{16,0},{20,4},{24,8},{28,12},{1,17},{... | collective-permute-start | bytes 258056 | tf_op jit(solution)/shard_map/ppermute | solution.py:80
  39.0 0.4 select_maximum_fusion
  39.4 4.3 %collective-permute-done.7 = f32[1,168,128]{2,1,0:T(8,128)S(1)} collective-permute-done((f32[1,168,128]{2,1,0:T(8,128)S(1)}, f32[1,168,128]{2,1,0:T(8,128)S(1)}, u32[]{:S(2)}, u32[]{:S(2)}) %collective-permute-start.7) | collective-permute-done | bytes 86048 | tf_op jit(solution)/shard_map/ppermute | solution.py:80
  43.7 0.6 %collective-permute-start.10 = (f32[1,168,128]{2,1,0:T(8,128)S(1)}, f32[1,168,128]{2,1,0:T(8,128)S(1)}, u32[]{:S(2)}, u32[]{:S(2)}) collective-permute-start(f32[1,168,128]{2,1,0:T(8,128)S(1)} %add.298), channel_id=1, source_target_pairs={{0,8},{4,12},{8,0},{12,4},{16,24},{20,28},{24,16},{28,20},{1,9},{5... | collective-permute-start | bytes 258056 | tf_op jit(solution)/shard_map/ppermute | solution.py:90
  44.3 4.7 %add_convert_fusion = bf16[1,96,6,128]{3,1,2,0:T(8,128)(2,1)} fusion(f32[1,96,12,134]{3,1,2,0:T(8,128)S(1)} %select_maximum_fusion, bf16[1,96,6,128]{3,1,2,0:T(8,128)(2,1)S(1)} %copy-done.1, f32[96]{0:T(128)S(1)} %get-tuple-element.142, f32[96]{0:T(128)S(1)} %get-tuple-element.143, f32[96]{0:T(128)S(1)} %get-tuple-element.96, f32[96]{0:T(128)S(1)} %get-tuple-element.97, ...), kind=kLoop, calls=%fused_computation.107 | loop fusion | flops 7372800 | bytes 14764416 | tf_op jit(solution)/shard_map/convert_element_type | solution.py:177
  49.1 1.4 %collective-permute-done.11 = f32[2,168,128]{2,1,0:T(8,128)S(1)} collective-permute-done((f32[2,168,128]{2,1,0:T(8,128)S(1)}, f32[2,168,128]{2,1,0:T(8,128)S(1)}, u32[]{:S(2)}, u32[]{:S(2)}) %collective-permute-start.11) | collective-permute-done | bytes 172064 | tf_op jit(solution)/shard_map/ppermute | solution.py:90
  50.6 0.3 slice.647
  50.8 0.5 fusion.60
  51.4 0.6 %slice.681 = f32[384]{0:T(512)} slice(f32[86016]{0:T(1024)S(1)} %bitcast.267), slice={[45056:45440]} | slice | bytes 3072 | tf_op jit(solution)/shard_map/slice | solution.py:98
  52.1 0.6 %slice_bitcast_fusion.1 = f32[96,7,7]{0,2,1:T(8,128)} fusion(f32[128,7,96]{2,1,0:T(8,128)S(1)} %slice.647), kind=kLoop, calls=%fused_computation.200 | loop fusion | bytes 37632 | tf_op jit(solution)/shard_map/transpose | solution.py:199
  52.7 0.7 %reshape.363 = f32[96,384]{1,0:T(8,128)} reshape(f32[36864]{0:T(1024)S(1)} %slice.680) | data formatting | bytes 294912 | tf_op jit(solution)/shard_map/reshape | solution.py:98
  53.4 0.7 %slice_bitcast_fusion = f32[384,96]{0,1:T(8,128)} fusion(f32[224,384]{1,0:T(8,128)S(1)} %slice.654), kind=kLoop, calls=%fused_computation.178 | loop fusion | bytes 294912 | tf_op jit(solution)/shard_map/transpose | solution.py:200
  (76 shorter events, 1.3 us)
Async XLA Ops:
  0.6 12.6 %copy-start = (bf16[96,384]{1,0:T(8,128)(2,1)S(1)}, bf16[96,384]{1,0:T(8,128)(2,1)}, u32[]{:S(2)}) copy-start(bf16[96,384]{1,0:T(8,128)(2,1)} %param.17) | copy-start | bytes 221188
  0.7 8.4 %collective-permute-start = (bf16[1,96,6,128]{3,1,2,0:T(8,128)(2,1)}, bf16[1,96,6,128]{3,1,2,0:T(8,128)(2,1)S(1)}, u32[]{:S(2)}, u32[]{:S(2)}) collective-permute-start(bf16[1,96,6,128]{3,1,2,0:T(8,128)(2,1)} %param.11), channel_id=1, source_target_pairs={{4,8},{12,16},{20,24},{8,4},{16,12},{24,20},{5,9},{13,17},{21,25},... | collective-permute-start | bytes 442376 | tf_op jit(solution)/shard_map/ppermute | solution.py:15
  2.6 6.5 %collective-permute-start.1 = (bf16[1,96,6,128]{3,1,2,0:T(8,128)(2,1)}, bf16[1,96,6,128]{3,1,2,0:T(8,128)(2,1)S(1)}, u32[]{:S(2)}, u32[]{:S(2)}) collective-permute-start(bf16[1,96,6,128]{3,1,2,0:T(8,128)(2,1)} %param.11), channel_id=1, source_target_pairs={{0,4},{4,0},{8,12},{12,8},{16,20},{20,16},{24,28},{28,24},{1,5},{5... | collective-permute-start | bytes 442376 | tf_op jit(solution)/shard_map/ppermute | solution.py:19
  10.5 0.8 %copy-start.3 = (f32[96,7,7]{0,2,1:T(8,128)S(1)}, f32[96,7,7]{0,2,1:T(8,128)}, u32[]{:S(2)}) copy-start(f32[96,7,7]{0,2,1:T(8,128)} %param.13) | copy-start | bytes 56452
  10.5 0.7 %copy-start.9 = (f32[96]{0:T(128)S(1)}, f32[96]{0:T(128)}, u32[]{:S(2)}) copy-start(f32[96]{0:T(128)} %param.14) | copy-start | bytes 1156
  10.5 0.7 %copy-start.11 = (pred[8,17]{0,1:T(8,128)(4,1)S(1)}, pred[8,17]{0,1:T(8,128)(4,1)}, u32[]{:S(2)}) copy-start(pred[8,17]{0,1:T(8,128)(4,1)} %constant.174) | copy-start | bytes 412
  12.9 0.7 %copy-start.4 = (f32[96]{0:T(128)S(1)}, f32[96]{0:T(128)}, u32[]{:S(2)}) copy-start(f32[96]{0:T(128)} %param.15) | copy-start | bytes 1156
  12.9 0.7 %copy-start.6 = (f32[96]{0:T(128)S(1)}, f32[96]{0:T(128)}, u32[]{:S(2)}) copy-start(f32[96]{0:T(128)} %param.16) | copy-start | bytes 1156
  12.9 0.7 %copy-start.8 = (f32[384]{0:T(512)S(1)}, f32[384]{0:T(512)}, u32[]{:S(2)}) copy-start(f32[384]{0:T(512)} %param.18) | copy-start | bytes 4612
  13.6 2.8 %copy-start.1 = (bf16[1,96,6,128]{3,1,2,0:T(8,128)(2,1)S(1)}, bf16[1,96,6,128]{3,1,2,0:T(8,128)(2,1)}, u32[]{:S(2)}) copy-start(bf16[1,96,6,128]{3,1,2,0:T(8,128)(2,1)} %param.12) | copy-start | bytes 442372
  13.6 2.9 %copy-start.5 = (f32[96]{0:T(128)S(1)}, f32[96]{0:T(128)}, u32[]{:S(2)}) copy-start(f32[96]{0:T(128)} %param.21) | copy-start | bytes 1156
  13.6 2.9 %copy-start.7 = (bf16[384,96]{0,1:T(8,128)(2,1)S(1)}, bf16[384,96]{0,1:T(8,128)(2,1)}, u32[]{:S(2)}) copy-start(bf16[384,96]{0,1:T(8,128)(2,1)} %param.19) | copy-start | bytes 221188
  17.6 1.9 %copy-start.2 = (bf16[1,96,6,128]{3,1,2,0:T(8,128)(2,1)S(1)}, bf16[1,96,6,128]{3,1,2,0:T(8,128)(2,1)}, u32[]{:S(2)}) copy-start(bf16[1,96,6,128]{3,1,2,0:T(8,128)(2,1)} %param.11) | copy-start | bytes 442372
  21.3 0.8 %copy-start.10 = (f32[96]{0:T(128)S(1)}, f32[96]{0:T(128)}, u32[]{:S(2)}) copy-start(f32[96]{0:T(128)} %param.20) | copy-start | bytes 1156
  22.7 1.5 %collective-permute-start.2 = (f32[2,168,128]{2,1,0:T(8,128)S(1)}, f32[2,168,128]{2,1,0:T(8,128)S(1)}, u32[]{:S(2)}, u32[]{:S(2)}) collective-permute-start(f32[2,168,128]{2,1,0:T(8,128)S(1)} %constant_dynamic-slice_fusion.1), channel_id=1, source_target_pairs={{0,4},{4,0},{8,12},{12,8},{16,20},{20,16},{24,28},{28,24},{1,5},{5... | collective-permute-start | bytes 516104 | tf_op jit(solution)/shard_map/ppermute | solution.py:74
  24.2 4.6 %collective-permute-start.3 = (f32[1,168,128]{2,1,0:T(8,128)S(1)}, f32[1,168,128]{2,1,0:T(8,128)S(1)}, u32[]{:S(2)}, u32[]{:S(2)}) collective-permute-start(f32[1,168,128]{2,1,0:T(8,128)S(1)} %constant_dynamic-slice_fusion), channel_id=1, source_target_pairs={{0,8},{4,12},{8,0},{12,4},{16,24},{20,28},{24,16},{28,20},{1,9},{5... | collective-permute-start | bytes 258056 | tf_op jit(solution)/shard_map/ppermute | solution.py:74
  25.8 6.5 %collective-permute-start.8 = (f32[1,96,3,128]{3,1,2,0:T(8,128)S(1)}, f32[1,96,3,128]{3,1,2,0:T(8,128)S(1)}, u32[]{:S(2)}, u32[]{:S(2)}) collective-permute-start(f32[1,96,3,128]{3,1,2,0:T(8,128)S(1)} %get-tuple-element.87), channel_id=1, source_target_pairs={{4,8},{12,16},{20,24},{8,4},{16,12},{24,20},{5,9},{13,17},{21,25},... | collective-permute-start | bytes 442376 | tf_op jit(solution)/shard_map/ppermute | solution.py:33
  26.7 5.7 %collective-permute-start.9 = (f32[1,96,3,128]{3,1,2,0:T(8,128)S(1)}, f32[1,96,3,128]{3,1,2,0:T(8,128)S(1)}, u32[]{:S(2)}, u32[]{:S(2)}) collective-permute-start(f32[1,96,3,128]{3,1,2,0:T(8,128)S(1)} %get-tuple-element.88), channel_id=1, source_target_pairs={{0,4},{4,0},{8,12},{12,8},{16,20},{20,16},{24,28},{28,24},{1,5},{5... | collective-permute-start | bytes 442376 | tf_op jit(solution)/shard_map/ppermute | solution.py:32
  28.8 5.5 %collective-permute-start.6 = (f32[1,168,128]{2,1,0:T(8,128)S(1)}, f32[1,168,128]{2,1,0:T(8,128)S(1)}, u32[]{:S(2)}, u32[]{:S(2)}) collective-permute-start(f32[1,168,128]{2,1,0:T(8,128)S(1)} %dynamic-slice_add_fusion.1), channel_id=1, source_target_pairs={{0,3},{1,2},{2,1},{3,0},{4,7},{5,6},{6,5},{7,4},{8,11},{9,10},{10,... | collective-permute-start | bytes 258056 | tf_op jit(solution)/shard_map/ppermute | solution.py:80
  31.3 4.8 %collective-permute-start.5 = (f32[1,168,128]{2,1,0:T(8,128)S(1)}, f32[1,168,128]{2,1,0:T(8,128)S(1)}, u32[]{:S(2)}, u32[]{:S(2)}) collective-permute-start(f32[1,168,128]{2,1,0:T(8,128)S(1)} %dynamic-slice_add_fusion.1), channel_id=1, source_target_pairs={{0,2},{1,3},{2,0},{3,1},{4,6},{5,7},{6,4},{7,5},{8,10},{9,11},{10,... | collective-permute-start | bytes 258056 | tf_op jit(solution)/shard_map/ppermute | solution.py:80
  31.9 4.5 %collective-permute-start.4 = (f32[1,168,128]{2,1,0:T(8,128)S(1)}, f32[1,168,128]{2,1,0:T(8,128)S(1)}, u32[]{:S(2)}, u32[]{:S(2)}) collective-permute-start(f32[1,168,128]{2,1,0:T(8,128)S(1)} %dynamic-slice_add_fusion.1), channel_id=1, source_target_pairs={{0,1},{1,0},{2,3},{3,2},{4,5},{5,4},{6,7},{7,6},{8,9},{9,8},{10,11... | collective-permute-start | bytes 258056 | tf_op jit(solution)/shard_map/ppermute | solution.py:80
  36.4 7.3 %collective-permute-start.7 = (f32[1,168,128]{2,1,0:T(8,128)S(1)}, f32[1,168,128]{2,1,0:T(8,128)S(1)}, u32[]{:S(2)}, u32[]{:S(2)}) collective-permute-start(f32[1,168,128]{2,1,0:T(8,128)S(1)} %add_add_fusion), channel_id=1, source_target_pairs={{0,16},{4,20},{8,24},{12,28},{16,0},{20,4},{24,8},{28,12},{1,17},{... | collective-permute-start | bytes 258056 | tf_op jit(solution)/shard_map/ppermute | solution.py:80
  43.7 5.3 %collective-permute-start.10 = (f32[1,168,128]{2,1,0:T(8,128)S(1)}, f32[1,168,128]{2,1,0:T(8,128)S(1)}, u32[]{:S(2)}, u32[]{:S(2)}) collective-permute-start(f32[1,168,128]{2,1,0:T(8,128)S(1)} %add.298), channel_id=1, source_target_pairs={{0,8},{4,12},{8,0},{12,4},{16,24},{20,28},{24,16},{28,20},{1,9},{5... | collective-permute-start | bytes 258056 | tf_op jit(solution)/shard_map/ppermute | solution.py:90
  49.0 1.5 %collective-permute-start.11 = (f32[2,168,128]{2,1,0:T(8,128)S(1)}, f32[2,168,128]{2,1,0:T(8,128)S(1)}, u32[]{:S(2)}, u32[]{:S(2)}) collective-permute-start(f32[2,168,128]{2,1,0:T(8,128)S(1)} %pad_maximum_fusion.2), channel_id=1, source_target_pairs={{0,4},{4,0},{8,12},{12,8},{16,20},{20,16},{24,28},{28,24},{1,5},{5... | collective-permute-start | bytes 516104 | tf_op jit(solution)/shard_map/ppermute | solution.py:90

commit v16 on v14

--- a/solution.py
+++ b/solution.py
@@ -159,16 +159,17 @@
         - normed * jnp.mean(d_normed * normed, axis=1, keepdims=True)
     )
     d_wide = with_halo(d_conv, (("strip", 2),), 3)
-    d_padded = jnp.pad(d_wide, ((0, 0), (0, 0), (0, 0), (3, 3)))
-    def image_grad_of(d_padded, cotangent):
-        image_grad = cotangent.astype(jnp.float32)
-        for a in range(kernel):
-            for b in range(kernel):
-                image_grad = (
-                    image_grad
-                    + conv_weight[:, a, b][None, :, None, None]
-                    * d_padded[:, :, 6 - a : 6 - a + rows, 6 - b : 6 - b + cols]
-                )
+    def image_grad_of(d_wide, cotangent):
+        spread = lax.conv_general_dilated(
+            d_wide,
+            conv_weight[:, ::-1, ::-1][:, None],
+            window_strides=(1, 1),
+            padding=((0, 0), (3, 3)),
+            dimension_numbers=("NCHW", "OIHW", "NCHW"),
+            feature_group_count=chans,
+            precision=lax.Precision.HIGHEST,
+        )
+        image_grad = cotangent.astype(jnp.float32) + spread
         return image_grad.astype(jnp.bfloat16)
 
     taps = []
@@ -189,7 +190,7 @@
         jnp.sum(upstream * branch, axis=(0, 2, 3)),
     )
     g, image_grad = tree_psum(
-        [item * scale for item in terms], image_grad_of, (d_padded, cotangent)
+        [item * scale for item in terms], image_grad_of, (d_wide, cotangent)
     )
     g[0] = g[0].reshape(kernel, kernel, chans).transpose(2, 0, 1)
     g[6] = g[6].T

time: 54.4 us -> 53.6 us (0.985)
  other arithmetic: 10.9 us -> 5.94 us
  starting transfers between devices: 16.3 us -> 18.3 us
  matrix products: 6.49 us -> 7.93 us
  waiting for transfers between devices: 11.4 us -> 12.1 us
    convert_element_type x1, other arithmetic: 4.7 us -> 0.06 us  [image_grad_of(): return image_grad.astype(jnp.bfloat16)]
    ppermute x2, starting transfers between devices: 5.98 us -> 8.02 us  [tree_psum(): flat = keep + lax.ppermute(give, axis, xor_pairs(size, bit))]
    mul x3 -> x0, local copies, waits for them, and re-layouts: 1.99 us -> none  [image_grad_of(): conv_weight[:, a, b][None, :, None, None]]
    conv_general_dilated x0 -> x1, matrix products: none -> 1.43 us  [image_grad_of(): lax.conv_general_dilated(d_wide, conv_weight[:, ::-1, ::-1][:, None], win...]
    unnamed x34 -> x36, local copies, waits for them, and re-layouts: 1.32 us -> 2.61 us
    optimization_barrier x0 -> x2, local copies, waits for them, and re-layouts: none -> 0.73 us  [tree_psum(): flat, side_in = lax.optimization_barrier((flat, side_in))]
  transfers between devices with their start and end apart: 12 -> 12, of which waited for: 7 -> 8; matrix products, arithmetic and copies ran while one was open for 15% -> 9% of each run, Pallas kernels for 0% -> 0%
where the time goes in v16:
time: 53.6 us; the launch traced here: 53.4 us
  starting transfers between devices  18.3 us (34%)
  waiting for transfers between devices  12.1 us (23%)
  matrix products  7.93 us (15%)
  local copies, waits for them, and re-layouts  7.86 us (15%)
  other arithmetic  5.94 us (11%)
  between operations  1.27 us (2%)
    ppermute x4, waiting for transfers between devices, tree_psum(): got = [lax.ppermute(flat, axis, xor_pairs(size, mask)) for mask in masks]  8.63 us
    ppermute x2, starting transfers between devices, tree_psum(): flat = keep + lax.ppermute(give, axis, xor_pairs(size, bit))  8.02 us
    ppermute x4, starting transfers between devices, tree_psum(): got = [lax.ppermute(flat, axis, xor_pairs(size, mask)) for mask in masks]  6.21 us
    reduce_sum x4, other arithmetic, on_device(): jnp.sum(d_conv * padded[:, :, a:a + rows, b:b + cols], axis=(0, 2, 3))  3.23 us
    dot_general x1, matrix products, on_device(): jnp.einsum('scrw,cf->sfrw', lifted, up_weight, preferred_element_type=jnp...  2.83 us
    unnamed x36, local copies, waits for them, and re-layouts  2.61 us
    ppermute x2, waiting for transfers between devices, tree_psum(): flat = keep + lax.ppermute(give, axis, xor_pairs(size, bit))  1.75 us
    ppermute x2, waiting for transfers between devices, tree_psum(): got = lax.ppermute(flat, axis, xor_pairs(size, bit))  1.67 us
  transfers between devices with their start and end apart: 12, of which 8 were waited for; matrix products, arithmetic and copies ran while one was open for 9% of the time, Pallas kernels for 0%

profile of v16, /device:TPU:0, one launch (start us, length us, event | category | flops | bytes accessed | tf_op | source)
XLA Modules:
  0.0 53.4 jit_solution(1286861599272514338)
XLA Ops:
  0.7 0.6 %collective-permute-start.1 = (bf16[1,96,6,128]{3,1,2,0:T(8,128)(2,1)}, bf16[1,96,6,128]{3,1,2,0:T(8,128)(2,1)S(1)}, u32[]{:S(2)}, u32[]{:S(2)}) collective-permute-start(bf16[1,96,6,128]{3,1,2,0:T(8,128)(2,1)} %param.11), channel_id=1, source_target_pairs={{0,4},{4,0},{8,12},{12,8},{16,20},{20,16},{24,28},{28,24},{1,5},{5... | collective-permute-start | bytes 442376 | tf_op jit(solution)/shard_map/ppermute | solution.py:15
  1.2 0.7 %collective-permute-start = (bf16[1,96,6,128]{3,1,2,0:T(8,128)(2,1)}, bf16[1,96,6,128]{3,1,2,0:T(8,128)(2,1)S(1)}, u32[]{:S(2)}, u32[]{:S(2)}) collective-permute-start(bf16[1,96,6,128]{3,1,2,0:T(8,128)(2,1)} %param.11), channel_id=1, source_target_pairs={{4,8},{12,16},{20,24},{8,4},{16,12},{24,20},{5,9},{13,17},{21,25},... | collective-permute-start | bytes 442376 | tf_op jit(solution)/shard_map/ppermute | solution.py:16
  1.9 1.1 %convert_reduce_fusion.1 = f32[96]{0:T(128)S(1)} fusion(bf16[1,96,6,128]{3,1,2,0:T(8,128)(2,1)} %param.12, f32[96]{0:T(128)} %param.21), kind=kLoop, calls=%fused_computation.113 | loop fusion | flops 368544 | bytes 148224 | tf_op jit(solution)/shard_map/reduce_sum | solution.py:189
  3.1 1.0 %fusion.69 = (bf16[96,12,1,128]{3,0,1,2:T(8,128)(2,1)S(1)}, bf16[1,96,12,128]{3,1,2,0:T(8,128)(2,1)S(1)}) fusion(bf16[1,96,3,128]{3,1,2,0:T(8,128)(2,1)S(1)} %get-tuple-element.100, bf16[1,96,6,128]{3,1,2,0:T(8,128)(2,1)} %param.11, bf16[1,96,3,128]{3,1,2,0:T(8,128)(2,1)S(1)} %get-tuple-element.99), kind=kLoop, calls=%fused_computation.236 | loop fusion | flops 294912 | bytes 884736 | tf_op jit(solution)/shard_map/concatenate | solution.py:22
  4.0 0.2 copy.51
  4.7 0.5 copy-done.3
  5.2 1.5 %fusion.19 = f32[6,8,17,96]{3,1,2,0:T(8,128)S(1)} fusion(bf16[96,12,1,7,6]{0,3,4,1,2:T(8,128)(2,1)S(1)} %slice.274, bf16[96,12,1,8,17]{0,3,4,1,2:T(8,128)(2,1)S(1)} %copy.31, f32[96]{0:T(128)S(1)} %copy-done.9, pred[8,17]{0,1:T(8,128)(4,1)S(1)} %copy-done.11, f32[96,1,7,7]{0,3,2,1:T(8,128)S(1)} %bitcast.186), kind=kOutput, calls=%fused_computation.76 | convolution fusion | flops 47490048 | bytes 742792 | tf_op jit(solution)/shard_map/conv_general_dilated | solution.py:127
  6.9 0.2 copy.50
  7.2 0.3 copy-done.4
  7.6 2.8 %fusion.9 = (bf16[384,6,128]{0,2,1:T(8,128)(2,1)S(1)}, f32[384,6,128]{0,2,1:T(8,128)S(1)}) fusion(f32[384]{0:T(512)S(1)} %copy-done.8, bf16[96,384]{1,0:T(8,128)(2,1)S(1)} %copy-done, f32[6,1,128,96]{2,3,0,1:T(8,128)S(1)} %copy.50, f32[96]{0:T(128)S(1)} %copy-done.6, f32[96]{0:T(128)S(1)} %copy-done.4, f32[6,128]{1,0:T(8,128)S(1)} %add_rsqrt_fusion, ...), kind=kOutput, calls=%fused_computation.55 | convolution fusion | flops 76455936 | bytes 2146560 | tf_op jit(solution)/shard_map/scrw,cf->sfrw/dot_general | solution.py:143
  10.4 0.7 %convert_reduce_fusion = (f32[384]{0:T(512)S(1)}, bf16[384,6,128]{0,2,1:T(8,128)(2,1)S(1)}) fusion(f32[384,6,128]{0,2,1:T(8,128)S(1)} %get-tuple-element.107, bf16[384,96]{0,1:T(8,128)(2,1)S(1)} %copy-done.7, bf16[1,96,6,128]{3,1,2,0:T(8,128)(2,1)S(1)} %copy-done.1, f32[96]{0:T(128)S(1)} %copy-done.5), kind=kOutput, calls=%fused_computation.69 | convolution fusion | flops 60382848 | bytes 1992576 | tf_op jit(solution)/shard_map/scrw,fc->sfrw/dot_general | solution.py:152
  11.2 0.4 fusion.39
  11.7 1.2 %multiply_reduce_fusion = (f32[96]{0:T(128)S(1)}, f32[96]{0:T(128)S(1)}, f32[96]{0:T(128)S(1)}, f32[96]{0:T(128)S(1)}, f32[96]{0:T(128)S(1)}, /*index=5*/f32[96]...) fusion(bf16[1,96,12,128]{3,1,2,0:T(8,128)(2,1)S(1)} %get-tuple-, ...), kind=kLoop, calls=%fused_computation.114 | loop fusion | flops 4495680 | bytes 1199232 | tf_op jit(solution)/shard_map/reduce_sum | solution.py:178
  12.9 0.5 multiply_reduce_fusion.42
  13.5 0.3 multiply_reduce_fusion.3
  13.7 1.2 %multiply_reduce_fusion.21 = (f32[96]{0:T(128)S(1)}, f32[96]{0:T(128)S(1)}, f32[96]{0:T(128)S(1)}, f32[96]{0:T(128)S(1)}, f32[96]{0:T(128)S(1)}, /*index=5*/f32[...) fusion(f32[1,96,6,128]{3,1,2,0:T(8,128)S(1)} %get-tuple-element, ...), kind=kLoop, calls=%fused_computation.135 | loop fusion | flops 3979584 | bytes 596736 | tf_op jit(solution)/shard_map/reduce_sum | solution.py:178
  14.9 0.3 fusion.21
  15.3 0.1 stack.199
  15.7 0.3 fusion.22
  16.0 0.4 fusion.20
  16.6 5.9 %collective-permute-start.2 = (f32[2,168,128]{2,1,0:T(8,128)S(1)}, f32[2,168,128]{2,1,0:T(8,128)S(1)}, u32[]{:S(2)}, u32[]{:S(2)}) collective-permute-start(f32[2,168,128]{2,1,0:T(8,128)S(1)} %constant_dynamic-slice_fusion.1), channel_id=1, source_target_pairs={{0,4},{4,0},{8,12},{12,8},{16,20},{20,16},{24,28},{28,24},{1,5},{5... | collective-permute-start | bytes 516104 | tf_op jit(solution)/shard_map/ppermute | solution.py:71
  22.5 1.0 %collective-permute-done.2 = f32[2,168,128]{2,1,0:T(8,128)S(1)} collective-permute-done((f32[2,168,128]{2,1,0:T(8,128)S(1)}, f32[2,168,128]{2,1,0:T(8,128)S(1)}, u32[]{:S(2)}, u32[]{:S(2)}) %collective-permute-start.2) | collective-permute-done | bytes 172064 | tf_op jit(solution)/shard_map/ppermute | solution.py:71
  23.6 2.2 %collective-permute-start.3 = (f32[1,168,128]{2,1,0:T(8,128)S(1)}, f32[1,168,128]{2,1,0:T(8,128)S(1)}, u32[]{:S(2)}, u32[]{:S(2)}) collective-permute-start(f32[1,168,128]{2,1,0:T(8,128)S(1)} %constant_dynamic-slice_fusion), channel_id=1, source_target_pairs={{0,8},{4,12},{8,0},{12,4},{16,24},{20,28},{24,16},{28,20},{1,9},{5... | collective-permute-start | bytes 258056 | tf_op jit(solution)/shard_map/ppermute | solution.py:71
  25.8 0.9 %collective-permute-start.8 = (f32[1,96,3,128]{3,1,2,0:T(8,128)S(1)}, f32[1,96,3,128]{3,1,2,0:T(8,128)S(1)}, u32[]{:S(2)}, u32[]{:S(2)}) collective-permute-start(f32[1,96,3,128]{3,1,2,0:T(8,128)S(1)} %get-tuple-element.95), channel_id=1, source_target_pairs={{4,8},{12,16},{20,24},{8,4},{16,12},{24,20},{5,9},{13,17},{21,25},... | collective-permute-start | bytes 442376 | tf_op jit(solution)/shard_map/ppermute | solution.py:30
  26.6 1.4 %collective-permute-start.9 = (f32[1,96,3,128]{3,1,2,0:T(8,128)S(1)}, f32[1,96,3,128]{3,1,2,0:T(8,128)S(1)}, u32[]{:S(2)}, u32[]{:S(2)}) collective-permute-start(f32[1,96,3,128]{3,1,2,0:T(8,128)S(1)} %get-tuple-element.96), channel_id=1, source_target_pairs={{0,4},{4,0},{8,12},{12,8},{16,20},{20,16},{24,28},{28,24},{1,5},{5... | collective-permute-start | bytes 442376 | tf_op jit(solution)/shard_map/ppermute | solution.py:29
  28.1 0.7 %collective-permute-done.3 = f32[1,168,128]{2,1,0:T(8,128)S(1)} collective-permute-done((f32[1,168,128]{2,1,0:T(8,128)S(1)}, f32[1,168,128]{2,1,0:T(8,128)S(1)}, u32[]{:S(2)}, u32[]{:S(2)}) %collective-permute-start.3) | collective-permute-done | bytes 86048 | tf_op jit(solution)/shard_map/ppermute | solution.py:71
  28.8 2.7 %collective-permute-start.6 = (f32[1,168,128]{2,1,0:T(8,128)S(1)}, f32[1,168,128]{2,1,0:T(8,128)S(1)}, u32[]{:S(2)}, u32[]{:S(2)}) collective-permute-start(f32[1,168,128]{2,1,0:T(8,128)S(1)} %dynamic-slice_add_fusion.1), channel_id=1, source_target_pairs={{0,3},{1,2},{2,1},{3,0},{4,7},{5,6},{6,5},{7,4},{8,11},{9,10},{10,... | collective-permute-start | bytes 258056 | tf_op jit(solution)/shard_map/ppermute | solution.py:77
  31.5 0.5 collective-permute-start.5
  32.0 0.4 collective-permute-start.4
  32.4 2.0 %collective-permute-done.6 = f32[1,168,128]{2,1,0:T(8,128)S(1)} collective-permute-done((f32[1,168,128]{2,1,0:T(8,128)S(1)}, f32[1,168,128]{2,1,0:T(8,128)S(1)}, u32[]{:S(2)}, u32[]{:S(2)}) %collective-permute-start.6) | collective-permute-done | bytes 86048 | tf_op jit(solution)/shard_map/ppermute | solution.py:77
  34.4 1.7 %collective-permute-done.5 = f32[1,168,128]{2,1,0:T(8,128)S(1)} collective-permute-done((f32[1,168,128]{2,1,0:T(8,128)S(1)}, f32[1,168,128]{2,1,0:T(8,128)S(1)}, u32[]{:S(2)}, u32[]{:S(2)}) %collective-permute-start.5) | collective-permute-done | bytes 86048 | tf_op jit(solution)/shard_map/ppermute | solution.py:77
  36.1 0.4 collective-permute-done.4
  36.5 2.7 %collective-permute-start.7 = (f32[1,168,128]{2,1,0:T(8,128)S(1)}, f32[1,168,128]{2,1,0:T(8,128)S(1)}, u32[]{:S(2)}, u32[]{:S(2)}) collective-permute-start(f32[1,168,128]{2,1,0:T(8,128)S(1)} %add_add_fusion), channel_id=1, source_target_pairs={{0,16},{4,20},{8,24},{12,28},{16,0},{20,4},{24,8},{28,12},{1,17},{... | collective-permute-start | bytes 258056 | tf_op jit(solution)/shard_map/ppermute | solution.py:77
  39.2 4.5 %collective-permute-done.7 = f32[1,168,128]{2,1,0:T(8,128)S(1)} collective-permute-done((f32[1,168,128]{2,1,0:T(8,128)S(1)}, f32[1,168,128]{2,1,0:T(8,128)S(1)}, u32[]{:S(2)}, u32[]{:S(2)}) %collective-permute-start.7) | collective-permute-done | bytes 86048 | tf_op jit(solution)/shard_map/ppermute | solution.py:77
  43.8 0.5 collective-permute-start.10
  44.3 0.5 copy.52
  44.8 0.6 %pad.43.clone = f32[96,12,1,136]{0,2,3,1:T(1,128)S(1)} pad(f32[96,12,1,128]{0,2,3,1:T(1,128)S(1)} %copy.52, f32[]{:T(128)} %constant.112.clone.1), padding=0_0x0_0x0_0x3_5 | pad | bytes 1216516 | tf_op jit(solution)/shard_map/optimization_barrier | solution.py:80
  45.4 1.4 %convolution_select_fusion.1 = f32[6,8,17,96]{3,1,2,0:T(8,128)S(1)} fusion(f32[96,12,1,7,6]{0,3,4,1,2:T(8,128)S(1)} %slice.286, f32[96,12,1,8,17]{0,3,4,1,2:T(8,128)S(1)} %copy.42, pred[8,17]{0,1:T(8,128)(4,1)S(1)} %copy-done.11, f32[96,1,7,7]{0,3,2,1:T(8,128)S(1)} %bitcast.187), kind=kOutput, calls=%fused_computation.77 | convolution fusion | flops 46775808 | bytes 1152520 | tf_op jit(solution)/shard_map/conv_general_dilated | solution.py:163
  47.0 0.2 copy.39
  47.2 1.1 %collective-permute-done.10 = f32[1,168,128]{2,1,0:T(8,128)S(1)} collective-permute-done((f32[1,168,128]{2,1,0:T(8,128)S(1)}, f32[1,168,128]{2,1,0:T(8,128)S(1)}, u32[]{:S(2)}, u32[]{:S(2)}) %collective-permute-start.10) | collective-permute-done | bytes 86048 | tf_op jit(solution)/shard_map/ppermute | solution.py:87
  48.4 0.8 %copy.45 = bf16[1,96,6,128]{3,1,2,0:T(8,128)(2,1)} copy(bf16[1,96,6,128]{1,3,2,0:T(8,128)(2,1)S(1)} %fusion.37) | data formatting | bytes 294912
  49.2 0.6 %collective-permute-done.11 = f32[2,168,128]{2,1,0:T(8,128)S(1)} collective-permute-done((f32[2,168,128]{2,1,0:T(8,128)S(1)}, f32[2,168,128]{2,1,0:T(8,128)S(1)}, u32[]{:S(2)}, u32[]{:S(2)}) %collective-permute-start.11) | collective-permute-done | bytes 172064 | tf_op jit(solution)/shard_map/ppermute | solution.py:87
  49.9 0.3 slice.255
  50.2 0.5 fusion.71
  50.7 0.6 %slice.293 = f32[384]{0:T(512)} slice(f32[86016]{0:T(1024)S(1)} %bitcast.181), slice={[45056:45440]} | slice | bytes 3072 | tf_op jit(solution)/shard_map/slice | solution.py:95
  51.4 0.6 %slice_bitcast_fusion.2 = f32[96,7,7]{0,2,1:T(8,128)} fusion(f32[128,7,96]{2,1,0:T(8,128)S(1)} %slice.255), kind=kLoop, calls=%fused_computation.205 | loop fusion | bytes 37632 | tf_op jit(solution)/shard_map/transpose | solution.py:195
  52.0 0.7 %reshape.216 = f32[96,384]{1,0:T(8,128)} reshape(f32[36864]{0:T(1024)S(1)} %slice.292) | data formatting | bytes 294912 | tf_op jit(solution)/shard_map/reshape | solution.py:95
  52.7 0.7 %slice_bitcast_fusion.1 = f32[384,96]{0,1:T(8,128)} fusion(f32[224,384]{1,0:T(8,128)S(1)} %slice.262), kind=kLoop, calls=%fused_computation.183 | loop fusion | bytes 294912 | tf_op jit(solution)/shard_map/transpose | solution.py:196
  (83 shorter events, 1.9 us)
Async XLA Ops:
  0.6 6.5 %copy-start = (bf16[96,384]{1,0:T(8,128)(2,1)S(1)}, bf16[96,384]{1,0:T(8,128)(2,1)}, u32[]{:S(2)}) copy-start(bf16[96,384]{1,0:T(8,128)(2,1)} %param.17) | copy-start | bytes 221188
  0.7 2.4 %collective-permute-start.1 = (bf16[1,96,6,128]{3,1,2,0:T(8,128)(2,1)}, bf16[1,96,6,128]{3,1,2,0:T(8,128)(2,1)S(1)}, u32[]{:S(2)}, u32[]{:S(2)}) collective-permute-start(bf16[1,96,6,128]{3,1,2,0:T(8,128)(2,1)} %param.11), channel_id=1, source_target_pairs={{0,4},{4,0},{8,12},{12,8},{16,20},{20,16},{24,28},{28,24},{1,5},{5... | collective-permute-start | bytes 442376 | tf_op jit(solution)/shard_map/ppermute | solution.py:15
  1.2 1.8 %collective-permute-start = (bf16[1,96,6,128]{3,1,2,0:T(8,128)(2,1)}, bf16[1,96,6,128]{3,1,2,0:T(8,128)(2,1)S(1)}, u32[]{:S(2)}, u32[]{:S(2)}) collective-permute-start(bf16[1,96,6,128]{3,1,2,0:T(8,128)(2,1)} %param.11), channel_id=1, source_target_pairs={{4,8},{12,16},{20,24},{8,4},{16,12},{24,20},{5,9},{13,17},{21,25},... | collective-permute-start | bytes 442376 | tf_op jit(solution)/shard_map/ppermute | solution.py:16
  4.4 0.8 %copy-start.3 = (f32[96,7,7]{0,2,1:T(8,128)S(1)}, f32[96,7,7]{0,2,1:T(8,128)}, u32[]{:S(2)}) copy-start(f32[96,7,7]{0,2,1:T(8,128)} %param.13) | copy-start | bytes 56452
  4.4 0.7 %copy-start.9 = (f32[96]{0:T(128)S(1)}, f32[96]{0:T(128)}, u32[]{:S(2)}) copy-start(f32[96]{0:T(128)} %param.14) | copy-start | bytes 1156
  4.5 0.7 %copy-start.11 = (pred[8,17]{0,1:T(8,128)(4,1)S(1)}, pred[8,17]{0,1:T(8,128)(4,1)}, u32[]{:S(2)}) copy-start(pred[8,17]{0,1:T(8,128)(4,1)} %constant.178) | copy-start | bytes 412
  6.8 0.7 %copy-start.4 = (f32[96]{0:T(128)S(1)}, f32[96]{0:T(128)}, u32[]{:S(2)}) copy-start(f32[96]{0:T(128)} %param.15) | copy-start | bytes 1156
  6.9 0.7 %copy-start.6 = (f32[96]{0:T(128)S(1)}, f32[96]{0:T(128)}, u32[]{:S(2)}) copy-start(f32[96]{0:T(128)} %param.16) | copy-start | bytes 1156
  6.9 0.7 %copy-start.8 = (f32[384]{0:T(512)S(1)}, f32[384]{0:T(512)}, u32[]{:S(2)}) copy-start(f32[384]{0:T(512)} %param.18) | copy-start | bytes 4612
  7.6 2.8 %copy-start.1 = (bf16[1,96,6,128]{3,1,2,0:T(8,128)(2,1)S(1)}, bf16[1,96,6,128]{3,1,2,0:T(8,128)(2,1)}, u32[]{:S(2)}) copy-start(bf16[1,96,6,128]{3,1,2,0:T(8,128)(2,1)} %param.12) | copy-start | bytes 442372
  7.6 2.9 %copy-start.5 = (f32[96]{0:T(128)S(1)}, f32[96]{0:T(128)}, u32[]{:S(2)}) copy-start(f32[96]{0:T(128)} %param.21) | copy-start | bytes 1156
  7.6 2.9 %copy-start.7 = (bf16[384,96]{0,1:T(8,128)(2,1)S(1)}, bf16[384,96]{0,1:T(8,128)(2,1)}, u32[]{:S(2)}) copy-start(bf16[384,96]{0,1:T(8,128)(2,1)} %param.19) | copy-start | bytes 221188
  11.6 1.9 %copy-start.2 = (bf16[1,96,6,128]{3,1,2,0:T(8,128)(2,1)S(1)}, bf16[1,96,6,128]{3,1,2,0:T(8,128)(2,1)}, u32[]{:S(2)}) copy-start(bf16[1,96,6,128]{3,1,2,0:T(8,128)(2,1)} %param.11) | copy-start | bytes 442372
  15.3 0.8 %copy-start.10 = (f32[96]{0:T(128)S(1)}, f32[96]{0:T(128)}, u32[]{:S(2)}) copy-start(f32[96]{0:T(128)} %param.20) | copy-start | bytes 1156
  16.6 6.9 %collective-permute-start.2 = (f32[2,168,128]{2,1,0:T(8,128)S(1)}, f32[2,168,128]{2,1,0:T(8,128)S(1)}, u32[]{:S(2)}, u32[]{:S(2)}) collective-permute-start(f32[2,168,128]{2,1,0:T(8,128)S(1)} %constant_dynamic-slice_fusion.1), channel_id=1, source_target_pairs={{0,4},{4,0},{8,12},{12,8},{16,20},{20,16},{24,28},{28,24},{1,5},{5... | collective-permute-start | bytes 516104 | tf_op jit(solution)/shard_map/ppermute | solution.py:71
  23.6 5.2 %collective-permute-start.3 = (f32[1,168,128]{2,1,0:T(8,128)S(1)}, f32[1,168,128]{2,1,0:T(8,128)S(1)}, u32[]{:S(2)}, u32[]{:S(2)}) collective-permute-start(f32[1,168,128]{2,1,0:T(8,128)S(1)} %constant_dynamic-slice_fusion), channel_id=1, source_target_pairs={{0,8},{4,12},{8,0},{12,4},{16,24},{20,28},{24,16},{28,20},{1,9},{5... | collective-permute-start | bytes 258056 | tf_op jit(solution)/shard_map/ppermute | solution.py:71
  25.8 6.6 %collective-permute-start.8 = (f32[1,96,3,128]{3,1,2,0:T(8,128)S(1)}, f32[1,96,3,128]{3,1,2,0:T(8,128)S(1)}, u32[]{:S(2)}, u32[]{:S(2)}) collective-permute-start(f32[1,96,3,128]{3,1,2,0:T(8,128)S(1)} %get-tuple-element.95), channel_id=1, source_target_pairs={{4,8},{12,16},{20,24},{8,4},{16,12},{24,20},{5,9},{13,17},{21,25},... | collective-permute-start | bytes 442376 | tf_op jit(solution)/shard_map/ppermute | solution.py:30
  26.6 5.8 %collective-permute-start.9 = (f32[1,96,3,128]{3,1,2,0:T(8,128)S(1)}, f32[1,96,3,128]{3,1,2,0:T(8,128)S(1)}, u32[]{:S(2)}, u32[]{:S(2)}) collective-permute-start(f32[1,96,3,128]{3,1,2,0:T(8,128)S(1)} %get-tuple-element.96), channel_id=1, source_target_pairs={{0,4},{4,0},{8,12},{12,8},{16,20},{20,16},{24,28},{28,24},{1,5},{5... | collective-permute-start | bytes 442376 | tf_op jit(solution)/shard_map/ppermute | solution.py:29
  28.8 5.5 %collective-permute-start.6 = (f32[1,168,128]{2,1,0:T(8,128)S(1)}, f32[1,168,128]{2,1,0:T(8,128)S(1)}, u32[]{:S(2)}, u32[]{:S(2)}) collective-permute-start(f32[1,168,128]{2,1,0:T(8,128)S(1)} %dynamic-slice_add_fusion.1), channel_id=1, source_target_pairs={{0,3},{1,2},{2,1},{3,0},{4,7},{5,6},{6,5},{7,4},{8,11},{9,10},{10,... | collective-permute-start | bytes 258056 | tf_op jit(solution)/shard_map/ppermute | solution.py:77
  31.5 4.6 %collective-permute-start.5 = (f32[1,168,128]{2,1,0:T(8,128)S(1)}, f32[1,168,128]{2,1,0:T(8,128)S(1)}, u32[]{:S(2)}, u32[]{:S(2)}) collective-permute-start(f32[1,168,128]{2,1,0:T(8,128)S(1)} %dynamic-slice_add_fusion.1), channel_id=1, source_target_pairs={{0,2},{1,3},{2,0},{3,1},{4,6},{5,7},{6,4},{7,5},{8,10},{9,11},{10,... | collective-permute-start | bytes 258056 | tf_op jit(solution)/shard_map/ppermute | solution.py:77
  32.0 4.5 %collective-permute-start.4 = (f32[1,168,128]{2,1,0:T(8,128)S(1)}, f32[1,168,128]{2,1,0:T(8,128)S(1)}, u32[]{:S(2)}, u32[]{:S(2)}) collective-permute-start(f32[1,168,128]{2,1,0:T(8,128)S(1)} %dynamic-slice_add_fusion.1), channel_id=1, source_target_pairs={{0,1},{1,0},{2,3},{3,2},{4,5},{5,4},{6,7},{7,6},{8,9},{9,8},{10,11... | collective-permute-start | bytes 258056 | tf_op jit(solution)/shard_map/ppermute | solution.py:77
  36.5 7.2 %collective-permute-start.7 = (f32[1,168,128]{2,1,0:T(8,128)S(1)}, f32[1,168,128]{2,1,0:T(8,128)S(1)}, u32[]{:S(2)}, u32[]{:S(2)}) collective-permute-start(f32[1,168,128]{2,1,0:T(8,128)S(1)} %add_add_fusion), channel_id=1, source_target_pairs={{0,16},{4,20},{8,24},{12,28},{16,0},{20,4},{24,8},{28,12},{1,17},{... | collective-permute-start | bytes 258056 | tf_op jit(solution)/shard_map/ppermute | solution.py:77
  43.8 4.6 %collective-permute-start.10 = (f32[1,168,128]{2,1,0:T(8,128)S(1)}, f32[1,168,128]{2,1,0:T(8,128)S(1)}, u32[]{:S(2)}, u32[]{:S(2)}) collective-permute-start(f32[1,168,128]{2,1,0:T(8,128)S(1)} %add.152), channel_id=1, source_target_pairs={{0,8},{4,12},{8,0},{12,4},{16,24},{20,28},{24,16},{28,20},{1,9},{5... | collective-permute-start | bytes 258056 | tf_op jit(solution)/shard_map/ppermute | solution.py:87
  48.4 1.5 %collective-permute-start.11 = (f32[2,168,128]{2,1,0:T(8,128)S(1)}, f32[2,168,128]{2,1,0:T(8,128)S(1)}, u32[]{:S(2)}, u32[]{:S(2)}) collective-permute-start(f32[2,168,128]{2,1,0:T(8,128)S(1)} %pad_maximum_fusion.3), channel_id=1, source_target_pairs={{0,4},{4,0},{8,12},{12,8},{16,20},{20,16},{24,28},{28,24},{1,5},{5... | collective-permute-start | bytes 516104 | tf_op jit(solution)/shard_map/ppermute | solution.py:87

commit v17 on v16

--- a/solution.py
+++ b/solution.py
@@ -6,14 +6,17 @@
 from jax.sharding import PartitionSpec as P
 
 
-def with_halo(array, sides, width, whole=False):
+def with_halo(array, sides, width, whole=False, pair_after=None):
     for axis, dim in sides:
         size, length = (lax.axis_size(axis), array.shape[dim])
         if whole:
             pairs = [(i, i + 1) for i in range(1, size - 1, 2)]
             pairs += [(j, i) for i, j in pairs]
-            from_pair = lax.ppermute(array, axis, [(i, i ^ 1) for i in range(size)])
             from_chip = lax.ppermute(array, axis, pairs)
+            paired = array
+            if pair_after is not None:
+                paired, _ = lax.optimization_barrier((array, pair_after))
+            from_pair = lax.ppermute(paired, axis, [(i, i ^ 1) for i in range(size)])
             even = lax.axis_index(axis) % 2 == 0
             above = jnp.where(even, from_chip, from_pair)
             below = jnp.where(even, from_pair, from_chip)
@@ -121,7 +124,10 @@
     rows = images.shape[2]
     cols = images.shape[3]
     kernel = conv_weight.shape[1]
-    extended = with_halo(images, (("strip", 2),), 3, whole=True)
+    upstream = cotangent.astype(jnp.float32)
+    d_branch = (layer_scale[None, :, None, None] * upstream).astype(jnp.bfloat16)
+    d_branch_sum = jnp.sum(d_branch.astype(jnp.float32), axis=(0, 2, 3))
+    extended = with_halo(images, (("strip", 2),), 3, whole=True, pair_after=d_branch_sum)
     upstream = cotangent.astype(jnp.float32)
     padded = jnp.pad(extended, ((0, 0), (0, 0), (0, 0), (3, 3)))
     conv = lax.conv_general_dilated(
@@ -148,7 +154,6 @@
         jnp.einsum("sfrw,fc->scrw", act, down_weight, preferred_element_type=jnp.float32)
         + down_bias[None, :, None, None]
     )
-    d_branch = (layer_scale[None, :, None, None] * upstream).astype(jnp.bfloat16)
     d_act = jnp.einsum("scrw,fc->sfrw", d_branch, down_weight, preferred_element_type=jnp.float32)
     d_pre = (d_act * gelu_slope(pre)).astype(jnp.bfloat16)
     d_lifted = jnp.einsum("sfrw,cf->scrw", d_pre, up_weight, preferred_element_type=jnp.float32)
@@ -186,7 +191,7 @@
         jnp.einsum("scrw,sfrw->cf", lifted, d_pre, preferred_element_type=jnp.float32),
         jnp.sum(d_pre.astype(jnp.float32), axis=(0, 2, 3)),
         jnp.einsum("scrw,sfrw->cf", d_branch, act, preferred_element_type=jnp.float32),
-        jnp.sum(d_branch.astype(jnp.float32), axis=(0, 2, 3)),
+        d_branch_sum,
         jnp.sum(upstream * branch, axis=(0, 2, 3)),
     )
     g, image_grad = tree_psum(

time: 53.6 us -> 52.5 us (0.979)
  waiting for transfers between devices: 12.1 us -> 10.7 us
    ppermute x2, starting transfers between devices: 8.02 us -> 2.74 us  [tree_psum(): flat = keep + lax.ppermute(give, axis, xor_pairs(size, bit))]
    ppermute x1, starting transfers between devices: 0.56 us -> 4.47 us  [with_halo(): from_pair = lax.ppermute(paired, axis, [(i, i ^ 1) for i in range(size)])]
    ppermute x2, starting transfers between devices: 0.55 us -> 1.84 us  [tree_psum(): got = lax.ppermute(flat, axis, xor_pairs(size, bit))]
    ppermute x1, waiting for transfers between devices: 0.01 us -> 1.21 us  [with_halo(): from_pair = lax.ppermute(paired, axis, [(i, i ^ 1) for i in range(size)])]
    ppermute x4, waiting for transfers between devices: 8.63 us -> 7.42 us  [tree_psum(): got = [lax.ppermute(flat, axis, xor_pairs(size, mask)) for mask in masks]]
    ppermute x2, waiting for transfers between devices: 1.67 us -> 0.59 us  [tree_psum(): got = lax.ppermute(flat, axis, xor_pairs(size, bit))]
where the time goes in v17:
time: 52.5 us; the launch traced here: 52.2 us
  starting transfers between devices  18.5 us (35%)
  waiting for transfers between devices  10.7 us (20%)
  matrix products  7.93 us (15%)
  local copies, waits for them, and re-layouts  7.86 us (15%)
  other arithmetic  5.94 us (11%)
  between operations  1.23 us (2%)
    ppermute x4, waiting for transfers between devices, tree_psum(): got = [lax.ppermute(flat, axis, xor_pairs(size, mask)) for mask in masks]  7.42 us
    ppermute x4, starting transfers between devices, tree_psum(): got = [lax.ppermute(flat, axis, xor_pairs(size, mask)) for mask in masks]  6.37 us
    ppermute x1, starting transfers between devices, with_halo(): from_pair = lax.ppermute(paired, axis, [(i, i ^ 1) for i in range(size)])  4.47 us
    reduce_sum x4, other arithmetic, on_device(): jnp.sum(d_conv * padded[:, :, a:a + rows, b:b + cols], axis=(0, 2, 3))  3.23 us
    dot_general x1, matrix products, on_device(): jnp.einsum('scrw,cf->sfrw', lifted, up_weight, preferred_element_type=jnp...  2.83 us
    ppermute x2, starting transfers between devices, tree_psum(): flat = keep + lax.ppermute(give, axis, xor_pairs(size, bit))  2.74 us
    unnamed x36, local copies, waits for them, and re-layouts  2.61 us
    ppermute x2, starting transfers between devices, tree_psum(): got = lax.ppermute(flat, axis, xor_pairs(size, bit))  1.84 us
  transfers between devices with their start and end apart: 12, of which 8 were waited for; matrix products, arithmetic and copies ran while one was open for 9% of the time, Pallas kernels for 0%

profile of v17, /device:TPU:0, one launch (start us, length us, event | category | flops | bytes accessed | tf_op | source)
XLA Modules:
  0.0 52.2 jit_solution(7426372614339793575)
XLA Ops:
  0.7 0.8 %collective-permute-start = (bf16[1,96,6,128]{3,1,2,0:T(8,128)(2,1)}, bf16[1,96,6,128]{3,1,2,0:T(8,128)(2,1)S(1)}, u32[]{:S(2)}, u32[]{:S(2)}) collective-permute-start(bf16[1,96,6,128]{3,1,2,0:T(8,128)(2,1)} %param.11), channel_id=1, source_target_pairs={{4,8},{12,16},{20,24},{8,4},{16,12},{24,20},{5,9},{13,17},{21,25},... | collective-permute-start | bytes 442376 | tf_op jit(solution)/shard_map/ppermute | solution.py:15
  1.5 1.1 %convert_reduce_fusion.1 = f32[96]{0:T(128)S(1)} fusion(bf16[1,96,6,128]{3,1,2,0:T(8,128)(2,1)} %param.12, f32[96]{0:T(128)} %param.21), kind=kLoop, calls=%fused_computation.164 | loop fusion | flops 368544 | bytes 148224 | tf_op jit(solution)/shard_map/reduce_sum | solution.py:129
  2.6 4.5 %collective-permute-start.1 = (bf16[1,96,6,128]{3,1,2,0:T(8,128)(2,1)}, bf16[1,96,6,128]{3,1,2,0:T(8,128)(2,1)S(1)}, u32[]{:S(2)}, u32[]{:S(2)}) collective-permute-start(bf16[1,96,6,128]{3,1,2,0:T(8,128)(2,1)} %param.11), channel_id=1, source_target_pairs={{0,4},{4,0},{8,12},{12,8},{16,20},{20,16},{24,28},{28,24},{1,5},{5... | collective-permute-start | bytes 442376 | tf_op jit(solution)/shard_map/ppermute | solution.py:19
  7.1 1.2 %collective-permute-done.1 = bf16[1,96,6,128]{3,1,2,0:T(8,128)(2,1)S(1)} collective-permute-done((bf16[1,96,6,128]{3,1,2,0:T(8,128)(2,1)}, bf16[1,96,6,128]{3,1,2,0:T(8,128)(2,1)S(1)}, u32[]{:S(2)}, u32[]{:S(2)}) %collective-permute-start.1) | collective-permute-done | bytes 147488 | tf_op jit(solution)/shard_map/ppermute | solution.py:19
  8.3 1.0 %fusion.69 = (bf16[96,12,1,128]{3,0,1,2:T(8,128)(2,1)S(1)}, bf16[1,96,12,128]{3,1,2,0:T(8,128)(2,1)S(1)}) fusion(bf16[1,96,3,128]{3,1,2,0:T(8,128)(2,1)S(1)} %get-tuple-element.102, bf16[1,96,6,128]{3,1,2,0:T(8,128)(2,1)} %param.11, bf16[1,96,3,128]{3,1,2,0:T(8,128)(2,1)S(1)} %get-tuple-element.101), kind=kLoop, calls=%fused_computation.236 | loop fusion | flops 294912 | bytes 884736 | tf_op jit(solution)/shard_map/concatenate | solution.py:25
  9.3 0.2 copy.51
  9.9 0.5 copy-done.3
  10.4 1.5 %fusion.19 = f32[6,8,17,96]{3,1,2,0:T(8,128)S(1)} fusion(bf16[96,12,1,7,6]{0,3,4,1,2:T(8,128)(2,1)S(1)} %slice.274, bf16[96,12,1,8,17]{0,3,4,1,2:T(8,128)(2,1)S(1)} %copy.31, f32[96]{0:T(128)S(1)} %copy-done.9, pred[8,17]{0,1:T(8,128)(4,1)S(1)} %copy-done.11, f32[96,1,7,7]{0,3,2,1:T(8,128)S(1)} %bitcast.186), kind=kOutput, calls=%fused_computation.76 | convolution fusion | flops 47490048 | bytes 742792 | tf_op jit(solution)/shard_map/conv_general_dilated | solution.py:133
  12.1 0.2 copy.50
  12.4 0.3 copy-done.4
  12.8 2.8 %fusion.9 = (bf16[384,6,128]{0,2,1:T(8,128)(2,1)S(1)}, f32[384,6,128]{0,2,1:T(8,128)S(1)}) fusion(f32[384]{0:T(512)S(1)} %copy-done.8, bf16[96,384]{1,0:T(8,128)(2,1)S(1)} %copy-done, f32[6,1,128,96]{2,3,0,1:T(8,128)S(1)} %copy.50, f32[96]{0:T(128)S(1)} %copy-done.6, f32[96]{0:T(128)S(1)} %copy-done.4, f32[6,128]{1,0:T(8,128)S(1)} %add_rsqrt_fusion, ...), kind=kOutput, calls=%fused_computation.55 | convolution fusion | flops 76455936 | bytes 2146560 | tf_op jit(solution)/shard_map/scrw,cf->sfrw/dot_general | solution.py:149
  15.6 0.7 %convert_reduce_fusion = (f32[384]{0:T(512)S(1)}, bf16[384,6,128]{0,2,1:T(8,128)(2,1)S(1)}) fusion(f32[384,6,128]{0,2,1:T(8,128)S(1)} %get-tuple-element.109, bf16[384,96]{0,1:T(8,128)(2,1)S(1)} %copy-done.7, bf16[1,96,6,128]{3,1,2,0:T(8,128)(2,1)S(1)} %copy-done.1, f32[96]{0:T(128)S(1)} %copy-done.5), kind=kOutput, calls=%fused_computation.69 | convolution fusion | flops 60382848 | bytes 1992576 | tf_op jit(solution)/shard_map/scrw,fc->sfrw/dot_general | solution.py:157
  16.4 0.4 fusion.39
  16.9 1.2 %multiply_reduce_fusion = (f32[96]{0:T(128)S(1)}, f32[96]{0:T(128)S(1)}, f32[96]{0:T(128)S(1)}, f32[96]{0:T(128)S(1)}, f32[96]{0:T(128)S(1)}, /*index=5*/f32[96]...) fusion(bf16[1,96,12,128]{3,1,2,0:T(8,128)(2,1)S(1)} %get-tuple-, ...), kind=kLoop, calls=%fused_computation.113 | loop fusion | flops 4495680 | bytes 1199232 | tf_op jit(solution)/shard_map/reduce_sum | solution.py:183
  18.1 0.5 multiply_reduce_fusion.42
  18.7 0.3 multiply_reduce_fusion.3
  19.0 1.2 %multiply_reduce_fusion.21 = (f32[96]{0:T(128)S(1)}, f32[96]{0:T(128)S(1)}, f32[96]{0:T(128)S(1)}, f32[96]{0:T(128)S(1)}, f32[96]{0:T(128)S(1)}, /*index=5*/f32[...) fusion(f32[1,96,6,128]{3,1,2,0:T(8,128)S(1)} %get-tuple-element, ...), kind=kLoop, calls=%fused_computation.134 | loop fusion | flops 3979584 | bytes 596736 | tf_op jit(solution)/shard_map/reduce_sum | solution.py:183
  20.2 0.3 fusion.21
  20.5 0.1 stack.199
  20.9 0.3 fusion.22
  21.2 0.4 fusion.20
  21.8 0.7 %collective-permute-start.2 = (f32[2,168,128]{2,1,0:T(8,128)S(1)}, f32[2,168,128]{2,1,0:T(8,128)S(1)}, u32[]{:S(2)}, u32[]{:S(2)}) collective-permute-start(f32[2,168,128]{2,1,0:T(8,128)S(1)} %constant_dynamic-slice_fusion.1), channel_id=1, source_target_pairs={{0,4},{4,0},{8,12},{12,8},{16,20},{20,16},{24,28},{28,24},{1,5},{5... | collective-permute-start | bytes 516104 | tf_op jit(solution)/shard_map/ppermute | solution.py:74
  22.6 1.0 %collective-permute-done.2 = f32[2,168,128]{2,1,0:T(8,128)S(1)} collective-permute-done((f32[2,168,128]{2,1,0:T(8,128)S(1)}, f32[2,168,128]{2,1,0:T(8,128)S(1)}, u32[]{:S(2)}, u32[]{:S(2)}) %collective-permute-start.2) | collective-permute-done | bytes 172064 | tf_op jit(solution)/shard_map/ppermute | solution.py:74
  23.6 2.1 %collective-permute-start.3 = (f32[1,168,128]{2,1,0:T(8,128)S(1)}, f32[1,168,128]{2,1,0:T(8,128)S(1)}, u32[]{:S(2)}, u32[]{:S(2)}) collective-permute-start(f32[1,168,128]{2,1,0:T(8,128)S(1)} %constant_dynamic-slice_fusion), channel_id=1, source_target_pairs={{0,8},{4,12},{8,0},{12,4},{16,24},{20,28},{24,16},{28,20},{1,9},{5... | collective-permute-start | bytes 258056 | tf_op jit(solution)/shard_map/ppermute | solution.py:74
  25.7 0.9 %collective-permute-start.8 = (f32[1,96,3,128]{3,1,2,0:T(8,128)S(1)}, f32[1,96,3,128]{3,1,2,0:T(8,128)S(1)}, u32[]{:S(2)}, u32[]{:S(2)}) collective-permute-start(f32[1,96,3,128]{3,1,2,0:T(8,128)S(1)} %get-tuple-element.97), channel_id=1, source_target_pairs={{4,8},{12,16},{20,24},{8,4},{16,12},{24,20},{5,9},{13,17},{21,25},... | collective-permute-start | bytes 442376 | tf_op jit(solution)/shard_map/ppermute | solution.py:33
  26.6 1.5 %collective-permute-start.9 = (f32[1,96,3,128]{3,1,2,0:T(8,128)S(1)}, f32[1,96,3,128]{3,1,2,0:T(8,128)S(1)}, u32[]{:S(2)}, u32[]{:S(2)}) collective-permute-start(f32[1,96,3,128]{3,1,2,0:T(8,128)S(1)} %get-tuple-element.98), channel_id=1, source_target_pairs={{0,4},{4,0},{8,12},{12,8},{16,20},{20,16},{24,28},{28,24},{1,5},{5... | collective-permute-start | bytes 442376 | tf_op jit(solution)/shard_map/ppermute | solution.py:32
  28.0 0.5 collective-permute-done.3
  28.5 2.5 %collective-permute-start.6 = (f32[1,168,128]{2,1,0:T(8,128)S(1)}, f32[1,168,128]{2,1,0:T(8,128)S(1)}, u32[]{:S(2)}, u32[]{:S(2)}) collective-permute-start(f32[1,168,128]{2,1,0:T(8,128)S(1)} %dynamic-slice_add_fusion.1), channel_id=1, source_target_pairs={{0,3},{1,2},{2,1},{3,0},{4,7},{5,6},{6,5},{7,4},{8,11},{9,10},{10,... | collective-permute-start | bytes 258056 | tf_op jit(solution)/shard_map/ppermute | solution.py:80
  31.0 0.5 collective-permute-start.5
  31.5 0.5 %collective-permute-start.4 = (f32[1,168,128]{2,1,0:T(8,128)S(1)}, f32[1,168,128]{2,1,0:T(8,128)S(1)}, u32[]{:S(2)}, u32[]{:S(2)}) collective-permute-start(f32[1,168,128]{2,1,0:T(8,128)S(1)} %dynamic-slice_add_fusion.1), channel_id=1, source_target_pairs={{0,1},{1,0},{2,3},{3,2},{4,5},{5,4},{6,7},{7,6},{8,9},{9,8},{10,11... | collective-permute-start | bytes 258056 | tf_op jit(solution)/shard_map/ppermute | solution.py:80
  32.1 2.0 %collective-permute-done.6 = f32[1,168,128]{2,1,0:T(8,128)S(1)} collective-permute-done((f32[1,168,128]{2,1,0:T(8,128)S(1)}, f32[1,168,128]{2,1,0:T(8,128)S(1)}, u32[]{:S(2)}, u32[]{:S(2)}) %collective-permute-start.6) | collective-permute-done | bytes 86048 | tf_op jit(solution)/shard_map/ppermute | solution.py:80
  34.1 1.6 %collective-permute-done.5 = f32[1,168,128]{2,1,0:T(8,128)S(1)} collective-permute-done((f32[1,168,128]{2,1,0:T(8,128)S(1)}, f32[1,168,128]{2,1,0:T(8,128)S(1)}, u32[]{:S(2)}, u32[]{:S(2)}) %collective-permute-start.5) | collective-permute-done | bytes 86048 | tf_op jit(solution)/shard_map/ppermute | solution.py:80
  35.7 0.4 collective-permute-done.4
  36.1 2.8 %collective-permute-start.7 = (f32[1,168,128]{2,1,0:T(8,128)S(1)}, f32[1,168,128]{2,1,0:T(8,128)S(1)}, u32[]{:S(2)}, u32[]{:S(2)}) collective-permute-start(f32[1,168,128]{2,1,0:T(8,128)S(1)} %add_add_fusion), channel_id=1, source_target_pairs={{0,16},{4,20},{8,24},{12,28},{16,0},{20,4},{24,8},{28,12},{1,17},{... | collective-permute-start | bytes 258056 | tf_op jit(solution)/shard_map/ppermute | solution.py:80
  38.9 3.5 %collective-permute-done.7 = f32[1,168,128]{2,1,0:T(8,128)S(1)} collective-permute-done((f32[1,168,128]{2,1,0:T(8,128)S(1)}, f32[1,168,128]{2,1,0:T(8,128)S(1)}, u32[]{:S(2)}, u32[]{:S(2)}) %collective-permute-start.7) | collective-permute-done | bytes 86048 | tf_op jit(solution)/shard_map/ppermute | solution.py:80
  42.4 1.8 %collective-permute-start.10 = (f32[1,168,128]{2,1,0:T(8,128)S(1)}, f32[1,168,128]{2,1,0:T(8,128)S(1)}, u32[]{:S(2)}, u32[]{:S(2)}) collective-permute-start(f32[1,168,128]{2,1,0:T(8,128)S(1)} %add.152), channel_id=1, source_target_pairs={{0,8},{4,12},{8,0},{12,4},{16,24},{20,28},{24,16},{28,20},{1,9},{5... | collective-permute-start | bytes 258056 | tf_op jit(solution)/shard_map/ppermute | solution.py:90
  44.2 0.5 copy.52
  44.7 0.6 %pad.43.clone = f32[96,12,1,136]{0,2,3,1:T(1,128)S(1)} pad(f32[96,12,1,128]{0,2,3,1:T(1,128)S(1)} %copy.52, f32[]{:T(128)} %constant.112.clone.1), padding=0_0x0_0x0_0x3_5 | pad | bytes 1216516 | tf_op jit(solution)/shard_map/optimization_barrier | solution.py:83
  45.4 1.4 %convolution_select_fusion.1 = f32[6,8,17,96]{3,1,2,0:T(8,128)S(1)} fusion(f32[96,12,1,7,6]{0,3,4,1,2:T(8,128)S(1)} %slice.286, f32[96,12,1,8,17]{0,3,4,1,2:T(8,128)S(1)} %copy.42, pred[8,17]{0,1:T(8,128)(4,1)S(1)} %copy-done.11, f32[96,1,7,7]{0,3,2,1:T(8,128)S(1)} %bitcast.187), kind=kOutput, calls=%fused_computation.77 | convolution fusion | flops 46775808 | bytes 1152520 | tf_op jit(solution)/shard_map/conv_general_dilated | solution.py:168
  46.9 0.2 copy.39
  47.3 0.8 %copy.45 = bf16[1,96,6,128]{3,1,2,0:T(8,128)(2,1)} copy(bf16[1,96,6,128]{1,3,2,0:T(8,128)(2,1)S(1)} %fusion.37) | data formatting | bytes 294912
  48.1 0.6 %collective-permute-done.11 = f32[2,168,128]{2,1,0:T(8,128)S(1)} collective-permute-done((f32[2,168,128]{2,1,0:T(8,128)S(1)}, f32[2,168,128]{2,1,0:T(8,128)S(1)}, u32[]{:S(2)}, u32[]{:S(2)}) %collective-permute-start.11) | collective-permute-done | bytes 172064 | tf_op jit(solution)/shard_map/ppermute | solution.py:90
  48.8 0.3 slice.255
  49.0 0.5 %fusion.71 = (f32[96]{0:T(128)}, f32[96]{0:T(128)}, f32[96]{0:T(128)}, f32[96]{0:T(128)}, f32[96]{0:T(128)}) fusion(f32[86016]{0:T(1024)S(1)} %bitcast.179), kind=kLoop, calls=%fused_computation.237 | loop fusion | bytes 3840 | tf_op jit(solution)/shard_map/slice | solution.py:98
  49.6 0.6 %slice.293 = f32[384]{0:T(512)} slice(f32[86016]{0:T(1024)S(1)} %bitcast.181), slice={[45056:45440]} | slice | bytes 3072 | tf_op jit(solution)/shard_map/slice | solution.py:98
  50.3 0.6 %slice_bitcast_fusion.2 = f32[96,7,7]{0,2,1:T(8,128)} fusion(f32[128,7,96]{2,1,0:T(8,128)S(1)} %slice.255), kind=kLoop, calls=%fused_computation.205 | loop fusion | bytes 37632 | tf_op jit(solution)/shard_map/transpose | solution.py:200
  50.9 0.7 %reshape.216 = f32[96,384]{1,0:T(8,128)} reshape(f32[36864]{0:T(1024)S(1)} %slice.292) | data formatting | bytes 294912 | tf_op jit(solution)/shard_map/reshape | solution.py:98
  51.6 0.7 %slice_bitcast_fusion.1 = f32[384,96]{0,1:T(8,128)} fusion(f32[224,384]{1,0:T(8,128)S(1)} %slice.262), kind=kLoop, calls=%fused_computation.183 | loop fusion | bytes 294912 | tf_op jit(solution)/shard_map/transpose | solution.py:201
  (83 shorter events, 1.9 us)
Async XLA Ops:
  0.6 11.8 %copy-start = (bf16[96,384]{1,0:T(8,128)(2,1)S(1)}, bf16[96,384]{1,0:T(8,128)(2,1)}, u32[]{:S(2)}) copy-start(bf16[96,384]{1,0:T(8,128)(2,1)} %param.17) | copy-start | bytes 221188
  0.7 7.6 %collective-permute-start = (bf16[1,96,6,128]{3,1,2,0:T(8,128)(2,1)}, bf16[1,96,6,128]{3,1,2,0:T(8,128)(2,1)S(1)}, u32[]{:S(2)}, u32[]{:S(2)}) collective-permute-start(bf16[1,96,6,128]{3,1,2,0:T(8,128)(2,1)} %param.11), channel_id=1, source_target_pairs={{4,8},{12,16},{20,24},{8,4},{16,12},{24,20},{5,9},{13,17},{21,25},... | collective-permute-start | bytes 442376 | tf_op jit(solution)/shard_map/ppermute | solution.py:15
  2.6 5.7 %collective-permute-start.1 = (bf16[1,96,6,128]{3,1,2,0:T(8,128)(2,1)}, bf16[1,96,6,128]{3,1,2,0:T(8,128)(2,1)S(1)}, u32[]{:S(2)}, u32[]{:S(2)}) collective-permute-start(bf16[1,96,6,128]{3,1,2,0:T(8,128)(2,1)} %param.11), channel_id=1, source_target_pairs={{0,4},{4,0},{8,12},{12,8},{16,20},{20,16},{24,28},{28,24},{1,5},{5... | collective-permute-start | bytes 442376 | tf_op jit(solution)/shard_map/ppermute | solution.py:19
  9.6 0.8 %copy-start.3 = (f32[96,7,7]{0,2,1:T(8,128)S(1)}, f32[96,7,7]{0,2,1:T(8,128)}, u32[]{:S(2)}) copy-start(f32[96,7,7]{0,2,1:T(8,128)} %param.13) | copy-start | bytes 56452
  9.7 0.7 %copy-start.9 = (f32[96]{0:T(128)S(1)}, f32[96]{0:T(128)}, u32[]{:S(2)}) copy-start(f32[96]{0:T(128)} %param.14) | copy-start | bytes 1156
  9.7 0.7 %copy-start.11 = (pred[8,17]{0,1:T(8,128)(4,1)S(1)}, pred[8,17]{0,1:T(8,128)(4,1)}, u32[]{:S(2)}) copy-start(pred[8,17]{0,1:T(8,128)(4,1)} %constant.178) | copy-start | bytes 412
  12.1 0.7 %copy-start.4 = (f32[96]{0:T(128)S(1)}, f32[96]{0:T(128)}, u32[]{:S(2)}) copy-start(f32[96]{0:T(128)} %param.15) | copy-start | bytes 1156
  12.1 0.7 %copy-start.6 = (f32[96]{0:T(128)S(1)}, f32[96]{0:T(128)}, u32[]{:S(2)}) copy-start(f32[96]{0:T(128)} %param.16) | copy-start | bytes 1156
  12.1 0.7 %copy-start.8 = (f32[384]{0:T(512)S(1)}, f32[384]{0:T(512)}, u32[]{:S(2)}) copy-start(f32[384]{0:T(512)} %param.18) | copy-start | bytes 4612
  12.8 2.8 %copy-start.1 = (bf16[1,96,6,128]{3,1,2,0:T(8,128)(2,1)S(1)}, bf16[1,96,6,128]{3,1,2,0:T(8,128)(2,1)}, u32[]{:S(2)}) copy-start(bf16[1,96,6,128]{3,1,2,0:T(8,128)(2,1)} %param.12) | copy-start | bytes 442372
  12.8 2.9 %copy-start.5 = (f32[96]{0:T(128)S(1)}, f32[96]{0:T(128)}, u32[]{:S(2)}) copy-start(f32[96]{0:T(128)} %param.21) | copy-start | bytes 1156
  12.8 2.9 %copy-start.7 = (bf16[384,96]{0,1:T(8,128)(2,1)S(1)}, bf16[384,96]{0,1:T(8,128)(2,1)}, u32[]{:S(2)}) copy-start(bf16[384,96]{0,1:T(8,128)(2,1)} %param.19) | copy-start | bytes 221188
  16.8 1.9 %copy-start.2 = (bf16[1,96,6,128]{3,1,2,0:T(8,128)(2,1)S(1)}, bf16[1,96,6,128]{3,1,2,0:T(8,128)(2,1)}, u32[]{:S(2)}) copy-start(bf16[1,96,6,128]{3,1,2,0:T(8,128)(2,1)} %param.11) | copy-start | bytes 442372
  20.5 0.8 %copy-start.10 = (f32[96]{0:T(128)S(1)}, f32[96]{0:T(128)}, u32[]{:S(2)}) copy-start(f32[96]{0:T(128)} %param.20) | copy-start | bytes 1156
  21.8 1.7 %collective-permute-start.2 = (f32[2,168,128]{2,1,0:T(8,128)S(1)}, f32[2,168,128]{2,1,0:T(8,128)S(1)}, u32[]{:S(2)}, u32[]{:S(2)}) collective-permute-start(f32[2,168,128]{2,1,0:T(8,128)S(1)} %constant_dynamic-slice_fusion.1), channel_id=1, source_target_pairs={{0,4},{4,0},{8,12},{12,8},{16,20},{20,16},{24,28},{28,24},{1,5},{5... | collective-permute-start | bytes 516104 | tf_op jit(solution)/shard_map/ppermute | solution.py:74
  23.6 4.9 %collective-permute-start.3 = (f32[1,168,128]{2,1,0:T(8,128)S(1)}, f32[1,168,128]{2,1,0:T(8,128)S(1)}, u32[]{:S(2)}, u32[]{:S(2)}) collective-permute-start(f32[1,168,128]{2,1,0:T(8,128)S(1)} %constant_dynamic-slice_fusion), channel_id=1, source_target_pairs={{0,8},{4,12},{8,0},{12,4},{16,24},{20,28},{24,16},{28,20},{1,9},{5... | collective-permute-start | bytes 258056 | tf_op jit(solution)/shard_map/ppermute | solution.py:74
  25.7 6.4 %collective-permute-start.8 = (f32[1,96,3,128]{3,1,2,0:T(8,128)S(1)}, f32[1,96,3,128]{3,1,2,0:T(8,128)S(1)}, u32[]{:S(2)}, u32[]{:S(2)}) collective-permute-start(f32[1,96,3,128]{3,1,2,0:T(8,128)S(1)} %get-tuple-element.97), channel_id=1, source_target_pairs={{4,8},{12,16},{20,24},{8,4},{16,12},{24,20},{5,9},{13,17},{21,25},... | collective-permute-start | bytes 442376 | tf_op jit(solution)/shard_map/ppermute | solution.py:33
  26.6 5.5 %collective-permute-start.9 = (f32[1,96,3,128]{3,1,2,0:T(8,128)S(1)}, f32[1,96,3,128]{3,1,2,0:T(8,128)S(1)}, u32[]{:S(2)}, u32[]{:S(2)}) collective-permute-start(f32[1,96,3,128]{3,1,2,0:T(8,128)S(1)} %get-tuple-element.98), channel_id=1, source_target_pairs={{0,4},{4,0},{8,12},{12,8},{16,20},{20,16},{24,28},{28,24},{1,5},{5... | collective-permute-start | bytes 442376 | tf_op jit(solution)/shard_map/ppermute | solution.py:32
  28.5 5.5 %collective-permute-start.6 = (f32[1,168,128]{2,1,0:T(8,128)S(1)}, f32[1,168,128]{2,1,0:T(8,128)S(1)}, u32[]{:S(2)}, u32[]{:S(2)}) collective-permute-start(f32[1,168,128]{2,1,0:T(8,128)S(1)} %dynamic-slice_add_fusion.1), channel_id=1, source_target_pairs={{0,3},{1,2},{2,1},{3,0},{4,7},{5,6},{6,5},{7,4},{8,11},{9,10},{10,... | collective-permute-start | bytes 258056 | tf_op jit(solution)/shard_map/ppermute | solution.py:80
  31.0 4.6 %collective-permute-start.5 = (f32[1,168,128]{2,1,0:T(8,128)S(1)}, f32[1,168,128]{2,1,0:T(8,128)S(1)}, u32[]{:S(2)}, u32[]{:S(2)}) collective-permute-start(f32[1,168,128]{2,1,0:T(8,128)S(1)} %dynamic-slice_add_fusion.1), channel_id=1, source_target_pairs={{0,2},{1,3},{2,0},{3,1},{4,6},{5,7},{6,4},{7,5},{8,10},{9,11},{10,... | collective-permute-start | bytes 258056 | tf_op jit(solution)/shard_map/ppermute | solution.py:80
  31.5 4.5 %collective-permute-start.4 = (f32[1,168,128]{2,1,0:T(8,128)S(1)}, f32[1,168,128]{2,1,0:T(8,128)S(1)}, u32[]{:S(2)}, u32[]{:S(2)}) collective-permute-start(f32[1,168,128]{2,1,0:T(8,128)S(1)} %dynamic-slice_add_fusion.1), channel_id=1, source_target_pairs={{0,1},{1,0},{2,3},{3,2},{4,5},{5,4},{6,7},{7,6},{8,9},{9,8},{10,11... | collective-permute-start | bytes 258056 | tf_op jit(solution)/shard_map/ppermute | solution.py:80
  36.1 6.4 %collective-permute-start.7 = (f32[1,168,128]{2,1,0:T(8,128)S(1)}, f32[1,168,128]{2,1,0:T(8,128)S(1)}, u32[]{:S(2)}, u32[]{:S(2)}) collective-permute-start(f32[1,168,128]{2,1,0:T(8,128)S(1)} %add_add_fusion), channel_id=1, source_target_pairs={{0,16},{4,20},{8,24},{12,28},{16,0},{20,4},{24,8},{28,12},{1,17},{... | collective-permute-start | bytes 258056 | tf_op jit(solution)/shard_map/ppermute | solution.py:80
  42.4 4.8 %collective-permute-start.10 = (f32[1,168,128]{2,1,0:T(8,128)S(1)}, f32[1,168,128]{2,1,0:T(8,128)S(1)}, u32[]{:S(2)}, u32[]{:S(2)}) collective-permute-start(f32[1,168,128]{2,1,0:T(8,128)S(1)} %add.152), channel_id=1, source_target_pairs={{0,8},{4,12},{8,0},{12,4},{16,24},{20,28},{24,16},{28,20},{1,9},{5... | collective-permute-start | bytes 258056 | tf_op jit(solution)/shard_map/ppermute | solution.py:90
  47.2 1.5 %collective-permute-start.11 = (f32[2,168,128]{2,1,0:T(8,128)S(1)}, f32[2,168,128]{2,1,0:T(8,128)S(1)}, u32[]{:S(2)}, u32[]{:S(2)}) collective-permute-start(f32[2,168,128]{2,1,0:T(8,128)S(1)} %pad_maximum_fusion.3), channel_id=1, source_target_pairs={{0,4},{4,0},{8,12},{12,8},{16,20},{20,16},{24,28},{28,24},{1,5},{5... | collective-permute-start | bytes 516104 | tf_op jit(solution)/shard_map/ppermute | solution.py:90

commit v18 on v17

--- a/solution.py
+++ b/solution.py
@@ -53,8 +53,7 @@
 def tree_psum(terms, side_fn, side_in):
     shapes = [t.shape for t in terms]
     sizes = [math.prod(s) for s in shapes]
-    rooms = [-(-size // 1024) * 1024 for size in sizes]
-    total = sum(rooms)
+    total = sum(sizes)
     strip_bits = low_bits(lax.axis_size("strip"))
     slide_bits = low_bits(lax.axis_size("slide"))
     scatter = [("strip", b) for b in strip_bits[:2]]
@@ -63,7 +62,8 @@
     pieces = 2 ** len(scatter)
     rows = -(-total // (pieces * 128))
     rows = -(-rows // 8) * 8
-    flat = jnp.concatenate([jnp.pad(t.reshape(-1), (0, room - size)) for t, size, room in zip(terms, sizes, rooms)])
+    order = sorted(range(len(terms)), key=lambda i: -sizes[i])
+    flat = jnp.concatenate([terms[i].reshape(-1) for i in order])
     flat = jnp.pad(flat, (0, pieces * rows * 128 - total)).reshape(pieces, rows, 128)
     for axis, bit in scatter:
         size = lax.axis_size(axis)
@@ -92,11 +92,11 @@
         high = jnp.where(mine == 0, got, flat)
         flat = jnp.concatenate([low, high], axis=0)
     flat = flat.reshape(-1)
-    out = []
+    out = [None] * len(terms)
     offset = 0
-    for shape, size, room in zip(shapes, sizes, rooms):
-        out.append(flat[offset : offset + size].reshape(shape))
-        offset += room
+    for i in order:
+        out[i] = flat[offset : offset + sizes[i]].reshape(shapes[i])
+        offset += sizes[i]
     return out, hold
 
 

time: 52.5 us -> 55 us (1.048)
  local copies, waits for them, and re-layouts: 7.86 us -> 9.45 us
  starting transfers between devices: 18.5 us -> 20 us
    ppermute x2, starting transfers between devices: 2.74 us -> 8.64 us  [tree_psum(): flat = keep + lax.ppermute(give, axis, xor_pairs(size, bit))]
    ppermute x1, starting transfers between devices: 4.47 us -> 0.56 us  [with_halo(): from_pair = lax.ppermute(paired, axis, [(i, i ^ 1) for i in range(size)])]
    concatenate x1, local copies, waits for them, and re-layouts: 0.01 us -> 1.74 us  [tree_psum(): flat = jnp.concatenate([terms[i].reshape(-1) for i in order])]
    transpose x2 -> x0, local copies, waits for them, and re-layouts: 1.28 us -> none  [the longest x1 0.67 us: on_device(): g[6] = g[6].T]
    reshape x3 -> x4, local copies, waits for them, and re-layouts: 0.72 us -> 1.41 us  [the longest x2 1.39 us: tree_psum(): out[i] = flat[offset:offset + sizes[i]].reshape(shapes[i])]
    ppermute x1, waiting for transfers between devices: 1.21 us -> 0.53 us  [with_halo(): from_pair = lax.ppermute(paired, axis, [(i, i ^ 1) for i in range(size)])]
    another operation x0 -> x1, local copies, waits for them, and re-layouts: none -> 0.68 us  [on_device(): g[0] = g[0].reshape(kernel, kernel, chans).transpose(2, 0, 1)]
    slice x5 -> x4, local copies, waits for them, and re-layouts: 1.46 us -> 1.27 us  [tree_psum(): out[i] = flat[offset:offset + sizes[i]].reshape(shapes[i])]
  transfers between devices with their start and end apart: 12 -> 12, of which waited for: 8 -> 8; matrix products, arithmetic and copies ran while one was open for 9% -> 7% of each run, Pallas kernels for 0% -> 0%
where the time goes in v18:
time: 55 us; the launch traced here: 54.7 us
  starting transfers between devices  20 us (36%)
  waiting for transfers between devices  10.2 us (19%)
  local copies, waits for them, and re-layouts  9.45 us (17%)
  matrix products  7.93 us (14%)
  other arithmetic  5.94 us (11%)
  between operations  1.18 us (2%)
    ppermute x2, starting transfers between devices, tree_psum(): flat = keep + lax.ppermute(give, axis, xor_pairs(size, bit))  8.64 us
    ppermute x4, waiting for transfers between devices, tree_psum(): got = [lax.ppermute(flat, axis, xor_pairs(size, mask)) for mask in masks]  7.44 us
    ppermute x4, starting transfers between devices, tree_psum(): got = [lax.ppermute(flat, axis, xor_pairs(size, mask)) for mask in masks]  6.21 us
    reduce_sum x4, other arithmetic, on_device(): jnp.sum(d_conv * padded[:, :, a:a + rows, b:b + cols], axis=(0, 2, 3))  3.23 us
    dot_general x1, matrix products, on_device(): jnp.einsum('scrw,cf->sfrw', lifted, up_weight, preferred_element_type=jnp...  2.83 us
    unnamed x28, local copies, waits for them, and re-layouts  2.56 us
    concatenate x1, local copies, waits for them, and re-layouts, tree_psum(): flat = jnp.concatenate([terms[i].reshape(-1) for i in order])  1.74 us
    ppermute x2, waiting for transfers between devices, tree_psum(): flat = keep + lax.ppermute(give, axis, xor_pairs(size, bit))  1.65 us
  transfers between devices with their start and end apart: 12, of which 8 were waited for; matrix products, arithmetic and copies ran while one was open for 7% of the time, Pallas kernels for 0%

profile of v18, /device:TPU:0, one launch (start us, length us, event | category | flops | bytes accessed | tf_op | source)
XLA Modules:
  0.0 54.7 jit_solution(1401408311942534355)
XLA Ops:
  0.7 1.1 %convert_reduce_fusion.1 = f32[96]{0:T(128)S(1)} fusion(bf16[1,96,6,128]{3,1,2,0:T(8,128)(2,1)} %param.12, f32[96]{0:T(128)} %param.21), kind=kLoop, calls=%fused_computation.164 | loop fusion | flops 368544 | bytes 148224 | tf_op jit(solution)/shard_map/reduce_sum | solution.py:129
  1.8 0.6 %collective-permute-start.1 = (bf16[1,96,6,128]{3,1,2,0:T(8,128)(2,1)}, bf16[1,96,6,128]{3,1,2,0:T(8,128)(2,1)S(1)}, u32[]{:S(2)}, u32[]{:S(2)}) collective-permute-start(bf16[1,96,6,128]{3,1,2,0:T(8,128)(2,1)} %param.11), channel_id=1, source_target_pairs={{0,4},{4,0},{8,12},{12,8},{16,20},{20,16},{24,28},{28,24},{1,5},{5... | collective-permute-start | bytes 442376 | tf_op jit(solution)/shard_map/ppermute | solution.py:19
  2.4 0.7 %collective-permute-start = (bf16[1,96,6,128]{3,1,2,0:T(8,128)(2,1)}, bf16[1,96,6,128]{3,1,2,0:T(8,128)(2,1)S(1)}, u32[]{:S(2)}, u32[]{:S(2)}) collective-permute-start(bf16[1,96,6,128]{3,1,2,0:T(8,128)(2,1)} %param.11), channel_id=1, source_target_pairs={{4,8},{12,16},{20,24},{8,4},{16,12},{24,20},{5,9},{13,17},{21,25},... | collective-permute-start | bytes 442376 | tf_op jit(solution)/shard_map/ppermute | solution.py:15
  3.0 0.5 collective-permute-done.1
  3.6 1.0 %pad_maximum_fusion.2 = (bf16[1,96,12,128]{3,1,2,0:T(8,128)(2,1)S(1)}, bf16[96,12,1,128]{3,0,1,2:T(8,128)(2,1)S(1)}) fusion(bf16[1,96,3,128]{3,1,2,0:T(8,128)(2,1)S(1)} %get-tuple-element.104, bf16[1,96,6,128]{3,1,2,0:T(8,128)(2,1)} %param.11, bf16[1,96,3,128]{3,1,2,0:T(8,128)(2,1)S(1)} %get-tuple-element.103), kind=kLoop, calls=%fused_computation.103 | loop fusion | flops 294912 | bytes 884736 | tf_op jit(solution)/shard_map/concatenate | solution.py:25
  4.6 0.2 copy.51
  5.2 0.5 copy-done.3
  5.7 1.5 %fusion.19 = f32[6,8,17,96]{3,1,2,0:T(8,128)S(1)} fusion(bf16[96,12,1,7,6]{0,3,4,1,2:T(8,128)(2,1)S(1)} %slice.266, bf16[96,12,1,8,17]{0,3,4,1,2:T(8,128)(2,1)S(1)} %copy.31, f32[96]{0:T(128)S(1)} %copy-done.9, pred[8,17]{0,1:T(8,128)(4,1)S(1)} %copy-done.11, f32[96,1,7,7]{0,3,2,1:T(8,128)S(1)} %bitcast.186), kind=kOutput, calls=%fused_computation.76 | convolution fusion | flops 47490048 | bytes 742792 | tf_op jit(solution)/shard_map/conv_general_dilated | solution.py:133
  7.4 0.2 copy.50
  7.7 0.3 copy-done.4
  8.1 2.8 %fusion.9 = (bf16[384,6,128]{0,2,1:T(8,128)(2,1)S(1)}, f32[384,6,128]{0,2,1:T(8,128)S(1)}) fusion(f32[384]{0:T(512)S(1)} %copy-done.8, bf16[96,384]{1,0:T(8,128)(2,1)S(1)} %copy-done, f32[6,1,128,96]{2,3,0,1:T(8,128)S(1)} %copy.50, f32[96]{0:T(128)S(1)} %copy-done.6, f32[96]{0:T(128)S(1)} %copy-done.4, f32[6,128]{1,0:T(8,128)S(1)} %add_rsqrt_fusion, ...), kind=kOutput, calls=%fused_computation.55 | convolution fusion | flops 76455936 | bytes 2146560 | tf_op jit(solution)/shard_map/scrw,cf->sfrw/dot_general | solution.py:149
  10.9 0.7 %convert_reduce_fusion = (f32[384]{0:T(512)S(1)}, bf16[384,6,128]{0,2,1:T(8,128)(2,1)S(1)}) fusion(f32[384,6,128]{0,2,1:T(8,128)S(1)} %get-tuple-element.108, bf16[384,96]{0,1:T(8,128)(2,1)S(1)} %copy-done.7, bf16[1,96,6,128]{3,1,2,0:T(8,128)(2,1)S(1)} %copy-done.1, f32[96]{0:T(128)S(1)} %copy-done.5), kind=kOutput, calls=%fused_computation.56 | convolution fusion | flops 60382848 | bytes 1992576 | tf_op jit(solution)/shard_map/scrw,fc->sfrw/dot_general | solution.py:157
  11.7 0.3 fusion.21
  12.0 0.4 fusion.39
  12.5 1.2 %multiply_reduce_fusion = (f32[96]{0:T(128)S(1)}, f32[96]{0:T(128)S(1)}, f32[96]{0:T(128)S(1)}, f32[96]{0:T(128)S(1)}, f32[96]{0:T(128)S(1)}, /*index=5*/f32[96]...) fusion(bf16[1,96,12,128]{3,1,2,0:T(8,128)(2,1)S(1)} %get-tuple-, ...), kind=kLoop, calls=%fused_computation.113 | loop fusion | flops 4495680 | bytes 1199232 | tf_op jit(solution)/shard_map/reduce_sum | solution.py:183
  13.8 0.5 multiply_reduce_fusion.42
  14.3 0.3 multiply_reduce_fusion.3
  14.6 1.2 %multiply_reduce_fusion.21 = (f32[96]{0:T(128)S(1)}, f32[96]{0:T(128)S(1)}, f32[96]{0:T(128)S(1)}, f32[96]{0:T(128)S(1)}, f32[96]{0:T(128)S(1)}, /*index=5*/f32[...) fusion(f32[1,96,6,128]{3,1,2,0:T(8,128)S(1)} %get-tuple-element, ...), kind=kLoop, calls=%fused_computation.134 | loop fusion | flops 3979584 | bytes 596736 | tf_op jit(solution)/shard_map/reduce_sum | solution.py:183
  15.8 0.3 fusion.22
  16.1 0.1 stack.199
  16.5 0.4 fusion.20
  16.9 1.7 %concatenate.28 = f32[79296]{0:T(1024)S(1)} concatenate(f32[36864]{0:T(1024)S(1)} %reshape.210, f32[36864]{0:T(1024)S(1)} %reshape.211, f32[4704]{0:T(1024)S(1)} %mul.363, f32[384]{0:T(512)S(1)} %broadcast_multiply_fusion.4, f32[96]{0:T(128)S(1)} %broadcast_multiply_fusion.9, f32[96]{0:T(128)S(1)} %get-tuple-element.117, f32[96]{0:T(128)S(1)} %get-tuple-element.116, ...), dimensions={0} | concatenate | bytes 634368 | tf_op jit(solution)/shard_map/concatenate | solution.py:66
  18.7 6.5 %collective-permute-start.2 = (f32[2,160,128]{2,1,0:T(8,128)S(1)}, f32[2,160,128]{2,1,0:T(8,128)S(1)}, u32[]{:S(2)}, u32[]{:S(2)}) collective-permute-start(f32[2,160,128]{2,1,0:T(8,128)S(1)} %constant_dynamic-slice_fusion.1), channel_id=1, source_target_pairs={{0,4},{4,0},{8,12},{12,8},{16,20},{20,16},{24,28},{28,24},{1,5},{5... | collective-permute-start | bytes 491528 | tf_op jit(solution)/shard_map/ppermute | solution.py:74
  25.2 1.0 %collective-permute-done.2 = f32[2,160,128]{2,1,0:T(8,128)S(1)} collective-permute-done((f32[2,160,128]{2,1,0:T(8,128)S(1)}, f32[2,160,128]{2,1,0:T(8,128)S(1)}, u32[]{:S(2)}, u32[]{:S(2)}) %collective-permute-start.2) | collective-permute-done | bytes 163872 | tf_op jit(solution)/shard_map/ppermute | solution.py:74
  26.3 2.2 %collective-permute-start.3 = (f32[1,160,128]{2,1,0:T(8,128)S(1)}, f32[1,160,128]{2,1,0:T(8,128)S(1)}, u32[]{:S(2)}, u32[]{:S(2)}) collective-permute-start(f32[1,160,128]{2,1,0:T(8,128)S(1)} %constant_dynamic-slice_fusion), channel_id=1, source_target_pairs={{0,8},{4,12},{8,0},{12,4},{16,24},{20,28},{24,16},{28,20},{1,9},{5... | collective-permute-start | bytes 245768 | tf_op jit(solution)/shard_map/ppermute | solution.py:74
  28.5 0.9 %collective-permute-start.8 = (f32[1,96,3,128]{3,1,2,0:T(8,128)S(1)}, f32[1,96,3,128]{3,1,2,0:T(8,128)S(1)}, u32[]{:S(2)}, u32[]{:S(2)}) collective-permute-start(f32[1,96,3,128]{3,1,2,0:T(8,128)S(1)} %get-tuple-element.99), channel_id=1, source_target_pairs={{4,8},{12,16},{20,24},{8,4},{16,12},{24,20},{5,9},{13,17},{21,25},... | collective-permute-start | bytes 442376 | tf_op jit(solution)/shard_map/ppermute | solution.py:33
  29.3 1.4 %collective-permute-start.9 = (f32[1,96,3,128]{3,1,2,0:T(8,128)S(1)}, f32[1,96,3,128]{3,1,2,0:T(8,128)S(1)}, u32[]{:S(2)}, u32[]{:S(2)}) collective-permute-start(f32[1,96,3,128]{3,1,2,0:T(8,128)S(1)} %get-tuple-element.100), channel_id=1, source_target_pairs={{0,4},{4,0},{8,12},{12,8},{16,20},{20,16},{24,28},{28,24},{1,5},{5... | collective-permute-start | bytes 442376 | tf_op jit(solution)/shard_map/ppermute | solution.py:32
  30.8 0.7 %collective-permute-done.3 = f32[1,160,128]{2,1,0:T(8,128)S(1)} collective-permute-done((f32[1,160,128]{2,1,0:T(8,128)S(1)}, f32[1,160,128]{2,1,0:T(8,128)S(1)}, u32[]{:S(2)}, u32[]{:S(2)}) %collective-permute-start.3) | collective-permute-done | bytes 81952 | tf_op jit(solution)/shard_map/ppermute | solution.py:74
  31.4 2.7 %collective-permute-start.6 = (f32[1,160,128]{2,1,0:T(8,128)S(1)}, f32[1,160,128]{2,1,0:T(8,128)S(1)}, u32[]{:S(2)}, u32[]{:S(2)}) collective-permute-start(f32[1,160,128]{2,1,0:T(8,128)S(1)} %dynamic-slice_add_fusion.1), channel_id=1, source_target_pairs={{0,3},{1,2},{2,1},{3,0},{4,7},{5,6},{6,5},{7,4},{8,11},{9,10},{10,... | collective-permute-start | bytes 245768 | tf_op jit(solution)/shard_map/ppermute | solution.py:80
  34.1 0.5 collective-permute-start.5
  34.6 0.4 collective-permute-start.4
  35.0 1.9 %collective-permute-done.6 = f32[1,160,128]{2,1,0:T(8,128)S(1)} collective-permute-done((f32[1,160,128]{2,1,0:T(8,128)S(1)}, f32[1,160,128]{2,1,0:T(8,128)S(1)}, u32[]{:S(2)}, u32[]{:S(2)}) %collective-permute-start.6) | collective-permute-done | bytes 81952 | tf_op jit(solution)/shard_map/ppermute | solution.py:80
  36.9 1.7 %collective-permute-done.5 = f32[1,160,128]{2,1,0:T(8,128)S(1)} collective-permute-done((f32[1,160,128]{2,1,0:T(8,128)S(1)}, f32[1,160,128]{2,1,0:T(8,128)S(1)}, u32[]{:S(2)}, u32[]{:S(2)}) %collective-permute-start.5) | collective-permute-done | bytes 81952 | tf_op jit(solution)/shard_map/ppermute | solution.py:80
  38.6 0.5 collective-permute-done.4
  39.1 2.7 %collective-permute-start.7 = (f32[1,160,128]{2,1,0:T(8,128)S(1)}, f32[1,160,128]{2,1,0:T(8,128)S(1)}, u32[]{:S(2)}, u32[]{:S(2)}) collective-permute-start(f32[1,160,128]{2,1,0:T(8,128)S(1)} %add_add_fusion), channel_id=1, source_target_pairs={{0,16},{4,20},{8,24},{12,28},{16,0},{20,4},{24,8},{28,12},{1,17},{... | collective-permute-start | bytes 245768 | tf_op jit(solution)/shard_map/ppermute | solution.py:80
  41.8 3.4 %collective-permute-done.7 = f32[1,160,128]{2,1,0:T(8,128)S(1)} collective-permute-done((f32[1,160,128]{2,1,0:T(8,128)S(1)}, f32[1,160,128]{2,1,0:T(8,128)S(1)}, u32[]{:S(2)}, u32[]{:S(2)}) %collective-permute-start.7) | collective-permute-done | bytes 81952 | tf_op jit(solution)/shard_map/ppermute | solution.py:80
  45.2 1.6 %collective-permute-start.10 = (f32[1,160,128]{2,1,0:T(8,128)S(1)}, f32[1,160,128]{2,1,0:T(8,128)S(1)}, u32[]{:S(2)}, u32[]{:S(2)}) collective-permute-start(f32[1,160,128]{2,1,0:T(8,128)S(1)} %add.138), channel_id=1, source_target_pairs={{0,8},{4,12},{8,0},{12,4},{16,24},{20,28},{24,16},{28,20},{1,9},{5... | collective-permute-start | bytes 245768 | tf_op jit(solution)/shard_map/ppermute | solution.py:90
  46.8 0.5 copy.52
  47.3 0.6 %pad.12.clone = f32[96,12,1,136]{0,2,3,1:T(1,128)S(1)} pad(f32[96,12,1,128]{0,2,3,1:T(1,128)S(1)} %copy.52, f32[]{:T(128)} %constant.112.clone.1), padding=0_0x0_0x0_0x3_5 | pad | bytes 1216516 | tf_op jit(solution)/shard_map/optimization_barrier | solution.py:83
  47.9 1.4 %convolution_select_fusion.1 = f32[6,8,17,96]{3,1,2,0:T(8,128)S(1)} fusion(f32[96,12,1,7,6]{0,3,4,1,2:T(8,128)S(1)} %slice.278, f32[96,12,1,8,17]{0,3,4,1,2:T(8,128)S(1)} %copy.42, pred[8,17]{0,1:T(8,128)(4,1)S(1)} %copy-done.11, f32[96,1,7,7]{0,3,2,1:T(8,128)S(1)} %bitcast.187), kind=kOutput, calls=%fused_computation.77 | convolution fusion | flops 46775808 | bytes 1152520 | tf_op jit(solution)/shard_map/conv_general_dilated | solution.py:168
  49.5 0.2 copy.39
  49.9 0.8 %copy.45 = bf16[1,96,6,128]{3,1,2,0:T(8,128)(2,1)} copy(bf16[1,96,6,128]{1,3,2,0:T(8,128)(2,1)S(1)} %fusion.37) | data formatting | bytes 294912
  50.7 0.6 %collective-permute-done.11 = f32[2,160,128]{2,1,0:T(8,128)S(1)} collective-permute-done((f32[2,160,128]{2,1,0:T(8,128)S(1)}, f32[2,160,128]{2,1,0:T(8,128)S(1)}, u32[]{:S(2)}, u32[]{:S(2)}) %collective-permute-start.11) | collective-permute-done | bytes 163872 | tf_op jit(solution)/shard_map/ppermute | solution.py:90
  51.4 0.6 %fusion.71 = (f32[96]{0:T(128)}, f32[96]{0:T(128)}, f32[96]{0:T(128)}, f32[96]{0:T(128)}, f32[96]{0:T(128)}) fusion(f32[81920]{0:T(1024)S(1)} %bitcast.182), kind=kLoop, calls=%fused_computation.226 | loop fusion | bytes 3840 | tf_op jit(solution)/shard_map/slice | solution.py:98
  52.0 0.6 %slice.285 = f32[384]{0:T(512)} slice(f32[81920]{0:T(1024)S(1)} %bitcast.184), slice={[78432:78816]} | slice | bytes 3072 | tf_op jit(solution)/shard_map/slice | solution.py:98
  52.6 0.7 %reshape_reshape.3 = f32[7,7,96]{2,1,0:T(8,128)} reshape(f32[4704]{0:T(1024)S(1)} %slice.280) | data formatting | bytes 37632 | tf_op jit(solution)/shard_map/reshape;reshape | solution.py:200
  53.3 0.7 %reshape.214 = f32[96,384]{1,0:T(8,128)} reshape(f32[36864]{0:T(1024)S(1)} %get-tuple-element.94) | data formatting | bytes 294912 | tf_op jit(solution)/shard_map/reshape | solution.py:98
  54.0 0.7 %reshape.215 = f32[96,384]{1,0:T(8,128)} reshape(f32[36864]{0:T(1024)S(1)} %get-tuple-element.93) | data formatting | bytes 294912 | tf_op jit(solution)/shard_map/reshape | solution.py:98
  (72 shorter events, 1.8 us)
Async XLA Ops:
  0.6 7.1 %copy-start = (bf16[96,384]{1,0:T(8,128)(2,1)S(1)}, bf16[96,384]{1,0:T(8,128)(2,1)}, u32[]{:S(2)}) copy-start(bf16[96,384]{1,0:T(8,128)(2,1)} %param.17) | copy-start | bytes 221188
  1.8 1.8 %collective-permute-start.1 = (bf16[1,96,6,128]{3,1,2,0:T(8,128)(2,1)}, bf16[1,96,6,128]{3,1,2,0:T(8,128)(2,1)S(1)}, u32[]{:S(2)}, u32[]{:S(2)}) collective-permute-start(bf16[1,96,6,128]{3,1,2,0:T(8,128)(2,1)} %param.11), channel_id=1, source_target_pairs={{0,4},{4,0},{8,12},{12,8},{16,20},{20,16},{24,28},{28,24},{1,5},{5... | collective-permute-start | bytes 442376 | tf_op jit(solution)/shard_map/ppermute | solution.py:19
  2.4 1.2 %collective-permute-start = (bf16[1,96,6,128]{3,1,2,0:T(8,128)(2,1)}, bf16[1,96,6,128]{3,1,2,0:T(8,128)(2,1)S(1)}, u32[]{:S(2)}, u32[]{:S(2)}) collective-permute-start(bf16[1,96,6,128]{3,1,2,0:T(8,128)(2,1)} %param.11), channel_id=1, source_target_pairs={{4,8},{12,16},{20,24},{8,4},{16,12},{24,20},{5,9},{13,17},{21,25},... | collective-permute-start | bytes 442376 | tf_op jit(solution)/shard_map/ppermute | solution.py:15
  4.9 0.8 %copy-start.3 = (f32[96,7,7]{0,2,1:T(8,128)S(1)}, f32[96,7,7]{0,2,1:T(8,128)}, u32[]{:S(2)}) copy-start(f32[96,7,7]{0,2,1:T(8,128)} %param.13) | copy-start | bytes 56452
  5.0 0.7 %copy-start.9 = (f32[96]{0:T(128)S(1)}, f32[96]{0:T(128)}, u32[]{:S(2)}) copy-start(f32[96]{0:T(128)} %param.14) | copy-start | bytes 1156
  5.0 0.7 %copy-start.11 = (pred[8,17]{0,1:T(8,128)(4,1)S(1)}, pred[8,17]{0,1:T(8,128)(4,1)}, u32[]{:S(2)}) copy-start(pred[8,17]{0,1:T(8,128)(4,1)} %constant.164) | copy-start | bytes 412
  7.4 0.7 %copy-start.4 = (f32[96]{0:T(128)S(1)}, f32[96]{0:T(128)}, u32[]{:S(2)}) copy-start(f32[96]{0:T(128)} %param.15) | copy-start | bytes 1156
  7.4 0.7 %copy-start.6 = (f32[96]{0:T(128)S(1)}, f32[96]{0:T(128)}, u32[]{:S(2)}) copy-start(f32[96]{0:T(128)} %param.16) | copy-start | bytes 1156
  7.4 0.7 %copy-start.8 = (f32[384]{0:T(512)S(1)}, f32[384]{0:T(512)}, u32[]{:S(2)}) copy-start(f32[384]{0:T(512)} %param.18) | copy-start | bytes 4612
  8.1 2.8 %copy-start.1 = (bf16[1,96,6,128]{3,1,2,0:T(8,128)(2,1)S(1)}, bf16[1,96,6,128]{3,1,2,0:T(8,128)(2,1)}, u32[]{:S(2)}) copy-start(bf16[1,96,6,128]{3,1,2,0:T(8,128)(2,1)} %param.12) | copy-start | bytes 442372
  8.1 2.9 %copy-start.5 = (f32[96]{0:T(128)S(1)}, f32[96]{0:T(128)}, u32[]{:S(2)}) copy-start(f32[96]{0:T(128)} %param.21) | copy-start | bytes 1156
  8.1 2.9 %copy-start.7 = (bf16[384,96]{0,1:T(8,128)(2,1)S(1)}, bf16[384,96]{0,1:T(8,128)(2,1)}, u32[]{:S(2)}) copy-start(bf16[384,96]{0,1:T(8,128)(2,1)} %param.19) | copy-start | bytes 221188
  12.4 1.9 %copy-start.2 = (bf16[1,96,6,128]{3,1,2,0:T(8,128)(2,1)S(1)}, bf16[1,96,6,128]{3,1,2,0:T(8,128)(2,1)}, u32[]{:S(2)}) copy-start(bf16[1,96,6,128]{3,1,2,0:T(8,128)(2,1)} %param.11) | copy-start | bytes 442372
  15.8 0.7 %copy-start.10 = (f32[96]{0:T(128)S(1)}, f32[96]{0:T(128)}, u32[]{:S(2)}) copy-start(f32[96]{0:T(128)} %param.20) | copy-start | bytes 1156
  18.7 7.5 %collective-permute-start.2 = (f32[2,160,128]{2,1,0:T(8,128)S(1)}, f32[2,160,128]{2,1,0:T(8,128)S(1)}, u32[]{:S(2)}, u32[]{:S(2)}) collective-permute-start(f32[2,160,128]{2,1,0:T(8,128)S(1)} %constant_dynamic-slice_fusion.1), channel_id=1, source_target_pairs={{0,4},{4,0},{8,12},{12,8},{16,20},{20,16},{24,28},{28,24},{1,5},{5... | collective-permute-start | bytes 491528 | tf_op jit(solution)/shard_map/ppermute | solution.py:74
  26.3 5.1 %collective-permute-start.3 = (f32[1,160,128]{2,1,0:T(8,128)S(1)}, f32[1,160,128]{2,1,0:T(8,128)S(1)}, u32[]{:S(2)}, u32[]{:S(2)}) collective-permute-start(f32[1,160,128]{2,1,0:T(8,128)S(1)} %constant_dynamic-slice_fusion), channel_id=1, source_target_pairs={{0,8},{4,12},{8,0},{12,4},{16,24},{20,28},{24,16},{28,20},{1,9},{5... | collective-permute-start | bytes 245768 | tf_op jit(solution)/shard_map/ppermute | solution.py:74
  28.5 6.5 %collective-permute-start.8 = (f32[1,96,3,128]{3,1,2,0:T(8,128)S(1)}, f32[1,96,3,128]{3,1,2,0:T(8,128)S(1)}, u32[]{:S(2)}, u32[]{:S(2)}) collective-permute-start(f32[1,96,3,128]{3,1,2,0:T(8,128)S(1)} %get-tuple-element.99), channel_id=1, source_target_pairs={{4,8},{12,16},{20,24},{8,4},{16,12},{24,20},{5,9},{13,17},{21,25},... | collective-permute-start | bytes 442376 | tf_op jit(solution)/shard_map/ppermute | solution.py:33
  29.3 5.7 %collective-permute-start.9 = (f32[1,96,3,128]{3,1,2,0:T(8,128)S(1)}, f32[1,96,3,128]{3,1,2,0:T(8,128)S(1)}, u32[]{:S(2)}, u32[]{:S(2)}) collective-permute-start(f32[1,96,3,128]{3,1,2,0:T(8,128)S(1)} %get-tuple-element.100), channel_id=1, source_target_pairs={{0,4},{4,0},{8,12},{12,8},{16,20},{20,16},{24,28},{28,24},{1,5},{5... | collective-permute-start | bytes 442376 | tf_op jit(solution)/shard_map/ppermute | solution.py:32
  31.4 5.5 %collective-permute-start.6 = (f32[1,160,128]{2,1,0:T(8,128)S(1)}, f32[1,160,128]{2,1,0:T(8,128)S(1)}, u32[]{:S(2)}, u32[]{:S(2)}) collective-permute-start(f32[1,160,128]{2,1,0:T(8,128)S(1)} %dynamic-slice_add_fusion.1), channel_id=1, source_target_pairs={{0,3},{1,2},{2,1},{3,0},{4,7},{5,6},{6,5},{7,4},{8,11},{9,10},{10,... | collective-permute-start | bytes 245768 | tf_op jit(solution)/shard_map/ppermute | solution.py:80
  34.1 4.5 %collective-permute-start.5 = (f32[1,160,128]{2,1,0:T(8,128)S(1)}, f32[1,160,128]{2,1,0:T(8,128)S(1)}, u32[]{:S(2)}, u32[]{:S(2)}) collective-permute-start(f32[1,160,128]{2,1,0:T(8,128)S(1)} %dynamic-slice_add_fusion.1), channel_id=1, source_target_pairs={{0,2},{1,3},{2,0},{3,1},{4,6},{5,7},{6,4},{7,5},{8,10},{9,11},{10,... | collective-permute-start | bytes 245768 | tf_op jit(solution)/shard_map/ppermute | solution.py:80
  34.6 4.4 %collective-permute-start.4 = (f32[1,160,128]{2,1,0:T(8,128)S(1)}, f32[1,160,128]{2,1,0:T(8,128)S(1)}, u32[]{:S(2)}, u32[]{:S(2)}) collective-permute-start(f32[1,160,128]{2,1,0:T(8,128)S(1)} %dynamic-slice_add_fusion.1), channel_id=1, source_target_pairs={{0,1},{1,0},{2,3},{3,2},{4,5},{5,4},{6,7},{7,6},{8,9},{9,8},{10,11... | collective-permute-start | bytes 245768 | tf_op jit(solution)/shard_map/ppermute | solution.py:80
  39.1 6.1 %collective-permute-start.7 = (f32[1,160,128]{2,1,0:T(8,128)S(1)}, f32[1,160,128]{2,1,0:T(8,128)S(1)}, u32[]{:S(2)}, u32[]{:S(2)}) collective-permute-start(f32[1,160,128]{2,1,0:T(8,128)S(1)} %add_add_fusion), channel_id=1, source_target_pairs={{0,16},{4,20},{8,24},{12,28},{16,0},{20,4},{24,8},{28,12},{1,17},{... | collective-permute-start | bytes 245768 | tf_op jit(solution)/shard_map/ppermute | solution.py:80
  45.2 4.6 %collective-permute-start.10 = (f32[1,160,128]{2,1,0:T(8,128)S(1)}, f32[1,160,128]{2,1,0:T(8,128)S(1)}, u32[]{:S(2)}, u32[]{:S(2)}) collective-permute-start(f32[1,160,128]{2,1,0:T(8,128)S(1)} %add.138), channel_id=1, source_target_pairs={{0,8},{4,12},{8,0},{12,4},{16,24},{20,28},{24,16},{28,20},{1,9},{5... | collective-permute-start | bytes 245768 | tf_op jit(solution)/shard_map/ppermute | solution.py:90
  49.8 1.5 %collective-permute-start.11 = (f32[2,160,128]{2,1,0:T(8,128)S(1)}, f32[2,160,128]{2,1,0:T(8,128)S(1)}, u32[]{:S(2)}, u32[]{:S(2)}) collective-permute-start(f32[2,160,128]{2,1,0:T(8,128)S(1)} %pad_maximum_fusion.3), channel_id=1, source_target_pairs={{0,4},{4,0},{8,12},{12,8},{16,20},{20,16},{24,28},{28,24},{1,5},{5... | collective-permute-start | bytes 491528 | tf_op jit(solution)/shard_map/ppermute | solution.py:90

commit v19 on v17

--- a/solution.py
+++ b/solution.py
@@ -128,6 +128,8 @@
     d_branch = (layer_scale[None, :, None, None] * upstream).astype(jnp.bfloat16)
     d_branch_sum = jnp.sum(d_branch.astype(jnp.float32), axis=(0, 2, 3))
     extended = with_halo(images, (("strip", 2),), 3, whole=True, pair_after=d_branch_sum)
+    d_act = jnp.einsum("scrw,fc->sfrw", d_branch, down_weight, preferred_element_type=jnp.float32)
+    extended, d_act = lax.optimization_barrier((extended, d_act))
     upstream = cotangent.astype(jnp.float32)
     padded = jnp.pad(extended, ((0, 0), (0, 0), (0, 0), (3, 3)))
     conv = lax.conv_general_dilated(
@@ -154,7 +156,6 @@
         jnp.einsum("sfrw,fc->scrw", act, down_weight, preferred_element_type=jnp.float32)
         + down_bias[None, :, None, None]
     )
-    d_act = jnp.einsum("scrw,fc->sfrw", d_branch, down_weight, preferred_element_type=jnp.float32)
     d_pre = (d_act * gelu_slope(pre)).astype(jnp.bfloat16)
     d_lifted = jnp.einsum("sfrw,cf->scrw", d_pre, up_weight, preferred_element_type=jnp.float32)
     d_normed = d_lifted * norm_gain[None, :, None, None]

time: 52.5 us -> 53.8 us (1.025)
  starting transfers between devices: 18.5 us -> 16.5 us
  other arithmetic: 5.94 us -> 7.42 us
  matrix products: 7.93 us -> 9 us
  waiting for transfers between devices: 10.7 us -> 11.5 us
    convert_element_type x0 -> x1, other arithmetic: none -> 2.6 us  [on_device(): act = jax.nn.gelu(pre, approximate=False).astype(jnp.bfloat16)]
    dot_general x1, matrix products: 0.73 us -> 2.4 us  [on_device(): jnp.einsum('scrw,fc->sfrw', d_branch, down_weight, preferred_element_type...]
    ppermute x2, starting transfers between devices: 1.84 us -> 0.54 us  [tree_psum(): got = lax.ppermute(flat, axis, xor_pairs(size, bit))]
    ppermute x1, waiting for transfers between devices: 1.21 us -> 0.01 us  [with_halo(): from_pair = lax.ppermute(paired, axis, [(i, i ^ 1) for i in range(size)])]
    ppermute x2, waiting for transfers between devices: 0.59 us -> 1.62 us  [tree_psum(): got = lax.ppermute(flat, axis, xor_pairs(size, bit))]
    ppermute x2, starting transfers between devices: 2.74 us -> 1.75 us  [tree_psum(): flat = keep + lax.ppermute(give, axis, xor_pairs(size, bit))]
    concatenate x2, other arithmetic: 1 us -> 0.08 us  [with_halo(): array = jnp.concatenate([before, array, after], axis=dim)]
    ppermute x4, waiting for transfers between devices: 7.42 us -> 8.29 us  [tree_psum(): got = [lax.ppermute(flat, axis, xor_pairs(size, mask)) for mask in masks]]
  transfers between devices with their start and end apart: 12 -> 12, of which waited for: 8 -> 8; matrix products, arithmetic and copies ran while one was open for 9% -> 14% of each run, Pallas kernels for 0% -> 0%
where the time goes in v19:
time: 53.8 us; the launch traced here: 53.5 us
  starting transfers between devices  16.5 us (31%)
  waiting for transfers between devices  11.5 us (21%)
  matrix products  9 us (17%)
  local copies, waits for them, and re-layouts  7.87 us (15%)
  other arithmetic  7.42 us (14%)
  between operations  1.27 us (2%)
    ppermute x4, waiting for transfers between devices, tree_psum(): got = [lax.ppermute(flat, axis, xor_pairs(size, mask)) for mask in masks]  8.29 us
    ppermute x4, starting transfers between devices, tree_psum(): got = [lax.ppermute(flat, axis, xor_pairs(size, mask)) for mask in masks]  6.21 us
    ppermute x1, starting transfers between devices, with_halo(): from_pair = lax.ppermute(paired, axis, [(i, i ^ 1) for i in range(size)])  4.47 us
    reduce_sum x3, other arithmetic, on_device(): jnp.sum(d_conv * padded[:, :, a:a + rows, b:b + cols], axis=(0, 2, 3))  3.03 us
    unnamed x36, local copies, waits for them, and re-layouts  2.62 us
    convert_element_type x1, other arithmetic, on_device(): act = jax.nn.gelu(pre, approximate=False).astype(jnp.bfloat16)  2.6 us
    dot_general x1, matrix products, on_device(): jnp.einsum('scrw,fc->sfrw', d_branch, down_weight, preferred_element_type...  2.4 us
    dot_general x1, matrix products, on_device(): jnp.einsum('scrw,cf->sfrw', lifted, up_weight, preferred_element_type=jnp...  2.13 us
  transfers between devices with their start and end apart: 12, of which 8 were waited for; matrix products, arithmetic and copies ran while one was open for 14% of the time, Pallas kernels for 0%

profile of v19, /device:TPU:0, one launch (start us, length us, event | category | flops | bytes accessed | tf_op | source)
XLA Modules:
  0.0 53.5 jit_solution(5794584874765168925)
XLA Ops:
  0.7 0.8 %collective-permute-start = (bf16[1,96,6,128]{3,1,2,0:T(8,128)(2,1)}, bf16[1,96,6,128]{3,1,2,0:T(8,128)(2,1)S(1)}, u32[]{:S(2)}, u32[]{:S(2)}) collective-permute-start(bf16[1,96,6,128]{3,1,2,0:T(8,128)(2,1)} %param.11), channel_id=1, source_target_pairs={{4,8},{12,16},{20,24},{8,4},{16,12},{24,20},{5,9},{13,17},{21,25},... | collective-permute-start | bytes 442376 | tf_op jit(solution)/shard_map/ppermute | solution.py:15
  1.5 1.1 %convert_reduce_fusion.1 = f32[96]{0:T(128)S(1)} fusion(bf16[1,96,6,128]{3,1,2,0:T(8,128)(2,1)} %param.12, f32[96]{0:T(128)} %param.21), kind=kLoop, calls=%fused_computation.168 | loop fusion | flops 368544 | bytes 148224 | tf_op jit(solution)/shard_map/reduce_sum | solution.py:129
  2.6 4.5 %collective-permute-start.1 = (bf16[1,96,6,128]{3,1,2,0:T(8,128)(2,1)}, bf16[1,96,6,128]{3,1,2,0:T(8,128)(2,1)S(1)}, u32[]{:S(2)}, u32[]{:S(2)}) collective-permute-start(bf16[1,96,6,128]{3,1,2,0:T(8,128)(2,1)} %param.11), channel_id=1, source_target_pairs={{0,4},{4,0},{8,12},{12,8},{16,20},{20,16},{24,28},{28,24},{1,5},{5... | collective-permute-start | bytes 442376 | tf_op jit(solution)/shard_map/ppermute | solution.py:19
  7.1 2.4 %convolution_bitcast_fusion = f32[1,384,6,128]{1,3,2,0:T(8,128)} fusion(bf16[384,96]{0,1:T(8,128)(2,1)} %param.19, bf16[1,96,6,128]{3,1,2,0:T(8,128)(2,1)} %param.12, f32[96]{0:T(128)} %param.21), kind=kOutput, calls=%fused_computation.46 | convolution fusion | flops 56844288 | bytes 1401216 | tf_op jit(solution)/shard_map/scrw,fc->sfrw/dot_general | solution.py:131
  9.5 0.2 copy.51
  9.8 0.1 pad.41.clone
  10.0 0.1 reshape.216
  10.2 0.5 copy-done.4
  10.7 1.5 %fusion.20 = f32[6,8,17,96]{3,1,2,0:T(8,128)S(1)} fusion(bf16[96,12,1,7,6]{0,3,4,1,2:T(8,128)(2,1)S(1)} %slice.271, bf16[96,12,1,8,17]{0,3,4,1,2:T(8,128)(2,1)S(1)} %copy.31, f32[96]{0:T(128)S(1)} %copy-done.9, pred[8,17]{0,1:T(8,128)(4,1)S(1)} %copy-done.11, f32[96,1,7,7]{0,3,2,1:T(8,128)S(1)} %bitcast.192), kind=kOutput, calls=%fused_computation.77 | convolution fusion | flops 47490048 | bytes 742792 | tf_op jit(solution)/shard_map/conv_general_dilated | solution.py:135
  12.5 0.2 copy.50
  12.7 0.3 copy-done.5
  13.1 2.1 %convert_reduce_fusion = (f32[384]{0:T(512)S(1)}, bf16[1,384,6,128]{1,3,2,0:T(8,128)(2,1)S(1)}, f32[384,6,128]{0,2,1:T(8,128)S(1)}) fusion(f32[1,384,6,128]{1,3,2,0:T(8,128)} %convolution_bitcast_fusion, f32[384]{0:T(512)S(1)} %copy-done.8, bf16[96,384]{1,0:T(8,128)(2,1)S(1)} %copy-done, f32[6,1,128,96]{2,3,0,1:T(8,128)S(1)} %copy.50, f32[96]{0:T(128)S(1)} %copy-done.7, ...), kind=kOutput, calls=%fused_computation.70 | convolution fusion | flops 60825216 | bytes 3327744 | tf_op jit(solution)/shard_map/scrw,cf->sfrw/dot_general | solution.py:151
  15.2 0.4 fusion.43
  15.8 1.1 %multiply_reduce_fusion = (f32[96]{0:T(128)S(1)}, f32[96]{0:T(128)S(1)}, f32[96]{0:T(128)S(1)}, f32[96]{0:T(128)S(1)}, f32[96]{0:T(128)S(1)}, /*index=5*/f32[96]...) fusion(bf16[1,96,12,128]{3,1,2,0:T(8,128)(2,1)S(1)} %pad_maximu, ...), kind=kLoop, calls=%fused_computation.117 | loop fusion | flops 4495680 | bytes 1645824 | tf_op jit(solution)/shard_map/reduce_sum | solution.py:184
  16.9 0.8 %multiply_reduce_fusion.36 = (f32[96]{0:T(128)S(1)}, f32[96]{0:T(128)S(1)}, f32[96]{0:T(128)S(1)}, f32[96]{0:T(128)S(1)}, f32[96]{0:T(128)S(1)}, /*index=5*/f32[...) fusion(f32[1,96,6,128]{3,1,2,0:T(8,128)S(1)} %get-tuple-element, ...), kind=kLoop, calls=%fused_computation.153 | loop fusion | flops 2947776 | bytes 890112 | tf_op jit(solution)/shard_map/reduce_sum | solution.py:184
  17.7 1.1 %multiply_reduce_fusion.18 = (f32[96]{0:T(128)S(1)}, f32[96]{0:T(128)S(1)}, f32[96]{0:T(128)S(1)}, f32[96]{0:T(128)S(1)}, f32[96]{0:T(128)S(1)}, /*index=5*/f32[...) fusion(f32[1,96,6,128]{3,1,2,0:T(8,128)S(1)} %get-tuple-element, ...), kind=kLoop, calls=%fused_computation.135 | loop fusion | flops 3979584 | bytes 891648 | tf_op jit(solution)/shard_map/reduce_sum | solution.py:184
  18.8 0.3 fusion.22
  19.1 0.1 stack.199
  19.6 2.6 %fusion.10 = bf16[384,6,128]{0,2,1:T(8,128)(2,1)S(1)} fusion(f32[384,6,128]{0,2,1:T(8,128)S(1)} %get-tuple-element.106), kind=kLoop, calls=%fused_computation.56 | loop fusion | flops 19169280 | bytes 1769472 | tf_op jit(solution)/shard_map/convert_element_type | solution.py:154
  22.2 0.3 fusion.23
  22.6 0.4 fusion.21
  23.3 1.3 %collective-permute-done.2 = f32[2,168,128]{2,1,0:T(8,128)S(1)} collective-permute-done((f32[2,168,128]{2,1,0:T(8,128)S(1)}, f32[2,168,128]{2,1,0:T(8,128)S(1)}, u32[]{:S(2)}, u32[]{:S(2)}) %collective-permute-start.2) | collective-permute-done | bytes 172064 | tf_op jit(solution)/shard_map/ppermute | solution.py:74
  24.7 1.6 %collective-permute-start.3 = (f32[1,168,128]{2,1,0:T(8,128)S(1)}, f32[1,168,128]{2,1,0:T(8,128)S(1)}, u32[]{:S(2)}, u32[]{:S(2)}) collective-permute-start(f32[1,168,128]{2,1,0:T(8,128)S(1)} %constant_dynamic-slice_fusion), channel_id=1, source_target_pairs={{0,8},{4,12},{8,0},{12,4},{16,24},{20,28},{24,16},{28,20},{1,9},{5... | collective-permute-start | bytes 258056 | tf_op jit(solution)/shard_map/ppermute | solution.py:74
  26.3 0.9 %collective-permute-start.8 = (f32[1,96,3,128]{3,1,2,0:T(8,128)S(1)}, f32[1,96,3,128]{3,1,2,0:T(8,128)S(1)}, u32[]{:S(2)}, u32[]{:S(2)}) collective-permute-start(f32[1,96,3,128]{3,1,2,0:T(8,128)S(1)} %get-tuple-element.100), channel_id=1, source_target_pairs={{4,8},{12,16},{20,24},{8,4},{16,12},{24,20},{5,9},{13,17},{21,25},... | collective-permute-start | bytes 442376 | tf_op jit(solution)/shard_map/ppermute | solution.py:33
  27.2 1.9 %collective-permute-start.9 = (f32[1,96,3,128]{3,1,2,0:T(8,128)S(1)}, f32[1,96,3,128]{3,1,2,0:T(8,128)S(1)}, u32[]{:S(2)}, u32[]{:S(2)}) collective-permute-start(f32[1,96,3,128]{3,1,2,0:T(8,128)S(1)} %get-tuple-element.101), channel_id=1, source_target_pairs={{0,4},{4,0},{8,12},{12,8},{16,20},{20,16},{24,28},{28,24},{1,5},{5... | collective-permute-start | bytes 442376 | tf_op jit(solution)/shard_map/ppermute | solution.py:32
  29.1 0.2 collective-permute-done.3
  29.3 2.5 %collective-permute-start.6 = (f32[1,168,128]{2,1,0:T(8,128)S(1)}, f32[1,168,128]{2,1,0:T(8,128)S(1)}, u32[]{:S(2)}, u32[]{:S(2)}) collective-permute-start(f32[1,168,128]{2,1,0:T(8,128)S(1)} %dynamic-slice_add_fusion.1), channel_id=1, source_target_pairs={{0,3},{1,2},{2,1},{3,0},{4,7},{5,6},{6,5},{7,4},{8,11},{9,10},{10,... | collective-permute-start | bytes 258056 | tf_op jit(solution)/shard_map/ppermute | solution.py:80
  31.8 0.5 collective-permute-start.5
  32.4 0.5 %collective-permute-start.4 = (f32[1,168,128]{2,1,0:T(8,128)S(1)}, f32[1,168,128]{2,1,0:T(8,128)S(1)}, u32[]{:S(2)}, u32[]{:S(2)}) collective-permute-start(f32[1,168,128]{2,1,0:T(8,128)S(1)} %dynamic-slice_add_fusion.1), channel_id=1, source_target_pairs={{0,1},{1,0},{2,3},{3,2},{4,5},{5,4},{6,7},{7,6},{8,9},{9,8},{10,11... | collective-permute-start | bytes 258056 | tf_op jit(solution)/shard_map/ppermute | solution.py:80
  32.9 1.9 %collective-permute-done.6 = f32[1,168,128]{2,1,0:T(8,128)S(1)} collective-permute-done((f32[1,168,128]{2,1,0:T(8,128)S(1)}, f32[1,168,128]{2,1,0:T(8,128)S(1)}, u32[]{:S(2)}, u32[]{:S(2)}) %collective-permute-start.6) | collective-permute-done | bytes 86048 | tf_op jit(solution)/shard_map/ppermute | solution.py:80
  34.9 1.8 %collective-permute-done.5 = f32[1,168,128]{2,1,0:T(8,128)S(1)} collective-permute-done((f32[1,168,128]{2,1,0:T(8,128)S(1)}, f32[1,168,128]{2,1,0:T(8,128)S(1)}, u32[]{:S(2)}, u32[]{:S(2)}) %collective-permute-start.5) | collective-permute-done | bytes 86048 | tf_op jit(solution)/shard_map/ppermute | solution.py:80
  36.6 0.2 collective-permute-done.4
  36.9 2.7 %collective-permute-start.7 = (f32[1,168,128]{2,1,0:T(8,128)S(1)}, f32[1,168,128]{2,1,0:T(8,128)S(1)}, u32[]{:S(2)}, u32[]{:S(2)}) collective-permute-start(f32[1,168,128]{2,1,0:T(8,128)S(1)} %add_add_fusion), channel_id=1, source_target_pairs={{0,16},{4,20},{8,24},{12,28},{16,0},{20,4},{24,8},{28,12},{1,17},{... | collective-permute-start | bytes 258056 | tf_op jit(solution)/shard_map/ppermute | solution.py:80
  39.6 4.4 %collective-permute-done.7 = f32[1,168,128]{2,1,0:T(8,128)S(1)} collective-permute-done((f32[1,168,128]{2,1,0:T(8,128)S(1)}, f32[1,168,128]{2,1,0:T(8,128)S(1)}, u32[]{:S(2)}, u32[]{:S(2)}) %collective-permute-start.7) | collective-permute-done | bytes 86048 | tf_op jit(solution)/shard_map/ppermute | solution.py:80
  44.0 0.5 collective-permute-start.10
  44.4 0.5 copy.52
  44.9 0.6 %pad.43.clone = f32[96,12,1,136]{0,2,3,1:T(1,128)S(1)} pad(f32[96,12,1,128]{0,2,3,1:T(1,128)S(1)} %copy.52, f32[]{:T(128)} %constant.112.clone.1), padding=0_0x0_0x0_0x3_5 | pad | bytes 1216516 | tf_op jit(solution)/shard_map/optimization_barrier | solution.py:83
  45.6 1.5 %convolution_select_fusion.1 = f32[6,8,17,96]{3,1,2,0:T(8,128)S(1)} fusion(f32[96,12,1,7,6]{0,3,4,1,2:T(8,128)S(1)} %slice.275, f32[96,12,1,8,17]{0,3,4,1,2:T(8,128)S(1)} %copy.42, pred[8,17]{0,1:T(8,128)(4,1)S(1)} %copy-done.11, f32[96,1,7,7]{0,3,2,1:T(8,128)S(1)} %bitcast.193), kind=kOutput, calls=%fused_computation.78 | convolution fusion | flops 46775808 | bytes 1152520 | tf_op jit(solution)/shard_map/conv_general_dilated | solution.py:169
  47.2 0.2 copy.39
  47.5 1.0 %collective-permute-done.10 = f32[1,168,128]{2,1,0:T(8,128)S(1)} collective-permute-done((f32[1,168,128]{2,1,0:T(8,128)S(1)}, f32[1,168,128]{2,1,0:T(8,128)S(1)}, u32[]{:S(2)}, u32[]{:S(2)}) %collective-permute-start.10) | collective-permute-done | bytes 86048 | tf_op jit(solution)/shard_map/ppermute | solution.py:90
  48.6 0.8 %copy.45 = bf16[1,96,6,128]{3,1,2,0:T(8,128)(2,1)} copy(bf16[1,96,6,128]{1,3,2,0:T(8,128)(2,1)S(1)} %fusion.41) | data formatting | bytes 294912
  49.4 0.6 %collective-permute-done.11 = f32[2,168,128]{2,1,0:T(8,128)S(1)} collective-permute-done((f32[2,168,128]{2,1,0:T(8,128)S(1)}, f32[2,168,128]{2,1,0:T(8,128)S(1)}, u32[]{:S(2)}, u32[]{:S(2)}) %collective-permute-start.11) | collective-permute-done | bytes 172064 | tf_op jit(solution)/shard_map/ppermute | solution.py:90
  50.1 0.3 slice.252
  50.4 0.5 fusion.70
  50.9 0.6 %slice.282 = f32[384]{0:T(512)} slice(f32[86016]{0:T(1024)S(1)} %bitcast.187), slice={[45056:45440]} | slice | bytes 3072 | tf_op jit(solution)/shard_map/slice | solution.py:98
  51.6 0.6 %slice_bitcast_fusion.2 = f32[96,7,7]{0,2,1:T(8,128)} fusion(f32[128,7,96]{2,1,0:T(8,128)S(1)} %slice.252), kind=kLoop, calls=%fused_computation.194 | loop fusion | bytes 37632 | tf_op jit(solution)/shard_map/transpose | solution.py:201
  52.2 0.7 %reshape.213 = f32[96,384]{1,0:T(8,128)} reshape(f32[36864]{0:T(1024)S(1)} %slice.281) | data formatting | bytes 294912 | tf_op jit(solution)/shard_map/reshape | solution.py:98
  52.9 0.7 %slice_bitcast_fusion.1 = f32[384,96]{0,1:T(8,128)} fusion(f32[224,384]{1,0:T(8,128)S(1)} %slice.259), kind=kLoop, calls=%fused_computation.175 | loop fusion | bytes 294912 | tf_op jit(solution)/shard_map/transpose | solution.py:202
  (83 shorter events, 1.8 us)
Async XLA Ops:
  0.6 12.1 %copy-start = (bf16[96,384]{1,0:T(8,128)(2,1)S(1)}, bf16[96,384]{1,0:T(8,128)(2,1)}, u32[]{:S(2)}) copy-start(bf16[96,384]{1,0:T(8,128)(2,1)} %param.17) | copy-start | bytes 221188
  0.7 8.8 %copy-start.2 = (bf16[1,96,6,128]{3,1,2,0:T(8,128)(2,1)S(1)}, bf16[1,96,6,128]{3,1,2,0:T(8,128)(2,1)}, u32[]{:S(2)}) copy-start(bf16[1,96,6,128]{3,1,2,0:T(8,128)(2,1)} %param.11) | copy-start | bytes 442372
  0.7 8.8 %collective-permute-start = (bf16[1,96,6,128]{3,1,2,0:T(8,128)(2,1)}, bf16[1,96,6,128]{3,1,2,0:T(8,128)(2,1)S(1)}, u32[]{:S(2)}, u32[]{:S(2)}) collective-permute-start(bf16[1,96,6,128]{3,1,2,0:T(8,128)(2,1)} %param.11), channel_id=1, source_target_pairs={{4,8},{12,16},{20,24},{8,4},{16,12},{24,20},{5,9},{13,17},{21,25},... | collective-permute-start | bytes 442376 | tf_op jit(solution)/shard_map/ppermute | solution.py:15
  2.6 6.9 %collective-permute-start.1 = (bf16[1,96,6,128]{3,1,2,0:T(8,128)(2,1)}, bf16[1,96,6,128]{3,1,2,0:T(8,128)(2,1)S(1)}, u32[]{:S(2)}, u32[]{:S(2)}) collective-permute-start(bf16[1,96,6,128]{3,1,2,0:T(8,128)(2,1)} %param.11), channel_id=1, source_target_pairs={{0,4},{4,0},{8,12},{12,8},{16,20},{20,16},{24,28},{28,24},{1,5},{5... | collective-permute-start | bytes 442376 | tf_op jit(solution)/shard_map/ppermute | solution.py:19
  9.9 0.8 %copy-start.4 = (f32[96,7,7]{0,2,1:T(8,128)S(1)}, f32[96,7,7]{0,2,1:T(8,128)}, u32[]{:S(2)}) copy-start(f32[96,7,7]{0,2,1:T(8,128)} %param.13) | copy-start | bytes 56452
  9.9 0.7 %copy-start.9 = (f32[96]{0:T(128)S(1)}, f32[96]{0:T(128)}, u32[]{:S(2)}) copy-start(f32[96]{0:T(128)} %param.14) | copy-start | bytes 1156
  10.0 0.7 %copy-start.11 = (pred[8,17]{0,1:T(8,128)(4,1)S(1)}, pred[8,17]{0,1:T(8,128)(4,1)}, u32[]{:S(2)}) copy-start(pred[8,17]{0,1:T(8,128)(4,1)} %constant.178) | copy-start | bytes 412
  12.4 0.7 %copy-start.5 = (f32[96]{0:T(128)S(1)}, f32[96]{0:T(128)}, u32[]{:S(2)}) copy-start(f32[96]{0:T(128)} %param.15) | copy-start | bytes 1156
  12.4 0.7 %copy-start.7 = (f32[96]{0:T(128)S(1)}, f32[96]{0:T(128)}, u32[]{:S(2)}) copy-start(f32[96]{0:T(128)} %param.16) | copy-start | bytes 1156
  12.4 0.7 %copy-start.8 = (f32[384]{0:T(512)S(1)}, f32[384]{0:T(512)}, u32[]{:S(2)}) copy-start(f32[384]{0:T(512)} %param.18) | copy-start | bytes 4612
  19.4 2.8 %copy-start.1 = (bf16[1,96,6,128]{3,1,2,0:T(8,128)(2,1)S(1)}, bf16[1,96,6,128]{3,1,2,0:T(8,128)(2,1)}, u32[]{:S(2)}) copy-start(bf16[1,96,6,128]{3,1,2,0:T(8,128)(2,1)} %param.12) | copy-start | bytes 442372
  19.4 2.8 %copy-start.6 = (f32[96]{0:T(128)S(1)}, f32[96]{0:T(128)}, u32[]{:S(2)}) copy-start(f32[96]{0:T(128)} %param.21) | copy-start | bytes 1156
  19.6 3.0 %copy-start.3 = (bf16[384,96]{0,1:T(8,128)(2,1)S(1)}, bf16[384,96]{0,1:T(8,128)(2,1)}, u32[]{:S(2)}) copy-start(bf16[384,96]{0,1:T(8,128)(2,1)} %param.19) | copy-start | bytes 221188
  19.6 3.0 %copy-start.10 = (f32[96]{0:T(128)S(1)}, f32[96]{0:T(128)}, u32[]{:S(2)}) copy-start(f32[96]{0:T(128)} %param.20) | copy-start | bytes 1156
  23.2 1.5 %collective-permute-start.2 = (f32[2,168,128]{2,1,0:T(8,128)S(1)}, f32[2,168,128]{2,1,0:T(8,128)S(1)}, u32[]{:S(2)}, u32[]{:S(2)}) collective-permute-start(f32[2,168,128]{2,1,0:T(8,128)S(1)} %constant_dynamic-slice_fusion.1), channel_id=1, source_target_pairs={{0,4},{4,0},{8,12},{12,8},{16,20},{20,16},{24,28},{28,24},{1,5},{5... | collective-permute-start | bytes 516104 | tf_op jit(solution)/shard_map/ppermute | solution.py:74
  24.7 4.6 %collective-permute-start.3 = (f32[1,168,128]{2,1,0:T(8,128)S(1)}, f32[1,168,128]{2,1,0:T(8,128)S(1)}, u32[]{:S(2)}, u32[]{:S(2)}) collective-permute-start(f32[1,168,128]{2,1,0:T(8,128)S(1)} %constant_dynamic-slice_fusion), channel_id=1, source_target_pairs={{0,8},{4,12},{8,0},{12,4},{16,24},{20,28},{24,16},{28,20},{1,9},{5... | collective-permute-start | bytes 258056 | tf_op jit(solution)/shard_map/ppermute | solution.py:74
  26.3 6.5 %collective-permute-start.8 = (f32[1,96,3,128]{3,1,2,0:T(8,128)S(1)}, f32[1,96,3,128]{3,1,2,0:T(8,128)S(1)}, u32[]{:S(2)}, u32[]{:S(2)}) collective-permute-start(f32[1,96,3,128]{3,1,2,0:T(8,128)S(1)} %get-tuple-element.100), channel_id=1, source_target_pairs={{4,8},{12,16},{20,24},{8,4},{16,12},{24,20},{5,9},{13,17},{21,25},... | collective-permute-start | bytes 442376 | tf_op jit(solution)/shard_map/ppermute | solution.py:33
  27.2 5.7 %collective-permute-start.9 = (f32[1,96,3,128]{3,1,2,0:T(8,128)S(1)}, f32[1,96,3,128]{3,1,2,0:T(8,128)S(1)}, u32[]{:S(2)}, u32[]{:S(2)}) collective-permute-start(f32[1,96,3,128]{3,1,2,0:T(8,128)S(1)} %get-tuple-element.101), channel_id=1, source_target_pairs={{0,4},{4,0},{8,12},{12,8},{16,20},{20,16},{24,28},{28,24},{1,5},{5... | collective-permute-start | bytes 442376 | tf_op jit(solution)/shard_map/ppermute | solution.py:32
  29.3 5.5 %collective-permute-start.6 = (f32[1,168,128]{2,1,0:T(8,128)S(1)}, f32[1,168,128]{2,1,0:T(8,128)S(1)}, u32[]{:S(2)}, u32[]{:S(2)}) collective-permute-start(f32[1,168,128]{2,1,0:T(8,128)S(1)} %dynamic-slice_add_fusion.1), channel_id=1, source_target_pairs={{0,3},{1,2},{2,1},{3,0},{4,7},{5,6},{6,5},{7,4},{8,11},{9,10},{10,... | collective-permute-start | bytes 258056 | tf_op jit(solution)/shard_map/ppermute | solution.py:80
  31.8 4.8 %collective-permute-start.5 = (f32[1,168,128]{2,1,0:T(8,128)S(1)}, f32[1,168,128]{2,1,0:T(8,128)S(1)}, u32[]{:S(2)}, u32[]{:S(2)}) collective-permute-start(f32[1,168,128]{2,1,0:T(8,128)S(1)} %dynamic-slice_add_fusion.1), channel_id=1, source_target_pairs={{0,2},{1,3},{2,0},{3,1},{4,6},{5,7},{6,4},{7,5},{8,10},{9,11},{10,... | collective-permute-start | bytes 258056 | tf_op jit(solution)/shard_map/ppermute | solution.py:80
  32.4 4.5 %collective-permute-start.4 = (f32[1,168,128]{2,1,0:T(8,128)S(1)}, f32[1,168,128]{2,1,0:T(8,128)S(1)}, u32[]{:S(2)}, u32[]{:S(2)}) collective-permute-start(f32[1,168,128]{2,1,0:T(8,128)S(1)} %dynamic-slice_add_fusion.1), channel_id=1, source_target_pairs={{0,1},{1,0},{2,3},{3,2},{4,5},{5,4},{6,7},{7,6},{8,9},{9,8},{10,11... | collective-permute-start | bytes 258056 | tf_op jit(solution)/shard_map/ppermute | solution.py:80
  36.9 7.1 %collective-permute-start.7 = (f32[1,168,128]{2,1,0:T(8,128)S(1)}, f32[1,168,128]{2,1,0:T(8,128)S(1)}, u32[]{:S(2)}, u32[]{:S(2)}) collective-permute-start(f32[1,168,128]{2,1,0:T(8,128)S(1)} %add_add_fusion), channel_id=1, source_target_pairs={{0,16},{4,20},{8,24},{12,28},{16,0},{20,4},{24,8},{28,12},{1,17},{... | collective-permute-start | bytes 258056 | tf_op jit(solution)/shard_map/ppermute | solution.py:80
  44.0 4.6 %collective-permute-start.10 = (f32[1,168,128]{2,1,0:T(8,128)S(1)}, f32[1,168,128]{2,1,0:T(8,128)S(1)}, u32[]{:S(2)}, u32[]{:S(2)}) collective-permute-start(f32[1,168,128]{2,1,0:T(8,128)S(1)} %add.155), channel_id=1, source_target_pairs={{0,8},{4,12},{8,0},{12,4},{16,24},{20,28},{24,16},{28,20},{1,9},{5... | collective-permute-start | bytes 258056 | tf_op jit(solution)/shard_map/ppermute | solution.py:90
  48.6 1.5 %collective-permute-start.11 = (f32[2,168,128]{2,1,0:T(8,128)S(1)}, f32[2,168,128]{2,1,0:T(8,128)S(1)}, u32[]{:S(2)}, u32[]{:S(2)}) collective-permute-start(f32[2,168,128]{2,1,0:T(8,128)S(1)} %pad_maximum_fusion.3), channel_id=1, source_target_pairs={{0,4},{4,0},{8,12},{12,8},{16,20},{20,16},{24,28},{28,24},{1,5},{5... | collective-permute-start | bytes 516104 | tf_op jit(solution)/shard_map/ppermute | solution.py:90
